TPU v7x, 32 devices: a whole 2x2x4 slice. The times are simulated.
32 devices in a mesh: tm: 8 (over y, x, core), src: 4 (over z).
Axes of the slice: x: 2, y: 2, z: 4, core: 2. Of those that a mesh axis runs over, the one named last changes fastest.
Arguments:
- observed_residual: float32 [12, 262144], P(None, ('tm', 'src')), may hold values from -6 to 6
- source_partials: float32 [5, 262144], P(None, ('tm', 'src')), may hold values from -6 to 6
- spread_derivative_table: float32 [12, 62], replicated, may hold values from -6 to 6
- detector_index: int32 [262144], P(('tm', 'src')), may hold values from 0 to 61
- first_knot_interval: int32 [262144], P(('tm', 'src')), may hold values from 0 to 1023
- interval_fraction: float32 [262144], P(('tm', 'src')), may hold values from 0 to 1
- live_slot_count: int32 [32, 32], P(('tm', 'src')), may hold values from 64 to 256, as said below
- slot_owned_source: int32 [32, 8192], P(('tm', 'src')), may hold values from 0 to 32767
Outputs:
- source_update: float32 [5, 1048576], P(None, ('tm', 'src'))
- attitude_update: float32 [8192], P('tm')
- residual: float32 [12, 262144], P(None, ('tm', 'src'))
Inputs may be any that keep to these rules, and one draw needn't show every extreme that they name: live_slot_count[d, o] counts the live slots among the 256 that device d holds for owner o; one owner, drawn from the seed, has 256 live slots from every device.
All inputs are finite; a program needn't handle non-finite values.
Results may differ from a plain program's by a relative error of at most 0.00011.
Values sent between devices are 32-bit elements; how exact they have to be, the bound alone decides.
No kernel may reach another device: no remote copies, remote signals or barrier semaphores. Data moves between devices by JAX's collectives and lax.ppermute only.
A program may use at most 64 MiB of HBM per device.

v0:
```python
import jax
import jax.numpy as jnp
from jax import lax
from jax.experimental import pallas as pl
from jax.experimental.pallas import tpu as pltpu
from jax.sharding import PartitionSpec as P

SRC_DEV = 32768
KN = 1024
ITERS = 2
HI = 256
CHUNK = 512


def passed_along(block, axis, distance):
    devices = range(lax.axis_size(axis))
    route = [(i - distance, i) for i in devices if i - distance in devices]
    return lax.ppermute(block, axis, route)


def spline_basis(frac):
    u2 = frac * frac
    u3 = u2 * frac
    one = 1.0 - frac
    return [
        one * one * one / 6.0,
        (3.0 * u3 - 6.0 * u2 + 4.0) / 6.0,
        (-3.0 * u3 + 3.0 * u2 + 3.0 * frac + 1.0) / 6.0,
        u3 / 6.0,
    ]


def pieces(x):
    h = x.astype(jnp.bfloat16)
    r = x - h.astype(jnp.float32)
    m = r.astype(jnp.bfloat16)
    l = (r - m.astype(jnp.float32)).astype(jnp.bfloat16)
    return h, m, l


def hot_rows(ids, width):
    low = jnp.bitwise_and(ids, HI - 1)
    return (lax.broadcasted_iota(jnp.int32, (HI, width), 0) == low).astype(jnp.bfloat16)


def group_mask(ids, rows, width, groups):
    high = lax.shift_right_logical(ids, 8)
    iota = lax.broadcasted_iota(jnp.int32, (rows, width), 0)
    return (iota % groups) == high


def chunks(total, body):
    def step(i, carry):
        body(pl.multiple_of(i * CHUNK, CHUNK))
        return carry

    lax.fori_loop(0, total // CHUNK, step, 0)


def split_into(src_ref, big_ref):
    rows = src_ref.shape[0]
    for k, part in enumerate(pieces(src_ref[...])):
        big_ref[k * rows:(k + 1) * rows, :] = part


def source_gather(table, ids):
    n, width = table.shape
    cols = width // HI
    rows = n * cols
    total = ids.shape[1]

    def kernel(tab_ref, ids_ref, out_ref, big_ref):
        split_into(tab_ref, big_ref)

        def body(off):
            idc = ids_ref[:, pl.ds(off, CHUNK)]
            picked = jnp.dot(big_ref[...], hot_rows(idc, CHUNK), preferred_element_type=jnp.float32)
            sel = group_mask(idc, cols, CHUNK, cols)
            for p in range(n):
                acc = (
                    picked[p * cols:(p + 1) * cols]
                    + picked[rows + p * cols:rows + (p + 1) * cols]
                ) + picked[2 * rows + p * cols:2 * rows + (p + 1) * cols]
                out_ref[pl.ds(p, 1), pl.ds(off, CHUNK)] = jnp.sum(
                    jnp.where(sel, acc, 0.0), axis=0, keepdims=True
                )

        chunks(total, body)

    return pl.pallas_call(
        kernel,
        out_shape=jax.ShapeDtypeStruct((n, total), jnp.float32),
        scratch_shapes=[pltpu.VMEM((3 * rows, HI), jnp.bfloat16)],
    )(table.reshape(rows, HI), ids)


def source_scatter(values, ids, width):
    n, total = values.shape
    cols = width // HI
    rows = n * cols

    def kernel(val_ref, ids_ref, out_ref):
        out_ref[...] = jnp.zeros(out_ref.shape, jnp.float32)

        def body(off):
            idc = ids_ref[:, pl.ds(off, CHUNK)]
            v = val_ref[:, pl.ds(off, CHUNK)]
            sel = group_mask(idc, cols, CHUNK, cols)
            parts = []
            for piece in pieces(v):
                for p in range(n):
                    parts.append(jnp.where(sel, piece[p:p + 1, :], jnp.zeros((), jnp.bfloat16)))
            spread = jnp.concatenate(parts, axis=0)
            res = lax.dot_general(
                spread, hot_rows(idc, CHUNK), (((1,), (1,)), ((), ())),
                preferred_element_type=jnp.float32,
            )
            out_ref[...] += (res[:rows] + res[rows:2 * rows]) + res[2 * rows:]

        chunks(total, body)

    out = pl.pallas_call(
        kernel, out_shape=jax.ShapeDtypeStruct((rows, HI), jnp.float32)
    )(values, ids)
    return out.reshape(n, width)


def knot_gather(extended, first_ids, basis16, knots):
    total = first_ids.shape[1]
    cols = knots // HI
    shifted = jnp.stack([extended[q:q + knots] for q in range(4)], axis=0)
    rows = 4 * cols

    def kernel(tab_ref, ids_ref, basis_ref, out_ref, big_ref):
        split_into(tab_ref, big_ref)

        def body(off):
            idc = ids_ref[:, pl.ds(off, CHUNK)]
            picked = jnp.dot(big_ref[...], hot_rows(idc, CHUNK), preferred_element_type=jnp.float32)
            acc = (picked[:rows] + picked[rows:2 * rows]) + picked[2 * rows:]
            sel = group_mask(idc, rows, CHUNK, cols)
            weight = jnp.where(sel, basis_ref[:, pl.ds(off, CHUNK)], 0.0)
            out_ref[:, pl.ds(off, CHUNK)] = jnp.sum(acc * weight, axis=0, keepdims=True)

        chunks(total, body)

    return pl.pallas_call(
        kernel,
        out_shape=jax.ShapeDtypeStruct((1, total), jnp.float32),
        scratch_shapes=[pltpu.VMEM((3 * rows, HI), jnp.bfloat16)],
    )(shifted.reshape(rows, HI), first_ids, basis16)


def knot_scatter(values, first_ids, basis16, knots):
    total = first_ids.shape[1]
    cols = knots // HI
    rows = 4 * cols

    def kernel(val_ref, ids_ref, basis_ref, out_ref):
        out_ref[...] = jnp.zeros(out_ref.shape, jnp.float32)

        def body(off):
            idc = ids_ref[:, pl.ds(off, CHUNK)]
            sel = group_mask(idc, rows, CHUNK, cols)
            v = jnp.where(sel, basis_ref[:, pl.ds(off, CHUNK)] * val_ref[:, pl.ds(off, CHUNK)], 0.0)
            spread = jnp.concatenate(pieces(v), axis=0)
            res = lax.dot_general(
                spread, hot_rows(idc, CHUNK), (((1,), (1,)), ((), ())),
                preferred_element_type=jnp.float32,
            )
            out_ref[...] += (res[:rows] + res[rows:2 * rows]) + res[2 * rows:]

        chunks(total, body)

    out = pl.pallas_call(
        kernel, out_shape=jax.ShapeDtypeStruct((rows, HI), jnp.float32)
    )(values, first_ids, basis16)
    per_shift = out.reshape(4, knots)
    grad = jnp.zeros((knots + 3,), jnp.float32)
    for q in range(4):
        grad = grad.at[q:q + knots].add(per_shift[q])
    return grad


def per_device(
    observed_residual,
    source_partials,
    spread_derivative_table,
    detector_index,
    first_knot_interval,
    interval_fraction,
    live_slot_count,
    slot_owned_source,
):
    rows = observed_residual.shape[1]
    n_time = lax.axis_size("tm")
    n_share = lax.axis_size("src")
    n_ranks = n_time * n_share
    capacity = rows // n_ranks
    n_params = source_partials.shape[0]
    detector_count = spread_derivative_table.shape[1]
    knots = KN
    owned = SRC_DEV
    place = jnp.arange(capacity, dtype=jnp.int32)[None, :]
    live = (place < live_slot_count[0][:, None]).astype(jnp.float32).reshape(rows)
    indicator = (
        detector_index[None, :] == jnp.arange(detector_count, dtype=jnp.int32)[:, None]
    ).astype(jnp.float32)
    weight_factor = jnp.dot(
        spread_derivative_table,
        indicator,
        precision=lax.Precision.HIGHEST,
        preferred_element_type=jnp.float32,
    )
    basis16 = jnp.repeat(jnp.stack(spline_basis(interval_fraction), axis=0), knots // HI, axis=0)
    first_ids = first_knot_interval.reshape(1, rows)
    ids = slot_owned_source[0].reshape(1, rows)
    held = lax.all_to_all(source_partials, ("tm", "src"), split_axis=1, concat_axis=1, tiled=True)

    def adjoint(resid):
        zbar = live * jnp.sum(weight_factor * resid, axis=0)
        returned = held * lax.all_to_all(zbar, ("tm", "src"), split_axis=0, concat_axis=0, tiled=True)[None, :]
        grad_s = source_scatter(returned, ids, owned)
        grad_a = knot_scatter(zbar.reshape(1, rows), first_ids, basis16, knots)
        grad_a = lax.psum(grad_a, "src")
        carried = passed_along(grad_a[knots:], "tm", 1)
        return (grad_s, grad_a[:knots].at[:3].add(carried))

    def local_inner(s_one, a_one, s_two, a_two):
        return jnp.sum(s_one * s_two) + jnp.sum(a_one * a_two) / n_share

    def total(value):
        return lax.psum(value, ("tm", "src"))

    sol_s = jnp.zeros((n_params, owned), jnp.float32)
    sol_a = jnp.zeros((knots,), jnp.float32)
    resid = observed_residual
    grad_s, grad_a = adjoint(resid)
    dir_s, dir_a = (grad_s, grad_a)
    gamma = total(local_inner(grad_s, grad_a, grad_s, grad_a))
    for step in range(ITERS):
        pulled = source_gather(dir_s, ids)
        column = jnp.sum(held * pulled, axis=0)
        zsrc = lax.all_to_all(column, ("tm", "src"), split_axis=0, concat_axis=0, tiled=True)
        rim = passed_along(dir_a[:3], "tm", -1)
        extended = jnp.concatenate([dir_a, rim])
        zatt = knot_gather(extended, first_ids, basis16, knots).reshape(rows)
        shift_total = (zsrc + zatt) * live
        image = weight_factor * shift_total[None, :]
        alpha = gamma / total(jnp.sum(image * image))
        sol_s = sol_s + alpha * dir_s
        sol_a = sol_a + alpha * dir_a
        resid = resid - alpha * image
        if step + 1 < ITERS:
            grad_s, grad_a = adjoint(resid)
            fresh = total(local_inner(grad_s, grad_a, grad_s, grad_a))
            dir_s = grad_s + fresh / gamma * dir_s
            dir_a = grad_a + fresh / gamma * dir_a
            gamma = fresh
    return (sol_s, sol_a, resid)


def solution(mesh):
    placed = (
        P(None, ("tm", "src")),
        P(None, ("tm", "src")),
        P(),
        P(("tm", "src")),
        P(("tm", "src")),
        P(("tm", "src")),
        P(("tm", "src"), None),
        P(("tm", "src"), None),
    )
    return jax.shard_map(
        per_device,
        mesh=mesh,
        in_specs=placed,
        out_specs=(P(None, ("tm", "src")), P("tm"), P(None, ("tm", "src"))),
        check_vma=False,
    )
```

profile of v0, /device:TPU:0, one launch (start us, length us, event | category | flops | bytes accessed | tf_op | source)
XLA Modules:
  0.0 292.5 jit_solution(6622164723703070566)
XLA Ops:
  0.6 0.7 fusion.11
  1.4 0.8 fusion.8
  2.3 0.1 pad_maximum_fusion
  2.4 0.1 broadcast_in_dim.2
  2.5 1.0 reshape.405.basis_ref
  3.5 0.8 multiply_reduce_fusion.5
  4.4 0.7 broadcast_select_fusion.1.val_ref
  5.0 5.5 %shard_map.104 = f32[16,256]{1,0:T(8,128)} custom-call(f32[1,8192]{1,0:T(1,128)} %broadcast_select_fusion.1.val_ref, s32[1,8192]{1,0:T(1,128)} %bitcast.65, f32[16,8192]{1,0:T(8,128)} %reshape.405.basis_ref), custom_call_target="tpu_custom_call" | custom-call | tf_op jit(solution)/shard_map/pallas_call | solution.py:175
  10.5 0.8 slice_bitcast_fusion.4
  11.3 0.1 add_dynamic-update-slice_fusion.1
  11.4 0.1 fusion.20
  11.6 0.1 fusion.19
  11.7 13.7 %psum.42 = f32[1027]{0:T(1024)S(1)} all-reduce(f32[1027]{0:T(1024)S(1)} %fusion.19), channel_id=1, replica_groups=mesh['tm'=8,'src'=4] {'src'}, use_global_device_ids=true, to_apply=%region_2.0 | all-reduce | flops 1027 | bytes 8216 | tf_op jit(solution)/shard_map/psum | solution.py:225
  25.4 1.3 collective-permute-start
  26.8 0.7 copy.11
  27.5 3.7 %all-to-all-start.1 = ((f32[32,256,1]{1,2,0:T(1,128)}), f32[32,256,1]{1,2,0:T(1,128)S(1)}, u32[]{:S(2)}, u32[]{:S(2)}) async-start(f32[32,256,1]{1,2,0:T(1,128)} %copy.11), calls=%async_computation.1 | async-start | bytes 65536 | tf_op jit(solution)/shard_map/all_to_all | solution.py:222
  31.3 1.3 collective-permute-start.1
  32.6 6.0 %all-to-all-done.1 = f32[32,256,1]{1,2,0:T(1,128)S(1)} async-done(((f32[32,256,1]{1,2,0:T(1,128)}), f32[32,256,1]{1,2,0:T(1,128)S(1)}, u32[]{:S(2)}, u32[]{:S(2)}) %all-to-all-start.1) | async-done | bytes 32800 | tf_op jit(solution)/shard_map/all_to_all | solution.py:222
  38.5 2.6 all-to-all-start
  41.1 0.6 fusion.16
  41.7 0.6 reshape.409.tab_ref
  42.4 4.7 %shard_map.106 = f32[1,8192]{1,0:T(1,128)} custom-call(f32[16,256]{1,0:T(8,128)} %reshape.409.tab_ref, s32[1,8192]{1,0:T(1,128)} %bitcast.66, f32[16,8192]{1,0:T(8,128)} %reshape.405.basis_ref), custom_call_target="tpu_custom_call" | custom-call | tf_op jit(solution)/shard_map/pallas_call | solution.py:147
  47.7 3.6 %all-to-all-done = f32[5,32,256]{2,0,1:T(8,128)S(1)} async-done(((f32[5,32,256]{2,0,1:T(8,128)}), f32[5,32,256]{2,0,1:T(8,128)S(1)}, u32[]{:S(2)}, u32[]{:S(2)}) %all-to-all-start) | async-done | bytes 163872 | tf_op jit(solution)/shard_map/all_to_all | solution.py:218
  51.3 0.7 broadcast_multiply_fusion.1.val_ref
  52.0 13.6 %shard_map.103.tab_ref = f32[640,256]{1,0:T(8,128)} custom-call(f32[5,8192]{1,0:T(8,128)} %broadcast_multiply_fusion.1.val_ref, s32[1,8192]{1,0:T(1,128)} %ids_ref.7), custom_call_target="tpu_custom_call" | custom-call | tf_op jit(solution)/shard_map/pallas_call | solution.py:122
  65.7 13.1 %shard_map.105 = f32[5,8192]{1,0:T(8,128)} custom-call(f32[640,256]{1,0:T(8,128)} %shard_map.103.tab_ref, s32[1,8192]{1,0:T(1,128)} %ids_ref.7), custom_call_target="tpu_custom_call" | custom-call | tf_op jit(solution)/shard_map/pallas_call | solution.py:90
  78.7 1.6 multiply_reduce_fusion.7
  80.4 2.7 all-to-all-start.2
  83.1 0.8 multiply_reduce_fusion.1
  84.5 5.9 %all-to-all-done.2 = f32[32,256,1]{1,2,0:T(1,128)S(1)} async-done(((f32[32,256,1]{1,2,0:T(1,128)}), f32[32,256,1]{1,2,0:T(1,128)S(1)}, u32[]{:S(2)}, u32[]{:S(2)}) %all-to-all-start.2) | async-done | bytes 32800 | tf_op jit(solution)/shard_map/all_to_all | solution.py:244
  90.4 0.7 multiply_reduce_fusion.4
  91.2 38.3 %all-reduce.2 = (f32[]{:T(128)}, f32[]{:T(128)}) all-reduce(f32[]{:T(128)S(6)} %add.142, f32[]{:T(128)} %multiply_reduce_fusion.4), channel_id=1, replica_groups=mesh['tm'=8,'src'=4] {'tm','src'}, use_global_device_ids=true, to_apply=%region_4.0 | all-reduce | flops 2 | bytes 16 | tf_op jit(solution)/shard_map/psum | solution.py:233
  130.8 0.2 multiply_reduce_fusion.3
  131.0 0.7 broadcast_select_fusion.val_ref
  131.6 5.5 %shard_map.108 = f32[16,256]{1,0:T(8,128)} custom-call(f32[1,8192]{1,0:T(1,128)} %broadcast_select_fusion.val_ref, s32[1,8192]{1,0:T(1,128)} %bitcast.67, f32[16,8192]{1,0:T(8,128)} %reshape.405.basis_ref), custom_call_target="tpu_custom_call" | custom-call | tf_op jit(solution)/shard_map/pallas_call | solution.py:175
  137.1 0.8 slice_bitcast_fusion
  137.9 0.1 add_dynamic-update-slice_fusion
  138.1 0.1 fusion.18
  138.2 0.1 fusion.17
  138.4 10.1 %psum.45 = f32[1027]{0:T(1024)S(1)} all-reduce(f32[1027]{0:T(1024)S(1)} %fusion.17), channel_id=1, replica_groups=mesh['tm'=8,'src'=4] {'src'}, use_global_device_ids=true, to_apply=%region_10.0 | all-reduce | flops 1027 | bytes 8216 | tf_op jit(solution)/shard_map/psum | solution.py:225
  148.6 1.3 collective-permute-start.2
  149.9 0.7 copy.12
  150.6 4.7 %all-to-all-start.3 = ((f32[32,256,1]{1,2,0:T(1,128)}), f32[32,256,1]{1,2,0:T(1,128)S(1)}, u32[]{:S(2)}, u32[]{:S(2)}) async-start(f32[32,256,1]{1,2,0:T(1,128)} %copy.12), calls=%async_computation.3 | async-start | bytes 65536 | tf_op jit(solution)/shard_map/all_to_all | solution.py:222
  155.3 0.6 multiply_reduce_fusion.8
  156.6 6.0 %all-to-all-done.3 = f32[32,256,1]{1,2,0:T(1,128)S(1)} async-done(((f32[32,256,1]{1,2,0:T(1,128)}), f32[32,256,1]{1,2,0:T(1,128)S(1)}, u32[]{:S(2)}, u32[]{:S(2)}) %all-to-all-start.3) | async-done | bytes 32800 | tf_op jit(solution)/shard_map/all_to_all | solution.py:222
  162.6 0.7 broadcast_multiply_fusion.val_ref
  163.3 13.6 %shard_map.107 = f32[640,256]{1,0:T(8,128)} custom-call(f32[5,8192]{1,0:T(8,128)} %broadcast_multiply_fusion.val_ref, s32[1,8192]{1,0:T(1,128)} %ids_ref.7), custom_call_target="tpu_custom_call" | custom-call | tf_op jit(solution)/shard_map/pallas_call | solution.py:122
  176.9 1.9 multiply_reduce_fusion
  179.5 38.1 %psum.46 = f32[]{:T(128)} all-reduce(f32[]{:T(128)S(6)} %add.149), channel_id=1, replica_groups=mesh['tm'=8,'src'=4] {'tm','src'}, use_global_device_ids=true, to_apply=%region_12.0 | all-reduce | flops 1 | bytes 8 | tf_op jit(solution)/shard_map/psum | solution.py:233
  219.0 0.9 multiply_add_fusion.1.tab_ref
  219.9 1.3 collective-permute-start.3
  221.2 13.0 %shard_map.109 = f32[5,8192]{1,0:T(8,128)} custom-call(f32[640,256]{1,0:T(8,128)} %multiply_add_fusion.1.tab_ref, s32[1,8192]{1,0:T(1,128)} %ids_ref.7), custom_call_target="tpu_custom_call" | custom-call | tf_op jit(solution)/shard_map/pallas_call | solution.py:90
  234.2 1.7 multiply_reduce_fusion.6
  235.9 4.8 %all-to-all-start.4 = ((f32[32,256,1]{1,2,0:T(1,128)}), f32[32,256,1]{1,2,0:T(1,128)S(1)}, u32[]{:S(2)}, u32[]{:S(2)}) async-start(f32[32,256,1]{1,2,0:T(1,128)} %bitcast.20), calls=%async_computation.4 | async-start | bytes 65536 | tf_op jit(solution)/shard_map/all_to_all | solution.py:244
  240.8 0.6 reshape.413.tab_ref
  241.4 4.7 %shard_map.110 = f32[1,8192]{1,0:T(1,128)} custom-call(f32[16,256]{1,0:T(8,128)} %reshape.413.tab_ref, s32[1,8192]{1,0:T(1,128)} %bitcast.68, f32[16,8192]{1,0:T(8,128)} %reshape.405.basis_ref), custom_call_target="tpu_custom_call" | custom-call | tf_op jit(solution)/shard_map/pallas_call | solution.py:147
  246.1 1.9 all-to-all-done.4
  248.0 0.8 add_select_fusion
  248.8 0.7 multiply_reduce_fusion.2
  249.6 38.8 %psum.47 = f32[]{:T(128)} all-reduce(f32[]{:T(128)} %multiply_reduce_fusion.2), channel_id=1, replica_groups=mesh['tm'=8,'src'=4] {'tm','src'}, use_global_device_ids=true, to_apply=%region_15.0 | all-reduce | flops 1 | bytes 8 | tf_op jit(solution)/shard_map/psum | solution.py:233
  289.7 0.1 multiply_add_fusion
  289.8 0.9 multiply_subtract_fusion
  290.7 0.6 multiply_add_fusion.2
  291.3 1.2 add.154
  (47 shorter events, 0.5 us)
Async XLA Ops:
  0.6 2.9 copy-start
  1.4 2.1 copy-start.4
  1.4 2.1 copy-start.6
  3.5 23.3 %copy-start.7 = (s32[1,32]{1,0:T(1,128)S(1)}, s32[1,32]{1,0:T(1,128)}, u32[]{:S(2)}) copy-start(s32[1,32]{1,0:T(1,128)} %param.34) | copy-start | bytes 388
  25.4 5.8 %collective-permute-start = (f32[3]{0:T(128)S(1)}, f32[3]{0:T(128)S(1)}, u32[]{:S(2)}, u32[]{:S(2)}) collective-permute-start(f32[3]{0:T(128)S(1)} %slice.237), channel_id=1, source_target_pairs={{0,4},{4,8},{8,12},{12,16},{16,20},{20,24},{24,28},{1,5},{5,9},{9,... | collective-permute-start | bytes 44 | tf_op jit(solution)/shard_map/ppermute | solution.py:18
  27.5 11.0 %all-to-all-start.1 = ((f32[32,256,1]{1,2,0:T(1,128)}), f32[32,256,1]{1,2,0:T(1,128)S(1)}, u32[]{:S(2)}, u32[]{:S(2)}) async-start(f32[32,256,1]{1,2,0:T(1,128)} %copy.11), calls=%async_computation.1 | async-start | bytes 65536 | tf_op jit(solution)/shard_map/all_to_all | solution.py:222
  31.3 9.9 %collective-permute-start.1 = (f32[3]{0:T(128)S(1)}, f32[3]{0:T(128)S(1)}, u32[]{:S(2)}, u32[]{:S(2)}) collective-permute-start(f32[3]{0:T(128)S(1)} %get-tuple-element.126), channel_id=1, source_target_pairs={{4,0},{8,4},{12,8},{16,12},{20,16},{24,20},{28,24},{5,1},{9,5},{13... | collective-permute-start | bytes 44 | tf_op jit(solution)/shard_map/ppermute | solution.py:18
  38.5 12.8 %all-to-all-start = ((f32[5,32,256]{2,0,1:T(8,128)}), f32[5,32,256]{2,0,1:T(8,128)S(1)}, u32[]{:S(2)}, u32[]{:S(2)}) async-start(f32[5,32,256]{2,0,1:T(8,128)} %bitcast), calls=%async_computation | async-start | bytes 524288 | tf_op jit(solution)/shard_map/all_to_all | solution.py:218
  65.7 17.4 %copy-start.1 = (f32[640,256]{1,0:T(8,128)S(1)}, f32[640,256]{1,0:T(8,128)}, u32[]{:S(2)}) copy-start(f32[640,256]{1,0:T(8,128)} %shard_map.103.tab_ref) | copy-start | bytes 1966084
  65.7 24.7 %copy-start.5 = (f32[1,8192]{1,0:T(1,128)S(1)}, f32[1,8192]{1,0:T(1,128)}, u32[]{:S(2)}) copy-start(f32[1,8192]{1,0:T(1,128)} %shard_map.106) | copy-start | bytes 98308
  80.4 10.0 %all-to-all-start.2 = ((f32[32,256,1]{1,2,0:T(1,128)}), f32[32,256,1]{1,2,0:T(1,128)S(1)}, u32[]{:S(2)}, u32[]{:S(2)}) async-start(f32[32,256,1]{1,2,0:T(1,128)} %bitcast.11), calls=%async_computation.2 | async-start | bytes 65536 | tf_op jit(solution)/shard_map/all_to_all | solution.py:244
  148.6 6.7 %collective-permute-start.2 = (f32[3]{0:T(128)S(1)}, f32[3]{0:T(128)S(1)}, u32[]{:S(2)}, u32[]{:S(2)}) collective-permute-start(f32[3]{0:T(128)S(1)} %slice.250), channel_id=1, source_target_pairs={{0,4},{4,8},{8,12},{12,16},{16,20},{20,24},{24,28},{1,5},{5,9},{9,... | collective-permute-start | bytes 44 | tf_op jit(solution)/shard_map/ppermute | solution.py:18
  150.6 12.0 %all-to-all-start.3 = ((f32[32,256,1]{1,2,0:T(1,128)}), f32[32,256,1]{1,2,0:T(1,128)S(1)}, u32[]{:S(2)}, u32[]{:S(2)}) async-start(f32[32,256,1]{1,2,0:T(1,128)} %copy.12), calls=%async_computation.3 | async-start | bytes 65536 | tf_op jit(solution)/shard_map/all_to_all | solution.py:222
  176.9 42.0 %copy-start.3 = (f32[640,256]{1,0:T(8,128)S(1)}, f32[640,256]{1,0:T(8,128)}, u32[]{:S(2)}) copy-start(f32[640,256]{1,0:T(8,128)} %shard_map.107) | copy-start | bytes 1966084
  219.9 20.8 %collective-permute-start.3 = (f32[3]{0:T(128)S(1)}, f32[3]{0:T(128)S(1)}, u32[]{:S(2)}, u32[]{:S(2)}) collective-permute-start(f32[3]{0:T(128)S(1)} %slice.225), channel_id=1, source_target_pairs={{4,0},{8,4},{12,8},{16,12},{20,16},{24,20},{28,24},{5,1},{9,5},{13... | collective-permute-start | bytes 44 | tf_op jit(solution)/shard_map/ppermute | solution.py:18
  234.2 55.5 %copy-start.2 = (f32[640,256]{1,0:T(8,128)S(1)}, f32[640,256]{1,0:T(8,128)}, u32[]{:S(2)}) copy-start(f32[640,256]{1,0:T(8,128)} %multiply_add_fusion.1.tab_ref) | copy-start | bytes 1966084
  235.9 12.1 %all-to-all-start.4 = ((f32[32,256,1]{1,2,0:T(1,128)}), f32[32,256,1]{1,2,0:T(1,128)S(1)}, u32[]{:S(2)}, u32[]{:S(2)}) async-start(f32[32,256,1]{1,2,0:T(1,128)} %bitcast.20), calls=%async_computation.4 | async-start | bytes 65536 | tf_op jit(solution)/shard_map/all_to_all | solution.py:244
where the time goes:
time: 294 us; the launch traced here: 292 us
  blocking collectives  139 us (47%)
  Pallas kernels  73.5 us (25%)
  starting transfers between devices  23.6 us (8%)
  waiting for transfers between devices  23.4 us (8%)
  other arithmetic  18 us (6%)
  between operations  7.6 us (3%)
  local copies, waits for them, and re-layouts  6.49 us (2%)
    psum x3, blocking collectives, total(): return lax.psum(value, ('tm', 'src'))  115 us
    pallas_call x2, Pallas kernels, source_scatter(): pl.pallas_call(kernel, out_shape=jax.ShapeDtypeStruct((rows, HI), jnp.flo...  27.2 us
    pallas_call x2, Pallas kernels, source_gather(): pl.pallas_call(kernel, out_shape=jax.ShapeDtypeStruct((n, total), jnp.flo...  26.1 us
    psum x2, blocking collectives, adjoint(): grad_a = lax.psum(grad_a, 'src')  23.8 us
    all_to_all x2, waiting for transfers between devices, adjoint(): lax.all_to_all(zbar, ('tm', 'src'), split_axis=0, concat_axis=0, tiled=True)  12 us
    pallas_call x2, Pallas kernels, knot_scatter(): pl.pallas_call(kernel, out_shape=jax.ShapeDtypeStruct((rows, HI), jnp.flo...  10.9 us
    pallas_call x2, Pallas kernels, knot_gather(): pl.pallas_call(kernel, out_shape=jax.ShapeDtypeStruct((1, total), jnp.flo...  9.3 us
    all_to_all x2, starting transfers between devices, adjoint(): lax.all_to_all(zbar, ('tm', 'src'), split_axis=0, concat_axis=0, tiled=True)  8.42 us
  transfers between devices with their start and end apart: 9, of which 5 were waited for; matrix products, arithmetic and copies ran while one was open for 2% of the time, Pallas kernels for 8%

commit v1 on v0

--- a/solution.py
+++ b/solution.py
@@ -125,7 +125,7 @@
     return out.reshape(n, width)
 
 
-def knot_gather(extended, first_ids, basis16, knots):
+def knot_gather(extended, first_ids, basis, knots):
     total = first_ids.shape[1]
     cols = knots // HI
     shifted = jnp.stack([extended[q:q + knots] for q in range(4)], axis=0)
@@ -138,9 +138,13 @@
             idc = ids_ref[:, pl.ds(off, CHUNK)]
             picked = jnp.dot(big_ref[...], hot_rows(idc, CHUNK), preferred_element_type=jnp.float32)
             acc = (picked[:rows] + picked[rows:2 * rows]) + picked[2 * rows:]
-            sel = group_mask(idc, rows, CHUNK, cols)
-            weight = jnp.where(sel, basis_ref[:, pl.ds(off, CHUNK)], 0.0)
-            out_ref[:, pl.ds(off, CHUNK)] = jnp.sum(acc * weight, axis=0, keepdims=True)
+            sel = group_mask(idc, cols, CHUNK, cols)
+            b = basis_ref[:, pl.ds(off, CHUNK)]
+            z = jnp.zeros((1, CHUNK), jnp.float32)
+            for q in range(4):
+                value = jnp.sum(jnp.where(sel, acc[q * cols:(q + 1) * cols], 0.0), axis=0, keepdims=True)
+                z = z + b[q:q + 1] * value
+            out_ref[:, pl.ds(off, CHUNK)] = z
 
         chunks(total, body)
 
@@ -148,7 +152,7 @@
         kernel,
         out_shape=jax.ShapeDtypeStruct((1, total), jnp.float32),
         scratch_shapes=[pltpu.VMEM((3 * rows, HI), jnp.bfloat16)],
-    )(shifted.reshape(rows, HI), first_ids, basis16)
+    )(shifted.reshape(rows, HI), first_ids, basis)
 
 
 def knot_scatter(values, first_ids, basis16, knots):
@@ -200,7 +204,9 @@
     n_params = source_partials.shape[0]
     detector_count = spread_derivative_table.shape[1]
     knots = KN
+    n_knots = n_time * knots
     owned = SRC_DEV
+    everyone = ("tm", "src")
     place = jnp.arange(capacity, dtype=jnp.int32)[None, :]
     live = (place < live_slot_count[0][:, None]).astype(jnp.float32).reshape(rows)
     indicator = (
@@ -212,52 +218,79 @@
         precision=lax.Precision.HIGHEST,
         preferred_element_type=jnp.float32,
     )
+    weight_sq = jnp.sum(weight_factor * weight_factor, axis=0)
     basis16 = jnp.repeat(jnp.stack(spline_basis(interval_fraction), axis=0), knots // HI, axis=0)
     first_ids = first_knot_interval.reshape(1, rows)
     ids = slot_owned_source[0].reshape(1, rows)
-    held = lax.all_to_all(source_partials, ("tm", "src"), split_axis=1, concat_axis=1, tiled=True)
-
-    def adjoint(resid):
-        zbar = live * jnp.sum(weight_factor * resid, axis=0)
-        returned = held * lax.all_to_all(zbar, ("tm", "src"), split_axis=0, concat_axis=0, tiled=True)[None, :]
-        grad_s = source_scatter(returned, ids, owned)
-        grad_a = knot_scatter(zbar.reshape(1, rows), first_ids, basis16, knots)
-        grad_a = lax.psum(grad_a, "src")
-        carried = passed_along(grad_a[knots:], "tm", 1)
-        return (grad_s, grad_a[:knots].at[:3].add(carried))
-
-    def local_inner(s_one, a_one, s_two, a_two):
-        return jnp.sum(s_one * s_two) + jnp.sum(a_one * a_two) / n_share
-
-    def total(value):
-        return lax.psum(value, ("tm", "src"))
+    zbar0 = live * jnp.sum(weight_factor * observed_residual, axis=0)
+
+    packed = jnp.concatenate(
+        [
+            source_partials,
+            zbar0[None],
+            weight_sq[None],
+            live[None],
+            interval_fraction[None],
+            first_knot_interval.astype(jnp.float32)[None],
+        ],
+        axis=0,
+    )
+    got = lax.all_to_all(packed, everyone, split_axis=1, concat_axis=1, tiled=True)
+    held = got[:n_params]
+    zbar0_own = got[n_params]
+    weight_sq_own = got[n_params + 1]
+    live_own = got[n_params + 2]
+    basis_own = jnp.stack(spline_basis(got[n_params + 3]), axis=0)
+    slot_device = jnp.arange(rows, dtype=jnp.int32) // capacity
+    base_own = ((slot_device // n_share) * knots + got[n_params + 4].astype(jnp.int32)).reshape(1, rows)
+
+    def adjoint(zbar_own, zbar_slot):
+        grad_s = source_scatter(held * zbar_own[None, :], ids, owned)
+        part_a = knot_scatter(zbar_slot.reshape(1, rows), first_ids, basis16, knots)
+        mine = jnp.concatenate([part_a, jnp.sum(grad_s * grad_s)[None]])
+        every = lax.all_to_all(
+            jnp.broadcast_to(mine[None, :], (n_ranks, knots + 4)), everyone, 0, 0, tiled=True
+        )
+        block = jnp.sum(every[:, :knots + 3].reshape(n_time, n_share, knots + 3), axis=1)
+        main = block[:, :knots].at[1:, :3].add(block[:-1, knots:])
+        grad_a = main.reshape(n_knots)
+        norm = jnp.sum(every[:, knots + 3]) + jnp.sum(grad_a * grad_a)
+        return grad_s, grad_a, norm
+
+    def forward(dir_s, dir_a):
+        pulled = source_gather(dir_s, ids)
+        zsrc = jnp.sum(held * pulled, axis=0)
+        extended = jnp.concatenate([dir_a, jnp.zeros((3,), jnp.float32)])
+        zatt = knot_gather(extended, base_own, basis_own, n_knots).reshape(rows)
+        shift_own = (zsrc + zatt) * live_own
+        partial = jnp.sum(weight_sq_own * shift_own * shift_own)
+        payload = jnp.concatenate(
+            [shift_own.reshape(n_ranks, capacity), jnp.broadcast_to(partial, (n_ranks, 1))], axis=1
+        )
+        back = lax.all_to_all(payload, everyone, 0, 0, tiled=True)
+        return shift_own, back[:, :capacity].reshape(rows), jnp.sum(back[:, capacity])
 
     sol_s = jnp.zeros((n_params, owned), jnp.float32)
-    sol_a = jnp.zeros((knots,), jnp.float32)
+    sol_a = jnp.zeros((n_knots,), jnp.float32)
     resid = observed_residual
-    grad_s, grad_a = adjoint(resid)
+    zbar_own, zbar_slot = zbar0_own, zbar0
+    grad_s, grad_a, gamma = adjoint(zbar_own, zbar_slot)
     dir_s, dir_a = (grad_s, grad_a)
-    gamma = total(local_inner(grad_s, grad_a, grad_s, grad_a))
     for step in range(ITERS):
-        pulled = source_gather(dir_s, ids)
-        column = jnp.sum(held * pulled, axis=0)
-        zsrc = lax.all_to_all(column, ("tm", "src"), split_axis=0, concat_axis=0, tiled=True)
-        rim = passed_along(dir_a[:3], "tm", -1)
-        extended = jnp.concatenate([dir_a, rim])
-        zatt = knot_gather(extended, first_ids, basis16, knots).reshape(rows)
-        shift_total = (zsrc + zatt) * live
-        image = weight_factor * shift_total[None, :]
-        alpha = gamma / total(jnp.sum(image * image))
+        shift_own, shift_slot, image_sq = forward(dir_s, dir_a)
+        alpha = gamma / image_sq
         sol_s = sol_s + alpha * dir_s
         sol_a = sol_a + alpha * dir_a
-        resid = resid - alpha * image
+        resid = resid - alpha * (weight_factor * shift_slot[None, :])
         if step + 1 < ITERS:
-            grad_s, grad_a = adjoint(resid)
-            fresh = total(local_inner(grad_s, grad_a, grad_s, grad_a))
+            zbar_own = zbar_own - alpha * (weight_sq_own * shift_own)
+            zbar_slot = zbar_slot - alpha * (weight_sq * shift_slot)
+            grad_s, grad_a, fresh = adjoint(zbar_own, zbar_slot)
             dir_s = grad_s + fresh / gamma * dir_s
             dir_a = grad_a + fresh / gamma * dir_a
             gamma = fresh
-    return (sol_s, sol_a, resid)
+    mine_a = lax.dynamic_slice(sol_a, (lax.axis_index("tm") * knots,), (knots,))
+    return (sol_s, mine_a, resid)
 
 
 def solution(mesh):

time: 294 us -> 173 us (0.59)
  blocking collectives: 139 us -> 10.3 us
  other arithmetic: 18 us -> 26.6 us
  local copies, waits for them, and re-layouts: 6.49 us -> 12.4 us
  waiting for transfers between devices: 23.4 us -> 18.4 us
  starting transfers between devices: 23.6 us -> 19.8 us
  Pallas kernels: 73.5 us -> 76.7 us
    psum x5 -> x0, blocking collectives: 139 us -> none  [the longest x3 115 us: total(): return lax.psum(value, ('tm', 'src'))]
    all_to_all x0 -> x1, blocking collectives: none -> 10.3 us  [adjoint(): lax.all_to_all(jnp.broadcast_to(mine[None, :], (n_ranks, knots + 4)), eve...]
    ppermute x4 -> x0, starting transfers between devices: 5.15 us -> none  [passed_along(): return lax.ppermute(block, axis, route)]
    all_to_all x5 -> x4, waiting for transfers between devices: 23.4 us -> 18.4 us  [the longest x2 12.8 us: forward(): back = lax.all_to_all(payload, everyone, 0, 0, tiled=True)]
    reduce_sum x8 -> x14, other arithmetic: 8.29 us -> 12.1 us  [the longest x2 3.82 us: adjoint(): mine = jnp.concatenate([part_a, jnp.sum(grad_s * grad_s)[None]])]
    pallas_call x2, Pallas kernels: 9.3 us -> 12.4 us  [knot_gather(): pl.pallas_call(kernel, out_shape=jax.ShapeDtypeStruct((1, total), jnp.flo...]
    all_to_all x5 -> x4, starting transfers between devices: 18.5 us -> 19.8 us  [the longest x2 8.4 us: forward(): back = lax.all_to_all(payload, everyone, 0, 0, tiled=True)]
  transfers between devices with their start and end apart: 9 -> 4, of which waited for: 5 -> 3; matrix products, arithmetic and copies ran while one was open for 2% -> 3% of each run, Pallas kernels for 8% -> 11%
where the time goes in v1:
time: 173 us; the launch traced here: 171 us
  Pallas kernels  76.7 us (44%)
  other arithmetic  26.6 us (15%)
  starting transfers between devices  19.8 us (11%)
  waiting for transfers between devices  18.4 us (11%)
  local copies, waits for them, and re-layouts  12.4 us (7%)
  blocking collectives  10.3 us (6%)
  between operations  5.21 us (3%)
  matrix products  2 us (1%)
    pallas_call x2, Pallas kernels, source_scatter(): pl.pallas_call(kernel, out_shape=jax.ShapeDtypeStruct((rows, HI), jnp.flo...  27.2 us
    pallas_call x2, Pallas kernels, source_gather(): pl.pallas_call(kernel, out_shape=jax.ShapeDtypeStruct((n, total), jnp.flo...  26.1 us
    all_to_all x2, waiting for transfers between devices, forward(): back = lax.all_to_all(payload, everyone, 0, 0, tiled=True)  12.8 us
    pallas_call x2, Pallas kernels, knot_gather(): pl.pallas_call(kernel, out_shape=jax.ShapeDtypeStruct((1, total), jnp.flo...  12.4 us
    pallas_call x2, Pallas kernels, knot_scatter(): pl.pallas_call(kernel, out_shape=jax.ShapeDtypeStruct((rows, HI), jnp.flo...  10.9 us
    all_to_all x1, blocking collectives, adjoint(): lax.all_to_all(jnp.broadcast_to(mine[None, :], (n_ranks, knots + 4)), eve...  10.3 us
    all_to_all x2, starting transfers between devices, forward(): back = lax.all_to_all(payload, everyone, 0, 0, tiled=True)  8.4 us
    all_to_all x1, starting transfers between devices, per_device(): lax.all_to_all(packed, everyone, split_axis=1, concat_axis=1, tiled=True)  7.3 us
  transfers between devices with their start and end apart: 4, of which 3 were waited for; matrix products, arithmetic and copies ran while one was open for 3% of the time, Pallas kernels for 11%

profile of v1, /device:TPU:0, one launch (start us, length us, event | category | flops | bytes accessed | tf_op | source)
XLA Modules:
  0.0 171.4 jit_solution(7970515749515205525)
XLA Ops:
  0.7 0.8 compare_convert_fusion
  1.5 0.8 convert_element_type.33
  2.2 2.0 %multiply_reduce_fusion.2 = (f32[8192]{0:T(1024)S(1)}, f32[8192]{0:T(1024)S(1)}, f32[12,8192]{1,0:T(8,128)S(1)}) fusion(f32[12,8192]{1,0:T(8,128)} %param.28, f32[12,62]{1,0:T(8,128)S(1)} %copy-done, s32[8192]{0:T(1024)} %param.31), kind=kOutput, calls=%fused_computation.8 | convolution fusion | flops 74022912 | bytes 887712 | tf_op jit(solution)/shard_map/dot_general | solution.py:215
  4.4 1.7 concatenate.54
  6.0 7.3 %all-to-all-start = ((f32[10,32,256]{2,0,1:T(8,128)}), f32[10,32,256]{2,0,1:T(8,128)S(1)}, u32[]{:S(2)}, u32[]{:S(2)}) async-start(f32[10,32,256]{2,0,1:T(8,128)} %concatenate.54), calls=%async_computation | async-start | bytes 1048576 | tf_op jit(solution)/shard_map/all_to_all | solution.py:238
  13.7 1.0 reshape.711.basis_ref
  14.7 0.7 broadcast_select_fusion.val_ref
  15.4 5.5 %shard_map.103 = f32[16,256]{1,0:T(8,128)} custom-call(f32[1,8192]{1,0:T(1,128)} %broadcast_select_fusion.val_ref, s32[1,8192]{1,0:T(1,128)} %bitcast.128, f32[16,8192]{1,0:T(8,128)} %reshape.711.basis_ref), custom_call_target="tpu_custom_call" | custom-call | tf_op jit(solution)/shard_map/pallas_call | solution.py:179
  20.8 0.8 slice_bitcast_fusion.7
  21.8 0.1 fusion.18
  22.0 0.1 fusion.17
  22.1 5.6 %all-to-all-done = f32[10,32,256]{2,0,1:T(8,128)S(1)} async-done(((f32[10,32,256]{2,0,1:T(8,128)}), f32[10,32,256]{2,0,1:T(8,128)S(1)}, u32[]{:S(2)}, u32[]{:S(2)}) %all-to-all-start) | async-done | bytes 327712 | tf_op jit(solution)/shard_map/all_to_all | solution.py:238
  27.8 0.7 multiply_add_fusion.3.ids_ref
  28.5 0.2 fusion.9
  28.7 0.7 broadcast_multiply_fusion.1.val_ref
  29.4 13.6 %shard_map.104.tab_ref = f32[640,256]{1,0:T(8,128)} custom-call(f32[5,8192]{1,0:T(8,128)} %broadcast_multiply_fusion.1.val_ref, s32[1,8192]{1,0:T(1,128)} %ids_ref.7), custom_call_target="tpu_custom_call" | custom-call | tf_op jit(solution)/shard_map/pallas_call | solution.py:122
  43.0 1.9 %multiply_reduce_fusion.1 = f32[]{:T(128)} fusion(f32[640,256]{1,0:T(8,128)} %shard_map.104.tab_ref), kind=kLoop, calls=%fused_computation.6 | loop fusion | flops 327679 | bytes 655364 | tf_op jit(solution)/shard_map/reduce_sum | solution.py:250
  44.9 0.7 pad_maximum_fusion.4
  45.6 0.7 broadcast_in_dim.12
  46.3 4.1 %all-to-all-start.1 = ((f32[32,1,1028]{2,1,0:T(1,128)}), f32[32,1,1028]{2,1,0:T(1,128)S(1)}, u32[]{:S(2)}, u32[]{:S(2)}) async-start(f32[32,1,1028]{2,1,0:T(1,128)} %broadcast_in_dim.12), calls=%async_computation.1 | async-start | bytes 294912 | tf_op jit(solution)/shard_map/all_to_all | solution.py:251
  50.4 0.8 pad_maximum_fusion.2.basis_ref
  51.2 13.0 %shard_map.105 = f32[5,8192]{1,0:T(8,128)} custom-call(f32[640,256]{1,0:T(8,128)} %shard_map.104.tab_ref, s32[1,8192]{1,0:T(1,128)} %ids_ref.7), custom_call_target="tpu_custom_call" | custom-call | tf_op jit(solution)/shard_map/pallas_call | solution.py:90
  64.2 1.0 multiply_reduce_fusion.5
  65.5 0.4 scatter-add.40
  65.9 0.7 multiply_reduce_fusion.7
  66.9 0.7 reshape.717.tab_ref
  67.7 6.2 %shard_map.106 = f32[1,8192]{1,0:T(1,128)} custom-call(f32[128,256]{1,0:T(8,128)} %reshape.717.tab_ref, s32[1,8192]{1,0:T(1,128)} %multiply_add_fusion.3.ids_ref, f32[4,8192]{1,0:T(4,128)} %pad_maximum_fusion.2.basis_ref), custom_call_target="tpu_custom_call" | custom-call | tf_op jit(solution)/shard_map/pallas_call | solution.py:151
  73.9 0.5 broadcast.488
  74.4 1.5 reduce.36
  75.9 1.5 fusion.11
  77.3 0.6 pad_bitcast_fusion.1
  78.0 0.7 copy.30
  78.6 5.8 %all-to-all-start.2 = ((f32[32,1,257]{2,1,0:T(1,128)}), f32[32,1,257]{2,1,0:T(1,128)S(1)}, u32[]{:S(2)}, u32[]{:S(2)}) async-start(f32[32,1,257]{2,1,0:T(1,128)} %copy.30), calls=%async_computation.2 | async-start | bytes 98304 | tf_op jit(solution)/shard_map/all_to_all | solution.py:270
  84.5 0.7 slice_reduce_fusion.3
  86.4 5.4 %all-to-all-done.2 = f32[32,1,257]{2,1,0:T(1,128)S(1)} async-done(((f32[32,1,257]{2,1,0:T(1,128)}), f32[32,1,257]{2,1,0:T(1,128)S(1)}, u32[]{:S(2)}, u32[]{:S(2)}) %all-to-all-start.2) | async-done | bytes 32928 | tf_op jit(solution)/shard_map/all_to_all | solution.py:270
  91.9 0.6 slice_reduce_fusion.2
  93.2 0.7 multiply_subtract_fusion.1
  94.0 5.5 %shard_map.107 = f32[16,256]{1,0:T(8,128)} custom-call(f32[1,8192]{1,0:T(1,128)} %get-tuple-element.157.val_ref, s32[1,8192]{1,0:T(1,128)} %bitcast.129, f32[16,8192]{1,0:T(8,128)} %reshape.711.basis_ref), custom_call_target="tpu_custom_call" | custom-call | tf_op jit(solution)/shard_map/pallas_call | solution.py:179
  99.4 0.8 slice_bitcast_fusion.3
  100.3 0.7 broadcast_multiply_fusion.val_ref
  101.0 13.6 %shard_map.108 = f32[640,256]{1,0:T(8,128)} custom-call(f32[5,8192]{1,0:T(8,128)} %broadcast_multiply_fusion.val_ref, s32[1,8192]{1,0:T(1,128)} %ids_ref.7), custom_call_target="tpu_custom_call" | custom-call | tf_op jit(solution)/shard_map/pallas_call | solution.py:122
  114.6 2.0 %multiply_reduce_fusion = f32[]{:T(128)} fusion(f32[640,256]{1,0:T(8,128)} %shard_map.108), kind=kLoop, calls=%fused_computation.5 | loop fusion | flops 327679 | bytes 655364 | tf_op jit(solution)/shard_map/reduce_sum | solution.py:250
  116.7 0.1 fusion.16
  116.9 0.1 fusion.15
  117.0 0.7 pad_maximum_fusion.5
  117.8 10.3 %all_to_all.48 = f32[32,1,1028]{2,1,0:T(1,128)S(1)} all-to-all(f32[32,1,1028]{2,1,0:T(1,128)S(1)} %broadcast_in_dim.14), channel_id=1, replica_groups=mesh['tm'=8,'src'=4] {'tm','src'}, dimensions={0} | all-to-all | bytes 263168 | tf_op jit(solution)/shard_map/all_to_all | solution.py:251
  128.2 0.7 slice_reduce_fusion.1
  129.0 0.4 scatter-add.49
  129.5 0.6 multiply_reduce_fusion.6
  131.4 0.9 multiply_add_fusion.1.tab_ref
  132.7 0.7 reshape.727.tab_ref
  133.4 6.2 %shard_map.110 = f32[1,8192]{1,0:T(1,128)} custom-call(f32[128,256]{1,0:T(8,128)} %reshape.727.tab_ref, s32[1,8192]{1,0:T(1,128)} %multiply_add_fusion.3.ids_ref, f32[4,8192]{1,0:T(4,128)} %pad_maximum_fusion.2.basis_ref), custom_call_target="tpu_custom_call" | custom-call | tf_op jit(solution)/shard_map/pallas_call | solution.py:151
  139.6 1.5 reduce.37
  141.1 13.1 %shard_map.109 = f32[5,8192]{1,0:T(8,128)} custom-call(f32[640,256]{1,0:T(8,128)} %multiply_add_fusion.1.tab_ref, s32[1,8192]{1,0:T(1,128)} %ids_ref.7), custom_call_target="tpu_custom_call" | custom-call | tf_op jit(solution)/shard_map/pallas_call | solution.py:90
  154.2 1.0 multiply_reduce_fusion.4
  155.3 0.7 fusion.12
  156.0 0.6 pad_bitcast_fusion
  156.6 0.7 copy.34
  157.3 2.6 %all-to-all-start.4 = ((f32[32,1,257]{2,1,0:T(1,128)}), f32[32,1,257]{2,1,0:T(1,128)S(1)}, u32[]{:S(2)}, u32[]{:S(2)}) async-start(f32[32,1,257]{2,1,0:T(1,128)} %copy.34), calls=%async_computation.4 | async-start | bytes 98304 | tf_op jit(solution)/shard_map/all_to_all | solution.py:270
  159.9 7.4 %all-to-all-done.4 = f32[32,1,257]{2,1,0:T(1,128)S(1)} async-done(((f32[32,1,257]{2,1,0:T(1,128)}), f32[32,1,257]{2,1,0:T(1,128)S(1)}, u32[]{:S(2)}, u32[]{:S(2)}) %all-to-all-start.4) | async-done | bytes 32928 | tf_op jit(solution)/shard_map/all_to_all | solution.py:270
  167.3 0.6 slice_reduce_fusion
  168.7 0.6 fusion.14
  169.3 1.2 add.250
  170.5 0.9 multiply_subtract_fusion
  (77 shorter events, 2.1 us)
Async XLA Ops:
  0.6 1.6 copy-start
  0.6 3.6 %copy-start.10 = (s32[1,32]{1,0:T(1,128)S(1)}, s32[1,32]{1,0:T(1,128)}, u32[]{:S(2)}) copy-start(s32[1,32]{1,0:T(1,128)} %param.34) | copy-start | bytes 388
  0.7 3.7 %copy-start.9 = (f32[8192]{0:T(1024)S(1)}, f32[8192]{0:T(1024)}, u32[]{:S(2)}) copy-start(f32[8192]{0:T(1024)} %param.33) | copy-start | bytes 98308
  0.7 3.7 %copy-start.8 = (f32[5,8192]{1,0:T(8,128)S(1)}, f32[5,8192]{1,0:T(8,128)}, u32[]{:S(2)}) copy-start(f32[5,8192]{1,0:T(8,128)} %param.29) | copy-start | bytes 491524
  6.0 21.7 %all-to-all-start = ((f32[10,32,256]{2,0,1:T(8,128)}), f32[10,32,256]{2,0,1:T(8,128)S(1)}, u32[]{:S(2)}, u32[]{:S(2)}) async-start(f32[10,32,256]{2,0,1:T(8,128)} %concatenate.54), calls=%async_computation | async-start | bytes 1048576 | tf_op jit(solution)/shard_map/all_to_all | solution.py:238
  46.3 19.0 %all-to-all-start.1 = ((f32[32,1,1028]{2,1,0:T(1,128)}), f32[32,1,1028]{2,1,0:T(1,128)S(1)}, u32[]{:S(2)}, u32[]{:S(2)}) async-start(f32[32,1,1028]{2,1,0:T(1,128)} %broadcast_in_dim.12), calls=%async_computation.1 | async-start | bytes 294912 | tf_op jit(solution)/shard_map/all_to_all | solution.py:251
  66.7 26.6 %copy-start.6 = (f32[1,8192]{1,0:T(1,128)S(1)}, f32[1,8192]{1,0:T(1,128)}, u32[]{:S(2)}) copy-start(f32[1,8192]{1,0:T(1,128)} %broadcast_select_fusion.val_ref) | copy-start | bytes 98308
  73.9 19.4 %copy-start.5 = (f32[1,8192]{1,0:T(1,128)S(1)}, f32[1,8192]{1,0:T(1,128)}, u32[]{:S(2)}) copy-start(f32[1,8192]{1,0:T(1,128)} %shard_map.106) | copy-start | bytes 98308
  78.6 13.2 %all-to-all-start.2 = ((f32[32,1,257]{2,1,0:T(1,128)}), f32[32,1,257]{2,1,0:T(1,128)S(1)}, u32[]{:S(2)}, u32[]{:S(2)}) async-start(f32[32,1,257]{2,1,0:T(1,128)} %copy.30), calls=%async_computation.2 | async-start | bytes 98304 | tf_op jit(solution)/shard_map/all_to_all | solution.py:270
  114.6 16.8 %copy-start.1 = (f32[640,256]{1,0:T(8,128)S(1)}, f32[640,256]{1,0:T(8,128)}, u32[]{:S(2)}) copy-start(f32[640,256]{1,0:T(8,128)} %shard_map.104.tab_ref) | copy-start | bytes 1966084
  114.6 16.8 %copy-start.3 = (f32[640,256]{1,0:T(8,128)S(1)}, f32[640,256]{1,0:T(8,128)}, u32[]{:S(2)}) copy-start(f32[640,256]{1,0:T(8,128)} %shard_map.108) | copy-start | bytes 1966084
  139.6 15.7 %copy-start.7 = (f32[1,8192]{1,0:T(1,128)S(1)}, f32[1,8192]{1,0:T(1,128)}, u32[]{:S(2)}) copy-start(f32[1,8192]{1,0:T(1,128)} %shard_map.110) | copy-start | bytes 98308
  141.1 27.5 %copy-start.2 = (f32[640,256]{1,0:T(8,128)S(1)}, f32[640,256]{1,0:T(8,128)}, u32[]{:S(2)}) copy-start(f32[640,256]{1,0:T(8,128)} %multiply_add_fusion.1.tab_ref) | copy-start | bytes 1966084
  157.3 10.0 %all-to-all-start.4 = ((f32[32,1,257]{2,1,0:T(1,128)}), f32[32,1,257]{2,1,0:T(1,128)S(1)}, u32[]{:S(2)}, u32[]{:S(2)}) async-start(f32[32,1,257]{2,1,0:T(1,128)} %copy.34), calls=%async_computation.4 | async-start | bytes 98304 | tf_op jit(solution)/shard_map/all_to_all | solution.py:270
  168.7 1.8 %copy-start.4 = (f32[12,8192]{1,0:T(8,128)S(1)}, f32[12,8192]{1,0:T(8,128)}, u32[]{:S(2)}) copy-start(f32[12,8192]{1,0:T(8,128)} %param.28) | copy-start | bytes 1179652

commit v2 on v1

--- a/solution.py
+++ b/solution.py
@@ -32,10 +32,8 @@
 
 def pieces(x):
     h = x.astype(jnp.bfloat16)
-    r = x - h.astype(jnp.float32)
-    m = r.astype(jnp.bfloat16)
-    l = (r - m.astype(jnp.float32)).astype(jnp.bfloat16)
-    return h, m, l
+    m = (x - h.astype(jnp.float32)).astype(jnp.bfloat16)
+    return h, m
 
 
 def hot_rows(ids, width):
@@ -80,7 +78,7 @@
                 acc = (
                     picked[p * cols:(p + 1) * cols]
                     + picked[rows + p * cols:rows + (p + 1) * cols]
-                ) + picked[2 * rows + p * cols:2 * rows + (p + 1) * cols]
+                )
                 out_ref[pl.ds(p, 1), pl.ds(off, CHUNK)] = jnp.sum(
                     jnp.where(sel, acc, 0.0), axis=0, keepdims=True
                 )
@@ -90,7 +88,7 @@
     return pl.pallas_call(
         kernel,
         out_shape=jax.ShapeDtypeStruct((n, total), jnp.float32),
-        scratch_shapes=[pltpu.VMEM((3 * rows, HI), jnp.bfloat16)],
+        scratch_shapes=[pltpu.VMEM((2 * rows, HI), jnp.bfloat16)],
     )(table.reshape(rows, HI), ids)
 
 
@@ -115,7 +113,7 @@
                 spread, hot_rows(idc, CHUNK), (((1,), (1,)), ((), ())),
                 preferred_element_type=jnp.float32,
             )
-            out_ref[...] += (res[:rows] + res[rows:2 * rows]) + res[2 * rows:]
+            out_ref[...] += res[:rows] + res[rows:]
 
         chunks(total, body)
 
@@ -137,7 +135,7 @@
         def body(off):
             idc = ids_ref[:, pl.ds(off, CHUNK)]
             picked = jnp.dot(big_ref[...], hot_rows(idc, CHUNK), preferred_element_type=jnp.float32)
-            acc = (picked[:rows] + picked[rows:2 * rows]) + picked[2 * rows:]
+            acc = picked[:rows] + picked[rows:]
             sel = group_mask(idc, cols, CHUNK, cols)
             b = basis_ref[:, pl.ds(off, CHUNK)]
             z = jnp.zeros((1, CHUNK), jnp.float32)
@@ -151,7 +149,7 @@
     return pl.pallas_call(
         kernel,
         out_shape=jax.ShapeDtypeStruct((1, total), jnp.float32),
-        scratch_shapes=[pltpu.VMEM((3 * rows, HI), jnp.bfloat16)],
+        scratch_shapes=[pltpu.VMEM((2 * rows, HI), jnp.bfloat16)],
     )(shifted.reshape(rows, HI), first_ids, basis)
 
 
@@ -172,7 +170,7 @@
                 spread, hot_rows(idc, CHUNK), (((1,), (1,)), ((), ())),
                 preferred_element_type=jnp.float32,
             )
-            out_ref[...] += (res[:rows] + res[rows:2 * rows]) + res[2 * rows:]
+            out_ref[...] += res[:rows] + res[rows:]
 
         chunks(total, body)
 

time: 173 us -> 161 us (0.931)
  Pallas kernels: 76.7 us -> 64.4 us
    pallas_call x2, Pallas kernels: 26.1 us -> 20.6 us  [source_gather(): pl.pallas_call(kernel, out_shape=jax.ShapeDtypeStruct((n, total), jnp.flo...]
    pallas_call x2, Pallas kernels: 27.2 us -> 22 us  [source_scatter(): pl.pallas_call(kernel, out_shape=jax.ShapeDtypeStruct((rows, HI), jnp.flo...]
  transfers between devices with their start and end apart: 4 -> 4, of which waited for: 3 -> 3; matrix products, arithmetic and copies ran while one was open for 3% -> 4% of each run, Pallas kernels for 11% -> 10%
where the time goes in v2:
time: 161 us; the launch traced here: 159 us
  Pallas kernels  64.4 us (40%)
  other arithmetic  26.6 us (17%)
  starting transfers between devices  19.8 us (12%)
  waiting for transfers between devices  18.6 us (12%)
  local copies, waits for them, and re-layouts  12.4 us (8%)
  blocking collectives  10.3 us (6%)
  between operations  5.21 us (3%)
  matrix products  2 us (1%)
    pallas_call x2, Pallas kernels, source_scatter(): pl.pallas_call(kernel, out_shape=jax.ShapeDtypeStruct((rows, HI), jnp.flo...  22 us
    pallas_call x2, Pallas kernels, source_gather(): pl.pallas_call(kernel, out_shape=jax.ShapeDtypeStruct((n, total), jnp.flo...  20.6 us
    all_to_all x2, waiting for transfers between devices, forward(): back = lax.all_to_all(payload, everyone, 0, 0, tiled=True)  12.8 us
    pallas_call x2, Pallas kernels, knot_gather(): pl.pallas_call(kernel, out_shape=jax.ShapeDtypeStruct((1, total), jnp.flo...  11.3 us
    pallas_call x2, Pallas kernels, knot_scatter(): pl.pallas_call(kernel, out_shape=jax.ShapeDtypeStruct((rows, HI), jnp.flo...  10.6 us
    all_to_all x1, blocking collectives, adjoint(): lax.all_to_all(jnp.broadcast_to(mine[None, :], (n_ranks, knots + 4)), eve...  10.3 us
    all_to_all x2, starting transfers between devices, forward(): back = lax.all_to_all(payload, everyone, 0, 0, tiled=True)  8.4 us
    all_to_all x1, starting transfers between devices, per_device(): lax.all_to_all(packed, everyone, split_axis=1, concat_axis=1, tiled=True)  7.3 us
  transfers between devices with their start and end apart: 4, of which 3 were waited for; matrix products, arithmetic and copies ran while one was open for 4% of the time, Pallas kernels for 10%

profile of v2, /device:TPU:0, one launch (start us, length us, event | category | flops | bytes accessed | tf_op | source)
XLA Modules:
  0.0 159.4 jit_solution(11118889782700127477)
XLA Ops:
  0.7 0.8 compare_convert_fusion
  1.5 0.8 convert_element_type.33
  2.2 2.0 %multiply_reduce_fusion.2 = (f32[8192]{0:T(1024)S(1)}, f32[8192]{0:T(1024)S(1)}, f32[12,8192]{1,0:T(8,128)S(1)}) fusion(f32[12,8192]{1,0:T(8,128)} %param.28, f32[12,62]{1,0:T(8,128)S(1)} %copy-done, s32[8192]{0:T(1024)} %param.31), kind=kOutput, calls=%fused_computation.8 | convolution fusion | flops 74022912 | bytes 887712 | tf_op jit(solution)/shard_map/dot_general | solution.py:213
  4.4 1.7 %concatenate.54 = f32[10,32,256]{2,0,1:T(8,128)} concatenate(f32[5,32,256]{2,0,1:T(8,128)S(1)} %bitcast.140, f32[1,32,256]{2,0,1:T(1,128)S(1)} %compare_select_fusion.3, f32[1,32,256]{2,0,1:T(1,128)S(1)} %bitcast.138, f32[1,32,256]{2,0,1:T(1,128)S(1)} %compare_convert_fusion, f32[1,32,256]{2,0,1:T(1,128)S(1)} %bitcast.166, f32[1,32,256]{2,0,1:T(1,128)S(1)} %bitcast.167), dimensions={0} | concatenate | bytes 655360 | tf_op jit(solution)/shard_map/concatenate | solution.py:225
  6.0 7.3 %all-to-all-start = ((f32[10,32,256]{2,0,1:T(8,128)}), f32[10,32,256]{2,0,1:T(8,128)S(1)}, u32[]{:S(2)}, u32[]{:S(2)}) async-start(f32[10,32,256]{2,0,1:T(8,128)} %concatenate.54), calls=%async_computation | async-start | bytes 1048576 | tf_op jit(solution)/shard_map/all_to_all | solution.py:236
  13.7 1.0 reshape.711.basis_ref
  14.7 0.7 broadcast_select_fusion.val_ref
  15.4 5.3 %shard_map.103 = f32[16,256]{1,0:T(8,128)} custom-call(f32[1,8192]{1,0:T(1,128)} %broadcast_select_fusion.val_ref, s32[1,8192]{1,0:T(1,128)} %bitcast.128, f32[16,8192]{1,0:T(8,128)} %reshape.711.basis_ref), custom_call_target="tpu_custom_call" | custom-call | tf_op jit(solution)/shard_map/pallas_call | solution.py:177
  20.7 0.8 slice_bitcast_fusion.7
  21.6 0.1 fusion.18
  21.8 0.1 fusion.17
  21.9 5.8 %all-to-all-done = f32[10,32,256]{2,0,1:T(8,128)S(1)} async-done(((f32[10,32,256]{2,0,1:T(8,128)}), f32[10,32,256]{2,0,1:T(8,128)S(1)}, u32[]{:S(2)}, u32[]{:S(2)}) %all-to-all-start) | async-done | bytes 327712 | tf_op jit(solution)/shard_map/all_to_all | solution.py:236
  27.8 0.7 multiply_add_fusion.3.ids_ref
  28.5 0.2 fusion.9
  28.7 0.7 broadcast_multiply_fusion.1.val_ref
  29.4 11.0 %shard_map.104.tab_ref = f32[640,256]{1,0:T(8,128)} custom-call(f32[5,8192]{1,0:T(8,128)} %broadcast_multiply_fusion.1.val_ref, s32[1,8192]{1,0:T(1,128)} %ids_ref.7), custom_call_target="tpu_custom_call" | custom-call | tf_op jit(solution)/shard_map/pallas_call | solution.py:120
  40.4 1.9 %multiply_reduce_fusion.1 = f32[]{:T(128)} fusion(f32[640,256]{1,0:T(8,128)} %shard_map.104.tab_ref), kind=kLoop, calls=%fused_computation.6 | loop fusion | flops 327679 | bytes 655364 | tf_op jit(solution)/shard_map/reduce_sum | solution.py:248
  42.2 0.7 pad_maximum_fusion.4
  43.0 0.7 broadcast_in_dim.12
  43.7 4.1 %all-to-all-start.1 = ((f32[32,1,1028]{2,1,0:T(1,128)}), f32[32,1,1028]{2,1,0:T(1,128)S(1)}, u32[]{:S(2)}, u32[]{:S(2)}) async-start(f32[32,1,1028]{2,1,0:T(1,128)} %broadcast_in_dim.12), calls=%async_computation.1 | async-start | bytes 294912 | tf_op jit(solution)/shard_map/all_to_all | solution.py:249
  47.8 0.8 pad_maximum_fusion.2.basis_ref
  48.6 10.3 %shard_map.105 = f32[5,8192]{1,0:T(8,128)} custom-call(f32[640,256]{1,0:T(8,128)} %shard_map.104.tab_ref, s32[1,8192]{1,0:T(1,128)} %ids_ref.7), custom_call_target="tpu_custom_call" | custom-call | tf_op jit(solution)/shard_map/pallas_call | solution.py:88
  58.8 1.0 multiply_reduce_fusion.5
  60.1 0.4 scatter-add.40
  60.5 0.7 multiply_reduce_fusion.7
  61.5 0.7 reshape.717.tab_ref
  62.3 5.7 %shard_map.106 = f32[1,8192]{1,0:T(1,128)} custom-call(f32[128,256]{1,0:T(8,128)} %reshape.717.tab_ref, s32[1,8192]{1,0:T(1,128)} %multiply_add_fusion.3.ids_ref, f32[4,8192]{1,0:T(4,128)} %pad_maximum_fusion.2.basis_ref), custom_call_target="tpu_custom_call" | custom-call | tf_op jit(solution)/shard_map/pallas_call | solution.py:149
  67.9 0.5 broadcast.488
  68.4 1.5 reduce.36
  69.9 1.5 fusion.11
  71.4 0.6 pad_bitcast_fusion.1
  72.0 0.7 copy.30
  72.7 5.8 %all-to-all-start.2 = ((f32[32,1,257]{2,1,0:T(1,128)}), f32[32,1,257]{2,1,0:T(1,128)S(1)}, u32[]{:S(2)}, u32[]{:S(2)}) async-start(f32[32,1,257]{2,1,0:T(1,128)} %copy.30), calls=%async_computation.2 | async-start | bytes 98304 | tf_op jit(solution)/shard_map/all_to_all | solution.py:268
  78.5 0.7 slice_reduce_fusion.3
  80.5 5.4 %all-to-all-done.2 = f32[32,1,257]{2,1,0:T(1,128)S(1)} async-done(((f32[32,1,257]{2,1,0:T(1,128)}), f32[32,1,257]{2,1,0:T(1,128)S(1)}, u32[]{:S(2)}, u32[]{:S(2)}) %all-to-all-start.2) | async-done | bytes 32928 | tf_op jit(solution)/shard_map/all_to_all | solution.py:268
  85.9 0.6 slice_reduce_fusion.2
  87.3 0.7 multiply_subtract_fusion.1
  88.0 5.3 %shard_map.107 = f32[16,256]{1,0:T(8,128)} custom-call(f32[1,8192]{1,0:T(1,128)} %get-tuple-element.157.val_ref, s32[1,8192]{1,0:T(1,128)} %bitcast.129, f32[16,8192]{1,0:T(8,128)} %reshape.711.basis_ref), custom_call_target="tpu_custom_call" | custom-call | tf_op jit(solution)/shard_map/pallas_call | solution.py:177
  93.3 0.8 slice_bitcast_fusion.3
  94.1 0.7 broadcast_multiply_fusion.val_ref
  94.9 11.0 %shard_map.108 = f32[640,256]{1,0:T(8,128)} custom-call(f32[5,8192]{1,0:T(8,128)} %broadcast_multiply_fusion.val_ref, s32[1,8192]{1,0:T(1,128)} %ids_ref.7), custom_call_target="tpu_custom_call" | custom-call | tf_op jit(solution)/shard_map/pallas_call | solution.py:120
  105.9 2.0 %multiply_reduce_fusion = f32[]{:T(128)} fusion(f32[640,256]{1,0:T(8,128)} %shard_map.108), kind=kLoop, calls=%fused_computation.5 | loop fusion | flops 327679 | bytes 655364 | tf_op jit(solution)/shard_map/reduce_sum | solution.py:248
  108.0 0.1 fusion.16
  108.1 0.1 fusion.15
  108.3 0.7 pad_maximum_fusion.5
  109.1 10.3 %all_to_all.48 = f32[32,1,1028]{2,1,0:T(1,128)S(1)} all-to-all(f32[32,1,1028]{2,1,0:T(1,128)S(1)} %broadcast_in_dim.14), channel_id=1, replica_groups=mesh['tm'=8,'src'=4] {'tm','src'}, dimensions={0} | all-to-all | bytes 263168 | tf_op jit(solution)/shard_map/all_to_all | solution.py:249
  119.4 0.7 slice_reduce_fusion.1
  120.3 0.4 scatter-add.49
  120.7 0.6 multiply_reduce_fusion.6
  122.7 0.9 multiply_add_fusion.1.tab_ref
  123.9 0.7 reshape.727.tab_ref
  124.7 5.6 %shard_map.110 = f32[1,8192]{1,0:T(1,128)} custom-call(f32[128,256]{1,0:T(8,128)} %reshape.727.tab_ref, s32[1,8192]{1,0:T(1,128)} %multiply_add_fusion.3.ids_ref, f32[4,8192]{1,0:T(4,128)} %pad_maximum_fusion.2.basis_ref), custom_call_target="tpu_custom_call" | custom-call | tf_op jit(solution)/shard_map/pallas_call | solution.py:149
  130.3 1.5 reduce.37
  131.8 10.3 %shard_map.109 = f32[5,8192]{1,0:T(8,128)} custom-call(f32[640,256]{1,0:T(8,128)} %multiply_add_fusion.1.tab_ref, s32[1,8192]{1,0:T(1,128)} %ids_ref.7), custom_call_target="tpu_custom_call" | custom-call | tf_op jit(solution)/shard_map/pallas_call | solution.py:88
  142.2 1.0 multiply_reduce_fusion.4
  143.2 0.7 fusion.12
  143.9 0.6 pad_bitcast_fusion
  144.6 0.7 copy.34
  145.3 2.6 %all-to-all-start.4 = ((f32[32,1,257]{2,1,0:T(1,128)}), f32[32,1,257]{2,1,0:T(1,128)S(1)}, u32[]{:S(2)}, u32[]{:S(2)}) async-start(f32[32,1,257]{2,1,0:T(1,128)} %copy.34), calls=%async_computation.4 | async-start | bytes 98304 | tf_op jit(solution)/shard_map/all_to_all | solution.py:268
  147.9 7.4 %all-to-all-done.4 = f32[32,1,257]{2,1,0:T(1,128)S(1)} async-done(((f32[32,1,257]{2,1,0:T(1,128)}), f32[32,1,257]{2,1,0:T(1,128)S(1)}, u32[]{:S(2)}, u32[]{:S(2)}) %all-to-all-start.4) | async-done | bytes 32928 | tf_op jit(solution)/shard_map/all_to_all | solution.py:268
  155.2 0.6 slice_reduce_fusion
  156.7 0.6 fusion.14
  157.3 1.2 add.250
  158.5 0.9 multiply_subtract_fusion
  (77 shorter events, 2.1 us)
Async XLA Ops:
  0.6 1.6 %copy-start = (f32[12,62]{1,0:T(8,128)S(1)}, f32[12,62]{1,0:T(8,128)}, u32[]{:S(2)}) copy-start(f32[12,62]{1,0:T(8,128)} %param.30) | copy-start | bytes 8932
  0.6 3.6 %copy-start.10 = (s32[1,32]{1,0:T(1,128)S(1)}, s32[1,32]{1,0:T(1,128)}, u32[]{:S(2)}) copy-start(s32[1,32]{1,0:T(1,128)} %param.34) | copy-start | bytes 388
  0.7 3.7 %copy-start.9 = (f32[8192]{0:T(1024)S(1)}, f32[8192]{0:T(1024)}, u32[]{:S(2)}) copy-start(f32[8192]{0:T(1024)} %param.33) | copy-start | bytes 98308
  0.7 3.7 %copy-start.8 = (f32[5,8192]{1,0:T(8,128)S(1)}, f32[5,8192]{1,0:T(8,128)}, u32[]{:S(2)}) copy-start(f32[5,8192]{1,0:T(8,128)} %param.29) | copy-start | bytes 491524
  6.0 21.7 %all-to-all-start = ((f32[10,32,256]{2,0,1:T(8,128)}), f32[10,32,256]{2,0,1:T(8,128)S(1)}, u32[]{:S(2)}, u32[]{:S(2)}) async-start(f32[10,32,256]{2,0,1:T(8,128)} %concatenate.54), calls=%async_computation | async-start | bytes 1048576 | tf_op jit(solution)/shard_map/all_to_all | solution.py:236
  43.7 16.2 %all-to-all-start.1 = ((f32[32,1,1028]{2,1,0:T(1,128)}), f32[32,1,1028]{2,1,0:T(1,128)S(1)}, u32[]{:S(2)}, u32[]{:S(2)}) async-start(f32[32,1,1028]{2,1,0:T(1,128)} %broadcast_in_dim.12), calls=%async_computation.1 | async-start | bytes 294912 | tf_op jit(solution)/shard_map/all_to_all | solution.py:249
  61.3 26.0 %copy-start.6 = (f32[1,8192]{1,0:T(1,128)S(1)}, f32[1,8192]{1,0:T(1,128)}, u32[]{:S(2)}) copy-start(f32[1,8192]{1,0:T(1,128)} %broadcast_select_fusion.val_ref) | copy-start | bytes 98308
  67.9 19.4 %copy-start.5 = (f32[1,8192]{1,0:T(1,128)S(1)}, f32[1,8192]{1,0:T(1,128)}, u32[]{:S(2)}) copy-start(f32[1,8192]{1,0:T(1,128)} %shard_map.106) | copy-start | bytes 98308
  72.7 13.2 %all-to-all-start.2 = ((f32[32,1,257]{2,1,0:T(1,128)}), f32[32,1,257]{2,1,0:T(1,128)S(1)}, u32[]{:S(2)}, u32[]{:S(2)}) async-start(f32[32,1,257]{2,1,0:T(1,128)} %copy.30), calls=%async_computation.2 | async-start | bytes 98304 | tf_op jit(solution)/shard_map/all_to_all | solution.py:268
  105.9 16.8 %copy-start.1 = (f32[640,256]{1,0:T(8,128)S(1)}, f32[640,256]{1,0:T(8,128)}, u32[]{:S(2)}) copy-start(f32[640,256]{1,0:T(8,128)} %shard_map.104.tab_ref) | copy-start | bytes 1966084
  105.9 16.8 %copy-start.3 = (f32[640,256]{1,0:T(8,128)S(1)}, f32[640,256]{1,0:T(8,128)}, u32[]{:S(2)}) copy-start(f32[640,256]{1,0:T(8,128)} %shard_map.108) | copy-start | bytes 1966084
  130.3 12.9 %copy-start.7 = (f32[1,8192]{1,0:T(1,128)S(1)}, f32[1,8192]{1,0:T(1,128)}, u32[]{:S(2)}) copy-start(f32[1,8192]{1,0:T(1,128)} %shard_map.110) | copy-start | bytes 98308
  131.8 24.7 %copy-start.2 = (f32[640,256]{1,0:T(8,128)S(1)}, f32[640,256]{1,0:T(8,128)}, u32[]{:S(2)}) copy-start(f32[640,256]{1,0:T(8,128)} %multiply_add_fusion.1.tab_ref) | copy-start | bytes 1966084
  145.3 10.0 %all-to-all-start.4 = ((f32[32,1,257]{2,1,0:T(1,128)}), f32[32,1,257]{2,1,0:T(1,128)S(1)}, u32[]{:S(2)}, u32[]{:S(2)}) async-start(f32[32,1,257]{2,1,0:T(1,128)} %copy.34), calls=%async_computation.4 | async-start | bytes 98304 | tf_op jit(solution)/shard_map/all_to_all | solution.py:268
  156.6 1.8 %copy-start.4 = (f32[12,8192]{1,0:T(8,128)S(1)}, f32[12,8192]{1,0:T(8,128)}, u32[]{:S(2)}) copy-start(f32[12,8192]{1,0:T(8,128)} %param.28) | copy-start | bytes 1179652

commit v3 on v2

--- a/solution.py
+++ b/solution.py
@@ -242,9 +242,7 @@
     slot_device = jnp.arange(rows, dtype=jnp.int32) // capacity
     base_own = ((slot_device // n_share) * knots + got[n_params + 4].astype(jnp.int32)).reshape(1, rows)
 
-    def adjoint(zbar_own, zbar_slot):
-        grad_s = source_scatter(held * zbar_own[None, :], ids, owned)
-        part_a = knot_scatter(zbar_slot.reshape(1, rows), first_ids, basis16, knots)
+    def combine(part_a, grad_s):
         mine = jnp.concatenate([part_a, jnp.sum(grad_s * grad_s)[None]])
         every = lax.all_to_all(
             jnp.broadcast_to(mine[None, :], (n_ranks, knots + 4)), everyone, 0, 0, tiled=True
@@ -253,10 +251,9 @@
         main = block[:, :knots].at[1:, :3].add(block[:-1, knots:])
         grad_a = main.reshape(n_knots)
         norm = jnp.sum(every[:, knots + 3]) + jnp.sum(grad_a * grad_a)
-        return grad_s, grad_a, norm
-
-    def forward(dir_s, dir_a):
-        pulled = source_gather(dir_s, ids)
+        return grad_a, norm
+
+    def forward(pulled, dir_a):
         zsrc = jnp.sum(held * pulled, axis=0)
         extended = jnp.concatenate([dir_a, jnp.zeros((3,), jnp.float32)])
         zatt = knot_gather(extended, base_own, basis_own, n_knots).reshape(rows)
@@ -271,21 +268,29 @@
     sol_s = jnp.zeros((n_params, owned), jnp.float32)
     sol_a = jnp.zeros((n_knots,), jnp.float32)
     resid = observed_residual
-    zbar_own, zbar_slot = zbar0_own, zbar0
-    grad_s, grad_a, gamma = adjoint(zbar_own, zbar_slot)
+    zbar_slot = zbar0
+    grad_s = source_scatter(held * zbar0_own[None, :], ids, owned)
+    grad_a, gamma = combine(knot_scatter(zbar_slot.reshape(1, rows), first_ids, basis16, knots), grad_s)
     dir_s, dir_a = (grad_s, grad_a)
+    pulled = source_gather(dir_s, ids)
     for step in range(ITERS):
-        shift_own, shift_slot, image_sq = forward(dir_s, dir_a)
+        shift_own, shift_slot, image_sq = forward(pulled, dir_a)
         alpha = gamma / image_sq
         sol_s = sol_s + alpha * dir_s
         sol_a = sol_a + alpha * dir_a
         resid = resid - alpha * (weight_factor * shift_slot[None, :])
         if step + 1 < ITERS:
-            zbar_own = zbar_own - alpha * (weight_sq_own * shift_own)
+            pushed = source_scatter(held * (weight_sq_own * shift_own)[None, :], ids, owned)
             zbar_slot = zbar_slot - alpha * (weight_sq * shift_slot)
-            grad_s, grad_a, fresh = adjoint(zbar_own, zbar_slot)
-            dir_s = grad_s + fresh / gamma * dir_s
-            dir_a = grad_a + fresh / gamma * dir_a
+            grad_s = grad_s - alpha * pushed
+            grad_a, fresh = combine(
+                knot_scatter(zbar_slot.reshape(1, rows), first_ids, basis16, knots), grad_s
+            )
+            raw = source_gather(grad_s, ids)
+            beta = fresh / gamma
+            dir_s = grad_s + beta * dir_s
+            dir_a = grad_a + beta * dir_a
+            pulled = raw + beta * pulled
             gamma = fresh
     mine_a = lax.dynamic_slice(sol_a, (lax.axis_index("tm") * knots,), (knots,))
     return (sol_s, mine_a, resid)

time: 161 us -> 152 us (0.944)
  blocking collectives: 10.3 us -> 0 us
  starting transfers between devices: 19.8 us -> 28.9 us
  waiting for transfers between devices: 18.6 us -> 13.2 us
  other arithmetic: 26.6 us -> 24.5 us
    all_to_all x1 -> x0, blocking collectives: 10.3 us -> none  [adjoint(): lax.all_to_all(jnp.broadcast_to(mine[None, :], (n_ranks, knots + 4)), eve...]
    all_to_all x1 -> x2, starting transfers between devices: 4.08 us -> 9.91 us  [combine(): lax.all_to_all(jnp.broadcast_to(mine[None, :], (n_ranks, knots + 4)), eve...]
    all_to_all x2, waiting for transfers between devices: 12.8 us -> 7.37 us  [forward(): back = lax.all_to_all(payload, everyone, 0, 0, tiled=True)]
    all_to_all x2, starting transfers between devices: 8.4 us -> 11.7 us  [forward(): back = lax.all_to_all(payload, everyone, 0, 0, tiled=True)]
  transfers between devices with their start and end apart: 4 -> 5, of which waited for: 3 -> 2; matrix products, arithmetic and copies ran while one was open for 4% -> 4% of each run, Pallas kernels for 10% -> 24%
where the time goes in v3:
time: 152 us; the launch traced here: 151 us
  Pallas kernels  64.5 us (42%)
  starting transfers between devices  28.9 us (19%)
  other arithmetic  24.5 us (16%)
  waiting for transfers between devices  13.2 us (9%)
  local copies, waits for them, and re-layouts  13.1 us (9%)
  between operations  5.13 us (3%)
  matrix products  2 us (1%)
    pallas_call x2, Pallas kernels, source_scatter(): pl.pallas_call(kernel, out_shape=jax.ShapeDtypeStruct((rows, HI), jnp.flo...  22.1 us
    pallas_call x2, Pallas kernels, source_gather(): pl.pallas_call(kernel, out_shape=jax.ShapeDtypeStruct((n, total), jnp.flo...  20.5 us
    all_to_all x2, starting transfers between devices, forward(): back = lax.all_to_all(payload, everyone, 0, 0, tiled=True)  11.7 us
    pallas_call x2, Pallas kernels, knot_gather(): pl.pallas_call(kernel, out_shape=jax.ShapeDtypeStruct((1, total), jnp.flo...  11.3 us
    pallas_call x2, Pallas kernels, knot_scatter(): pl.pallas_call(kernel, out_shape=jax.ShapeDtypeStruct((rows, HI), jnp.flo...  10.6 us
    all_to_all x2, starting transfers between devices, combine(): lax.all_to_all(jnp.broadcast_to(mine[None, :], (n_ranks, knots + 4)), eve...  9.91 us
    all_to_all x2, waiting for transfers between devices, forward(): back = lax.all_to_all(payload, everyone, 0, 0, tiled=True)  7.37 us
    all_to_all x1, starting transfers between devices, per_device(): lax.all_to_all(packed, everyone, split_axis=1, concat_axis=1, tiled=True)  7.3 us
  transfers between devices with their start and end apart: 5, of which 2 were waited for; matrix products, arithmetic and copies ran while one was open for 4% of the time, Pallas kernels for 24%

profile of v3, /device:TPU:0, one launch (start us, length us, event | category | flops | bytes accessed | tf_op | source)
XLA Modules:
  0.0 151.2 jit_solution(10717714455043190817)
XLA Ops:
  0.7 0.8 compare_convert_fusion
  1.5 0.8 convert_element_type.33
  2.2 2.0 %multiply_reduce_fusion.2 = (f32[8192]{0:T(1024)S(1)}, f32[8192]{0:T(1024)S(1)}, f32[12,8192]{1,0:T(8,128)S(1)}) fusion(f32[12,8192]{1,0:T(8,128)} %param.28, f32[12,62]{1,0:T(8,128)S(1)} %copy-done, s32[8192]{0:T(1024)} %param.31), kind=kOutput, calls=%fused_computation.8 | convolution fusion | flops 74022912 | bytes 887712 | tf_op jit(solution)/shard_map/dot_general | solution.py:213
  4.4 1.7 %concatenate.54 = f32[10,32,256]{2,0,1:T(8,128)} concatenate(f32[5,32,256]{2,0,1:T(8,128)S(1)} %bitcast.137, f32[1,32,256]{2,0,1:T(1,128)S(1)} %compare_select_fusion.3, f32[1,32,256]{2,0,1:T(1,128)S(1)} %bitcast.135, f32[1,32,256]{2,0,1:T(1,128)S(1)} %compare_convert_fusion, f32[1,32,256]{2,0,1:T(1,128)S(1)} %bitcast.164, f32[1,32,256]{2,0,1:T(1,128)S(1)} %bitcast.165), dimensions={0} | concatenate | bytes 655360 | tf_op jit(solution)/shard_map/concatenate | solution.py:225
  6.0 7.3 %all-to-all-start = ((f32[10,32,256]{2,0,1:T(8,128)}), f32[10,32,256]{2,0,1:T(8,128)S(1)}, u32[]{:S(2)}, u32[]{:S(2)}) async-start(f32[10,32,256]{2,0,1:T(8,128)} %concatenate.54), calls=%async_computation | async-start | bytes 1048576 | tf_op jit(solution)/shard_map/all_to_all | solution.py:236
  13.7 1.0 reshape.713.basis_ref
  14.7 0.7 broadcast_select_fusion.val_ref
  15.4 5.3 %shard_map.103 = f32[16,256]{1,0:T(8,128)} custom-call(f32[1,8192]{1,0:T(1,128)} %broadcast_select_fusion.val_ref, s32[1,8192]{1,0:T(1,128)} %bitcast.126, f32[16,8192]{1,0:T(8,128)} %reshape.713.basis_ref), custom_call_target="tpu_custom_call" | custom-call | tf_op jit(solution)/shard_map/pallas_call | solution.py:177
  20.7 0.8 slice_bitcast_fusion.7
  21.5 0.1 add_dynamic-update-slice_fusion.1
  21.6 0.1 fusion.18
  21.8 0.1 fusion.17
  21.9 5.8 %all-to-all-done = f32[10,32,256]{2,0,1:T(8,128)S(1)} async-done(((f32[10,32,256]{2,0,1:T(8,128)}), f32[10,32,256]{2,0,1:T(8,128)S(1)}, u32[]{:S(2)}, u32[]{:S(2)}) %all-to-all-start) | async-done | bytes 327712 | tf_op jit(solution)/shard_map/all_to_all | solution.py:236
  27.8 0.7 multiply_add_fusion.2.ids_ref
  28.5 0.2 fusion.9
  28.6 0.7 broadcast_multiply_fusion.1.val_ref
  29.4 11.0 %shard_map.104.tab_ref = f32[640,256]{1,0:T(8,128)} custom-call(f32[5,8192]{1,0:T(8,128)} %broadcast_multiply_fusion.1.val_ref, s32[1,8192]{1,0:T(1,128)} %ids_ref.7), custom_call_target="tpu_custom_call" | custom-call | tf_op jit(solution)/shard_map/pallas_call | solution.py:120
  40.4 1.9 %multiply_reduce_fusion.1 = f32[]{:T(128)} fusion(f32[640,256]{1,0:T(8,128)} %shard_map.104.tab_ref), kind=kLoop, calls=%fused_computation.6 | loop fusion | flops 327679 | bytes 655364 | tf_op jit(solution)/shard_map/reduce_sum | solution.py:246
  42.2 0.7 pad_maximum_fusion.4
  43.0 0.7 broadcast_in_dim.12
  43.7 4.1 %all-to-all-start.1 = ((f32[32,1,1028]{2,1,0:T(1,128)}), f32[32,1,1028]{2,1,0:T(1,128)S(1)}, u32[]{:S(2)}, u32[]{:S(2)}) async-start(f32[32,1,1028]{2,1,0:T(1,128)} %broadcast_in_dim.12), calls=%async_computation.1 | async-start | bytes 294912 | tf_op jit(solution)/shard_map/all_to_all | solution.py:247
  47.8 0.8 pad_maximum_fusion.2.basis_ref
  48.6 10.3 %shard_map.105 = f32[5,8192]{1,0:T(8,128)} custom-call(f32[640,256]{1,0:T(8,128)} %shard_map.104.tab_ref, s32[1,8192]{1,0:T(1,128)} %ids_ref.7), custom_call_target="tpu_custom_call" | custom-call | tf_op jit(solution)/shard_map/pallas_call | solution.py:88
  58.8 1.0 multiply_reduce_fusion.5
  60.1 0.4 scatter-add.40
  60.5 0.7 multiply_reduce_fusion.7
  61.5 0.7 reshape.719.tab_ref
  62.2 5.6 %shard_map.106 = f32[1,8192]{1,0:T(1,128)} custom-call(f32[128,256]{1,0:T(8,128)} %reshape.719.tab_ref, s32[1,8192]{1,0:T(1,128)} %multiply_add_fusion.2.ids_ref, f32[4,8192]{1,0:T(4,128)} %pad_maximum_fusion.2.basis_ref), custom_call_target="tpu_custom_call" | custom-call | tf_op jit(solution)/shard_map/pallas_call | solution.py:149
  67.9 1.5 fusion.11
  69.3 0.5 broadcast.490
  69.8 1.5 %fusion.20 = (f32[8192]{0:T(1024)S(1)}, f32[1,8192]{1,0:T(1,128)S(1)}) fusion(f32[1,8192]{1,0:T(1,128)} %shard_map.106, f32[]{:T(128)} %broadcast.490, f32[1,8192]{1,0:T(1,128)S(1)} %bitcast.153, f32[1,8192]{1,0:T(1,128)S(1)} %bitcast.125, f32[1,8192]{1,0:T(1,128)S(1)} %bitcast.124), kind=kLoop, calls=%fused_computation.110 | loop fusion | flops 24576 | bytes 196612 | tf_op jit(solution)/shard_map/pallas_call | solution.py:149
  71.4 0.6 pad_bitcast_fusion.1
  72.1 0.7 copy.30
  72.7 5.8 %all-to-all-start.2 = ((f32[32,1,257]{2,1,0:T(1,128)}), f32[32,1,257]{2,1,0:T(1,128)S(1)}, u32[]{:S(2)}, u32[]{:S(2)}) async-start(f32[32,1,257]{2,1,0:T(1,128)} %copy.30), calls=%async_computation.2 | async-start | bytes 98304 | tf_op jit(solution)/shard_map/all_to_all | solution.py:265
  78.6 0.7 broadcast_multiply_fusion.val_ref
  79.3 11.1 %shard_map.108 = f32[640,256]{1,0:T(8,128)} custom-call(f32[5,8192]{1,0:T(8,128)} %broadcast_multiply_fusion.val_ref, s32[1,8192]{1,0:T(1,128)} %ids_ref.7), custom_call_target="tpu_custom_call" | custom-call | tf_op jit(solution)/shard_map/pallas_call | solution.py:120
  90.4 0.7 slice_reduce_fusion.3
  92.4 0.6 slice_reduce_fusion.2
  93.7 0.6 multiply_subtract_fusion.2.val_ref
  94.4 5.3 %shard_map.107 = f32[16,256]{1,0:T(8,128)} custom-call(f32[1,8192]{1,0:T(1,128)} %multiply_subtract_fusion.2.val_ref, s32[1,8192]{1,0:T(1,128)} %bitcast.127, f32[16,8192]{1,0:T(8,128)} %reshape.713.basis_ref), custom_call_target="tpu_custom_call" | custom-call | tf_op jit(solution)/shard_map/pallas_call | solution.py:177
  99.6 0.8 slice_bitcast_fusion.3
  100.5 1.6 %multiply_reduce_fusion = (f32[]{:T(128)}, f32[640,256]{1,0:T(8,128)}) fusion(f32[640,256]{1,0:T(8,128)S(1)} %copy-done.1, f32[640,256]{1,0:T(8,128)S(1)} %copy-done.3, f32[]{:T(128)S(6)} %div.65), kind=kLoop, calls=%fused_computation.4 | loop fusion | flops 655359 | bytes 1966088 | tf_op jit(solution)/shard_map/reduce_sum | solution.py:246
  102.1 0.1 add_dynamic-update-slice_fusion
  102.2 0.1 fusion.16
  102.4 0.1 fusion.15
  102.5 0.7 pad_maximum_fusion.5
  103.2 0.7 broadcast_in_dim.14
  103.9 5.8 %all-to-all-start.3 = ((f32[32,1,1028]{2,1,0:T(1,128)}), f32[32,1,1028]{2,1,0:T(1,128)S(1)}, u32[]{:S(2)}, u32[]{:S(2)}) async-start(f32[32,1,1028]{2,1,0:T(1,128)} %broadcast_in_dim.14), calls=%async_computation.3 | async-start | bytes 294912 | tf_op jit(solution)/shard_map/all_to_all | solution.py:247
  109.8 10.3 %shard_map.109 = f32[5,8192]{1,0:T(8,128)} custom-call(f32[640,256]{1,0:T(8,128)} %get-tuple-element.126.tab_ref, s32[1,8192]{1,0:T(1,128)} %ids_ref.7), custom_call_target="tpu_custom_call" | custom-call | tf_op jit(solution)/shard_map/pallas_call | solution.py:88
  120.1 0.7 slice_reduce_fusion.1
  120.9 0.4 scatter-add.49
  121.4 0.7 multiply_reduce_fusion.6
  123.7 0.8 reshape.729.tab_ref
  124.4 5.7 %shard_map.110 = f32[1,8192]{1,0:T(1,128)} custom-call(f32[128,256]{1,0:T(8,128)} %reshape.729.tab_ref, s32[1,8192]{1,0:T(1,128)} %multiply_add_fusion.2.ids_ref, f32[4,8192]{1,0:T(4,128)} %pad_maximum_fusion.2.basis_ref), custom_call_target="tpu_custom_call" | custom-call | tf_op jit(solution)/shard_map/pallas_call | solution.py:149
  130.1 1.5 reduce.37
  131.8 0.7 fusion.12
  132.5 0.6 pad_bitcast_fusion
  133.2 0.7 copy.34
  133.8 5.8 %all-to-all-start.4 = ((f32[32,1,257]{2,1,0:T(1,128)}), f32[32,1,257]{2,1,0:T(1,128)S(1)}, u32[]{:S(2)}, u32[]{:S(2)}) async-start(f32[32,1,257]{2,1,0:T(1,128)} %copy.34), calls=%async_computation.4 | async-start | bytes 98304 | tf_op jit(solution)/shard_map/all_to_all | solution.py:265
  139.7 7.4 %all-to-all-done.4 = f32[32,1,257]{2,1,0:T(1,128)S(1)} async-done(((f32[32,1,257]{2,1,0:T(1,128)}), f32[32,1,257]{2,1,0:T(1,128)S(1)}, u32[]{:S(2)}, u32[]{:S(2)}) %all-to-all-start.4) | async-done | bytes 32928 | tf_op jit(solution)/shard_map/all_to_all | solution.py:265
  147.1 0.6 slice_reduce_fusion
  148.5 0.6 fusion.14
  149.1 1.2 reshape.732
  150.3 0.9 multiply_subtract_fusion.1
  (79 shorter events, 1.9 us)
Async XLA Ops:
  0.6 1.6 %copy-start = (f32[12,62]{1,0:T(8,128)S(1)}, f32[12,62]{1,0:T(8,128)}, u32[]{:S(2)}) copy-start(f32[12,62]{1,0:T(8,128)} %param.30) | copy-start | bytes 8932
  0.6 3.6 %copy-start.11 = (s32[1,32]{1,0:T(1,128)S(1)}, s32[1,32]{1,0:T(1,128)}, u32[]{:S(2)}) copy-start(s32[1,32]{1,0:T(1,128)} %param.34) | copy-start | bytes 388
  0.7 3.7 %copy-start.10 = (f32[8192]{0:T(1024)S(1)}, f32[8192]{0:T(1024)}, u32[]{:S(2)}) copy-start(f32[8192]{0:T(1024)} %param.33) | copy-start | bytes 98308
  0.7 3.7 %copy-start.9 = (f32[5,8192]{1,0:T(8,128)S(1)}, f32[5,8192]{1,0:T(8,128)}, u32[]{:S(2)}) copy-start(f32[5,8192]{1,0:T(8,128)} %param.29) | copy-start | bytes 491524
  6.0 21.7 %all-to-all-start = ((f32[10,32,256]{2,0,1:T(8,128)}), f32[10,32,256]{2,0,1:T(8,128)S(1)}, u32[]{:S(2)}, u32[]{:S(2)}) async-start(f32[10,32,256]{2,0,1:T(8,128)} %concatenate.54), calls=%async_computation | async-start | bytes 1048576 | tf_op jit(solution)/shard_map/all_to_all | solution.py:236
  43.7 16.2 %all-to-all-start.1 = ((f32[32,1,1028]{2,1,0:T(1,128)}), f32[32,1,1028]{2,1,0:T(1,128)S(1)}, u32[]{:S(2)}, u32[]{:S(2)}) async-start(f32[32,1,1028]{2,1,0:T(1,128)} %broadcast_in_dim.12), calls=%async_computation.1 | async-start | bytes 294912 | tf_op jit(solution)/shard_map/all_to_all | solution.py:247
  71.4 22.3 %copy-start.7 = (f32[1,8192]{1,0:T(1,128)S(1)}, f32[1,8192]{1,0:T(1,128)}, u32[]{:S(2)}) copy-start(f32[1,8192]{1,0:T(1,128)} %broadcast_select_fusion.val_ref) | copy-start | bytes 98308
  72.7 19.6 %all-to-all-start.2 = ((f32[32,1,257]{2,1,0:T(1,128)}), f32[32,1,257]{2,1,0:T(1,128)S(1)}, u32[]{:S(2)}, u32[]{:S(2)}) async-start(f32[32,1,257]{2,1,0:T(1,128)} %copy.30), calls=%async_computation.2 | async-start | bytes 98304 | tf_op jit(solution)/shard_map/all_to_all | solution.py:265
  79.3 21.2 %copy-start.1 = (f32[640,256]{1,0:T(8,128)S(1)}, f32[640,256]{1,0:T(8,128)}, u32[]{:S(2)}) copy-start(f32[640,256]{1,0:T(8,128)} %shard_map.104.tab_ref) | copy-start | bytes 1966084
  90.4 10.1 %copy-start.3 = (f32[640,256]{1,0:T(8,128)S(1)}, f32[640,256]{1,0:T(8,128)}, u32[]{:S(2)}) copy-start(f32[640,256]{1,0:T(8,128)} %shard_map.108) | copy-start | bytes 1966084
  103.9 16.1 %all-to-all-start.3 = ((f32[32,1,1028]{2,1,0:T(1,128)}), f32[32,1,1028]{2,1,0:T(1,128)S(1)}, u32[]{:S(2)}, u32[]{:S(2)}) async-start(f32[32,1,1028]{2,1,0:T(1,128)} %broadcast_in_dim.14), calls=%async_computation.3 | async-start | bytes 294912 | tf_op jit(solution)/shard_map/all_to_all | solution.py:247
  120.0 11.6 %copy-start.4 = (f32[5,8192]{1,0:T(8,128)S(1)}, f32[5,8192]{1,0:T(8,128)}, u32[]{:S(2)}) copy-start(f32[5,8192]{1,0:T(8,128)} %shard_map.105) | copy-start | bytes 491524
  120.0 11.6 %copy-start.6 = (f32[5,8192]{1,0:T(8,128)S(1)}, f32[5,8192]{1,0:T(8,128)}, u32[]{:S(2)}) copy-start(f32[5,8192]{1,0:T(8,128)} %shard_map.109) | copy-start | bytes 491524
  124.4 24.0 %copy-start.2 = (f32[640,256]{1,0:T(8,128)S(1)}, f32[640,256]{1,0:T(8,128)}, u32[]{:S(2)}) copy-start(f32[640,256]{1,0:T(8,128)} %get-tuple-element.126.tab_ref) | copy-start | bytes 1966084
  130.1 1.7 %copy-start.8 = (f32[1,8192]{1,0:T(1,128)S(1)}, f32[1,8192]{1,0:T(1,128)}, u32[]{:S(2)}) copy-start(f32[1,8192]{1,0:T(1,128)} %shard_map.110) | copy-start | bytes 98308
  133.8 13.2 %all-to-all-start.4 = ((f32[32,1,257]{2,1,0:T(1,128)}), f32[32,1,257]{2,1,0:T(1,128)S(1)}, u32[]{:S(2)}, u32[]{:S(2)}) async-start(f32[32,1,257]{2,1,0:T(1,128)} %copy.34), calls=%async_computation.4 | async-start | bytes 98304 | tf_op jit(solution)/shard_map/all_to_all | solution.py:265
  148.5 1.8 %copy-start.5 = (f32[12,8192]{1,0:T(8,128)S(1)}, f32[12,8192]{1,0:T(8,128)}, u32[]{:S(2)}) copy-start(f32[12,8192]{1,0:T(8,128)} %param.28) | copy-start | bytes 1179652

commit v4 on v3

--- a/solution.py
+++ b/solution.py
@@ -9,7 +9,7 @@
 KN = 1024
 ITERS = 2
 HI = 256
-CHUNK = 512
+CHUNK = 2048
 
 
 def passed_along(block, axis, distance):

time: 152 us -> 137 us (0.901)
  Pallas kernels: 64.5 us -> 46.7 us
  waiting for transfers between devices: 13.2 us -> 15.3 us
    pallas_call x2, Pallas kernels: 22.1 us -> 16.2 us  [source_scatter(): pl.pallas_call(kernel, out_shape=jax.ShapeDtypeStruct((rows, HI), jnp.flo...]
    pallas_call x2, Pallas kernels: 20.5 us -> 16.4 us  [source_gather(): pl.pallas_call(kernel, out_shape=jax.ShapeDtypeStruct((n, total), jnp.flo...]
    pallas_call x2, Pallas kernels: 11.3 us -> 7.33 us  [knot_gather(): pl.pallas_call(kernel, out_shape=jax.ShapeDtypeStruct((1, total), jnp.flo...]
    pallas_call x2, Pallas kernels: 10.6 us -> 6.72 us  [knot_scatter(): pl.pallas_call(kernel, out_shape=jax.ShapeDtypeStruct((rows, HI), jnp.flo...]
    all_to_all x1, waiting for transfers between devices: 5.8 us -> 7.71 us  [per_device(): lax.all_to_all(packed, everyone, split_axis=1, concat_axis=1, tiled=True)]
  transfers between devices with their start and end apart: 5 -> 5, of which waited for: 2 -> 3; matrix products, arithmetic and copies ran while one was open for 4% -> 5% of each run, Pallas kernels for 24% -> 21%
where the time goes in v4:
time: 137 us; the launch traced here: 135 us
  Pallas kernels  46.7 us (34%)
  starting transfers between devices  28.6 us (21%)
  other arithmetic  24.5 us (18%)
  waiting for transfers between devices  15.3 us (11%)
  local copies, waits for them, and re-layouts  13.1 us (10%)
  between operations  5.13 us (4%)
  matrix products  2 us (1%)
    pallas_call x2, Pallas kernels, source_gather(): pl.pallas_call(kernel, out_shape=jax.ShapeDtypeStruct((n, total), jnp.flo...  16.4 us
    pallas_call x2, Pallas kernels, source_scatter(): pl.pallas_call(kernel, out_shape=jax.ShapeDtypeStruct((rows, HI), jnp.flo...  16.2 us
    all_to_all x2, starting transfers between devices, forward(): back = lax.all_to_all(payload, everyone, 0, 0, tiled=True)  11.2 us
    all_to_all x2, starting transfers between devices, combine(): lax.all_to_all(jnp.broadcast_to(mine[None, :], (n_ranks, knots + 4)), eve...  10.1 us
    all_to_all x1, waiting for transfers between devices, per_device(): lax.all_to_all(packed, everyone, split_axis=1, concat_axis=1, tiled=True)  7.71 us
    all_to_all x2, waiting for transfers between devices, forward(): back = lax.all_to_all(payload, everyone, 0, 0, tiled=True)  7.37 us
    pallas_call x2, Pallas kernels, knot_gather(): pl.pallas_call(kernel, out_shape=jax.ShapeDtypeStruct((1, total), jnp.flo...  7.33 us
    all_to_all x1, starting transfers between devices, per_device(): lax.all_to_all(packed, everyone, split_axis=1, concat_axis=1, tiled=True)  7.3 us
  transfers between devices with their start and end apart: 5, of which 3 were waited for; matrix products, arithmetic and copies ran while one was open for 5% of the time, Pallas kernels for 21%

profile of v4, /device:TPU:0, one launch (start us, length us, event | category | flops | bytes accessed | tf_op | source)
XLA Modules:
  0.0 135.3 jit_solution(6203780130951130951)
XLA Ops:
  0.7 0.8 compare_convert_fusion
  1.5 0.8 convert_element_type.33
  2.2 2.0 %multiply_reduce_fusion.2 = (f32[8192]{0:T(1024)S(1)}, f32[8192]{0:T(1024)S(1)}, f32[12,8192]{1,0:T(8,128)S(1)}) fusion(f32[12,8192]{1,0:T(8,128)} %param.28, f32[12,62]{1,0:T(8,128)S(1)} %copy-done, s32[8192]{0:T(1024)} %param.31), kind=kOutput, calls=%fused_computation.8 | convolution fusion | flops 74022912 | bytes 887712 | tf_op jit(solution)/shard_map/dot_general | solution.py:213
  4.4 1.7 %concatenate.54 = f32[10,32,256]{2,0,1:T(8,128)} concatenate(f32[5,32,256]{2,0,1:T(8,128)S(1)} %bitcast.137, f32[1,32,256]{2,0,1:T(1,128)S(1)} %compare_select_fusion.3, f32[1,32,256]{2,0,1:T(1,128)S(1)} %bitcast.135, f32[1,32,256]{2,0,1:T(1,128)S(1)} %compare_convert_fusion, f32[1,32,256]{2,0,1:T(1,128)S(1)} %bitcast.164, f32[1,32,256]{2,0,1:T(1,128)S(1)} %bitcast.165), dimensions={0} | concatenate | bytes 655360 | tf_op jit(solution)/shard_map/concatenate | solution.py:225
  6.0 7.3 %all-to-all-start = ((f32[10,32,256]{2,0,1:T(8,128)}), f32[10,32,256]{2,0,1:T(8,128)S(1)}, u32[]{:S(2)}, u32[]{:S(2)}) async-start(f32[10,32,256]{2,0,1:T(8,128)} %concatenate.54), calls=%async_computation | async-start | bytes 1048576 | tf_op jit(solution)/shard_map/all_to_all | solution.py:236
  13.7 1.0 reshape.713.basis_ref
  14.7 0.7 broadcast_select_fusion.val_ref
  15.4 3.4 %shard_map.103 = f32[16,256]{1,0:T(8,128)} custom-call(f32[1,8192]{1,0:T(1,128)} %broadcast_select_fusion.val_ref, s32[1,8192]{1,0:T(1,128)} %bitcast.126, f32[16,8192]{1,0:T(8,128)} %reshape.713.basis_ref), custom_call_target="tpu_custom_call" | custom-call | tf_op jit(solution)/shard_map/pallas_call | solution.py:177
  18.7 0.8 slice_bitcast_fusion.7
  19.6 0.1 add_dynamic-update-slice_fusion.1
  19.7 0.1 fusion.18
  19.9 0.1 fusion.17
  20.0 7.7 %all-to-all-done = f32[10,32,256]{2,0,1:T(8,128)S(1)} async-done(((f32[10,32,256]{2,0,1:T(8,128)}), f32[10,32,256]{2,0,1:T(8,128)S(1)}, u32[]{:S(2)}, u32[]{:S(2)}) %all-to-all-start) | async-done | bytes 327712 | tf_op jit(solution)/shard_map/all_to_all | solution.py:236
  27.8 0.7 multiply_add_fusion.2.ids_ref
  28.5 0.2 fusion.9
  28.6 0.7 broadcast_multiply_fusion.1.val_ref
  29.4 8.1 %shard_map.104.tab_ref = f32[640,256]{1,0:T(8,128)} custom-call(f32[5,8192]{1,0:T(8,128)} %broadcast_multiply_fusion.1.val_ref, s32[1,8192]{1,0:T(1,128)} %ids_ref.7), custom_call_target="tpu_custom_call" | custom-call | tf_op jit(solution)/shard_map/pallas_call | solution.py:120
  37.4 1.9 %multiply_reduce_fusion.1 = f32[]{:T(128)} fusion(f32[640,256]{1,0:T(8,128)} %shard_map.104.tab_ref), kind=kLoop, calls=%fused_computation.6 | loop fusion | flops 327679 | bytes 655364 | tf_op jit(solution)/shard_map/reduce_sum | solution.py:246
  39.3 0.7 pad_maximum_fusion.4
  40.0 0.7 broadcast_in_dim.12
  40.8 4.1 %all-to-all-start.1 = ((f32[32,1,1028]{2,1,0:T(1,128)}), f32[32,1,1028]{2,1,0:T(1,128)S(1)}, u32[]{:S(2)}, u32[]{:S(2)}) async-start(f32[32,1,1028]{2,1,0:T(1,128)} %broadcast_in_dim.12), calls=%async_computation.1 | async-start | bytes 294912 | tf_op jit(solution)/shard_map/all_to_all | solution.py:247
  44.8 0.8 pad_maximum_fusion.2.basis_ref
  45.6 8.2 %shard_map.105 = f32[5,8192]{1,0:T(8,128)} custom-call(f32[640,256]{1,0:T(8,128)} %shard_map.104.tab_ref, s32[1,8192]{1,0:T(1,128)} %ids_ref.7), custom_call_target="tpu_custom_call" | custom-call | tf_op jit(solution)/shard_map/pallas_call | solution.py:88
  53.8 1.0 multiply_reduce_fusion.5
  55.1 0.4 scatter-add.40
  55.5 0.7 multiply_reduce_fusion.7
  56.5 0.7 reshape.719.tab_ref
  57.2 3.6 %shard_map.106 = f32[1,8192]{1,0:T(1,128)} custom-call(f32[128,256]{1,0:T(8,128)} %reshape.719.tab_ref, s32[1,8192]{1,0:T(1,128)} %multiply_add_fusion.2.ids_ref, f32[4,8192]{1,0:T(4,128)} %pad_maximum_fusion.2.basis_ref), custom_call_target="tpu_custom_call" | custom-call | tf_op jit(solution)/shard_map/pallas_call | solution.py:149
  60.9 1.5 %fusion.11 = (f32[]{:T(128)}, f32[1,32,256]{2,0,1:T(1,128)S(1)}, f32[1,32,256]{2,0,1:T(1,128)S(1)}) fusion(f32[1,32,256]{2,0,1:T(1,128)S(1)} %bitcast.123, f32[1,32,256]{2,0,1:T(1,128)} %bitcast.132, f32[10,32,256]{2,0,1:T(8,128)S(1)} %all-to-all-done), kind=kLoop, calls=%fused_computation.72 | loop fusion | flops 40959 | bytes 196612 | tf_op jit(solution)/shard_map/reduce_sum | solution.py:261
  62.3 0.5 broadcast.490
  62.9 1.5 %fusion.20 = (f32[8192]{0:T(1024)S(1)}, f32[1,8192]{1,0:T(1,128)S(1)}) fusion(f32[1,8192]{1,0:T(1,128)} %shard_map.106, f32[]{:T(128)} %broadcast.490, f32[1,8192]{1,0:T(1,128)S(1)} %bitcast.153, f32[1,8192]{1,0:T(1,128)S(1)} %bitcast.125, f32[1,8192]{1,0:T(1,128)S(1)} %bitcast.124), kind=kLoop, calls=%fused_computation.110 | loop fusion | flops 24576 | bytes 196612 | tf_op jit(solution)/shard_map/pallas_call | solution.py:149
  64.4 0.6 pad_bitcast_fusion.1
  65.1 0.7 copy.30
  65.8 5.8 %all-to-all-start.2 = ((f32[32,1,257]{2,1,0:T(1,128)}), f32[32,1,257]{2,1,0:T(1,128)S(1)}, u32[]{:S(2)}, u32[]{:S(2)}) async-start(f32[32,1,257]{2,1,0:T(1,128)} %copy.30), calls=%async_computation.2 | async-start | bytes 98304 | tf_op jit(solution)/shard_map/all_to_all | solution.py:265
  71.6 0.7 broadcast_multiply_fusion.val_ref
  72.3 8.1 %shard_map.108 = f32[640,256]{1,0:T(8,128)} custom-call(f32[5,8192]{1,0:T(8,128)} %broadcast_multiply_fusion.val_ref, s32[1,8192]{1,0:T(1,128)} %ids_ref.7), custom_call_target="tpu_custom_call" | custom-call | tf_op jit(solution)/shard_map/pallas_call | solution.py:120
  80.5 0.7 slice_reduce_fusion.3
  82.5 0.6 slice_reduce_fusion.2
  83.8 0.6 multiply_subtract_fusion.2.val_ref
  84.5 3.4 %shard_map.107 = f32[16,256]{1,0:T(8,128)} custom-call(f32[1,8192]{1,0:T(1,128)} %multiply_subtract_fusion.2.val_ref, s32[1,8192]{1,0:T(1,128)} %bitcast.127, f32[16,8192]{1,0:T(8,128)} %reshape.713.basis_ref), custom_call_target="tpu_custom_call" | custom-call | tf_op jit(solution)/shard_map/pallas_call | solution.py:177
  87.8 0.8 slice_bitcast_fusion.3
  88.7 1.6 %multiply_reduce_fusion = (f32[]{:T(128)}, f32[640,256]{1,0:T(8,128)}) fusion(f32[640,256]{1,0:T(8,128)S(1)} %copy-done.1, f32[640,256]{1,0:T(8,128)S(1)} %copy-done.3, f32[]{:T(128)S(6)} %div.65), kind=kLoop, calls=%fused_computation.4 | loop fusion | flops 655359 | bytes 1966088 | tf_op jit(solution)/shard_map/reduce_sum | solution.py:246
  90.4 0.1 fusion.16
  90.5 0.1 fusion.15
  90.7 0.7 pad_maximum_fusion.5
  91.3 0.7 broadcast_in_dim.14
  92.1 6.0 %all-to-all-start.3 = ((f32[32,1,1028]{2,1,0:T(1,128)}), f32[32,1,1028]{2,1,0:T(1,128)S(1)}, u32[]{:S(2)}, u32[]{:S(2)}) async-start(f32[32,1,1028]{2,1,0:T(1,128)} %broadcast_in_dim.14), calls=%async_computation.3 | async-start | bytes 294912 | tf_op jit(solution)/shard_map/all_to_all | solution.py:247
  98.1 8.2 %shard_map.109 = f32[5,8192]{1,0:T(8,128)} custom-call(f32[640,256]{1,0:T(8,128)} %get-tuple-element.126.tab_ref, s32[1,8192]{1,0:T(1,128)} %ids_ref.7), custom_call_target="tpu_custom_call" | custom-call | tf_op jit(solution)/shard_map/pallas_call | solution.py:88
  106.3 0.2 all-to-all-done.3
  106.6 0.7 slice_reduce_fusion.1
  107.5 0.4 scatter-add.49
  107.9 0.7 multiply_reduce_fusion.6
  110.2 0.8 reshape.729.tab_ref
  111.0 3.7 %shard_map.110 = f32[1,8192]{1,0:T(1,128)} custom-call(f32[128,256]{1,0:T(8,128)} %reshape.729.tab_ref, s32[1,8192]{1,0:T(1,128)} %multiply_add_fusion.2.ids_ref, f32[4,8192]{1,0:T(4,128)} %pad_maximum_fusion.2.basis_ref), custom_call_target="tpu_custom_call" | custom-call | tf_op jit(solution)/shard_map/pallas_call | solution.py:149
  114.7 1.5 %reduce.37 = f32[8192]{0:T(1024)S(1)} reduce(f32[1,8192]{1,0:T(1,128)} %shard_map.110, f32[]{:T(128)} %broadcast.490), dimensions={0}, to_apply=%pallas_call.31.reduce_sub_computation.3 | reduce | bytes 65540 | tf_op jit(solution)/shard_map/pallas_call | solution.py:149
  116.3 0.7 fusion.12
  117.0 0.6 pad_bitcast_fusion
  117.7 0.7 copy.34
  118.4 5.4 %all-to-all-start.4 = ((f32[32,1,257]{2,1,0:T(1,128)}), f32[32,1,257]{2,1,0:T(1,128)S(1)}, u32[]{:S(2)}, u32[]{:S(2)}) async-start(f32[32,1,257]{2,1,0:T(1,128)} %copy.34), calls=%async_computation.4 | async-start | bytes 98304 | tf_op jit(solution)/shard_map/all_to_all | solution.py:265
  123.8 7.4 %all-to-all-done.4 = f32[32,1,257]{2,1,0:T(1,128)S(1)} async-done(((f32[32,1,257]{2,1,0:T(1,128)}), f32[32,1,257]{2,1,0:T(1,128)S(1)}, u32[]{:S(2)}, u32[]{:S(2)}) %all-to-all-start.4) | async-done | bytes 32928 | tf_op jit(solution)/shard_map/all_to_all | solution.py:265
  131.2 0.6 slice_reduce_fusion
  132.6 0.6 fusion.14
  133.3 1.2 reshape.732
  134.4 0.9 multiply_subtract_fusion.1
  (79 shorter events, 2.0 us)
Async XLA Ops:
  0.6 1.6 %copy-start = (f32[12,62]{1,0:T(8,128)S(1)}, f32[12,62]{1,0:T(8,128)}, u32[]{:S(2)}) copy-start(f32[12,62]{1,0:T(8,128)} %param.30) | copy-start | bytes 8932
  0.6 3.6 %copy-start.11 = (s32[1,32]{1,0:T(1,128)S(1)}, s32[1,32]{1,0:T(1,128)}, u32[]{:S(2)}) copy-start(s32[1,32]{1,0:T(1,128)} %param.34) | copy-start | bytes 388
  0.7 3.7 %copy-start.10 = (f32[8192]{0:T(1024)S(1)}, f32[8192]{0:T(1024)}, u32[]{:S(2)}) copy-start(f32[8192]{0:T(1024)} %param.33) | copy-start | bytes 98308
  0.7 3.7 %copy-start.9 = (f32[5,8192]{1,0:T(8,128)S(1)}, f32[5,8192]{1,0:T(8,128)}, u32[]{:S(2)}) copy-start(f32[5,8192]{1,0:T(8,128)} %param.29) | copy-start | bytes 491524
  6.0 21.7 %all-to-all-start = ((f32[10,32,256]{2,0,1:T(8,128)}), f32[10,32,256]{2,0,1:T(8,128)S(1)}, u32[]{:S(2)}, u32[]{:S(2)}) async-start(f32[10,32,256]{2,0,1:T(8,128)} %concatenate.54), calls=%async_computation | async-start | bytes 1048576 | tf_op jit(solution)/shard_map/all_to_all | solution.py:236
  40.8 14.2 %all-to-all-start.1 = ((f32[32,1,1028]{2,1,0:T(1,128)}), f32[32,1,1028]{2,1,0:T(1,128)S(1)}, u32[]{:S(2)}, u32[]{:S(2)}) async-start(f32[32,1,1028]{2,1,0:T(1,128)} %broadcast_in_dim.12), calls=%async_computation.1 | async-start | bytes 294912 | tf_op jit(solution)/shard_map/all_to_all | solution.py:247
  64.4 19.4 %copy-start.7 = (f32[1,8192]{1,0:T(1,128)S(1)}, f32[1,8192]{1,0:T(1,128)}, u32[]{:S(2)}) copy-start(f32[1,8192]{1,0:T(1,128)} %broadcast_select_fusion.val_ref) | copy-start | bytes 98308
  65.8 16.7 %all-to-all-start.2 = ((f32[32,1,257]{2,1,0:T(1,128)}), f32[32,1,257]{2,1,0:T(1,128)S(1)}, u32[]{:S(2)}, u32[]{:S(2)}) async-start(f32[32,1,257]{2,1,0:T(1,128)} %copy.30), calls=%async_computation.2 | async-start | bytes 98304 | tf_op jit(solution)/shard_map/all_to_all | solution.py:265
  72.3 16.3 %copy-start.1 = (f32[640,256]{1,0:T(8,128)S(1)}, f32[640,256]{1,0:T(8,128)}, u32[]{:S(2)}) copy-start(f32[640,256]{1,0:T(8,128)} %shard_map.104.tab_ref) | copy-start | bytes 1966084
  80.5 8.2 %copy-start.3 = (f32[640,256]{1,0:T(8,128)S(1)}, f32[640,256]{1,0:T(8,128)}, u32[]{:S(2)}) copy-start(f32[640,256]{1,0:T(8,128)} %shard_map.108) | copy-start | bytes 1966084
  92.1 14.5 %all-to-all-start.3 = ((f32[32,1,1028]{2,1,0:T(1,128)}), f32[32,1,1028]{2,1,0:T(1,128)S(1)}, u32[]{:S(2)}, u32[]{:S(2)}) async-start(f32[32,1,1028]{2,1,0:T(1,128)} %broadcast_in_dim.14), calls=%async_computation.3 | async-start | bytes 294912 | tf_op jit(solution)/shard_map/all_to_all | solution.py:247
  106.6 9.6 %copy-start.4 = (f32[5,8192]{1,0:T(8,128)S(1)}, f32[5,8192]{1,0:T(8,128)}, u32[]{:S(2)}) copy-start(f32[5,8192]{1,0:T(8,128)} %shard_map.105) | copy-start | bytes 491524
  106.6 9.6 %copy-start.6 = (f32[5,8192]{1,0:T(8,128)S(1)}, f32[5,8192]{1,0:T(8,128)}, u32[]{:S(2)}) copy-start(f32[5,8192]{1,0:T(8,128)} %shard_map.109) | copy-start | bytes 491524
  111.0 21.5 %copy-start.2 = (f32[640,256]{1,0:T(8,128)S(1)}, f32[640,256]{1,0:T(8,128)}, u32[]{:S(2)}) copy-start(f32[640,256]{1,0:T(8,128)} %get-tuple-element.126.tab_ref) | copy-start | bytes 1966084
  114.7 1.7 %copy-start.8 = (f32[1,8192]{1,0:T(1,128)S(1)}, f32[1,8192]{1,0:T(1,128)}, u32[]{:S(2)}) copy-start(f32[1,8192]{1,0:T(1,128)} %shard_map.110) | copy-start | bytes 98308
  118.4 12.8 %all-to-all-start.4 = ((f32[32,1,257]{2,1,0:T(1,128)}), f32[32,1,257]{2,1,0:T(1,128)S(1)}, u32[]{:S(2)}, u32[]{:S(2)}) async-start(f32[32,1,257]{2,1,0:T(1,128)} %copy.34), calls=%async_computation.4 | async-start | bytes 98304 | tf_op jit(solution)/shard_map/all_to_all | solution.py:265
  132.6 1.8 %copy-start.5 = (f32[12,8192]{1,0:T(8,128)S(1)}, f32[12,8192]{1,0:T(8,128)}, u32[]{:S(2)}) copy-start(f32[12,8192]{1,0:T(8,128)} %param.28) | copy-start | bytes 1179652

commit v5 on v4

--- a/solution.py
+++ b/solution.py
@@ -61,35 +61,36 @@
         big_ref[k * rows:(k + 1) * rows, :] = part
 
 
-def source_gather(table, ids):
-    n, width = table.shape
-    cols = width // HI
-    rows = n * cols
-    total = ids.shape[1]
-
-    def kernel(tab_ref, ids_ref, out_ref, big_ref):
+def source_gather(table, ids, held):
+    n, total = held.shape
+    rows = table.shape[0]
+    cols = rows // n
+
+    def kernel(tab_ref, ids_ref, held_ref, out_ref, big_ref):
         split_into(tab_ref, big_ref)
 
         def body(off):
             idc = ids_ref[:, pl.ds(off, CHUNK)]
             picked = jnp.dot(big_ref[...], hot_rows(idc, CHUNK), preferred_element_type=jnp.float32)
             sel = group_mask(idc, cols, CHUNK, cols)
+            weights = held_ref[:, pl.ds(off, CHUNK)]
+            column = jnp.zeros((1, CHUNK), jnp.float32)
             for p in range(n):
                 acc = (
                     picked[p * cols:(p + 1) * cols]
                     + picked[rows + p * cols:rows + (p + 1) * cols]
                 )
-                out_ref[pl.ds(p, 1), pl.ds(off, CHUNK)] = jnp.sum(
-                    jnp.where(sel, acc, 0.0), axis=0, keepdims=True
-                )
+                value = jnp.sum(jnp.where(sel, acc, 0.0), axis=0, keepdims=True)
+                column = column + weights[p:p + 1] * value
+            out_ref[:, pl.ds(off, CHUNK)] = column
 
         chunks(total, body)
 
     return pl.pallas_call(
         kernel,
-        out_shape=jax.ShapeDtypeStruct((n, total), jnp.float32),
+        out_shape=jax.ShapeDtypeStruct((1, total), jnp.float32),
         scratch_shapes=[pltpu.VMEM((2 * rows, HI), jnp.bfloat16)],
-    )(table.reshape(rows, HI), ids)
+    )(table, ids, held)
 
 
 def source_scatter(values, ids, width):
@@ -117,20 +118,20 @@
 
         chunks(total, body)
 
-    out = pl.pallas_call(
+    return pl.pallas_call(
         kernel, out_shape=jax.ShapeDtypeStruct((rows, HI), jnp.float32)
     )(values, ids)
-    return out.reshape(n, width)
-
-
-def knot_gather(extended, first_ids, basis, knots):
+
+
+def knot_gather(extended, first_ids, basis, zsrc, weight, knots):
     total = first_ids.shape[1]
     cols = knots // HI
     shifted = jnp.stack([extended[q:q + knots] for q in range(4)], axis=0)
     rows = 4 * cols
 
-    def kernel(tab_ref, ids_ref, basis_ref, out_ref, big_ref):
+    def kernel(tab_ref, ids_ref, basis_ref, zsrc_ref, weight_ref, out_ref, norm_ref, big_ref):
         split_into(tab_ref, big_ref)
+        norm_ref[...] = jnp.zeros(norm_ref.shape, jnp.float32)
 
         def body(off):
             idc = ids_ref[:, pl.ds(off, CHUNK)]
@@ -142,15 +143,20 @@
             for q in range(4):
                 value = jnp.sum(jnp.where(sel, acc[q * cols:(q + 1) * cols], 0.0), axis=0, keepdims=True)
                 z = z + b[q:q + 1] * value
-            out_ref[:, pl.ds(off, CHUNK)] = z
+            shift = zsrc_ref[:, pl.ds(off, CHUNK)] + z
+            out_ref[:, pl.ds(off, CHUNK)] = shift
+            norm_ref[...] += jnp.sum(weight_ref[:, pl.ds(off, CHUNK)] * shift * shift, axis=1, keepdims=True)
 
         chunks(total, body)
 
     return pl.pallas_call(
         kernel,
-        out_shape=jax.ShapeDtypeStruct((1, total), jnp.float32),
+        out_shape=(
+            jax.ShapeDtypeStruct((1, total), jnp.float32),
+            jax.ShapeDtypeStruct((1, 1), jnp.float32),
+        ),
         scratch_shapes=[pltpu.VMEM((2 * rows, HI), jnp.bfloat16)],
-    )(shifted.reshape(rows, HI), first_ids, basis)
+    )(shifted.reshape(rows, HI), first_ids, basis, zsrc, weight)
 
 
 def knot_scatter(values, first_ids, basis16, knots):
@@ -216,7 +222,7 @@
         precision=lax.Precision.HIGHEST,
         preferred_element_type=jnp.float32,
     )
-    weight_sq = jnp.sum(weight_factor * weight_factor, axis=0)
+    weight_sq = live * jnp.sum(weight_factor * weight_factor, axis=0)
     basis16 = jnp.repeat(jnp.stack(spline_basis(interval_fraction), axis=0), knots // HI, axis=0)
     first_ids = first_knot_interval.reshape(1, rows)
     ids = slot_owned_source[0].reshape(1, rows)
@@ -227,7 +233,6 @@
             source_partials,
             zbar0[None],
             weight_sq[None],
-            live[None],
             interval_fraction[None],
             first_knot_interval.astype(jnp.float32)[None],
         ],
@@ -237,10 +242,10 @@
     held = got[:n_params]
     zbar0_own = got[n_params]
     weight_sq_own = got[n_params + 1]
-    live_own = got[n_params + 2]
-    basis_own = jnp.stack(spline_basis(got[n_params + 3]), axis=0)
+    basis_own = jnp.stack(spline_basis(got[n_params + 2]), axis=0)
     slot_device = jnp.arange(rows, dtype=jnp.int32) // capacity
-    base_own = ((slot_device // n_share) * knots + got[n_params + 4].astype(jnp.int32)).reshape(1, rows)
+    base_own = ((slot_device // n_share) * knots + got[n_params + 3].astype(jnp.int32)).reshape(1, rows)
+    table_rows = n_params * (owned // HI)
 
     def combine(part_a, grad_s):
         mine = jnp.concatenate([part_a, jnp.sum(grad_s * grad_s)[None]])
@@ -253,26 +258,26 @@
         norm = jnp.sum(every[:, knots + 3]) + jnp.sum(grad_a * grad_a)
         return grad_a, norm
 
-    def forward(pulled, dir_a):
-        zsrc = jnp.sum(held * pulled, axis=0)
+    def forward(zsrc, dir_a):
         extended = jnp.concatenate([dir_a, jnp.zeros((3,), jnp.float32)])
-        zatt = knot_gather(extended, base_own, basis_own, n_knots).reshape(rows)
-        shift_own = (zsrc + zatt) * live_own
-        partial = jnp.sum(weight_sq_own * shift_own * shift_own)
+        shift_own, partial = knot_gather(
+            extended, base_own, basis_own, zsrc, weight_sq_own.reshape(1, rows), n_knots
+        )
+        shift_own = shift_own.reshape(rows)
         payload = jnp.concatenate(
             [shift_own.reshape(n_ranks, capacity), jnp.broadcast_to(partial, (n_ranks, 1))], axis=1
         )
         back = lax.all_to_all(payload, everyone, 0, 0, tiled=True)
-        return shift_own, back[:, :capacity].reshape(rows), jnp.sum(back[:, capacity])
-
-    sol_s = jnp.zeros((n_params, owned), jnp.float32)
+        return shift_own, back[:, :capacity].reshape(rows) * live, jnp.sum(back[:, capacity])
+
+    sol_s = jnp.zeros((table_rows, HI), jnp.float32)
     sol_a = jnp.zeros((n_knots,), jnp.float32)
     resid = observed_residual
     zbar_slot = zbar0
     grad_s = source_scatter(held * zbar0_own[None, :], ids, owned)
     grad_a, gamma = combine(knot_scatter(zbar_slot.reshape(1, rows), first_ids, basis16, knots), grad_s)
     dir_s, dir_a = (grad_s, grad_a)
-    pulled = source_gather(dir_s, ids)
+    pulled = source_gather(dir_s, ids, held)
     for step in range(ITERS):
         shift_own, shift_slot, image_sq = forward(pulled, dir_a)
         alpha = gamma / image_sq
@@ -286,14 +291,14 @@
             grad_a, fresh = combine(
                 knot_scatter(zbar_slot.reshape(1, rows), first_ids, basis16, knots), grad_s
             )
-            raw = source_gather(grad_s, ids)
+            raw = source_gather(grad_s, ids, held)
             beta = fresh / gamma
             dir_s = grad_s + beta * dir_s
             dir_a = grad_a + beta * dir_a
             pulled = raw + beta * pulled
             gamma = fresh
     mine_a = lax.dynamic_slice(sol_a, (lax.axis_index("tm") * knots,), (knots,))
-    return (sol_s, mine_a, resid)
+    return (sol_s.reshape(n_params, owned), mine_a, resid)
 
 
 def solution(mesh):

time: 137 us -> 134 us (0.978)
  other arithmetic: 24.5 us -> 21.8 us
    reduce_sum x4 -> x0, other arithmetic: 3.31 us -> none  [the longest x2 2.16 us: forward(): partial = jnp.sum(weight_sq_own * shift_own * shift_own)]
    concatenate x1 -> x3, local copies, waits for them, and re-layouts: 1.66 us -> 2.92 us  [the longest x1 1.61 us: per_device(): jnp.concatenate([source_partials, zbar0[None], weight_sq[None], interval_...]
  transfers between devices with their start and end apart: 5 -> 5, of which waited for: 3 -> 3; matrix products, arithmetic and copies ran while one was open for 5% -> 4% of each run, Pallas kernels for 21% -> 21%
where the time goes in v5:
time: 134 us; the launch traced here: 133 us
  Pallas kernels  47.2 us (35%)
  starting transfers between devices  28.7 us (21%)
  other arithmetic  21.8 us (16%)
  waiting for transfers between devices  15.3 us (11%)
  local copies, waits for them, and re-layouts  13 us (10%)
  between operations  5.28 us (4%)
  matrix products  2 us (1%)
    pallas_call x2, Pallas kernels, source_gather(): pl.pallas_call(kernel, out_shape=jax.ShapeDtypeStruct((1, total), jnp.flo...  16.4 us
    pallas_call x2, Pallas kernels, source_scatter(): pl.pallas_call(kernel, out_shape=jax.ShapeDtypeStruct((rows, HI), jnp.flo...  16.2 us
    all_to_all x2, starting transfers between devices, forward(): back = lax.all_to_all(payload, everyone, 0, 0, tiled=True)  11.3 us
    all_to_all x2, starting transfers between devices, combine(): lax.all_to_all(jnp.broadcast_to(mine[None, :], (n_ranks, knots + 4)), eve...  10.1 us
    pallas_call x2, Pallas kernels, knot_gather(): pl.pallas_call(kernel, out_shape=(jax.ShapeDtypeStruct((1, total), jnp.fl...  7.85 us
    all_to_all x1, waiting for transfers between devices, per_device(): lax.all_to_all(packed, everyone, split_axis=1, concat_axis=1, tiled=True)  7.72 us
    all_to_all x2, waiting for transfers between devices, forward(): back = lax.all_to_all(payload, everyone, 0, 0, tiled=True)  7.37 us
    all_to_all x1, starting transfers between devices, per_device(): lax.all_to_all(packed, everyone, split_axis=1, concat_axis=1, tiled=True)  7.3 us
  transfers between devices with their start and end apart: 5, of which 3 were waited for; matrix products, arithmetic and copies ran while one was open for 4% of the time, Pallas kernels for 21%

profile of v5, /device:TPU:0, one launch (start us, length us, event | category | flops | bytes accessed | tf_op | source)
XLA Modules:
  0.0 133.3 jit_solution(876770707764866739)
XLA Ops:
  0.7 0.8 convert_element_type.26
  1.5 2.0 %multiply_reduce_fusion.2 = (f32[8192]{0:T(1024)S(1)}, f32[8192]{0:T(1024)S(1)}, f32[12,8192]{1,0:T(8,128)S(1)}) fusion(f32[12,8192]{1,0:T(8,128)} %param.28, f32[12,62]{1,0:T(8,128)S(1)} %copy-done, s32[8192]{0:T(1024)} %param.31), kind=kOutput, calls=%fused_computation.8 | convolution fusion | flops 74022912 | bytes 887712 | tf_op jit(solution)/shard_map/dot_general | solution.py:219
  3.6 1.6 %concatenate.51 = f32[9,32,256]{2,0,1:T(8,128)} concatenate(f32[5,32,256]{2,0,1:T(8,128)S(1)} %bitcast.126, f32[1,32,256]{2,0,1:T(1,128)S(1)} %get-tuple-element.166, f32[1,32,256]{2,0,1:T(1,128)S(1)} %get-tuple-element.165, f32[1,32,256]{2,0,1:T(1,128)S(1)} %bitcast.133, f32[1,32,256]{2,0,1:T(1,128)S(1)} %bitcast.135), dimensions={0} | concatenate | bytes 589824 | tf_op jit(solution)/shard_map/concatenate | solution.py:231
  5.3 7.3 %all-to-all-start = ((f32[9,32,256]{2,0,1:T(8,128)}), f32[9,32,256]{2,0,1:T(8,128)S(1)}, u32[]{:S(2)}, u32[]{:S(2)}) async-start(f32[9,32,256]{2,0,1:T(8,128)} %concatenate.51), calls=%async_computation | async-start | bytes 1048576 | tf_op jit(solution)/shard_map/all_to_all | solution.py:241
  12.9 1.0 reshape.701.basis_ref
  13.9 0.7 broadcast_select_fusion.val_ref
  14.6 3.4 %shard_map.103 = f32[16,256]{1,0:T(8,128)} custom-call(f32[1,8192]{1,0:T(1,128)} %broadcast_select_fusion.val_ref, s32[1,8192]{1,0:T(1,128)} %bitcast.120, f32[16,8192]{1,0:T(8,128)} %reshape.701.basis_ref), custom_call_target="tpu_custom_call" | custom-call | tf_op jit(solution)/shard_map/pallas_call | solution.py:183
  17.9 0.8 slice_bitcast_fusion.5
  18.8 0.1 add_dynamic-update-slice_fusion.1
  18.9 0.1 fusion.17
  19.1 0.1 fusion.16
  19.2 7.7 %all-to-all-done = f32[9,32,256]{2,0,1:T(8,128)S(1)} async-done(((f32[9,32,256]{2,0,1:T(8,128)}), f32[9,32,256]{2,0,1:T(8,128)S(1)}, u32[]{:S(2)}, u32[]{:S(2)}) %all-to-all-start) | async-done | bytes 294944 | tf_op jit(solution)/shard_map/all_to_all | solution.py:241
  26.9 0.7 fusion.18
  27.6 0.7 multiply_add_fusion.3.ids_ref
  28.3 0.2 fusion.9
  28.5 0.8 broadcast_multiply_fusion.1.val_ref
  29.3 8.1 %shard_map.104.tab_ref = f32[640,256]{1,0:T(8,128)} custom-call(f32[5,8192]{1,0:T(8,128)} %broadcast_multiply_fusion.1.val_ref, s32[1,8192]{1,0:T(1,128)} %ids_ref.7), custom_call_target="tpu_custom_call" | custom-call | tf_op jit(solution)/shard_map/pallas_call | solution.py:121
  37.3 1.9 %multiply_reduce_fusion.1 = f32[]{:T(128)} fusion(f32[640,256]{1,0:T(8,128)} %shard_map.104.tab_ref), kind=kLoop, calls=%fused_computation.6 | loop fusion | flops 327679 | bytes 655364 | tf_op jit(solution)/shard_map/reduce_sum | solution.py:251
  39.2 0.7 pad_maximum_fusion.4
  39.9 0.7 broadcast_in_dim.16
  40.7 4.1 %all-to-all-start.1 = ((f32[32,1,1028]{2,1,0:T(1,128)}), f32[32,1,1028]{2,1,0:T(1,128)S(1)}, u32[]{:S(2)}, u32[]{:S(2)}) async-start(f32[32,1,1028]{2,1,0:T(1,128)} %broadcast_in_dim.16), calls=%async_computation.1 | async-start | bytes 294912 | tf_op jit(solution)/shard_map/all_to_all | solution.py:252
  44.7 0.8 pad_maximum_fusion.2.basis_ref
  45.5 8.2 %shard_map.105.zsrc_ref = f32[1,8192]{1,0:T(1,128)} custom-call(f32[640,256]{1,0:T(8,128)} %shard_map.104.tab_ref, s32[1,8192]{1,0:T(1,128)} %ids_ref.7, f32[5,8192]{1,0:T(8,128)} %bitcast.100), custom_call_target="tpu_custom_call" | custom-call | tf_op jit(solution)/shard_map/pallas_call | solution.py:89
  54.0 0.4 scatter-add.40
  54.4 0.7 multiply_reduce_fusion.5
  55.2 0.1 pad_maximum_fusion.1
  55.3 0.7 reshape.707.tab_ref
  56.1 3.9 %shard_map.106 = (f32[1,8192]{1,0:T(1,128)}, f32[1,1]{1,0:T(1,128)}) custom-call(f32[128,256]{1,0:T(8,128)} %reshape.707.tab_ref, s32[1,8192]{1,0:T(1,128)} %multiply_add_fusion.3.ids_ref, f32[4,8192]{1,0:T(4,128)} %pad_maximum_fusion.2.basis_ref, f32[1,8192]{1,0:T(1,128)} %shard_map.105.zsrc_ref, f32[1,8192]{1,0:T(1,128)} %bitcast.115), custom_call_target="tpu_custom_call" | custom-call | tf_op jit(solution)/shard_map/pallas_call | solution.py:152
  60.0 0.6 broadcast.523
  60.6 1.5 %fusion.19 = (f32[8192]{0:T(1024)S(1)}, f32[1,8192]{1,0:T(1,128)S(1)}) fusion(f32[1,8192]{1,0:T(1,128)} %get-tuple-element.127, f32[]{:T(128)} %broadcast.523, f32[1,8192]{1,0:T(1,128)S(1)} %bitcast.117), kind=kLoop, calls=%fused_computation.101 | loop fusion | flops 8192 | bytes 131076 | tf_op jit(solution)/shard_map/pallas_call | solution.py:152
  62.2 0.7 concatenate.54
  62.8 0.7 all_to_all.35
  63.5 5.8 %all-to-all-start.2 = ((f32[32,1,257]{2,1,0:T(1,128)}), f32[32,1,257]{2,1,0:T(1,128)S(1)}, u32[]{:S(2)}, u32[]{:S(2)}) async-start(f32[32,1,257]{2,1,0:T(1,128)} %all_to_all.35), calls=%async_computation.2 | async-start | bytes 98304 | tf_op jit(solution)/shard_map/all_to_all | solution.py:270
  69.3 0.7 broadcast_multiply_fusion.val_ref
  70.1 8.1 %shard_map.108 = f32[640,256]{1,0:T(8,128)} custom-call(f32[5,8192]{1,0:T(8,128)} %broadcast_multiply_fusion.val_ref, s32[1,8192]{1,0:T(1,128)} %ids_ref.7), custom_call_target="tpu_custom_call" | custom-call | tf_op jit(solution)/shard_map/pallas_call | solution.py:121
  78.2 0.7 slice_reduce_fusion.3
  80.2 0.6 slice_reduce_fusion.2
  81.6 0.7 multiply_subtract_fusion.2.val_ref
  82.3 3.4 %shard_map.107 = f32[16,256]{1,0:T(8,128)} custom-call(f32[1,8192]{1,0:T(1,128)} %multiply_subtract_fusion.2.val_ref, s32[1,8192]{1,0:T(1,128)} %bitcast.121, f32[16,8192]{1,0:T(8,128)} %reshape.701.basis_ref), custom_call_target="tpu_custom_call" | custom-call | tf_op jit(solution)/shard_map/pallas_call | solution.py:183
  85.7 0.8 slice_bitcast_fusion.1
  86.5 1.5 %multiply_reduce_fusion = (f32[]{:T(128)}, f32[640,256]{1,0:T(8,128)}) fusion(f32[640,256]{1,0:T(8,128)S(1)} %copy-done.1, f32[640,256]{1,0:T(8,128)S(1)} %copy-done.5, f32[]{:T(128)S(6)} %div.65), kind=kLoop, calls=%fused_computation.4 | loop fusion | flops 655359 | bytes 1966088 | tf_op jit(solution)/shard_map/reduce_sum | solution.py:251
  88.1 0.1 add_dynamic-update-slice_fusion
  88.2 0.1 fusion.15
  88.4 0.1 fusion.14
  88.5 0.7 pad_maximum_fusion.5
  89.2 0.7 broadcast_in_dim.19
  90.0 6.0 %all-to-all-start.3 = ((f32[32,1,1028]{2,1,0:T(1,128)}), f32[32,1,1028]{2,1,0:T(1,128)S(1)}, u32[]{:S(2)}, u32[]{:S(2)}) async-start(f32[32,1,1028]{2,1,0:T(1,128)} %broadcast_in_dim.19), calls=%async_computation.3 | async-start | bytes 294912 | tf_op jit(solution)/shard_map/all_to_all | solution.py:252
  96.0 8.2 %shard_map.109 = f32[1,8192]{1,0:T(1,128)} custom-call(f32[640,256]{1,0:T(8,128)} %get-tuple-element.134.tab_ref, s32[1,8192]{1,0:T(1,128)} %ids_ref.7, f32[5,8192]{1,0:T(8,128)} %bitcast.101), custom_call_target="tpu_custom_call" | custom-call | tf_op jit(solution)/shard_map/pallas_call | solution.py:89
  104.2 0.2 all-to-all-done.3
  104.5 0.7 slice_reduce_fusion.1
  105.3 0.4 scatter-add.49
  105.7 0.6 multiply_reduce_fusion.4
  107.9 0.7 multiply_add_fusion.1
  108.7 0.7 reshape.715.tab_ref
  109.5 3.9 %shard_map.110 = (f32[1,8192]{1,0:T(1,128)}, f32[1,1]{1,0:T(1,128)}) custom-call(f32[128,256]{1,0:T(8,128)} %reshape.715.tab_ref, s32[1,8192]{1,0:T(1,128)} %multiply_add_fusion.3.ids_ref, f32[4,8192]{1,0:T(4,128)} %pad_maximum_fusion.2.basis_ref, f32[1,8192]{1,0:T(1,128)} %get-tuple-element.168.zsrc_ref, f32[1,8192]{1,0:T(1,128)} %bitcast.116), custom_call_target="tpu_custom_call" | custom-call | tf_op jit(solution)/shard_map/pallas_call | solution.py:152
  113.4 1.5 %reduce.33 = f32[8192]{0:T(1024)S(1)} reduce(f32[1,8192]{1,0:T(1,128)} %get-tuple-element.129, f32[]{:T(128)} %broadcast.523), dimensions={0}, to_apply=%get-tuple-element.129.reduce_sub_computation.3 | reduce | bytes 65540 | tf_op jit(solution)/shard_map/pallas_call | solution.py:152
  114.9 0.7 concatenate.57
  115.6 0.7 all_to_all.40
  116.3 5.4 %all-to-all-start.4 = ((f32[32,1,257]{2,1,0:T(1,128)}), f32[32,1,257]{2,1,0:T(1,128)S(1)}, u32[]{:S(2)}, u32[]{:S(2)}) async-start(f32[32,1,257]{2,1,0:T(1,128)} %all_to_all.40), calls=%async_computation.4 | async-start | bytes 98304 | tf_op jit(solution)/shard_map/all_to_all | solution.py:270
  121.7 7.4 %all-to-all-done.4 = f32[32,1,257]{2,1,0:T(1,128)S(1)} async-done(((f32[32,1,257]{2,1,0:T(1,128)}), f32[32,1,257]{2,1,0:T(1,128)S(1)}, u32[]{:S(2)}, u32[]{:S(2)}) %all-to-all-start.4) | async-done | bytes 32928 | tf_op jit(solution)/shard_map/all_to_all | solution.py:270
  129.1 0.6 slice_reduce_fusion
  130.6 0.6 fusion.13
  131.3 1.2 reshape.716
  132.4 0.9 multiply_subtract_fusion.1
  (72 shorter events, 1.6 us)
Async XLA Ops:
  0.6 0.9 copy-start
  0.6 2.8 %copy-start.12 = (s32[1,32]{1,0:T(1,128)S(1)}, s32[1,32]{1,0:T(1,128)}, u32[]{:S(2)}) copy-start(s32[1,32]{1,0:T(1,128)} %param.34) | copy-start | bytes 388
  0.7 3.0 %copy-start.10 = (f32[8192]{0:T(1024)S(1)}, f32[8192]{0:T(1024)}, u32[]{:S(2)}) copy-start(f32[8192]{0:T(1024)} %param.33) | copy-start | bytes 98308
  0.7 3.0 %copy-start.9 = (f32[5,8192]{1,0:T(8,128)S(1)}, f32[5,8192]{1,0:T(8,128)}, u32[]{:S(2)}) copy-start(f32[5,8192]{1,0:T(8,128)} %param.29) | copy-start | bytes 491524
  5.3 21.7 %all-to-all-start = ((f32[9,32,256]{2,0,1:T(8,128)}), f32[9,32,256]{2,0,1:T(8,128)S(1)}, u32[]{:S(2)}, u32[]{:S(2)}) async-start(f32[9,32,256]{2,0,1:T(8,128)} %concatenate.51), calls=%async_computation | async-start | bytes 1048576 | tf_op jit(solution)/shard_map/all_to_all | solution.py:241
  28.5 10.7 %copy-start.2 = (f32[5,32,256]{2,0,1:T(8,128)}, f32[5,32,256]{2,0,1:T(8,128)S(1)}, u32[]{:S(2)}) copy-start(f32[5,32,256]{2,0,1:T(8,128)S(1)} %slice.316) | copy-start | bytes 491524
  40.7 13.1 %all-to-all-start.1 = ((f32[32,1,1028]{2,1,0:T(1,128)}), f32[32,1,1028]{2,1,0:T(1,128)S(1)}, u32[]{:S(2)}, u32[]{:S(2)}) async-start(f32[32,1,1028]{2,1,0:T(1,128)} %broadcast_in_dim.16), calls=%async_computation.1 | async-start | bytes 294912 | tf_op jit(solution)/shard_map/all_to_all | solution.py:252
  53.8 6.8 %copy-start.7 = (f32[1,32,256]{2,0,1:T(1,128)S(1)}, f32[1,32,256]{2,0,1:T(1,128)}, u32[]{:S(2)}) copy-start(f32[1,32,256]{2,0,1:T(1,128)} %get-tuple-element.136) | copy-start | bytes 98308
  53.8 15.5 %copy-start.3 = (f32[5,32,256]{2,0,1:T(8,128)S(1)}, f32[5,32,256]{2,0,1:T(8,128)}, u32[]{:S(2)}) copy-start(f32[5,32,256]{2,0,1:T(8,128)} %copy-done.2) | copy-start | bytes 491524
  63.5 16.7 %all-to-all-start.2 = ((f32[32,1,257]{2,1,0:T(1,128)}), f32[32,1,257]{2,1,0:T(1,128)S(1)}, u32[]{:S(2)}, u32[]{:S(2)}) async-start(f32[32,1,257]{2,1,0:T(1,128)} %all_to_all.35), calls=%async_computation.2 | async-start | bytes 98304 | tf_op jit(solution)/shard_map/all_to_all | solution.py:270
  70.1 16.5 %copy-start.1 = (f32[640,256]{1,0:T(8,128)S(1)}, f32[640,256]{1,0:T(8,128)}, u32[]{:S(2)}) copy-start(f32[640,256]{1,0:T(8,128)} %shard_map.104.tab_ref) | copy-start | bytes 1966084
  78.2 8.3 %copy-start.5 = (f32[640,256]{1,0:T(8,128)S(1)}, f32[640,256]{1,0:T(8,128)}, u32[]{:S(2)}) copy-start(f32[640,256]{1,0:T(8,128)} %shard_map.108) | copy-start | bytes 1966084
  90.0 14.5 %all-to-all-start.3 = ((f32[32,1,1028]{2,1,0:T(1,128)}), f32[32,1,1028]{2,1,0:T(1,128)S(1)}, u32[]{:S(2)}, u32[]{:S(2)}) async-start(f32[32,1,1028]{2,1,0:T(1,128)} %broadcast_in_dim.19), calls=%async_computation.3 | async-start | bytes 294912 | tf_op jit(solution)/shard_map/all_to_all | solution.py:252
  96.0 11.9 %copy-start.8 = (f32[1,8192]{1,0:T(1,128)S(1)}, f32[1,8192]{1,0:T(1,128)}, u32[]{:S(2)}) copy-start(f32[1,8192]{1,0:T(1,128)} %shard_map.105.zsrc_ref) | copy-start | bytes 98308
  104.2 3.7 %copy-start.11 = (f32[1,8192]{1,0:T(1,128)S(1)}, f32[1,8192]{1,0:T(1,128)}, u32[]{:S(2)}) copy-start(f32[1,8192]{1,0:T(1,128)} %shard_map.109) | copy-start | bytes 98308
  106.4 24.1 %copy-start.4 = (f32[640,256]{1,0:T(8,128)S(1)}, f32[640,256]{1,0:T(8,128)}, u32[]{:S(2)}) copy-start(f32[640,256]{1,0:T(8,128)} %get-tuple-element.134.tab_ref) | copy-start | bytes 1966084
  116.3 12.8 %all-to-all-start.4 = ((f32[32,1,257]{2,1,0:T(1,128)}), f32[32,1,257]{2,1,0:T(1,128)S(1)}, u32[]{:S(2)}, u32[]{:S(2)}) async-start(f32[32,1,257]{2,1,0:T(1,128)} %all_to_all.40), calls=%async_computation.4 | async-start | bytes 98304 | tf_op jit(solution)/shard_map/all_to_all | solution.py:270
  130.6 1.8 %copy-start.6 = (f32[12,8192]{1,0:T(8,128)S(1)}, f32[12,8192]{1,0:T(8,128)}, u32[]{:S(2)}) copy-start(f32[12,8192]{1,0:T(8,128)} %param.28) | copy-start | bytes 1179652

commit v6 on v5

--- a/solution.py
+++ b/solution.py
@@ -9,7 +9,7 @@
 KN = 1024
 ITERS = 2
 HI = 256
-CHUNK = 2048
+CHUNK = 4096
 
 
 def passed_along(block, axis, distance):
@@ -247,8 +247,8 @@
     base_own = ((slot_device // n_share) * knots + got[n_params + 3].astype(jnp.int32)).reshape(1, rows)
     table_rows = n_params * (owned // HI)
 
-    def combine(part_a, grad_s):
-        mine = jnp.concatenate([part_a, jnp.sum(grad_s * grad_s)[None]])
+    def combine(part_a, s_norm):
+        mine = jnp.concatenate([part_a, s_norm[None]])
         every = lax.all_to_all(
             jnp.broadcast_to(mine[None, :], (n_ranks, knots + 4)), everyone, 0, 0, tiled=True
         )
@@ -258,28 +258,35 @@
         norm = jnp.sum(every[:, knots + 3]) + jnp.sum(grad_a * grad_a)
         return grad_a, norm
 
-    def forward(zsrc, dir_a):
+    def forward(zsrc, dir_a, extra):
         extended = jnp.concatenate([dir_a, jnp.zeros((3,), jnp.float32)])
         shift_own, partial = knot_gather(
             extended, base_own, basis_own, zsrc, weight_sq_own.reshape(1, rows), n_knots
         )
         shift_own = shift_own.reshape(rows)
+        sums = jnp.concatenate([partial.reshape(1), extra.reshape(1)])
         payload = jnp.concatenate(
-            [shift_own.reshape(n_ranks, capacity), jnp.broadcast_to(partial, (n_ranks, 1))], axis=1
+            [shift_own.reshape(n_ranks, capacity), jnp.broadcast_to(sums[None, :], (n_ranks, 2))], axis=1
         )
         back = lax.all_to_all(payload, everyone, 0, 0, tiled=True)
-        return shift_own, back[:, :capacity].reshape(rows) * live, jnp.sum(back[:, capacity])
+        totals = jnp.sum(back[:, capacity:], axis=0)
+        return shift_own, back[:, :capacity].reshape(rows) * live, totals[0], totals[1]
 
     sol_s = jnp.zeros((table_rows, HI), jnp.float32)
     sol_a = jnp.zeros((n_knots,), jnp.float32)
     resid = observed_residual
     zbar_slot = zbar0
+    part_a = knot_scatter(zbar_slot.reshape(1, rows), first_ids, basis16, knots)
+    part_a, held, zbar0_own = lax.optimization_barrier((part_a, held, zbar0_own))
+    grad_a, gamma_a = combine(part_a, jnp.zeros((), jnp.float32))
     grad_s = source_scatter(held * zbar0_own[None, :], ids, owned)
-    grad_a, gamma = combine(knot_scatter(zbar_slot.reshape(1, rows), first_ids, basis16, knots), grad_s)
+    extra = jnp.sum(grad_s * grad_s)
     dir_s, dir_a = (grad_s, grad_a)
     pulled = source_gather(dir_s, ids, held)
     for step in range(ITERS):
-        shift_own, shift_slot, image_sq = forward(pulled, dir_a)
+        shift_own, shift_slot, image_sq, extra_sum = forward(pulled, dir_a, extra)
+        if step == 0:
+            gamma = extra_sum + gamma_a
         alpha = gamma / image_sq
         sol_s = sol_s + alpha * dir_s
         sol_a = sol_a + alpha * dir_a
@@ -289,7 +296,8 @@
             zbar_slot = zbar_slot - alpha * (weight_sq * shift_slot)
             grad_s = grad_s - alpha * pushed
             grad_a, fresh = combine(
-                knot_scatter(zbar_slot.reshape(1, rows), first_ids, basis16, knots), grad_s
+                knot_scatter(zbar_slot.reshape(1, rows), first_ids, basis16, knots),
+                jnp.sum(grad_s * grad_s),
             )
             raw = source_gather(grad_s, ids, held)
             beta = fresh / gamma
@@ -297,6 +305,7 @@
             dir_a = grad_a + beta * dir_a
             pulled = raw + beta * pulled
             gamma = fresh
+            extra = jnp.zeros((), jnp.float32)
     mine_a = lax.dynamic_slice(sol_a, (lax.axis_index("tm") * knots,), (knots,))
     return (sol_s.reshape(n_params, owned), mine_a, resid)
 

time: 134 us -> 131 us (0.978)
  Pallas kernels: 47.2 us -> 44.8 us
    reduce_sum x4, other arithmetic: 4.61 us -> 2.38 us  [the longest x1 1.54 us: per_device(): jnp.sum(grad_s * grad_s)]
    concatenate x2 -> x6, other arithmetic: 1.44 us -> 2.89 us  [the longest x2 2.08 us: forward(): sums = jnp.concatenate([partial.reshape(1), extra.reshape(1)])]
  transfers between devices with their start and end apart: 5 -> 5, of which waited for: 3 -> 3; matrix products, arithmetic and copies ran while one was open for 4% -> 5% of each run, Pallas kernels for 21% -> 26%
where the time goes in v6:
time: 131 us; the launch traced here: 130 us
  Pallas kernels  44.8 us (34%)
  starting transfers between devices  28.1 us (21%)
  other arithmetic  20.9 us (16%)
  waiting for transfers between devices  16.1 us (12%)
  local copies, waits for them, and re-layouts  12.3 us (9%)
  between operations  5.26 us (4%)
  matrix products  2 us (2%)
    pallas_call x2, Pallas kernels, source_gather(): pl.pallas_call(kernel, out_shape=jax.ShapeDtypeStruct((1, total), jnp.flo...  15.8 us
    pallas_call x2, Pallas kernels, source_scatter(): pl.pallas_call(kernel, out_shape=jax.ShapeDtypeStruct((rows, HI), jnp.flo...  15.3 us
    all_to_all x2, starting transfers between devices, forward(): back = lax.all_to_all(payload, everyone, 0, 0, tiled=True)  11.1 us
    all_to_all x2, starting transfers between devices, combine(): lax.all_to_all(jnp.broadcast_to(mine[None, :], (n_ranks, knots + 4)), eve...  9.74 us
    all_to_all x1, waiting for transfers between devices, per_device(): lax.all_to_all(packed, everyone, split_axis=1, concat_axis=1, tiled=True)  7.97 us
    pallas_call x2, Pallas kernels, knot_gather(): pl.pallas_call(kernel, out_shape=(jax.ShapeDtypeStruct((1, total), jnp.fl...  7.53 us
    all_to_all x2, waiting for transfers between devices, forward(): back = lax.all_to_all(payload, everyone, 0, 0, tiled=True)  7.37 us
    all_to_all x1, starting transfers between devices, per_device(): lax.all_to_all(packed, everyone, split_axis=1, concat_axis=1, tiled=True)  7.3 us
  transfers between devices with their start and end apart: 5, of which 3 were waited for; matrix products, arithmetic and copies ran while one was open for 5% of the time, Pallas kernels for 26%

profile of v6, /device:TPU:0, one launch (start us, length us, event | category | flops | bytes accessed | tf_op | source)
XLA Modules:
  0.0 129.6 jit_solution(1185072145829804769)
XLA Ops:
  0.7 0.8 convert_element_type.26
  1.5 2.0 %multiply_reduce_fusion.2 = (f32[8192]{0:T(1024)S(1)}, f32[8192]{0:T(1024)S(1)}, f32[12,8192]{1,0:T(8,128)S(1)}) fusion(f32[12,8192]{1,0:T(8,128)} %param.28, f32[12,62]{1,0:T(8,128)S(1)} %copy-done, s32[8192]{0:T(1024)} %param.31), kind=kOutput, calls=%fused_computation.8 | convolution fusion | flops 74022912 | bytes 887712 | tf_op jit(solution)/shard_map/dot_general | solution.py:219
  3.6 1.6 %concatenate.57 = f32[9,32,256]{2,0,1:T(8,128)} concatenate(f32[5,32,256]{2,0,1:T(8,128)S(1)} %bitcast.130, f32[1,32,256]{2,0,1:T(1,128)S(1)} %get-tuple-element.174, f32[1,32,256]{2,0,1:T(1,128)S(1)} %get-tuple-element.173, f32[1,32,256]{2,0,1:T(1,128)S(1)} %bitcast.137, f32[1,32,256]{2,0,1:T(1,128)S(1)} %bitcast.140), dimensions={0} | concatenate | bytes 589824 | tf_op jit(solution)/shard_map/concatenate | solution.py:231
  5.3 7.3 %all-to-all-start = ((f32[9,32,256]{2,0,1:T(8,128)}), f32[9,32,256]{2,0,1:T(8,128)S(1)}, u32[]{:S(2)}, u32[]{:S(2)}) async-start(f32[9,32,256]{2,0,1:T(8,128)} %concatenate.57), calls=%async_computation | async-start | bytes 1048576 | tf_op jit(solution)/shard_map/all_to_all | solution.py:241
  12.7 0.1 pad_maximum_fusion
  12.9 1.0 reshape.709.basis_ref
  13.9 0.7 broadcast_select_fusion.val_ref
  14.6 3.1 %shard_map.103 = f32[16,256]{1,0:T(8,128)} custom-call(f32[1,8192]{1,0:T(1,128)} %broadcast_select_fusion.val_ref, s32[1,8192]{1,0:T(1,128)} %bitcast.124, f32[16,8192]{1,0:T(8,128)} %reshape.709.basis_ref), custom_call_target="tpu_custom_call" | custom-call | tf_op jit(solution)/shard_map/pallas_call | solution.py:183
  17.7 0.8 slice_bitcast_fusion.5
  18.5 0.1 add_dynamic-update-slice_fusion.1
  18.7 0.1 fusion.17
  18.8 0.1 fusion.16
  19.0 8.0 %all-to-all-done = f32[9,32,256]{2,0,1:T(8,128)S(1)} async-done(((f32[9,32,256]{2,0,1:T(8,128)}), f32[9,32,256]{2,0,1:T(8,128)S(1)}, u32[]{:S(2)}, u32[]{:S(2)}) %all-to-all-start) | async-done | bytes 294944 | tf_op jit(solution)/shard_map/all_to_all | solution.py:241
  26.9 0.7 fusion.18
  27.7 0.7 multiply_add_fusion.3.ids_ref
  28.4 0.2 fusion.9
  28.6 0.7 broadcast_in_dim.13
  29.4 4.1 %all-to-all-start.1 = ((f32[32,1,1028]{2,1,0:T(1,128)}), f32[32,1,1028]{2,1,0:T(1,128)S(1)}, u32[]{:S(2)}, u32[]{:S(2)}) async-start(f32[32,1,1028]{2,1,0:T(1,128)} %broadcast_in_dim.13), calls=%async_computation.1 | async-start | bytes 294912 | tf_op jit(solution)/shard_map/all_to_all | solution.py:252
  33.5 0.7 broadcast_multiply_fusion.1.val_ref
  34.2 0.8 pad_maximum_fusion.2.basis_ref
  35.0 7.6 %shard_map.104.tab_ref = f32[640,256]{1,0:T(8,128)} custom-call(f32[5,8192]{1,0:T(8,128)} %broadcast_multiply_fusion.1.val_ref, s32[1,8192]{1,0:T(1,128)} %ids_ref.7), custom_call_target="tpu_custom_call" | custom-call | tf_op jit(solution)/shard_map/pallas_call | solution.py:121
  42.6 7.9 %shard_map.105.zsrc_ref = f32[1,8192]{1,0:T(1,128)} custom-call(f32[640,256]{1,0:T(8,128)} %shard_map.104.tab_ref, s32[1,8192]{1,0:T(1,128)} %ids_ref.7, f32[5,8192]{1,0:T(8,128)} %bitcast.104), custom_call_target="tpu_custom_call" | custom-call | tf_op jit(solution)/shard_map/pallas_call | solution.py:89
  50.6 0.8 multiply_reduce_fusion.1
  51.6 0.4 scatter-add.40
  52.0 0.6 multiply_reduce_fusion.5
  52.8 0.1 pad_maximum_fusion.1
  52.9 0.7 reshape.715.tab_ref
  53.7 3.8 %shard_map.106 = (f32[1,8192]{1,0:T(1,128)}, f32[1,1]{1,0:T(1,128)}) custom-call(f32[128,256]{1,0:T(8,128)} %reshape.715.tab_ref, s32[1,8192]{1,0:T(1,128)} %multiply_add_fusion.3.ids_ref, f32[4,8192]{1,0:T(4,128)} %pad_maximum_fusion.2.basis_ref, f32[1,8192]{1,0:T(1,128)} %shard_map.105.zsrc_ref, f32[1,8192]{1,0:T(1,128)} %bitcast.119), custom_call_target="tpu_custom_call" | custom-call | tf_op jit(solution)/shard_map/pallas_call | solution.py:152
  57.4 0.6 broadcast.524
  58.0 1.5 %fusion.19 = (f32[8192]{0:T(1024)S(1)}, f32[1,8192]{1,0:T(1,128)S(1)}) fusion(f32[1,8192]{1,0:T(1,128)} %get-tuple-element.133, f32[]{:T(128)} %broadcast.524, f32[1,8192]{1,0:T(1,128)S(1)} %bitcast.121), kind=kLoop, calls=%fused_computation.105 | loop fusion | flops 8192 | bytes 131076 | tf_op jit(solution)/shard_map/pallas_call | solution.py:152
  59.5 1.4 %pad_maximum_fusion.9 = f32[258]{0:T(512)S(1)} fusion(f32[1]{0:T(128)} %bitcast.22, f32[1]{0:T(128)} %bitcast.21), kind=kLoop, calls=%fused_computation.103 | loop fusion | flops 258 | bytes 1040 | tf_op jit(solution)/shard_map/concatenate | solution.py:267
  60.9 0.7 all_to_all.35
  61.5 6.0 %all-to-all-start.2 = ((f32[32,1,258]{2,1,0:T(1,128)}), f32[32,1,258]{2,1,0:T(1,128)S(1)}, u32[]{:S(2)}, u32[]{:S(2)}) async-start(f32[32,1,258]{2,1,0:T(1,128)} %all_to_all.35), calls=%async_computation.2 | async-start | bytes 98304 | tf_op jit(solution)/shard_map/all_to_all | solution.py:271
  67.6 0.7 broadcast_multiply_fusion.val_ref
  68.3 7.6 %shard_map.108 = f32[640,256]{1,0:T(8,128)} custom-call(f32[5,8192]{1,0:T(8,128)} %broadcast_multiply_fusion.val_ref, s32[1,8192]{1,0:T(1,128)} %ids_ref.7), custom_call_target="tpu_custom_call" | custom-call | tf_op jit(solution)/shard_map/pallas_call | solution.py:121
  76.0 0.7 slice_reduce_fusion.2
  78.0 0.6 fusion.20
  80.0 0.7 multiply_subtract_fusion.2.val_ref
  80.7 3.1 %shard_map.107 = f32[16,256]{1,0:T(8,128)} custom-call(f32[1,8192]{1,0:T(1,128)} %multiply_subtract_fusion.2.val_ref, s32[1,8192]{1,0:T(1,128)} %bitcast.125, f32[16,8192]{1,0:T(8,128)} %reshape.709.basis_ref), custom_call_target="tpu_custom_call" | custom-call | tf_op jit(solution)/shard_map/pallas_call | solution.py:183
  83.8 0.8 slice_bitcast_fusion.1
  84.7 1.5 %multiply_reduce_fusion = (f32[]{:T(128)}, f32[640,256]{1,0:T(8,128)}) fusion(f32[640,256]{1,0:T(8,128)S(1)} %copy-done.1, f32[640,256]{1,0:T(8,128)S(1)} %copy-done.5, f32[]{:T(128)S(6)} %div.65), kind=kLoop, calls=%fused_computation.4 | loop fusion | flops 655359 | bytes 1966088 | tf_op jit(solution)/shard_map/reduce_sum | solution.py:300
  86.2 0.1 add_dynamic-update-slice_fusion
  86.3 0.1 fusion.15
  86.5 0.1 fusion.14
  86.6 0.7 pad_maximum_fusion.7
  87.4 0.7 broadcast_in_dim.16
  88.1 5.7 %all-to-all-start.3 = ((f32[32,1,1028]{2,1,0:T(1,128)}), f32[32,1,1028]{2,1,0:T(1,128)S(1)}, u32[]{:S(2)}, u32[]{:S(2)}) async-start(f32[32,1,1028]{2,1,0:T(1,128)} %broadcast_in_dim.16), calls=%async_computation.3 | async-start | bytes 294912 | tf_op jit(solution)/shard_map/all_to_all | solution.py:252
  93.8 7.9 %shard_map.109 = f32[1,8192]{1,0:T(1,128)} custom-call(f32[640,256]{1,0:T(8,128)} %get-tuple-element.140.tab_ref, s32[1,8192]{1,0:T(1,128)} %ids_ref.7, f32[5,8192]{1,0:T(8,128)} %bitcast.105), custom_call_target="tpu_custom_call" | custom-call | tf_op jit(solution)/shard_map/pallas_call | solution.py:89
  101.6 0.8 all-to-all-done.3
  102.4 0.7 slice_reduce_fusion.1
  103.3 0.4 scatter-add.49
  103.7 0.6 multiply_reduce_fusion.4
  105.9 0.7 multiply_add_fusion.1
  106.6 0.1 pad_maximum_fusion.3
  106.7 0.7 reshape.725.tab_ref
  107.4 3.8 %shard_map.110 = (f32[1,8192]{1,0:T(1,128)}, f32[1,1]{1,0:T(1,128)}) custom-call(f32[128,256]{1,0:T(8,128)} %reshape.725.tab_ref, s32[1,8192]{1,0:T(1,128)} %multiply_add_fusion.3.ids_ref, f32[4,8192]{1,0:T(4,128)} %pad_maximum_fusion.2.basis_ref, f32[1,8192]{1,0:T(1,128)} %get-tuple-element.176.zsrc_ref, f32[1,8192]{1,0:T(1,128)} %bitcast.120), custom_call_target="tpu_custom_call" | custom-call | tf_op jit(solution)/shard_map/pallas_call | solution.py:152
  111.2 1.5 %reduce.31 = f32[8192]{0:T(1024)S(1)} reduce(f32[1,8192]{1,0:T(1,128)} %get-tuple-element.135, f32[]{:T(128)} %broadcast.524), dimensions={0}, to_apply=%get-tuple-element.135.reduce_sub_computation.3 | reduce | bytes 65540 | tf_op jit(solution)/shard_map/pallas_call | solution.py:152
  112.7 0.7 pad_maximum_fusion.8
  113.4 0.7 all_to_all.40
  114.1 5.1 %all-to-all-start.4 = ((f32[32,1,258]{2,1,0:T(1,128)}), f32[32,1,258]{2,1,0:T(1,128)S(1)}, u32[]{:S(2)}, u32[]{:S(2)}) async-start(f32[32,1,258]{2,1,0:T(1,128)} %all_to_all.40), calls=%async_computation.4 | async-start | bytes 98304 | tf_op jit(solution)/shard_map/all_to_all | solution.py:271
  119.2 7.4 %all-to-all-done.4 = f32[32,1,258]{2,1,0:T(1,128)S(1)} async-done(((f32[32,1,258]{2,1,0:T(1,128)}), f32[32,1,258]{2,1,0:T(1,128)S(1)}, u32[]{:S(2)}, u32[]{:S(2)}) %all-to-all-start.4) | async-done | bytes 33056 | tf_op jit(solution)/shard_map/all_to_all | solution.py:271
  126.9 0.6 fusion.13
  127.5 1.2 reshape.727
  128.7 0.9 multiply_subtract_fusion.1
  (75 shorter events, 1.5 us)
Async XLA Ops:
  0.6 0.9 copy-start
  0.6 2.8 %copy-start.12 = (s32[1,32]{1,0:T(1,128)S(1)}, s32[1,32]{1,0:T(1,128)}, u32[]{:S(2)}) copy-start(s32[1,32]{1,0:T(1,128)} %param.34) | copy-start | bytes 388
  0.7 3.0 %copy-start.10 = (f32[8192]{0:T(1024)S(1)}, f32[8192]{0:T(1024)}, u32[]{:S(2)}) copy-start(f32[8192]{0:T(1024)} %param.33) | copy-start | bytes 98308
  0.7 3.0 %copy-start.9 = (f32[5,8192]{1,0:T(8,128)S(1)}, f32[5,8192]{1,0:T(8,128)}, u32[]{:S(2)}) copy-start(f32[5,8192]{1,0:T(8,128)} %param.29) | copy-start | bytes 491524
  5.3 21.7 %all-to-all-start = ((f32[9,32,256]{2,0,1:T(8,128)}), f32[9,32,256]{2,0,1:T(8,128)S(1)}, u32[]{:S(2)}, u32[]{:S(2)}) async-start(f32[9,32,256]{2,0,1:T(8,128)} %concatenate.57), calls=%async_computation | async-start | bytes 1048576 | tf_op jit(solution)/shard_map/all_to_all | solution.py:241
  27.7 15.0 %copy-start.2 = (f32[5,32,256]{2,0,1:T(8,128)}, f32[5,32,256]{2,0,1:T(8,128)S(1)}, u32[]{:S(2)}) copy-start(f32[5,32,256]{2,0,1:T(8,128)S(1)} %slice.328) | copy-start | bytes 491524
  29.4 22.0 %all-to-all-start.1 = ((f32[32,1,1028]{2,1,0:T(1,128)}), f32[32,1,1028]{2,1,0:T(1,128)S(1)}, u32[]{:S(2)}, u32[]{:S(2)}) async-start(f32[32,1,1028]{2,1,0:T(1,128)} %broadcast_in_dim.13), calls=%async_computation.1 | async-start | bytes 294912 | tf_op jit(solution)/shard_map/all_to_all | solution.py:252
  42.6 7.9 %copy-start.1 = (f32[640,256]{1,0:T(8,128)S(1)}, f32[640,256]{1,0:T(8,128)}, u32[]{:S(2)}) copy-start(f32[640,256]{1,0:T(8,128)} %shard_map.104.tab_ref) | copy-start | bytes 1966084
  51.4 6.6 %copy-start.7 = (f32[1,32,256]{2,0,1:T(1,128)S(1)}, f32[1,32,256]{2,0,1:T(1,128)}, u32[]{:S(2)}) copy-start(f32[1,32,256]{2,0,1:T(1,128)} %get-tuple-element.142) | copy-start | bytes 98308
  51.4 16.1 %copy-start.3 = (f32[5,32,256]{2,0,1:T(8,128)S(1)}, f32[5,32,256]{2,0,1:T(8,128)}, u32[]{:S(2)}) copy-start(f32[5,32,256]{2,0,1:T(8,128)} %copy-done.2) | copy-start | bytes 491524
  61.5 16.4 %all-to-all-start.2 = ((f32[32,1,258]{2,1,0:T(1,128)}), f32[32,1,258]{2,1,0:T(1,128)S(1)}, u32[]{:S(2)}, u32[]{:S(2)}) async-start(f32[32,1,258]{2,1,0:T(1,128)} %all_to_all.35), calls=%async_computation.2 | async-start | bytes 98304 | tf_op jit(solution)/shard_map/all_to_all | solution.py:271
  76.0 8.7 %copy-start.5 = (f32[640,256]{1,0:T(8,128)S(1)}, f32[640,256]{1,0:T(8,128)}, u32[]{:S(2)}) copy-start(f32[640,256]{1,0:T(8,128)} %shard_map.108) | copy-start | bytes 1966084
  88.1 14.3 %all-to-all-start.3 = ((f32[32,1,1028]{2,1,0:T(1,128)}), f32[32,1,1028]{2,1,0:T(1,128)S(1)}, u32[]{:S(2)}, u32[]{:S(2)}) async-start(f32[32,1,1028]{2,1,0:T(1,128)} %broadcast_in_dim.16), calls=%async_computation.3 | async-start | bytes 294912 | tf_op jit(solution)/shard_map/all_to_all | solution.py:252
  93.8 12.1 %copy-start.8 = (f32[1,8192]{1,0:T(1,128)S(1)}, f32[1,8192]{1,0:T(1,128)}, u32[]{:S(2)}) copy-start(f32[1,8192]{1,0:T(1,128)} %shard_map.105.zsrc_ref) | copy-start | bytes 98308
  101.6 4.2 %copy-start.11 = (f32[1,8192]{1,0:T(1,128)S(1)}, f32[1,8192]{1,0:T(1,128)}, u32[]{:S(2)}) copy-start(f32[1,8192]{1,0:T(1,128)} %shard_map.109) | copy-start | bytes 98308
  104.3 22.4 %copy-start.4 = (f32[640,256]{1,0:T(8,128)S(1)}, f32[640,256]{1,0:T(8,128)}, u32[]{:S(2)}) copy-start(f32[640,256]{1,0:T(8,128)} %get-tuple-element.140.tab_ref) | copy-start | bytes 1966084
  114.1 12.5 %all-to-all-start.4 = ((f32[32,1,258]{2,1,0:T(1,128)}), f32[32,1,258]{2,1,0:T(1,128)S(1)}, u32[]{:S(2)}, u32[]{:S(2)}) async-start(f32[32,1,258]{2,1,0:T(1,128)} %all_to_all.40), calls=%async_computation.4 | async-start | bytes 98304 | tf_op jit(solution)/shard_map/all_to_all | solution.py:271
  126.9 1.8 %copy-start.6 = (f32[12,8192]{1,0:T(8,128)S(1)}, f32[12,8192]{1,0:T(8,128)}, u32[]{:S(2)}) copy-start(f32[12,8192]{1,0:T(8,128)} %param.28) | copy-start | bytes 1179652

commit v7 on v6

--- a/solution.py
+++ b/solution.py
@@ -238,7 +238,10 @@
         ],
         axis=0,
     )
-    got = lax.all_to_all(packed, everyone, split_axis=1, concat_axis=1, tiled=True)
+    n_rows = packed.shape[0]
+    blocks = packed.reshape(n_rows, n_ranks, capacity).transpose(1, 0, 2).reshape(n_ranks, n_rows * capacity)
+    got = lax.all_to_all(blocks, everyone, 0, 0, tiled=True)
+    got = got.reshape(n_ranks, n_rows, capacity).transpose(1, 0, 2).reshape(n_rows, rows)
     held = got[:n_params]
     zbar0_own = got[n_params]
     weight_sq_own = got[n_params + 1]

time: 131 us -> 126 us (0.962)
  waiting for transfers between devices: 16.1 us -> 12.3 us
    all_to_all x1, waiting for transfers between devices: 7.97 us -> 4.2 us  [per_device(): got = lax.all_to_all(blocks, everyone, 0, 0, tiled=True)]
    concatenate x1, local copies, waits for them, and re-layouts: 1.61 us -> 0.23 us  [per_device(): jnp.concatenate([source_partials, zbar0[None], weight_sq[None], interval_...]
  transfers between devices with their start and end apart: 5 -> 5, of which waited for: 3 -> 3; matrix products, arithmetic and copies ran while one was open for 5% -> 6% of each run, Pallas kernels for 26% -> 27%
where the time goes in v7:
time: 126 us; the launch traced here: 125 us
  Pallas kernels  44.8 us (36%)
  starting transfers between devices  27.1 us (22%)
  other arithmetic  21.4 us (17%)
  waiting for transfers between devices  12.3 us (10%)
  local copies, waits for them, and re-layouts  12 us (10%)
  between operations  5.11 us (4%)
  matrix products  2 us (2%)
    pallas_call x2, Pallas kernels, source_gather(): pl.pallas_call(kernel, out_shape=jax.ShapeDtypeStruct((1, total), jnp.flo...  15.8 us
    pallas_call x2, Pallas kernels, source_scatter(): pl.pallas_call(kernel, out_shape=jax.ShapeDtypeStruct((rows, HI), jnp.flo...  15.3 us
    all_to_all x2, starting transfers between devices, forward(): back = lax.all_to_all(payload, everyone, 0, 0, tiled=True)  11.1 us
    all_to_all x2, starting transfers between devices, combine(): lax.all_to_all(jnp.broadcast_to(mine[None, :], (n_ranks, knots + 4)), eve...  8.68 us
    pallas_call x2, Pallas kernels, knot_gather(): pl.pallas_call(kernel, out_shape=(jax.ShapeDtypeStruct((1, total), jnp.fl...  7.52 us
    all_to_all x2, waiting for transfers between devices, forward(): back = lax.all_to_all(payload, everyone, 0, 0, tiled=True)  7.37 us
    all_to_all x1, starting transfers between devices, per_device(): got = lax.all_to_all(blocks, everyone, 0, 0, tiled=True)  7.3 us
    pallas_call x2, Pallas kernels, knot_scatter(): pl.pallas_call(kernel, out_shape=jax.ShapeDtypeStruct((rows, HI), jnp.flo...  6.23 us
  transfers between devices with their start and end apart: 5, of which 3 were waited for; matrix products, arithmetic and copies ran while one was open for 6% of the time, Pallas kernels for 27%

profile of v7, /device:TPU:0, one launch (start us, length us, event | category | flops | bytes accessed | tf_op | source)
XLA Modules:
  0.0 124.7 jit_solution(10107362757601680615)
XLA Ops:
  0.7 0.8 convert_element_type.26
  1.5 2.0 %multiply_reduce_fusion.2 = (f32[8192]{0:T(1024)S(1)}, f32[8192]{0:T(1024)S(1)}, f32[12,8192]{1,0:T(8,128)S(1)}) fusion(f32[12,8192]{1,0:T(8,128)} %param.28, f32[12,62]{1,0:T(8,128)S(1)} %copy-done, s32[8192]{0:T(1024)} %param.31), kind=kOutput, calls=%fused_computation.8 | convolution fusion | flops 74022912 | bytes 887712 | tf_op jit(solution)/shard_map/dot_general | solution.py:219
  3.6 0.2 concatenate.57
  3.9 1.0 all_to_all.46
  4.9 7.3 %all-to-all-start = ((f32[32,1,2304]{2,1,0:T(1,128)}), f32[32,1,2304]{2,1,0:T(1,128)S(1)}, u32[]{:S(2)}, u32[]{:S(2)}) async-start(f32[32,1,2304]{2,1,0:T(1,128)} %all_to_all.46), calls=%async_computation | async-start | bytes 589824 | tf_op jit(solution)/shard_map/all_to_all | solution.py:243
  12.6 1.0 reshape.726.basis_ref
  13.6 0.7 broadcast_select_fusion.val_ref
  14.2 3.1 %shard_map.103 = f32[16,256]{1,0:T(8,128)} custom-call(f32[1,8192]{1,0:T(1,128)} %broadcast_select_fusion.val_ref, s32[1,8192]{1,0:T(1,128)} %bitcast.129, f32[16,8192]{1,0:T(8,128)} %reshape.726.basis_ref), custom_call_target="tpu_custom_call" | custom-call | tf_op jit(solution)/shard_map/pallas_call | solution.py:183
  17.3 0.8 slice_bitcast_fusion.5
  18.2 0.1 add_dynamic-update-slice_fusion.1
  18.3 0.1 fusion.17
  18.5 0.1 fusion.16
  18.6 4.2 %all-to-all-done = f32[32,1,2304]{2,1,0:T(1,128)S(1)} async-done(((f32[32,1,2304]{2,1,0:T(1,128)}), f32[32,1,2304]{2,1,0:T(1,128)S(1)}, u32[]{:S(2)}, u32[]{:S(2)}) %all-to-all-start) | async-done | bytes 294944 | tf_op jit(solution)/shard_map/all_to_all | solution.py:243
  22.8 0.7 reduce.24
  23.6 0.7 fusion.18
  24.3 0.7 multiply_add_fusion.3.ids_ref
  25.0 0.2 fusion.9
  25.3 0.7 broadcast_in_dim.13
  26.0 3.0 %all-to-all-start.1 = ((f32[32,1,1028]{2,1,0:T(1,128)}), f32[32,1,1028]{2,1,0:T(1,128)S(1)}, u32[]{:S(2)}, u32[]{:S(2)}) async-start(f32[32,1,1028]{2,1,0:T(1,128)} %broadcast_in_dim.13), calls=%async_computation.1 | async-start | bytes 294912 | tf_op jit(solution)/shard_map/all_to_all | solution.py:255
  29.0 0.7 broadcast_multiply_fusion.1.val_ref
  29.8 0.8 pad_maximum_fusion.2.basis_ref
  30.6 7.6 %shard_map.104.tab_ref = f32[640,256]{1,0:T(8,128)} custom-call(f32[5,8192]{1,0:T(8,128)} %broadcast_multiply_fusion.1.val_ref, s32[1,8192]{1,0:T(1,128)} %ids_ref.7), custom_call_target="tpu_custom_call" | custom-call | tf_op jit(solution)/shard_map/pallas_call | solution.py:121
  38.2 7.9 %shard_map.105.zsrc_ref = f32[1,8192]{1,0:T(1,128)} custom-call(f32[640,256]{1,0:T(8,128)} %shard_map.104.tab_ref, s32[1,8192]{1,0:T(1,128)} %ids_ref.7, f32[5,8192]{1,0:T(8,128)} %bitcast.106), custom_call_target="tpu_custom_call" | custom-call | tf_op jit(solution)/shard_map/pallas_call | solution.py:89
  46.1 0.7 multiply_reduce_fusion.1
  47.1 0.4 scatter-add.40
  47.5 0.6 multiply_reduce_fusion.5
  48.3 0.1 pad_maximum_fusion.1
  48.4 0.7 reshape.733.tab_ref
  49.1 3.8 %shard_map.106 = (f32[1,8192]{1,0:T(1,128)}, f32[1,1]{1,0:T(1,128)}) custom-call(f32[128,256]{1,0:T(8,128)} %reshape.733.tab_ref, s32[1,8192]{1,0:T(1,128)} %multiply_add_fusion.3.ids_ref, f32[4,8192]{1,0:T(4,128)} %pad_maximum_fusion.2.basis_ref, f32[1,8192]{1,0:T(1,128)} %shard_map.105.zsrc_ref, f32[1,8192]{1,0:T(1,128)} %bitcast.124), custom_call_target="tpu_custom_call" | custom-call | tf_op jit(solution)/shard_map/pallas_call | solution.py:152
  52.9 0.5 broadcast.525
  53.5 1.5 %fusion.19 = (f32[8192]{0:T(1024)S(1)}, f32[1,8192]{1,0:T(1,128)S(1)}) fusion(f32[1,8192]{1,0:T(1,128)} %get-tuple-element.133, f32[]{:T(128)} %broadcast.525, f32[1,8192]{1,0:T(1,128)S(1)} %bitcast.126), kind=kLoop, calls=%fused_computation.105 | loop fusion | flops 8192 | bytes 131076 | tf_op jit(solution)/shard_map/pallas_call | solution.py:152
  54.9 1.3 %pad_maximum_fusion.9 = f32[258]{0:T(512)S(1)} fusion(f32[1]{0:T(128)} %bitcast.24, f32[1]{0:T(128)} %bitcast.23), kind=kLoop, calls=%fused_computation.103 | loop fusion | flops 258 | bytes 1040 | tf_op jit(solution)/shard_map/concatenate | solution.py:270
  56.2 0.7 all_to_all.38
  56.9 6.0 %all-to-all-start.2 = ((f32[32,1,258]{2,1,0:T(1,128)}), f32[32,1,258]{2,1,0:T(1,128)S(1)}, u32[]{:S(2)}, u32[]{:S(2)}) async-start(f32[32,1,258]{2,1,0:T(1,128)} %all_to_all.38), calls=%async_computation.2 | async-start | bytes 98304 | tf_op jit(solution)/shard_map/all_to_all | solution.py:274
  62.9 0.7 broadcast_multiply_fusion.val_ref
  63.6 7.6 %shard_map.108 = f32[640,256]{1,0:T(8,128)} custom-call(f32[5,8192]{1,0:T(8,128)} %broadcast_multiply_fusion.val_ref, s32[1,8192]{1,0:T(1,128)} %ids_ref.7), custom_call_target="tpu_custom_call" | custom-call | tf_op jit(solution)/shard_map/pallas_call | solution.py:121
  71.3 0.7 slice_reduce_fusion.2
  73.3 0.6 fusion.20
  75.1 0.7 multiply_subtract_fusion.2.val_ref
  75.8 3.1 %shard_map.107 = f32[16,256]{1,0:T(8,128)} custom-call(f32[1,8192]{1,0:T(1,128)} %multiply_subtract_fusion.2.val_ref, s32[1,8192]{1,0:T(1,128)} %bitcast.130, f32[16,8192]{1,0:T(8,128)} %reshape.726.basis_ref), custom_call_target="tpu_custom_call" | custom-call | tf_op jit(solution)/shard_map/pallas_call | solution.py:183
  79.0 0.8 slice_bitcast_fusion.1
  79.8 1.5 %multiply_reduce_fusion = (f32[]{:T(128)}, f32[640,256]{1,0:T(8,128)}) fusion(f32[640,256]{1,0:T(8,128)S(1)} %copy-done.1, f32[640,256]{1,0:T(8,128)S(1)} %copy-done.5, f32[]{:T(128)S(6)} %div.65), kind=kLoop, calls=%fused_computation.4 | loop fusion | flops 655359 | bytes 1966088 | tf_op jit(solution)/shard_map/reduce_sum | solution.py:303
  81.3 0.1 add_dynamic-update-slice_fusion
  81.5 0.1 fusion.15
  81.6 0.1 fusion.14
  81.8 0.7 pad_maximum_fusion.7
  82.5 0.7 broadcast_in_dim.16
  83.2 5.7 %all-to-all-start.3 = ((f32[32,1,1028]{2,1,0:T(1,128)}), f32[32,1,1028]{2,1,0:T(1,128)S(1)}, u32[]{:S(2)}, u32[]{:S(2)}) async-start(f32[32,1,1028]{2,1,0:T(1,128)} %broadcast_in_dim.16), calls=%async_computation.3 | async-start | bytes 294912 | tf_op jit(solution)/shard_map/all_to_all | solution.py:255
  88.9 7.9 %shard_map.109 = f32[1,8192]{1,0:T(1,128)} custom-call(f32[640,256]{1,0:T(8,128)} %get-tuple-element.140.tab_ref, s32[1,8192]{1,0:T(1,128)} %ids_ref.7, f32[5,8192]{1,0:T(8,128)} %bitcast.107), custom_call_target="tpu_custom_call" | custom-call | tf_op jit(solution)/shard_map/pallas_call | solution.py:89
  96.8 0.8 all-to-all-done.3
  97.5 0.7 slice_reduce_fusion.1
  98.4 0.4 scatter-add.49
  98.8 0.6 multiply_reduce_fusion.4
  101.0 0.7 multiply_add_fusion.1
  101.8 0.7 reshape.743.tab_ref
  102.6 3.8 %shard_map.110 = (f32[1,8192]{1,0:T(1,128)}, f32[1,1]{1,0:T(1,128)}) custom-call(f32[128,256]{1,0:T(8,128)} %reshape.743.tab_ref, s32[1,8192]{1,0:T(1,128)} %multiply_add_fusion.3.ids_ref, f32[4,8192]{1,0:T(4,128)} %pad_maximum_fusion.2.basis_ref, f32[1,8192]{1,0:T(1,128)} %get-tuple-element.176.zsrc_ref, f32[1,8192]{1,0:T(1,128)} %bitcast.125), custom_call_target="tpu_custom_call" | custom-call | tf_op jit(solution)/shard_map/pallas_call | solution.py:152
  106.3 1.4 %reduce.32 = f32[8192]{0:T(1024)S(1)} reduce(f32[1,8192]{1,0:T(1,128)} %get-tuple-element.135, f32[]{:T(128)} %broadcast.525), dimensions={0}, to_apply=%get-tuple-element.135.reduce_sub_computation.3 | reduce | bytes 65540 | tf_op jit(solution)/shard_map/pallas_call | solution.py:152
  107.8 0.7 pad_maximum_fusion.8
  108.5 0.7 all_to_all.43
  109.2 5.1 %all-to-all-start.4 = ((f32[32,1,258]{2,1,0:T(1,128)}), f32[32,1,258]{2,1,0:T(1,128)S(1)}, u32[]{:S(2)}, u32[]{:S(2)}) async-start(f32[32,1,258]{2,1,0:T(1,128)} %all_to_all.43), calls=%async_computation.4 | async-start | bytes 98304 | tf_op jit(solution)/shard_map/all_to_all | solution.py:274
  114.3 7.4 %all-to-all-done.4 = f32[32,1,258]{2,1,0:T(1,128)S(1)} async-done(((f32[32,1,258]{2,1,0:T(1,128)}), f32[32,1,258]{2,1,0:T(1,128)S(1)}, u32[]{:S(2)}, u32[]{:S(2)}) %all-to-all-start.4) | async-done | bytes 33056 | tf_op jit(solution)/shard_map/all_to_all | solution.py:274
  122.0 0.6 fusion.13
  122.6 1.2 reshape.745
  123.8 0.9 multiply_subtract_fusion.1
  (78 shorter events, 1.8 us)
Async XLA Ops:
  0.6 0.9 copy-start
  0.6 2.8 %copy-start.12 = (s32[1,32]{1,0:T(1,128)S(1)}, s32[1,32]{1,0:T(1,128)}, u32[]{:S(2)}) copy-start(s32[1,32]{1,0:T(1,128)} %param.34) | copy-start | bytes 388
  0.7 3.0 %copy-start.10 = (f32[8192]{0:T(1024)S(1)}, f32[8192]{0:T(1024)}, u32[]{:S(2)}) copy-start(f32[8192]{0:T(1024)} %param.33) | copy-start | bytes 98308
  0.7 3.0 %copy-start.9 = (f32[5,8192]{1,0:T(8,128)S(1)}, f32[5,8192]{1,0:T(8,128)}, u32[]{:S(2)}) copy-start(f32[5,8192]{1,0:T(8,128)} %param.29) | copy-start | bytes 491524
  4.9 17.9 %all-to-all-start = ((f32[32,1,2304]{2,1,0:T(1,128)}), f32[32,1,2304]{2,1,0:T(1,128)S(1)}, u32[]{:S(2)}, u32[]{:S(2)}) async-start(f32[32,1,2304]{2,1,0:T(1,128)} %all_to_all.46), calls=%async_computation | async-start | bytes 589824 | tf_op jit(solution)/shard_map/all_to_all | solution.py:243
  24.3 13.9 %copy-start.2 = (f32[5,32,256]{2,0,1:T(8,128)}, f32[5,32,256]{2,0,1:T(8,128)S(1)}, u32[]{:S(2)}) copy-start(f32[5,32,256]{2,0,1:T(8,128)S(1)} %slice.325) | copy-start | bytes 491524
  26.0 20.9 %all-to-all-start.1 = ((f32[32,1,1028]{2,1,0:T(1,128)}), f32[32,1,1028]{2,1,0:T(1,128)S(1)}, u32[]{:S(2)}, u32[]{:S(2)}) async-start(f32[32,1,1028]{2,1,0:T(1,128)} %broadcast_in_dim.13), calls=%async_computation.1 | async-start | bytes 294912 | tf_op jit(solution)/shard_map/all_to_all | solution.py:255
  38.2 7.9 %copy-start.1 = (f32[640,256]{1,0:T(8,128)S(1)}, f32[640,256]{1,0:T(8,128)}, u32[]{:S(2)}) copy-start(f32[640,256]{1,0:T(8,128)} %shard_map.104.tab_ref) | copy-start | bytes 1966084
  46.9 6.6 %copy-start.7 = (f32[1,32,256]{2,0,1:T(1,128)S(1)}, f32[1,32,256]{2,0,1:T(1,128)}, u32[]{:S(2)}) copy-start(f32[1,32,256]{2,0,1:T(1,128)} %get-tuple-element.142) | copy-start | bytes 98308
  47.0 15.9 %copy-start.3 = (f32[5,32,256]{2,0,1:T(8,128)S(1)}, f32[5,32,256]{2,0,1:T(8,128)}, u32[]{:S(2)}) copy-start(f32[5,32,256]{2,0,1:T(8,128)} %copy-done.2) | copy-start | bytes 491524
  56.9 16.3 %all-to-all-start.2 = ((f32[32,1,258]{2,1,0:T(1,128)}), f32[32,1,258]{2,1,0:T(1,128)S(1)}, u32[]{:S(2)}, u32[]{:S(2)}) async-start(f32[32,1,258]{2,1,0:T(1,128)} %all_to_all.38), calls=%async_computation.2 | async-start | bytes 98304 | tf_op jit(solution)/shard_map/all_to_all | solution.py:274
  71.3 8.5 %copy-start.5 = (f32[640,256]{1,0:T(8,128)S(1)}, f32[640,256]{1,0:T(8,128)}, u32[]{:S(2)}) copy-start(f32[640,256]{1,0:T(8,128)} %shard_map.108) | copy-start | bytes 1966084
  83.2 14.3 %all-to-all-start.3 = ((f32[32,1,1028]{2,1,0:T(1,128)}), f32[32,1,1028]{2,1,0:T(1,128)S(1)}, u32[]{:S(2)}, u32[]{:S(2)}) async-start(f32[32,1,1028]{2,1,0:T(1,128)} %broadcast_in_dim.16), calls=%async_computation.3 | async-start | bytes 294912 | tf_op jit(solution)/shard_map/all_to_all | solution.py:255
  88.9 12.1 %copy-start.8 = (f32[1,8192]{1,0:T(1,128)S(1)}, f32[1,8192]{1,0:T(1,128)}, u32[]{:S(2)}) copy-start(f32[1,8192]{1,0:T(1,128)} %shard_map.105.zsrc_ref) | copy-start | bytes 98308
  96.8 4.2 %copy-start.11 = (f32[1,8192]{1,0:T(1,128)S(1)}, f32[1,8192]{1,0:T(1,128)}, u32[]{:S(2)}) copy-start(f32[1,8192]{1,0:T(1,128)} %shard_map.109) | copy-start | bytes 98308
  99.4 22.4 %copy-start.4 = (f32[640,256]{1,0:T(8,128)S(1)}, f32[640,256]{1,0:T(8,128)}, u32[]{:S(2)}) copy-start(f32[640,256]{1,0:T(8,128)} %get-tuple-element.140.tab_ref) | copy-start | bytes 1966084
  109.2 12.5 %all-to-all-start.4 = ((f32[32,1,258]{2,1,0:T(1,128)}), f32[32,1,258]{2,1,0:T(1,128)S(1)}, u32[]{:S(2)}, u32[]{:S(2)}) async-start(f32[32,1,258]{2,1,0:T(1,128)} %all_to_all.43), calls=%async_computation.4 | async-start | bytes 98304 | tf_op jit(solution)/shard_map/all_to_all | solution.py:274
  122.0 1.8 %copy-start.6 = (f32[12,8192]{1,0:T(8,128)S(1)}, f32[12,8192]{1,0:T(8,128)}, u32[]{:S(2)}) copy-start(f32[12,8192]{1,0:T(8,128)} %param.28) | copy-start | bytes 1179652

commit v8 on v7

--- a/solution.py
+++ b/solution.py
@@ -212,7 +212,7 @@
     owned = SRC_DEV
     everyone = ("tm", "src")
     place = jnp.arange(capacity, dtype=jnp.int32)[None, :]
-    live = (place < live_slot_count[0][:, None]).astype(jnp.float32).reshape(rows)
+    live = (place < live_slot_count[0][:, None]).astype(jnp.float32).reshape(1, rows)
     indicator = (
         detector_index[None, :] == jnp.arange(detector_count, dtype=jnp.int32)[:, None]
     ).astype(jnp.float32)
@@ -222,17 +222,17 @@
         precision=lax.Precision.HIGHEST,
         preferred_element_type=jnp.float32,
     )
-    weight_sq = live * jnp.sum(weight_factor * weight_factor, axis=0)
+    weight_sq = live * jnp.sum(weight_factor * weight_factor, axis=0, keepdims=True)
     basis16 = jnp.repeat(jnp.stack(spline_basis(interval_fraction), axis=0), knots // HI, axis=0)
     first_ids = first_knot_interval.reshape(1, rows)
     ids = slot_owned_source[0].reshape(1, rows)
-    zbar0 = live * jnp.sum(weight_factor * observed_residual, axis=0)
+    zbar0 = live * jnp.sum(weight_factor * observed_residual, axis=0, keepdims=True)
 
     packed = jnp.concatenate(
         [
             source_partials,
-            zbar0[None],
-            weight_sq[None],
+            zbar0,
+            weight_sq,
             interval_fraction[None],
             first_knot_interval.astype(jnp.float32)[None],
         ],
@@ -243,11 +243,11 @@
     got = lax.all_to_all(blocks, everyone, 0, 0, tiled=True)
     got = got.reshape(n_ranks, n_rows, capacity).transpose(1, 0, 2).reshape(n_rows, rows)
     held = got[:n_params]
-    zbar0_own = got[n_params]
-    weight_sq_own = got[n_params + 1]
-    basis_own = jnp.stack(spline_basis(got[n_params + 2]), axis=0)
-    slot_device = jnp.arange(rows, dtype=jnp.int32) // capacity
-    base_own = ((slot_device // n_share) * knots + got[n_params + 3].astype(jnp.int32)).reshape(1, rows)
+    zbar0_own = got[n_params:n_params + 1]
+    weight_sq_own = got[n_params + 1:n_params + 2]
+    basis_own = jnp.concatenate(spline_basis(got[n_params + 2:n_params + 3]), axis=0)
+    slot_device = jnp.arange(rows, dtype=jnp.int32)[None, :] // capacity
+    base_own = (slot_device // n_share) * knots + got[n_params + 3:n_params + 4].astype(jnp.int32)
     table_rows = n_params * (owned // HI)
 
     def combine(part_a, s_norm):
@@ -263,26 +263,23 @@
 
     def forward(zsrc, dir_a, extra):
         extended = jnp.concatenate([dir_a, jnp.zeros((3,), jnp.float32)])
-        shift_own, partial = knot_gather(
-            extended, base_own, basis_own, zsrc, weight_sq_own.reshape(1, rows), n_knots
-        )
-        shift_own = shift_own.reshape(rows)
+        shift_own, partial = knot_gather(extended, base_own, basis_own, zsrc, weight_sq_own, n_knots)
         sums = jnp.concatenate([partial.reshape(1), extra.reshape(1)])
         payload = jnp.concatenate(
             [shift_own.reshape(n_ranks, capacity), jnp.broadcast_to(sums[None, :], (n_ranks, 2))], axis=1
         )
         back = lax.all_to_all(payload, everyone, 0, 0, tiled=True)
         totals = jnp.sum(back[:, capacity:], axis=0)
-        return shift_own, back[:, :capacity].reshape(rows) * live, totals[0], totals[1]
+        return shift_own, back[:, :capacity].reshape(1, rows) * live, totals[0], totals[1]
 
     sol_s = jnp.zeros((table_rows, HI), jnp.float32)
     sol_a = jnp.zeros((n_knots,), jnp.float32)
     resid = observed_residual
     zbar_slot = zbar0
-    part_a = knot_scatter(zbar_slot.reshape(1, rows), first_ids, basis16, knots)
+    part_a = knot_scatter(zbar_slot, first_ids, basis16, knots)
     part_a, held, zbar0_own = lax.optimization_barrier((part_a, held, zbar0_own))
     grad_a, gamma_a = combine(part_a, jnp.zeros((), jnp.float32))
-    grad_s = source_scatter(held * zbar0_own[None, :], ids, owned)
+    grad_s = source_scatter(held * zbar0_own, ids, owned)
     extra = jnp.sum(grad_s * grad_s)
     dir_s, dir_a = (grad_s, grad_a)
     pulled = source_gather(dir_s, ids, held)
@@ -293,13 +290,13 @@
         alpha = gamma / image_sq
         sol_s = sol_s + alpha * dir_s
         sol_a = sol_a + alpha * dir_a
-        resid = resid - alpha * (weight_factor * shift_slot[None, :])
+        resid = resid - alpha * (weight_factor * shift_slot)
         if step + 1 < ITERS:
-            pushed = source_scatter(held * (weight_sq_own * shift_own)[None, :], ids, owned)
+            pushed = source_scatter(held * (weight_sq_own * shift_own), ids, owned)
             zbar_slot = zbar_slot - alpha * (weight_sq * shift_slot)
             grad_s = grad_s - alpha * pushed
             grad_a, fresh = combine(
-                knot_scatter(zbar_slot.reshape(1, rows), first_ids, basis16, knots),
+                knot_scatter(zbar_slot, first_ids, basis16, knots),
                 jnp.sum(grad_s * grad_s),
             )
             raw = source_gather(grad_s, ids, held)

time: 126 us -> 126 us (level)
  no operation moved by 1% of the time
where the time goes in v8:
time: 126 us; the launch traced here: 125 us
  Pallas kernels  44.8 us (36%)
  starting transfers between devices  27.1 us (22%)
  other arithmetic  21.4 us (17%)
  waiting for transfers between devices  12.3 us (10%)
  local copies, waits for them, and re-layouts  12 us (10%)
  between operations  5.11 us (4%)
  matrix products  2 us (2%)
    pallas_call x2, Pallas kernels, source_gather(): pl.pallas_call(kernel, out_shape=jax.ShapeDtypeStruct((1, total), jnp.flo...  15.8 us
    pallas_call x2, Pallas kernels, source_scatter(): pl.pallas_call(kernel, out_shape=jax.ShapeDtypeStruct((rows, HI), jnp.flo...  15.3 us
    all_to_all x2, starting transfers between devices, forward(): back = lax.all_to_all(payload, everyone, 0, 0, tiled=True)  11.1 us
    all_to_all x2, starting transfers between devices, combine(): lax.all_to_all(jnp.broadcast_to(mine[None, :], (n_ranks, knots + 4)), eve...  8.68 us
    pallas_call x2, Pallas kernels, knot_gather(): pl.pallas_call(kernel, out_shape=(jax.ShapeDtypeStruct((1, total), jnp.fl...  7.52 us
    all_to_all x2, waiting for transfers between devices, forward(): back = lax.all_to_all(payload, everyone, 0, 0, tiled=True)  7.37 us
    all_to_all x1, starting transfers between devices, per_device(): got = lax.all_to_all(blocks, everyone, 0, 0, tiled=True)  7.3 us
    pallas_call x2, Pallas kernels, knot_scatter(): pl.pallas_call(kernel, out_shape=jax.ShapeDtypeStruct((rows, HI), jnp.flo...  6.23 us
  transfers between devices with their start and end apart: 5, of which 3 were waited for; matrix products, arithmetic and copies ran while one was open for 6% of the time, Pallas kernels for 27%

profile of v8, /device:TPU:0, one launch (start us, length us, event | category | flops | bytes accessed | tf_op | source)
XLA Modules:
  0.0 124.7 jit_solution(10107362757601680615)
XLA Ops:
  0.7 0.8 convert_element_type.32
  1.5 2.0 %multiply_reduce_fusion.2 = (f32[8192]{0:T(1024)S(1)}, f32[8192]{0:T(1024)S(1)}, f32[12,8192]{1,0:T(8,128)S(1)}) fusion(f32[12,8192]{1,0:T(8,128)} %param.28, f32[12,62]{1,0:T(8,128)S(1)} %copy-done, s32[8192]{0:T(1024)} %param.31), kind=kOutput, calls=%fused_computation.8 | convolution fusion | flops 74022912 | bytes 887712 | tf_op jit(solution)/shard_map/dot_general | solution.py:219
  3.6 0.2 concatenate.60
  3.9 1.0 all_to_all.46
  4.9 7.3 %all-to-all-start = ((f32[32,1,2304]{2,1,0:T(1,128)}), f32[32,1,2304]{2,1,0:T(1,128)S(1)}, u32[]{:S(2)}, u32[]{:S(2)}) async-start(f32[32,1,2304]{2,1,0:T(1,128)} %all_to_all.46), calls=%async_computation | async-start | bytes 589824 | tf_op jit(solution)/shard_map/all_to_all | solution.py:243
  12.6 1.0 reshape.818.basis_ref
  13.6 0.7 broadcast_select_fusion.val_ref
  14.2 3.1 %shard_map.103 = f32[16,256]{1,0:T(8,128)} custom-call(f32[1,8192]{1,0:T(1,128)} %broadcast_select_fusion.val_ref, s32[1,8192]{1,0:T(1,128)} %bitcast.130, f32[16,8192]{1,0:T(8,128)} %reshape.818.basis_ref), custom_call_target="tpu_custom_call" | custom-call | tf_op jit(solution)/shard_map/pallas_call | solution.py:183
  17.3 0.8 slice_bitcast_fusion.5
  18.2 0.1 add_dynamic-update-slice_fusion.1
  18.3 0.1 fusion.17
  18.5 0.1 fusion.16
  18.6 4.2 %all-to-all-done = f32[32,1,2304]{2,1,0:T(1,128)S(1)} async-done(((f32[32,1,2304]{2,1,0:T(1,128)}), f32[32,1,2304]{2,1,0:T(1,128)S(1)}, u32[]{:S(2)}, u32[]{:S(2)}) %all-to-all-start) | async-done | bytes 294944 | tf_op jit(solution)/shard_map/all_to_all | solution.py:243
  22.8 0.7 reduce.24
  23.6 0.7 fusion.18
  24.3 0.7 multiply_add_fusion.3.ids_ref
  25.0 0.2 fusion.9
  25.3 0.7 broadcast_in_dim.13
  26.0 3.0 %all-to-all-start.1 = ((f32[32,1,1028]{2,1,0:T(1,128)}), f32[32,1,1028]{2,1,0:T(1,128)S(1)}, u32[]{:S(2)}, u32[]{:S(2)}) async-start(f32[32,1,1028]{2,1,0:T(1,128)} %broadcast_in_dim.13), calls=%async_computation.1 | async-start | bytes 294912 | tf_op jit(solution)/shard_map/all_to_all | solution.py:255
  29.0 0.7 broadcast_multiply_fusion.1.val_ref
  29.8 0.8 pad_maximum_fusion.2.basis_ref
  30.6 7.6 %shard_map.104.tab_ref = f32[640,256]{1,0:T(8,128)} custom-call(f32[5,8192]{1,0:T(8,128)} %broadcast_multiply_fusion.1.val_ref, s32[1,8192]{1,0:T(1,128)} %ids_ref.7), custom_call_target="tpu_custom_call" | custom-call | tf_op jit(solution)/shard_map/pallas_call | solution.py:121
  38.2 7.9 %shard_map.105.zsrc_ref = f32[1,8192]{1,0:T(1,128)} custom-call(f32[640,256]{1,0:T(8,128)} %shard_map.104.tab_ref, s32[1,8192]{1,0:T(1,128)} %ids_ref.7, f32[5,8192]{1,0:T(8,128)} %bitcast.107), custom_call_target="tpu_custom_call" | custom-call | tf_op jit(solution)/shard_map/pallas_call | solution.py:89
  46.1 0.7 multiply_reduce_fusion.1
  47.1 0.4 scatter-add.40
  47.5 0.6 multiply_reduce_fusion.5
  48.3 0.1 pad_maximum_fusion.1
  48.4 0.7 reshape.825.tab_ref
  49.1 3.8 %shard_map.106 = (f32[1,8192]{1,0:T(1,128)}, f32[1,1]{1,0:T(1,128)}) custom-call(f32[128,256]{1,0:T(8,128)} %reshape.825.tab_ref, s32[1,8192]{1,0:T(1,128)} %multiply_add_fusion.3.ids_ref, f32[4,8192]{1,0:T(4,128)} %pad_maximum_fusion.2.basis_ref, f32[1,8192]{1,0:T(1,128)} %shard_map.105.zsrc_ref, f32[1,8192]{1,0:T(1,128)} %bitcast.125), custom_call_target="tpu_custom_call" | custom-call | tf_op jit(solution)/shard_map/pallas_call | solution.py:152
  52.9 0.5 broadcast.543
  53.5 1.5 %fusion.19 = (f32[8192]{0:T(1024)S(1)}, f32[1,8192]{1,0:T(1,128)S(1)}) fusion(f32[1,8192]{1,0:T(1,128)} %get-tuple-element.133, f32[]{:T(128)} %broadcast.543, f32[1,8192]{1,0:T(1,128)S(1)} %bitcast.127), kind=kLoop, calls=%fused_computation.105 | loop fusion | flops 8192 | bytes 131076 | tf_op jit(solution)/shard_map/pallas_call | solution.py:152
  54.9 1.3 %pad_maximum_fusion.9 = f32[258]{0:T(512)S(1)} fusion(f32[1]{0:T(128)} %bitcast.25, f32[1]{0:T(128)} %bitcast.24), kind=kLoop, calls=%fused_computation.103 | loop fusion | flops 258 | bytes 1040 | tf_op jit(solution)/shard_map/concatenate | solution.py:267
  56.2 0.7 all_to_all.38
  56.9 6.0 %all-to-all-start.2 = ((f32[32,1,258]{2,1,0:T(1,128)}), f32[32,1,258]{2,1,0:T(1,128)S(1)}, u32[]{:S(2)}, u32[]{:S(2)}) async-start(f32[32,1,258]{2,1,0:T(1,128)} %all_to_all.38), calls=%async_computation.2 | async-start | bytes 98304 | tf_op jit(solution)/shard_map/all_to_all | solution.py:271
  62.9 0.7 broadcast_multiply_fusion.val_ref
  63.6 7.6 %shard_map.108 = f32[640,256]{1,0:T(8,128)} custom-call(f32[5,8192]{1,0:T(8,128)} %broadcast_multiply_fusion.val_ref, s32[1,8192]{1,0:T(1,128)} %ids_ref.7), custom_call_target="tpu_custom_call" | custom-call | tf_op jit(solution)/shard_map/pallas_call | solution.py:121
  71.3 0.7 slice_reduce_fusion.2
  73.3 0.6 fusion.20
  75.1 0.7 multiply_subtract_fusion.2.val_ref
  75.8 3.1 %shard_map.107 = f32[16,256]{1,0:T(8,128)} custom-call(f32[1,8192]{1,0:T(1,128)} %multiply_subtract_fusion.2.val_ref, s32[1,8192]{1,0:T(1,128)} %bitcast.131, f32[16,8192]{1,0:T(8,128)} %reshape.818.basis_ref), custom_call_target="tpu_custom_call" | custom-call | tf_op jit(solution)/shard_map/pallas_call | solution.py:183
  79.0 0.8 slice_bitcast_fusion.1
  79.8 1.5 %multiply_reduce_fusion = (f32[]{:T(128)}, f32[640,256]{1,0:T(8,128)}) fusion(f32[640,256]{1,0:T(8,128)S(1)} %copy-done.1, f32[640,256]{1,0:T(8,128)S(1)} %copy-done.5, f32[]{:T(128)S(6)} %div.65), kind=kLoop, calls=%fused_computation.4 | loop fusion | flops 655359 | bytes 1966088 | tf_op jit(solution)/shard_map/reduce_sum | solution.py:300
  81.3 0.1 add_dynamic-update-slice_fusion
  81.5 0.1 fusion.15
  81.6 0.1 fusion.14
  81.8 0.7 pad_maximum_fusion.7
  82.5 0.7 broadcast_in_dim.16
  83.2 5.7 %all-to-all-start.3 = ((f32[32,1,1028]{2,1,0:T(1,128)}), f32[32,1,1028]{2,1,0:T(1,128)S(1)}, u32[]{:S(2)}, u32[]{:S(2)}) async-start(f32[32,1,1028]{2,1,0:T(1,128)} %broadcast_in_dim.16), calls=%async_computation.3 | async-start | bytes 294912 | tf_op jit(solution)/shard_map/all_to_all | solution.py:255
  88.9 7.9 %shard_map.109 = f32[1,8192]{1,0:T(1,128)} custom-call(f32[640,256]{1,0:T(8,128)} %get-tuple-element.140.tab_ref, s32[1,8192]{1,0:T(1,128)} %ids_ref.7, f32[5,8192]{1,0:T(8,128)} %bitcast.108), custom_call_target="tpu_custom_call" | custom-call | tf_op jit(solution)/shard_map/pallas_call | solution.py:89
  96.8 0.8 all-to-all-done.3
  97.5 0.7 slice_reduce_fusion.1
  98.4 0.4 scatter-add.49
  98.8 0.6 multiply_reduce_fusion.4
  101.0 0.7 multiply_add_fusion.1
  101.8 0.7 reshape.836.tab_ref
  102.6 3.8 %shard_map.110 = (f32[1,8192]{1,0:T(1,128)}, f32[1,1]{1,0:T(1,128)}) custom-call(f32[128,256]{1,0:T(8,128)} %reshape.836.tab_ref, s32[1,8192]{1,0:T(1,128)} %multiply_add_fusion.3.ids_ref, f32[4,8192]{1,0:T(4,128)} %pad_maximum_fusion.2.basis_ref, f32[1,8192]{1,0:T(1,128)} %get-tuple-element.176.zsrc_ref, f32[1,8192]{1,0:T(1,128)} %bitcast.126), custom_call_target="tpu_custom_call" | custom-call | tf_op jit(solution)/shard_map/pallas_call | solution.py:152
  106.3 1.4 %reduce.32 = f32[8192]{0:T(1024)S(1)} reduce(f32[1,8192]{1,0:T(1,128)} %get-tuple-element.135, f32[]{:T(128)} %broadcast.543), dimensions={0}, to_apply=%get-tuple-element.135.reduce_sub_computation.3 | reduce | bytes 65540 | tf_op jit(solution)/shard_map/pallas_call | solution.py:152
  107.8 0.7 pad_maximum_fusion.8
  108.5 0.7 all_to_all.43
  109.2 5.1 %all-to-all-start.4 = ((f32[32,1,258]{2,1,0:T(1,128)}), f32[32,1,258]{2,1,0:T(1,128)S(1)}, u32[]{:S(2)}, u32[]{:S(2)}) async-start(f32[32,1,258]{2,1,0:T(1,128)} %all_to_all.43), calls=%async_computation.4 | async-start | bytes 98304 | tf_op jit(solution)/shard_map/all_to_all | solution.py:271
  114.3 7.4 %all-to-all-done.4 = f32[32,1,258]{2,1,0:T(1,128)S(1)} async-done(((f32[32,1,258]{2,1,0:T(1,128)}), f32[32,1,258]{2,1,0:T(1,128)S(1)}, u32[]{:S(2)}, u32[]{:S(2)}) %all-to-all-start.4) | async-done | bytes 33056 | tf_op jit(solution)/shard_map/all_to_all | solution.py:271
  122.0 0.6 fusion.13
  122.6 1.2 reshape.839
  123.8 0.9 multiply_subtract_fusion.1
  (78 shorter events, 1.8 us)
Async XLA Ops:
  0.6 0.9 copy-start
  0.6 2.8 %copy-start.12 = (s32[1,32]{1,0:T(1,128)S(1)}, s32[1,32]{1,0:T(1,128)}, u32[]{:S(2)}) copy-start(s32[1,32]{1,0:T(1,128)} %param.34) | copy-start | bytes 388
  0.7 3.0 %copy-start.10 = (f32[8192]{0:T(1024)S(1)}, f32[8192]{0:T(1024)}, u32[]{:S(2)}) copy-start(f32[8192]{0:T(1024)} %param.33) | copy-start | bytes 98308
  0.7 3.0 %copy-start.9 = (f32[5,8192]{1,0:T(8,128)S(1)}, f32[5,8192]{1,0:T(8,128)}, u32[]{:S(2)}) copy-start(f32[5,8192]{1,0:T(8,128)} %param.29) | copy-start | bytes 491524
  4.9 17.9 %all-to-all-start = ((f32[32,1,2304]{2,1,0:T(1,128)}), f32[32,1,2304]{2,1,0:T(1,128)S(1)}, u32[]{:S(2)}, u32[]{:S(2)}) async-start(f32[32,1,2304]{2,1,0:T(1,128)} %all_to_all.46), calls=%async_computation | async-start | bytes 589824 | tf_op jit(solution)/shard_map/all_to_all | solution.py:243
  24.3 13.9 %copy-start.2 = (f32[5,32,256]{2,0,1:T(8,128)}, f32[5,32,256]{2,0,1:T(8,128)S(1)}, u32[]{:S(2)}) copy-start(f32[5,32,256]{2,0,1:T(8,128)S(1)} %slice.331) | copy-start | bytes 491524
  26.0 20.9 %all-to-all-start.1 = ((f32[32,1,1028]{2,1,0:T(1,128)}), f32[32,1,1028]{2,1,0:T(1,128)S(1)}, u32[]{:S(2)}, u32[]{:S(2)}) async-start(f32[32,1,1028]{2,1,0:T(1,128)} %broadcast_in_dim.13), calls=%async_computation.1 | async-start | bytes 294912 | tf_op jit(solution)/shard_map/all_to_all | solution.py:255
  38.2 7.9 %copy-start.1 = (f32[640,256]{1,0:T(8,128)S(1)}, f32[640,256]{1,0:T(8,128)}, u32[]{:S(2)}) copy-start(f32[640,256]{1,0:T(8,128)} %shard_map.104.tab_ref) | copy-start | bytes 1966084
  46.9 6.6 %copy-start.7 = (f32[1,32,256]{2,0,1:T(1,128)S(1)}, f32[1,32,256]{2,0,1:T(1,128)}, u32[]{:S(2)}) copy-start(f32[1,32,256]{2,0,1:T(1,128)} %get-tuple-element.142) | copy-start | bytes 98308
  47.0 15.9 %copy-start.3 = (f32[5,32,256]{2,0,1:T(8,128)S(1)}, f32[5,32,256]{2,0,1:T(8,128)}, u32[]{:S(2)}) copy-start(f32[5,32,256]{2,0,1:T(8,128)} %copy-done.2) | copy-start | bytes 491524
  56.9 16.3 %all-to-all-start.2 = ((f32[32,1,258]{2,1,0:T(1,128)}), f32[32,1,258]{2,1,0:T(1,128)S(1)}, u32[]{:S(2)}, u32[]{:S(2)}) async-start(f32[32,1,258]{2,1,0:T(1,128)} %all_to_all.38), calls=%async_computation.2 | async-start | bytes 98304 | tf_op jit(solution)/shard_map/all_to_all | solution.py:271
  71.3 8.5 %copy-start.5 = (f32[640,256]{1,0:T(8,128)S(1)}, f32[640,256]{1,0:T(8,128)}, u32[]{:S(2)}) copy-start(f32[640,256]{1,0:T(8,128)} %shard_map.108) | copy-start | bytes 1966084
  83.2 14.3 %all-to-all-start.3 = ((f32[32,1,1028]{2,1,0:T(1,128)}), f32[32,1,1028]{2,1,0:T(1,128)S(1)}, u32[]{:S(2)}, u32[]{:S(2)}) async-start(f32[32,1,1028]{2,1,0:T(1,128)} %broadcast_in_dim.16), calls=%async_computation.3 | async-start | bytes 294912 | tf_op jit(solution)/shard_map/all_to_all | solution.py:255
  88.9 12.1 %copy-start.8 = (f32[1,8192]{1,0:T(1,128)S(1)}, f32[1,8192]{1,0:T(1,128)}, u32[]{:S(2)}) copy-start(f32[1,8192]{1,0:T(1,128)} %shard_map.105.zsrc_ref) | copy-start | bytes 98308
  96.8 4.2 %copy-start.11 = (f32[1,8192]{1,0:T(1,128)S(1)}, f32[1,8192]{1,0:T(1,128)}, u32[]{:S(2)}) copy-start(f32[1,8192]{1,0:T(1,128)} %shard_map.109) | copy-start | bytes 98308
  99.4 22.4 %copy-start.4 = (f32[640,256]{1,0:T(8,128)S(1)}, f32[640,256]{1,0:T(8,128)}, u32[]{:S(2)}) copy-start(f32[640,256]{1,0:T(8,128)} %get-tuple-element.140.tab_ref) | copy-start | bytes 1966084
  109.2 12.5 %all-to-all-start.4 = ((f32[32,1,258]{2,1,0:T(1,128)}), f32[32,1,258]{2,1,0:T(1,128)S(1)}, u32[]{:S(2)}, u32[]{:S(2)}) async-start(f32[32,1,258]{2,1,0:T(1,128)} %all_to_all.43), calls=%async_computation.4 | async-start | bytes 98304 | tf_op jit(solution)/shard_map/all_to_all | solution.py:271
  122.0 1.8 %copy-start.6 = (f32[12,8192]{1,0:T(8,128)S(1)}, f32[12,8192]{1,0:T(8,128)}, u32[]{:S(2)}) copy-start(f32[12,8192]{1,0:T(8,128)} %param.28) | copy-start | bytes 1179652

commit v9 on v8

--- a/solution.py
+++ b/solution.py
@@ -123,17 +123,19 @@
     )(values, ids)
 
 
-def knot_gather(extended, first_ids, basis, zsrc, weight, knots):
+def knot_gather(extended, first_ids, basis, zsrc, weight, extra, knots, parts, width):
     total = first_ids.shape[1]
     cols = knots // HI
     shifted = jnp.stack([extended[q:q + knots] for q in range(4)], axis=0)
     rows = 4 * cols
-
-    def kernel(tab_ref, ids_ref, basis_ref, zsrc_ref, weight_ref, out_ref, norm_ref, big_ref):
+    per_chunk = CHUNK // width
+
+    def kernel(tab_ref, ids_ref, basis_ref, zsrc_ref, weight_ref, extra_ref, out_ref, pay_ref, big_ref, norm_ref):
         split_into(tab_ref, big_ref)
         norm_ref[...] = jnp.zeros(norm_ref.shape, jnp.float32)
 
-        def body(off):
+        for i in range(total // CHUNK):
+            off = i * CHUNK
             idc = ids_ref[:, pl.ds(off, CHUNK)]
             picked = jnp.dot(big_ref[...], hot_rows(idc, CHUNK), preferred_element_type=jnp.float32)
             acc = picked[:rows] + picked[rows:]
@@ -145,18 +147,24 @@
                 z = z + b[q:q + 1] * value
             shift = zsrc_ref[:, pl.ds(off, CHUNK)] + z
             out_ref[:, pl.ds(off, CHUNK)] = shift
+            for r in range(per_chunk):
+                row = i * per_chunk + r
+                pay_ref[row:row + 1, 128:128 + width] = shift[:, r * width:(r + 1) * width]
             norm_ref[...] += jnp.sum(weight_ref[:, pl.ds(off, CHUNK)] * shift * shift, axis=1, keepdims=True)
 
-        chunks(total, body)
+        lane = lax.broadcasted_iota(jnp.int32, (parts, 128), 1)
+        pay_ref[:, 0:128] = jnp.where(
+            lane == 0, norm_ref[...], jnp.where(lane == 1, extra_ref[...], 0.0)
+        )
 
     return pl.pallas_call(
         kernel,
         out_shape=(
             jax.ShapeDtypeStruct((1, total), jnp.float32),
-            jax.ShapeDtypeStruct((1, 1), jnp.float32),
+            jax.ShapeDtypeStruct((parts, 128 + width), jnp.float32),
         ),
-        scratch_shapes=[pltpu.VMEM((2 * rows, HI), jnp.bfloat16)],
-    )(shifted.reshape(rows, HI), first_ids, basis, zsrc, weight)
+        scratch_shapes=[pltpu.VMEM((2 * rows, HI), jnp.bfloat16), pltpu.VMEM((1, 1), jnp.float32)],
+    )(shifted.reshape(rows, HI), first_ids, basis, zsrc, weight, extra.reshape(1, 1))
 
 
 def knot_scatter(values, first_ids, basis16, knots):
@@ -263,14 +271,12 @@
 
     def forward(zsrc, dir_a, extra):
         extended = jnp.concatenate([dir_a, jnp.zeros((3,), jnp.float32)])
-        shift_own, partial = knot_gather(extended, base_own, basis_own, zsrc, weight_sq_own, n_knots)
-        sums = jnp.concatenate([partial.reshape(1), extra.reshape(1)])
-        payload = jnp.concatenate(
-            [shift_own.reshape(n_ranks, capacity), jnp.broadcast_to(sums[None, :], (n_ranks, 2))], axis=1
+        shift_own, payload = knot_gather(
+            extended, base_own, basis_own, zsrc, weight_sq_own, extra, n_knots, n_ranks, capacity
         )
         back = lax.all_to_all(payload, everyone, 0, 0, tiled=True)
-        totals = jnp.sum(back[:, capacity:], axis=0)
-        return shift_own, back[:, :capacity].reshape(1, rows) * live, totals[0], totals[1]
+        totals = jnp.sum(back[:, :2], axis=0)
+        return shift_own, back[:, 128:].reshape(1, rows) * live, totals[0], totals[1]
 
     sol_s = jnp.zeros((table_rows, HI), jnp.float32)
     sol_a = jnp.zeros((n_knots,), jnp.float32)

time: 126 us -> 124 us (0.984)
  other arithmetic: 21.4 us -> 17.4 us
    pallas_call x2 -> x0, other arithmetic: 2.91 us -> none  [knot_gather(): pl.pallas_call(kernel, out_shape=(jax.ShapeDtypeStruct((1, total), jnp.fl...]
    concatenate x4 -> x0, other arithmetic: 2.01 us -> none  [the longest x2 1.99 us: forward(): sums = jnp.concatenate([partial.reshape(1), extra.reshape(1)])]
    all_to_all x2, local copies, waits for them, and re-layouts: 1.3 us -> 2.93 us  [forward(): back = lax.all_to_all(payload, everyone, 0, 0, tiled=True)]
  transfers between devices with their start and end apart: 5 -> 5, of which waited for: 3 -> 3; matrix products, arithmetic and copies ran while one was open for 6% -> 6% of each run, Pallas kernels for 27% -> 28%
where the time goes in v9:
time: 124 us; the launch traced here: 123 us
  Pallas kernels  45.8 us (37%)
  starting transfers between devices  27.3 us (22%)
  other arithmetic  17.4 us (14%)
  local copies, waits for them, and re-layouts  13.1 us (11%)
  waiting for transfers between devices  12.1 us (10%)
  between operations  5.16 us (4%)
  matrix products  2 us (2%)
    pallas_call x2, Pallas kernels, source_gather(): pl.pallas_call(kernel, out_shape=jax.ShapeDtypeStruct((1, total), jnp.flo...  15.8 us
    pallas_call x2, Pallas kernels, source_scatter(): pl.pallas_call(kernel, out_shape=jax.ShapeDtypeStruct((rows, HI), jnp.flo...  15.3 us
    all_to_all x2, starting transfers between devices, forward(): back = lax.all_to_all(payload, everyone, 0, 0, tiled=True)  10.7 us
    all_to_all x2, starting transfers between devices, combine(): lax.all_to_all(jnp.broadcast_to(mine[None, :], (n_ranks, knots + 4)), eve...  9.25 us
    pallas_call x2, Pallas kernels, knot_gather(): pl.pallas_call(kernel, out_shape=(jax.ShapeDtypeStruct((1, total), jnp.fl...  8.53 us
    all_to_all x2, waiting for transfers between devices, forward(): back = lax.all_to_all(payload, everyone, 0, 0, tiled=True)  7.37 us
    all_to_all x1, starting transfers between devices, per_device(): got = lax.all_to_all(blocks, everyone, 0, 0, tiled=True)  7.3 us
    pallas_call x2, Pallas kernels, knot_scatter(): pl.pallas_call(kernel, out_shape=jax.ShapeDtypeStruct((rows, HI), jnp.flo...  6.23 us
  transfers between devices with their start and end apart: 5, of which 3 were waited for; matrix products, arithmetic and copies ran while one was open for 6% of the time, Pallas kernels for 28%

profile of v9, /device:TPU:0, one launch (start us, length us, event | category | flops | bytes accessed | tf_op | source)
XLA Modules:
  0.0 122.9 jit_solution(13201304234684560017)
XLA Ops:
  0.7 0.8 convert_element_type.32
  1.5 2.0 %multiply_reduce_fusion.2 = (f32[8192]{0:T(1024)S(1)}, f32[8192]{0:T(1024)S(1)}, f32[12,8192]{1,0:T(8,128)S(1)}) fusion(f32[12,8192]{1,0:T(8,128)} %param.28, f32[12,62]{1,0:T(8,128)S(1)} %copy-done, s32[8192]{0:T(1024)} %param.31), kind=kOutput, calls=%fused_computation.8 | convolution fusion | flops 74022912 | bytes 887712 | tf_op jit(solution)/shard_map/dot_general | solution.py:227
  3.5 0.1 compare_select_fusion.3
  3.6 0.2 concatenate.48
  3.9 1.0 all_to_all.46
  4.9 7.3 %all-to-all-start = ((f32[32,1,2304]{2,1,0:T(1,128)}), f32[32,1,2304]{2,1,0:T(1,128)S(1)}, u32[]{:S(2)}, u32[]{:S(2)}) async-start(f32[32,1,2304]{2,1,0:T(1,128)} %all_to_all.46), calls=%async_computation | async-start | bytes 589824 | tf_op jit(solution)/shard_map/all_to_all | solution.py:251
  12.4 0.1 pad_maximum_fusion
  12.6 1.0 reshape.804.basis_ref
  13.6 0.7 broadcast_select_fusion.val_ref
  14.2 3.1 %shard_map.103 = f32[16,256]{1,0:T(8,128)} custom-call(f32[1,8192]{1,0:T(1,128)} %broadcast_select_fusion.val_ref, s32[1,8192]{1,0:T(1,128)} %bitcast.130, f32[16,8192]{1,0:T(8,128)} %reshape.804.basis_ref), custom_call_target="tpu_custom_call" | custom-call | tf_op jit(solution)/shard_map/pallas_call | solution.py:191
  17.3 0.8 slice_bitcast_fusion.5
  18.2 0.1 add_dynamic-update-slice_fusion.1
  18.3 0.1 fusion.17
  18.5 0.1 fusion.16
  18.6 4.2 %all-to-all-done = f32[32,1,2304]{2,1,0:T(1,128)S(1)} async-done(((f32[32,1,2304]{2,1,0:T(1,128)}), f32[32,1,2304]{2,1,0:T(1,128)S(1)}, u32[]{:S(2)}, u32[]{:S(2)}) %all-to-all-start) | async-done | bytes 294944 | tf_op jit(solution)/shard_map/all_to_all | solution.py:251
  22.8 0.7 reduce.24
  23.6 0.7 fusion.18
  24.3 0.7 multiply_add_fusion.3.ids_ref
  25.0 0.2 fusion.9
  25.3 0.7 broadcast_in_dim.9
  26.0 3.2 %all-to-all-start.1 = ((f32[32,1,1028]{2,1,0:T(1,128)}), f32[32,1,1028]{2,1,0:T(1,128)S(1)}, u32[]{:S(2)}, u32[]{:S(2)}) async-start(f32[32,1,1028]{2,1,0:T(1,128)} %broadcast_in_dim.9), calls=%async_computation.1 | async-start | bytes 294912 | tf_op jit(solution)/shard_map/all_to_all | solution.py:263
  29.2 0.7 broadcast_multiply_fusion.1.val_ref
  30.0 0.8 pad_maximum_fusion.2.basis_ref
  30.7 7.6 %shard_map.104.tab_ref = f32[640,256]{1,0:T(8,128)} custom-call(f32[5,8192]{1,0:T(8,128)} %broadcast_multiply_fusion.1.val_ref, s32[1,8192]{1,0:T(1,128)} %ids_ref.7), custom_call_target="tpu_custom_call" | custom-call | tf_op jit(solution)/shard_map/pallas_call | solution.py:121
  38.4 7.9 %shard_map.105.zsrc_ref = f32[1,8192]{1,0:T(1,128)} custom-call(f32[640,256]{1,0:T(8,128)} %shard_map.104.tab_ref, s32[1,8192]{1,0:T(1,128)} %ids_ref.7, f32[5,8192]{1,0:T(8,128)} %bitcast.107), custom_call_target="tpu_custom_call" | custom-call | tf_op jit(solution)/shard_map/pallas_call | solution.py:89
  46.3 0.8 multiply_reduce_fusion.1
  47.3 0.4 scatter-add.40
  47.7 0.6 multiply_reduce_fusion.5
  48.5 0.1 pad_maximum_fusion.1
  48.6 0.7 reshape.811.tab_ref
  49.4 4.6 %shard_map.106 = (f32[1,8192]{1,0:T(1,128)}, f32[32,384]{1,0:T(8,128)}) custom-call(f32[128,256]{1,0:T(8,128)} %reshape.811.tab_ref, s32[1,8192]{1,0:T(1,128)} %multiply_add_fusion.3.ids_ref, f32[4,8192]{1,0:T(4,128)} %pad_maximum_fusion.2.basis_ref, f32[1,8192]{1,0:T(1,128)} %shard_map.105.zsrc_ref, f32[1,8192]{1,0:T(1,128)} %bitcast.125, ...), custom_call_target="tpu_custom_call" | custom-call | tf_op jit(solution)/shard_map/pallas_call | solution.py:160
  54.0 1.5 %copy.32 = f32[32,1,384]{2,1,0:T(1,128)} copy(f32[32,1,384]{2,0,1:T(8,128)} %bitcast.164) | data formatting | bytes 98304 | tf_op jit(solution)/shard_map/all_to_all | solution.py:277
  55.4 5.7 %all-to-all-start.2 = ((f32[32,1,384]{2,1,0:T(1,128)}), f32[32,1,384]{2,1,0:T(1,128)S(1)}, u32[]{:S(2)}, u32[]{:S(2)}) async-start(f32[32,1,384]{2,1,0:T(1,128)} %copy.32), calls=%async_computation.2 | async-start | bytes 98304 | tf_op jit(solution)/shard_map/all_to_all | solution.py:277
  61.1 0.8 mul.386
  61.9 0.7 broadcast_multiply_fusion.val_ref
  62.7 7.6 %shard_map.108 = f32[640,256]{1,0:T(8,128)} custom-call(f32[5,8192]{1,0:T(8,128)} %broadcast_multiply_fusion.val_ref, s32[1,8192]{1,0:T(1,128)} %ids_ref.7), custom_call_target="tpu_custom_call" | custom-call | tf_op jit(solution)/shard_map/pallas_call | solution.py:121
  70.3 0.7 slice_reduce_fusion.2
  72.4 0.6 fusion.19
  74.4 0.7 multiply_subtract_fusion.2.val_ref
  75.1 3.1 %shard_map.107 = f32[16,256]{1,0:T(8,128)} custom-call(f32[1,8192]{1,0:T(1,128)} %multiply_subtract_fusion.2.val_ref, s32[1,8192]{1,0:T(1,128)} %bitcast.131, f32[16,8192]{1,0:T(8,128)} %reshape.804.basis_ref), custom_call_target="tpu_custom_call" | custom-call | tf_op jit(solution)/shard_map/pallas_call | solution.py:191
  78.2 0.8 slice_bitcast_fusion.1
  79.0 1.5 %multiply_reduce_fusion = (f32[]{:T(128)}, f32[640,256]{1,0:T(8,128)}) fusion(f32[640,256]{1,0:T(8,128)S(1)} %copy-done.1, f32[640,256]{1,0:T(8,128)S(1)} %copy-done.5, f32[]{:T(128)S(6)} %div.65), kind=kLoop, calls=%fused_computation.4 | loop fusion | flops 655359 | bytes 1966088 | tf_op jit(solution)/shard_map/reduce_sum | solution.py:306
  80.6 0.1 add_dynamic-update-slice_fusion
  80.7 0.1 fusion.15
  80.9 0.1 fusion.14
  81.0 0.7 pad_maximum_fusion.5
  81.7 0.7 broadcast_in_dim.11
  82.5 6.1 %all-to-all-start.3 = ((f32[32,1,1028]{2,1,0:T(1,128)}), f32[32,1,1028]{2,1,0:T(1,128)S(1)}, u32[]{:S(2)}, u32[]{:S(2)}) async-start(f32[32,1,1028]{2,1,0:T(1,128)} %broadcast_in_dim.11), calls=%async_computation.3 | async-start | bytes 294912 | tf_op jit(solution)/shard_map/all_to_all | solution.py:263
  88.5 7.9 %shard_map.109 = f32[1,8192]{1,0:T(1,128)} custom-call(f32[640,256]{1,0:T(8,128)} %get-tuple-element.138.tab_ref, s32[1,8192]{1,0:T(1,128)} %ids_ref.7, f32[5,8192]{1,0:T(8,128)} %bitcast.108), custom_call_target="tpu_custom_call" | custom-call | tf_op jit(solution)/shard_map/pallas_call | solution.py:89
  96.4 0.5 all-to-all-done.3
  97.0 0.7 slice_reduce_fusion.1
  97.8 0.4 scatter-add.49
  98.2 0.6 multiply_reduce_fusion.4
  100.4 0.7 multiply_add_fusion.1
  101.0 0.1 pad_maximum_fusion.3
  101.2 0.7 reshape.820.tab_ref
  101.9 3.9 %shard_map.110 = (f32[1,8192]{1,0:T(1,128)}, f32[32,384]{1,0:T(8,128)}) custom-call(f32[128,256]{1,0:T(8,128)} %reshape.820.tab_ref, s32[1,8192]{1,0:T(1,128)} %multiply_add_fusion.3.ids_ref, f32[4,8192]{1,0:T(4,128)} %pad_maximum_fusion.2.basis_ref, f32[1,8192]{1,0:T(1,128)} %get-tuple-element.172.zsrc_ref, f32[1,8192]{1,0:T(1,128)} %bitcast.126, ...), custom_call_target="tpu_custom_call" | custom-call | tf_op jit(solution)/shard_map/pallas_call | solution.py:160
  105.9 1.5 %copy.36 = f32[32,1,384]{2,1,0:T(1,128)} copy(f32[32,1,384]{2,0,1:T(8,128)} %bitcast.163) | data formatting | bytes 98304 | tf_op jit(solution)/shard_map/all_to_all | solution.py:277
  107.3 5.1 %all-to-all-start.4 = ((f32[32,1,384]{2,1,0:T(1,128)}), f32[32,1,384]{2,1,0:T(1,128)S(1)}, u32[]{:S(2)}, u32[]{:S(2)}) async-start(f32[32,1,384]{2,1,0:T(1,128)} %copy.36), calls=%async_computation.4 | async-start | bytes 98304 | tf_op jit(solution)/shard_map/all_to_all | solution.py:277
  112.5 7.4 %all-to-all-done.4 = f32[32,1,384]{2,1,0:T(1,128)S(1)} async-done(((f32[32,1,384]{2,1,0:T(1,128)}), f32[32,1,384]{2,1,0:T(1,128)S(1)}, u32[]{:S(2)}, u32[]{:S(2)}) %all-to-all-start.4) | async-done | bytes 49184 | tf_op jit(solution)/shard_map/all_to_all | solution.py:277
  120.0 0.1 multiply_add_fusion
  120.1 0.6 fusion.13
  120.8 1.2 reshape.821
  122.0 0.9 multiply_subtract_fusion.1
  (70 shorter events, 1.3 us)
Async XLA Ops:
  0.6 0.9 copy-start
  0.6 2.8 %copy-start.12 = (s32[1,32]{1,0:T(1,128)S(1)}, s32[1,32]{1,0:T(1,128)}, u32[]{:S(2)}) copy-start(s32[1,32]{1,0:T(1,128)} %param.34) | copy-start | bytes 388
  0.7 3.0 %copy-start.10 = (f32[8192]{0:T(1024)S(1)}, f32[8192]{0:T(1024)}, u32[]{:S(2)}) copy-start(f32[8192]{0:T(1024)} %param.33) | copy-start | bytes 98308
  0.7 3.0 %copy-start.9 = (f32[5,8192]{1,0:T(8,128)S(1)}, f32[5,8192]{1,0:T(8,128)}, u32[]{:S(2)}) copy-start(f32[5,8192]{1,0:T(8,128)} %param.29) | copy-start | bytes 491524
  4.9 17.9 %all-to-all-start = ((f32[32,1,2304]{2,1,0:T(1,128)}), f32[32,1,2304]{2,1,0:T(1,128)S(1)}, u32[]{:S(2)}, u32[]{:S(2)}) async-start(f32[32,1,2304]{2,1,0:T(1,128)} %all_to_all.46), calls=%async_computation | async-start | bytes 589824 | tf_op jit(solution)/shard_map/all_to_all | solution.py:251
  24.3 14.1 %copy-start.2 = (f32[5,32,256]{2,0,1:T(8,128)}, f32[5,32,256]{2,0,1:T(8,128)S(1)}, u32[]{:S(2)}) copy-start(f32[5,32,256]{2,0,1:T(8,128)S(1)} %slice.331) | copy-start | bytes 491524
  26.0 21.1 %all-to-all-start.1 = ((f32[32,1,1028]{2,1,0:T(1,128)}), f32[32,1,1028]{2,1,0:T(1,128)S(1)}, u32[]{:S(2)}, u32[]{:S(2)}) async-start(f32[32,1,1028]{2,1,0:T(1,128)} %broadcast_in_dim.9), calls=%async_computation.1 | async-start | bytes 294912 | tf_op jit(solution)/shard_map/all_to_all | solution.py:263
  38.4 7.9 %copy-start.1 = (f32[640,256]{1,0:T(8,128)S(1)}, f32[640,256]{1,0:T(8,128)}, u32[]{:S(2)}) copy-start(f32[640,256]{1,0:T(8,128)} %shard_map.104.tab_ref) | copy-start | bytes 1966084
  47.1 14.0 %copy-start.7 = (f32[1,32,256]{2,0,1:T(1,128)S(1)}, f32[1,32,256]{2,0,1:T(1,128)}, u32[]{:S(2)}) copy-start(f32[1,32,256]{2,0,1:T(1,128)} %get-tuple-element.140) | copy-start | bytes 98308
  47.1 14.8 %copy-start.3 = (f32[5,32,256]{2,0,1:T(8,128)S(1)}, f32[5,32,256]{2,0,1:T(8,128)}, u32[]{:S(2)}) copy-start(f32[5,32,256]{2,0,1:T(8,128)} %copy-done.2) | copy-start | bytes 491524
  55.4 16.8 %all-to-all-start.2 = ((f32[32,1,384]{2,1,0:T(1,128)}), f32[32,1,384]{2,1,0:T(1,128)S(1)}, u32[]{:S(2)}, u32[]{:S(2)}) async-start(f32[32,1,384]{2,1,0:T(1,128)} %copy.32), calls=%async_computation.2 | async-start | bytes 98304 | tf_op jit(solution)/shard_map/all_to_all | solution.py:277
  70.3 8.7 %copy-start.5 = (f32[640,256]{1,0:T(8,128)S(1)}, f32[640,256]{1,0:T(8,128)}, u32[]{:S(2)}) copy-start(f32[640,256]{1,0:T(8,128)} %shard_map.108) | copy-start | bytes 1966084
  82.5 14.5 %all-to-all-start.3 = ((f32[32,1,1028]{2,1,0:T(1,128)}), f32[32,1,1028]{2,1,0:T(1,128)S(1)}, u32[]{:S(2)}, u32[]{:S(2)}) async-start(f32[32,1,1028]{2,1,0:T(1,128)} %broadcast_in_dim.11), calls=%async_computation.3 | async-start | bytes 294912 | tf_op jit(solution)/shard_map/all_to_all | solution.py:263
  88.5 11.8 %copy-start.8 = (f32[1,8192]{1,0:T(1,128)S(1)}, f32[1,8192]{1,0:T(1,128)}, u32[]{:S(2)}) copy-start(f32[1,8192]{1,0:T(1,128)} %shard_map.105.zsrc_ref) | copy-start | bytes 98308
  96.4 4.0 %copy-start.11 = (f32[1,8192]{1,0:T(1,128)S(1)}, f32[1,8192]{1,0:T(1,128)}, u32[]{:S(2)}) copy-start(f32[1,8192]{1,0:T(1,128)} %shard_map.109) | copy-start | bytes 98308
  97.7 22.3 %copy-start.4 = (f32[640,256]{1,0:T(8,128)S(1)}, f32[640,256]{1,0:T(8,128)}, u32[]{:S(2)}) copy-start(f32[640,256]{1,0:T(8,128)} %get-tuple-element.138.tab_ref) | copy-start | bytes 1966084
  107.3 12.5 %all-to-all-start.4 = ((f32[32,1,384]{2,1,0:T(1,128)}), f32[32,1,384]{2,1,0:T(1,128)S(1)}, u32[]{:S(2)}, u32[]{:S(2)}) async-start(f32[32,1,384]{2,1,0:T(1,128)} %copy.36), calls=%async_computation.4 | async-start | bytes 98304 | tf_op jit(solution)/shard_map/all_to_all | solution.py:277
  120.1 1.8 %copy-start.6 = (f32[12,8192]{1,0:T(8,128)S(1)}, f32[12,8192]{1,0:T(8,128)}, u32[]{:S(2)}) copy-start(f32[12,8192]{1,0:T(8,128)} %param.28) | copy-start | bytes 1179652

commit v10 on v9

--- a/solution.py
+++ b/solution.py
@@ -129,6 +129,7 @@
     shifted = jnp.stack([extended[q:q + knots] for q in range(4)], axis=0)
     rows = 4 * cols
     per_chunk = CHUNK // width
+    line = 128 + -(-width // 128) * 128
 
     def kernel(tab_ref, ids_ref, basis_ref, zsrc_ref, weight_ref, extra_ref, out_ref, pay_ref, big_ref, norm_ref):
         split_into(tab_ref, big_ref)
@@ -148,20 +149,22 @@
             shift = zsrc_ref[:, pl.ds(off, CHUNK)] + z
             out_ref[:, pl.ds(off, CHUNK)] = shift
             for r in range(per_chunk):
-                row = i * per_chunk + r
-                pay_ref[row:row + 1, 128:128 + width] = shift[:, r * width:(r + 1) * width]
+                start = (i * per_chunk + r) * line + 128
+                pay_ref[:, start:start + width] = shift[:, r * width:(r + 1) * width]
             norm_ref[...] += jnp.sum(weight_ref[:, pl.ds(off, CHUNK)] * shift * shift, axis=1, keepdims=True)
 
-        lane = lax.broadcasted_iota(jnp.int32, (parts, 128), 1)
-        pay_ref[:, 0:128] = jnp.where(
-            lane == 0, norm_ref[...], jnp.where(lane == 1, extra_ref[...], 0.0)
-        )
+        lane = lax.broadcasted_iota(jnp.int32, (1, 128), 1)
+        sums = jnp.where(lane == 0, norm_ref[...], jnp.where(lane == 1, extra_ref[...], 0.0))
+        for r in range(parts):
+            pay_ref[:, r * line:r * line + 128] = sums
+            if line > 128 + width:
+                pay_ref[:, r * line + 128 + width:(r + 1) * line] = jnp.zeros((1, line - 128 - width), jnp.float32)
 
     return pl.pallas_call(
         kernel,
         out_shape=(
             jax.ShapeDtypeStruct((1, total), jnp.float32),
-            jax.ShapeDtypeStruct((parts, 128 + width), jnp.float32),
+            jax.ShapeDtypeStruct((1, parts * line), jnp.float32),
         ),
         scratch_shapes=[pltpu.VMEM((2 * rows, HI), jnp.bfloat16), pltpu.VMEM((1, 1), jnp.float32)],
     )(shifted.reshape(rows, HI), first_ids, basis, zsrc, weight, extra.reshape(1, 1))
@@ -274,9 +277,9 @@
         shift_own, payload = knot_gather(
             extended, base_own, basis_own, zsrc, weight_sq_own, extra, n_knots, n_ranks, capacity
         )
-        back = lax.all_to_all(payload, everyone, 0, 0, tiled=True)
+        back = lax.all_to_all(payload.reshape(n_ranks, -1), everyone, 0, 0, tiled=True)
         totals = jnp.sum(back[:, :2], axis=0)
-        return shift_own, back[:, 128:].reshape(1, rows) * live, totals[0], totals[1]
+        return shift_own, back[:, 128:128 + capacity].reshape(1, rows) * live, totals[0], totals[1]
 
     sol_s = jnp.zeros((table_rows, HI), jnp.float32)
     sol_a = jnp.zeros((n_knots,), jnp.float32)

time: 124 us -> 121 us (0.976)
  local copies, waits for them, and re-layouts: 13.1 us -> 10.2 us
    all_to_all x2 -> x0, local copies, waits for them, and re-layouts: 2.93 us -> none  [forward(): back = lax.all_to_all(payload, everyone, 0, 0, tiled=True)]
where the time goes in v10:
time: 121 us; the launch traced here: 120 us
  Pallas kernels  45.9 us (38%)
  starting transfers between devices  27.1 us (22%)
  other arithmetic  17.4 us (14%)
  waiting for transfers between devices  12.3 us (10%)
  local copies, waits for them, and re-layouts  10.2 us (8%)
  between operations  5.2 us (4%)
  matrix products  2 us (2%)
    pallas_call x2, Pallas kernels, source_gather(): pl.pallas_call(kernel, out_shape=jax.ShapeDtypeStruct((1, total), jnp.flo...  15.8 us
    pallas_call x2, Pallas kernels, source_scatter(): pl.pallas_call(kernel, out_shape=jax.ShapeDtypeStruct((rows, HI), jnp.flo...  15.3 us
    all_to_all x2, starting transfers between devices, forward(): lax.all_to_all(payload.reshape(n_ranks, -1), everyone, 0, 0, tiled=True)  10.9 us
    all_to_all x2, starting transfers between devices, combine(): lax.all_to_all(jnp.broadcast_to(mine[None, :], (n_ranks, knots + 4)), eve...  8.85 us
    pallas_call x2, Pallas kernels, knot_gather(): pl.pallas_call(kernel, out_shape=(jax.ShapeDtypeStruct((1, total), jnp.fl...  8.54 us
    all_to_all x2, waiting for transfers between devices, forward(): lax.all_to_all(payload.reshape(n_ranks, -1), everyone, 0, 0, tiled=True)  7.37 us
    all_to_all x1, starting transfers between devices, per_device(): got = lax.all_to_all(blocks, everyone, 0, 0, tiled=True)  7.3 us
    pallas_call x2, Pallas kernels, knot_scatter(): pl.pallas_call(kernel, out_shape=jax.ShapeDtypeStruct((rows, HI), jnp.flo...  6.23 us
  transfers between devices with their start and end apart: 5, of which 3 were waited for; matrix products, arithmetic and copies ran while one was open for 6% of the time, Pallas kernels for 28%

profile of v10, /device:TPU:0, one launch (start us, length us, event | category | flops | bytes accessed | tf_op | source)
XLA Modules:
  0.0 120.0 jit_solution(18076954183821191130)
XLA Ops:
  0.7 0.8 convert_element_type.32
  1.5 2.0 %multiply_reduce_fusion.2 = (f32[8192]{0:T(1024)S(1)}, f32[8192]{0:T(1024)S(1)}, f32[12,8192]{1,0:T(8,128)S(1)}) fusion(f32[12,8192]{1,0:T(8,128)} %param.28, f32[12,62]{1,0:T(8,128)S(1)} %copy-done, s32[8192]{0:T(1024)} %param.31), kind=kOutput, calls=%fused_computation.8 | convolution fusion | flops 74022912 | bytes 887712 | tf_op jit(solution)/shard_map/dot_general | solution.py:230
  3.5 0.1 compare_select_fusion.3
  3.6 0.2 concatenate.48
  3.9 1.0 all_to_all.46
  4.9 7.3 %all-to-all-start = ((f32[32,1,2304]{2,1,0:T(1,128)}), f32[32,1,2304]{2,1,0:T(1,128)S(1)}, u32[]{:S(2)}, u32[]{:S(2)}) async-start(f32[32,1,2304]{2,1,0:T(1,128)} %all_to_all.46), calls=%async_computation | async-start | bytes 589824 | tf_op jit(solution)/shard_map/all_to_all | solution.py:254
  12.4 0.1 pad_maximum_fusion
  12.5 0.1 broadcast_in_dim.8
  12.6 1.0 reshape.808.basis_ref
  13.6 0.7 broadcast_select_fusion.val_ref
  14.2 3.1 %shard_map.103 = f32[16,256]{1,0:T(8,128)} custom-call(f32[1,8192]{1,0:T(1,128)} %broadcast_select_fusion.val_ref, s32[1,8192]{1,0:T(1,128)} %bitcast.130, f32[16,8192]{1,0:T(8,128)} %reshape.808.basis_ref), custom_call_target="tpu_custom_call" | custom-call | tf_op jit(solution)/shard_map/pallas_call | solution.py:194
  17.3 0.8 slice_bitcast_fusion.5
  18.2 0.1 add_dynamic-update-slice_fusion.1
  18.3 0.1 fusion.17
  18.5 0.1 fusion.16
  18.6 4.2 %all-to-all-done = f32[32,1,2304]{2,1,0:T(1,128)S(1)} async-done(((f32[32,1,2304]{2,1,0:T(1,128)}), f32[32,1,2304]{2,1,0:T(1,128)S(1)}, u32[]{:S(2)}, u32[]{:S(2)}) %all-to-all-start) | async-done | bytes 294944 | tf_op jit(solution)/shard_map/all_to_all | solution.py:254
  22.8 0.7 reduce.24
  23.6 0.7 fusion.18
  24.3 0.7 multiply_add_fusion.3.ids_ref
  25.0 0.2 fusion.9
  25.3 0.7 broadcast_in_dim.9
  26.0 3.0 %all-to-all-start.1 = ((f32[32,1,1028]{2,1,0:T(1,128)}), f32[32,1,1028]{2,1,0:T(1,128)S(1)}, u32[]{:S(2)}, u32[]{:S(2)}) async-start(f32[32,1,1028]{2,1,0:T(1,128)} %broadcast_in_dim.9), calls=%async_computation.1 | async-start | bytes 294912 | tf_op jit(solution)/shard_map/all_to_all | solution.py:266
  29.0 0.7 broadcast_multiply_fusion.1.val_ref
  29.8 0.8 pad_maximum_fusion.2.basis_ref
  30.6 7.6 %shard_map.104.tab_ref = f32[640,256]{1,0:T(8,128)} custom-call(f32[5,8192]{1,0:T(8,128)} %broadcast_multiply_fusion.1.val_ref, s32[1,8192]{1,0:T(1,128)} %ids_ref.7), custom_call_target="tpu_custom_call" | custom-call | tf_op jit(solution)/shard_map/pallas_call | solution.py:121
  38.2 7.9 %shard_map.105.zsrc_ref = f32[1,8192]{1,0:T(1,128)} custom-call(f32[640,256]{1,0:T(8,128)} %shard_map.104.tab_ref, s32[1,8192]{1,0:T(1,128)} %ids_ref.7, f32[5,8192]{1,0:T(8,128)} %bitcast.107), custom_call_target="tpu_custom_call" | custom-call | tf_op jit(solution)/shard_map/pallas_call | solution.py:89
  46.1 0.8 multiply_reduce_fusion.1
  47.0 0.1 reduce_sum.121
  47.1 0.4 scatter-add.40
  47.6 0.7 multiply_reduce_fusion.5
  48.4 0.1 pad_maximum_fusion.1
  48.5 0.7 reshape.815.tab_ref
  49.2 4.6 %shard_map.106 = (f32[1,8192]{1,0:T(1,128)}, f32[1,12288]{1,0:T(1,128)}) custom-call(f32[128,256]{1,0:T(8,128)} %reshape.815.tab_ref, s32[1,8192]{1,0:T(1,128)} %multiply_add_fusion.3.ids_ref, f32[4,8192]{1,0:T(4,128)} %pad_maximum_fusion.2.basis_ref, f32[1,8192]{1,0:T(1,128)} %shard_map.105.zsrc_ref, f32[1,8192]{1,0:T(1,128)} %bitcast.125, ...), custom_call_target="tpu_custom_call" | custom-call | tf_op jit(solution)/shard_map/pallas_call | solution.py:163
  53.8 5.8 %all-to-all-start.2 = ((f32[32,1,384]{2,1,0:T(1,128)}), f32[32,1,384]{2,1,0:T(1,128)S(1)}, u32[]{:S(2)}, u32[]{:S(2)}) async-start(f32[32,1,384]{2,1,0:T(1,128)} %bitcast.164), calls=%async_computation.2 | async-start | bytes 98304 | tf_op jit(solution)/shard_map/all_to_all | solution.py:280
  59.7 0.8 mul.386
  60.5 0.7 broadcast_multiply_fusion.val_ref
  61.3 7.6 %shard_map.108 = f32[640,256]{1,0:T(8,128)} custom-call(f32[5,8192]{1,0:T(8,128)} %broadcast_multiply_fusion.val_ref, s32[1,8192]{1,0:T(1,128)} %ids_ref.7), custom_call_target="tpu_custom_call" | custom-call | tf_op jit(solution)/shard_map/pallas_call | solution.py:121
  68.9 0.7 slice_reduce_fusion.2
  71.0 0.6 fusion.19
  73.0 0.7 multiply_subtract_fusion.2.val_ref
  73.7 3.1 %shard_map.107 = f32[16,256]{1,0:T(8,128)} custom-call(f32[1,8192]{1,0:T(1,128)} %multiply_subtract_fusion.2.val_ref, s32[1,8192]{1,0:T(1,128)} %bitcast.131, f32[16,8192]{1,0:T(8,128)} %reshape.808.basis_ref), custom_call_target="tpu_custom_call" | custom-call | tf_op jit(solution)/shard_map/pallas_call | solution.py:194
  76.8 0.8 slice_bitcast_fusion.1
  77.7 1.5 %multiply_reduce_fusion = (f32[]{:T(128)}, f32[640,256]{1,0:T(8,128)}) fusion(f32[640,256]{1,0:T(8,128)S(1)} %copy-done.1, f32[640,256]{1,0:T(8,128)S(1)} %copy-done.5, f32[]{:T(128)S(6)} %div.65), kind=kLoop, calls=%fused_computation.4 | loop fusion | flops 655359 | bytes 1966088 | tf_op jit(solution)/shard_map/reduce_sum | solution.py:309
  79.2 0.1 add_dynamic-update-slice_fusion
  79.4 0.1 fusion.15
  79.5 0.1 fusion.14
  79.6 0.7 pad_maximum_fusion.5
  80.4 0.7 broadcast_in_dim.11
  81.1 5.8 %all-to-all-start.3 = ((f32[32,1,1028]{2,1,0:T(1,128)}), f32[32,1,1028]{2,1,0:T(1,128)S(1)}, u32[]{:S(2)}, u32[]{:S(2)}) async-start(f32[32,1,1028]{2,1,0:T(1,128)} %broadcast_in_dim.11), calls=%async_computation.3 | async-start | bytes 294912 | tf_op jit(solution)/shard_map/all_to_all | solution.py:266
  87.0 7.9 %shard_map.109 = f32[1,8192]{1,0:T(1,128)} custom-call(f32[640,256]{1,0:T(8,128)} %get-tuple-element.138.tab_ref, s32[1,8192]{1,0:T(1,128)} %ids_ref.7, f32[5,8192]{1,0:T(8,128)} %bitcast.108), custom_call_target="tpu_custom_call" | custom-call | tf_op jit(solution)/shard_map/pallas_call | solution.py:89
  94.8 0.8 all-to-all-done.3
  95.6 0.7 slice_reduce_fusion.1
  96.4 0.4 scatter-add.49
  96.9 0.6 multiply_reduce_fusion.4
  99.0 0.7 multiply_add_fusion.1
  99.7 0.1 pad_maximum_fusion.3
  99.8 0.7 reshape.824.tab_ref
  100.6 3.9 %shard_map.110 = (f32[1,8192]{1,0:T(1,128)}, f32[1,12288]{1,0:T(1,128)}) custom-call(f32[128,256]{1,0:T(8,128)} %reshape.824.tab_ref, s32[1,8192]{1,0:T(1,128)} %multiply_add_fusion.3.ids_ref, f32[4,8192]{1,0:T(4,128)} %pad_maximum_fusion.2.basis_ref, f32[1,8192]{1,0:T(1,128)} %get-tuple-element.172.zsrc_ref, f32[1,8192]{1,0:T(1,128)} %bitcast.126, ...), custom_call_target="tpu_custom_call" | custom-call | tf_op jit(solution)/shard_map/pallas_call | solution.py:163
  104.5 5.1 %all-to-all-start.4 = ((f32[32,1,384]{2,1,0:T(1,128)}), f32[32,1,384]{2,1,0:T(1,128)S(1)}, u32[]{:S(2)}, u32[]{:S(2)}) async-start(f32[32,1,384]{2,1,0:T(1,128)} %bitcast.163), calls=%async_computation.4 | async-start | bytes 98304 | tf_op jit(solution)/shard_map/all_to_all | solution.py:280
  109.6 7.4 %all-to-all-done.4 = f32[32,1,384]{2,1,0:T(1,128)S(1)} async-done(((f32[32,1,384]{2,1,0:T(1,128)}), f32[32,1,384]{2,1,0:T(1,128)S(1)}, u32[]{:S(2)}, u32[]{:S(2)}) %all-to-all-start.4) | async-done | bytes 49184 | tf_op jit(solution)/shard_map/all_to_all | solution.py:280
  117.2 0.1 multiply_add_fusion
  117.3 0.6 fusion.13
  118.0 1.2 reshape.825
  119.1 0.9 multiply_subtract_fusion.1
  (68 shorter events, 1.1 us)
Async XLA Ops:
  0.6 0.9 copy-start
  0.6 2.8 %copy-start.12 = (s32[1,32]{1,0:T(1,128)S(1)}, s32[1,32]{1,0:T(1,128)}, u32[]{:S(2)}) copy-start(s32[1,32]{1,0:T(1,128)} %param.34) | copy-start | bytes 388
  0.7 3.0 %copy-start.10 = (f32[8192]{0:T(1024)S(1)}, f32[8192]{0:T(1024)}, u32[]{:S(2)}) copy-start(f32[8192]{0:T(1024)} %param.33) | copy-start | bytes 98308
  0.7 3.0 %copy-start.9 = (f32[5,8192]{1,0:T(8,128)S(1)}, f32[5,8192]{1,0:T(8,128)}, u32[]{:S(2)}) copy-start(f32[5,8192]{1,0:T(8,128)} %param.29) | copy-start | bytes 491524
  4.9 17.9 %all-to-all-start = ((f32[32,1,2304]{2,1,0:T(1,128)}), f32[32,1,2304]{2,1,0:T(1,128)S(1)}, u32[]{:S(2)}, u32[]{:S(2)}) async-start(f32[32,1,2304]{2,1,0:T(1,128)} %all_to_all.46), calls=%async_computation | async-start | bytes 589824 | tf_op jit(solution)/shard_map/all_to_all | solution.py:254
  24.3 13.9 %copy-start.2 = (f32[5,32,256]{2,0,1:T(8,128)}, f32[5,32,256]{2,0,1:T(8,128)S(1)}, u32[]{:S(2)}) copy-start(f32[5,32,256]{2,0,1:T(8,128)S(1)} %slice.331) | copy-start | bytes 491524
  26.0 20.9 %all-to-all-start.1 = ((f32[32,1,1028]{2,1,0:T(1,128)}), f32[32,1,1028]{2,1,0:T(1,128)S(1)}, u32[]{:S(2)}, u32[]{:S(2)}) async-start(f32[32,1,1028]{2,1,0:T(1,128)} %broadcast_in_dim.9), calls=%async_computation.1 | async-start | bytes 294912 | tf_op jit(solution)/shard_map/all_to_all | solution.py:266
  38.2 7.9 %copy-start.1 = (f32[640,256]{1,0:T(8,128)S(1)}, f32[640,256]{1,0:T(8,128)}, u32[]{:S(2)}) copy-start(f32[640,256]{1,0:T(8,128)} %shard_map.104.tab_ref) | copy-start | bytes 1966084
  46.9 12.8 %copy-start.7 = (f32[1,32,256]{2,0,1:T(1,128)S(1)}, f32[1,32,256]{2,0,1:T(1,128)}, u32[]{:S(2)}) copy-start(f32[1,32,256]{2,0,1:T(1,128)} %get-tuple-element.140) | copy-start | bytes 98308
  46.9 13.6 %copy-start.3 = (f32[5,32,256]{2,0,1:T(8,128)S(1)}, f32[5,32,256]{2,0,1:T(8,128)}, u32[]{:S(2)}) copy-start(f32[5,32,256]{2,0,1:T(8,128)} %copy-done.2) | copy-start | bytes 491524
  53.8 17.1 %all-to-all-start.2 = ((f32[32,1,384]{2,1,0:T(1,128)}), f32[32,1,384]{2,1,0:T(1,128)S(1)}, u32[]{:S(2)}, u32[]{:S(2)}) async-start(f32[32,1,384]{2,1,0:T(1,128)} %bitcast.164), calls=%async_computation.2 | async-start | bytes 98304 | tf_op jit(solution)/shard_map/all_to_all | solution.py:280
  68.9 8.8 %copy-start.5 = (f32[640,256]{1,0:T(8,128)S(1)}, f32[640,256]{1,0:T(8,128)}, u32[]{:S(2)}) copy-start(f32[640,256]{1,0:T(8,128)} %shard_map.108) | copy-start | bytes 1966084
  81.1 14.5 %all-to-all-start.3 = ((f32[32,1,1028]{2,1,0:T(1,128)}), f32[32,1,1028]{2,1,0:T(1,128)S(1)}, u32[]{:S(2)}, u32[]{:S(2)}) async-start(f32[32,1,1028]{2,1,0:T(1,128)} %broadcast_in_dim.11), calls=%async_computation.3 | async-start | bytes 294912 | tf_op jit(solution)/shard_map/all_to_all | solution.py:266
  86.9 12.0 %copy-start.8 = (f32[1,8192]{1,0:T(1,128)S(1)}, f32[1,8192]{1,0:T(1,128)}, u32[]{:S(2)}) copy-start(f32[1,8192]{1,0:T(1,128)} %shard_map.105.zsrc_ref) | copy-start | bytes 98308
  94.8 4.2 %copy-start.11 = (f32[1,8192]{1,0:T(1,128)S(1)}, f32[1,8192]{1,0:T(1,128)}, u32[]{:S(2)}) copy-start(f32[1,8192]{1,0:T(1,128)} %shard_map.109) | copy-start | bytes 98308
  96.3 20.9 %copy-start.4 = (f32[640,256]{1,0:T(8,128)S(1)}, f32[640,256]{1,0:T(8,128)}, u32[]{:S(2)}) copy-start(f32[640,256]{1,0:T(8,128)} %get-tuple-element.138.tab_ref) | copy-start | bytes 1966084
  104.5 12.5 %all-to-all-start.4 = ((f32[32,1,384]{2,1,0:T(1,128)}), f32[32,1,384]{2,1,0:T(1,128)S(1)}, u32[]{:S(2)}, u32[]{:S(2)}) async-start(f32[32,1,384]{2,1,0:T(1,128)} %bitcast.163), calls=%async_computation.4 | async-start | bytes 98304 | tf_op jit(solution)/shard_map/all_to_all | solution.py:280
  117.3 1.8 %copy-start.6 = (f32[12,8192]{1,0:T(8,128)S(1)}, f32[12,8192]{1,0:T(8,128)}, u32[]{:S(2)}) copy-start(f32[12,8192]{1,0:T(8,128)} %param.28) | copy-start | bytes 1179652

commit v11 on v10

--- a/solution.py
+++ b/solution.py
@@ -93,12 +93,12 @@
     )(table, ids, held)
 
 
-def source_scatter(values, ids, width):
+def source_scatter(values, ids, width, with_norm=False):
     n, total = values.shape
     cols = width // HI
     rows = n * cols
 
-    def kernel(val_ref, ids_ref, out_ref):
+    def kernel(val_ref, ids_ref, out_ref, *norm_ref):
         out_ref[...] = jnp.zeros(out_ref.shape, jnp.float32)
 
         def body(off):
@@ -117,10 +117,17 @@
             out_ref[...] += res[:rows] + res[rows:]
 
         chunks(total, body)
-
-    return pl.pallas_call(
-        kernel, out_shape=jax.ShapeDtypeStruct((rows, HI), jnp.float32)
+        if with_norm:
+            grad = out_ref[...]
+            norm_ref[0][...] = jnp.sum(jnp.sum(grad * grad, axis=0, keepdims=True), axis=1, keepdims=True)
+
+    shape = jax.ShapeDtypeStruct((rows, HI), jnp.float32)
+    if not with_norm:
+        return pl.pallas_call(kernel, out_shape=shape)(values, ids)
+    grad, norm = pl.pallas_call(
+        kernel, out_shape=(shape, jax.ShapeDtypeStruct((1, 1), jnp.float32))
     )(values, ids)
+    return grad, norm.reshape(())
 
 
 def knot_gather(extended, first_ids, basis, zsrc, weight, extra, knots, parts, width):
@@ -261,11 +268,12 @@
     base_own = (slot_device // n_share) * knots + got[n_params + 3:n_params + 4].astype(jnp.int32)
     table_rows = n_params * (owned // HI)
 
-    def combine(part_a, s_norm):
+    def outgoing(part_a, s_norm):
         mine = jnp.concatenate([part_a, s_norm[None]])
-        every = lax.all_to_all(
-            jnp.broadcast_to(mine[None, :], (n_ranks, knots + 4)), everyone, 0, 0, tiled=True
-        )
+        return jnp.broadcast_to(mine[None, :], (n_ranks, knots + 4))
+
+    def combine(sent):
+        every = lax.all_to_all(sent, everyone, 0, 0, tiled=True)
         block = jnp.sum(every[:, :knots + 3].reshape(n_time, n_share, knots + 3), axis=1)
         main = block[:, :knots].at[1:, :3].add(block[:-1, knots:])
         grad_a = main.reshape(n_knots)
@@ -281,15 +289,14 @@
         totals = jnp.sum(back[:, :2], axis=0)
         return shift_own, back[:, 128:128 + capacity].reshape(1, rows) * live, totals[0], totals[1]
 
-    sol_s = jnp.zeros((table_rows, HI), jnp.float32)
+    sol_s = jnp.zeros((n_params, owned), jnp.float32)
     sol_a = jnp.zeros((n_knots,), jnp.float32)
     resid = observed_residual
     zbar_slot = zbar0
-    part_a = knot_scatter(zbar_slot, first_ids, basis16, knots)
-    part_a, held, zbar0_own = lax.optimization_barrier((part_a, held, zbar0_own))
-    grad_a, gamma_a = combine(part_a, jnp.zeros((), jnp.float32))
-    grad_s = source_scatter(held * zbar0_own, ids, owned)
-    extra = jnp.sum(grad_s * grad_s)
+    sent = outgoing(knot_scatter(zbar_slot, first_ids, basis16, knots), jnp.zeros((), jnp.float32))
+    sent, held, zbar0_own = lax.optimization_barrier((sent, held, zbar0_own))
+    grad_a, gamma_a = combine(sent)
+    grad_s, extra = source_scatter(held * zbar0_own, ids, owned, with_norm=True)
     dir_s, dir_a = (grad_s, grad_a)
     pulled = source_gather(dir_s, ids, held)
     for step in range(ITERS):
@@ -297,7 +304,7 @@
         if step == 0:
             gamma = extra_sum + gamma_a
         alpha = gamma / image_sq
-        sol_s = sol_s + alpha * dir_s
+        sol_s = sol_s + alpha * dir_s.reshape(n_params, owned)
         sol_a = sol_a + alpha * dir_a
         resid = resid - alpha * (weight_factor * shift_slot)
         if step + 1 < ITERS:
@@ -305,8 +312,7 @@
             zbar_slot = zbar_slot - alpha * (weight_sq * shift_slot)
             grad_s = grad_s - alpha * pushed
             grad_a, fresh = combine(
-                knot_scatter(zbar_slot, first_ids, basis16, knots),
-                jnp.sum(grad_s * grad_s),
+                outgoing(knot_scatter(zbar_slot, first_ids, basis16, knots), jnp.sum(grad_s * grad_s))
             )
             raw = source_gather(grad_s, ids, held)
             beta = fresh / gamma
@@ -316,7 +322,7 @@
             gamma = fresh
             extra = jnp.zeros((), jnp.float32)
     mine_a = lax.dynamic_slice(sol_a, (lax.axis_index("tm") * knots,), (knots,))
-    return (sol_s.reshape(n_params, owned), mine_a, resid)
+    return (sol_s, mine_a, resid)
 
 
 def solution(mesh):

time: 121 us -> 120 us (level)
  transfers between devices with their start and end apart: 5 -> 5, of which waited for: 3 -> 3; matrix products, arithmetic and copies ran while one was open for 6% -> 7% of each run, Pallas kernels for 28% -> 29%
where the time goes in v11:
time: 120 us; the launch traced here: 119 us
  Pallas kernels  45.8 us (38%)
  starting transfers between devices  27.3 us (23%)
  other arithmetic  16.5 us (14%)
  waiting for transfers between devices  12 us (10%)
  local copies, waits for them, and re-layouts  10.2 us (8%)
  between operations  5.18 us (4%)
  matrix products  2 us (2%)
    pallas_call x2, Pallas kernels, source_gather(): pl.pallas_call(kernel, out_shape=jax.ShapeDtypeStruct((1, total), jnp.flo...  15.7 us
    all_to_all x2, starting transfers between devices, forward(): lax.all_to_all(payload.reshape(n_ranks, -1), everyone, 0, 0, tiled=True)  10.8 us
    all_to_all x2, starting transfers between devices, combine(): every = lax.all_to_all(sent, everyone, 0, 0, tiled=True)  9.25 us
    pallas_call x2, Pallas kernels, knot_gather(): pl.pallas_call(kernel, out_shape=(jax.ShapeDtypeStruct((1, total), jnp.fl...  8.53 us
    pallas_call x1, Pallas kernels, source_scatter(): return pl.pallas_call(kernel, out_shape=shape)(values, ids)  7.7 us
    pallas_call x1, Pallas kernels, source_scatter(): pl.pallas_call(kernel, out_shape=(shape, jax.ShapeDtypeStruct((1, 1), jnp...  7.64 us
    all_to_all x2, waiting for transfers between devices, forward(): lax.all_to_all(payload.reshape(n_ranks, -1), everyone, 0, 0, tiled=True)  7.37 us
    all_to_all x1, starting transfers between devices, per_device(): got = lax.all_to_all(blocks, everyone, 0, 0, tiled=True)  7.3 us
  transfers between devices with their start and end apart: 5, of which 3 were waited for; matrix products, arithmetic and copies ran while one was open for 7% of the time, Pallas kernels for 29%

profile of v11, /device:TPU:0, one launch (start us, length us, event | category | flops | bytes accessed | tf_op | source)
XLA Modules:
  0.0 119.1 jit_solution(11607899815946792773)
XLA Ops:
  0.7 0.8 convert_element_type.32
  1.5 2.0 %multiply_reduce_fusion.1 = (f32[8192]{0:T(1024)S(1)}, f32[8192]{0:T(1024)S(1)}, f32[12,8192]{1,0:T(8,128)S(1)}) fusion(f32[12,8192]{1,0:T(8,128)} %param.28, f32[12,62]{1,0:T(8,128)S(1)} %copy-done, s32[8192]{0:T(1024)} %param.31), kind=kOutput, calls=%fused_computation.7 | convolution fusion | flops 74022912 | bytes 887712 | tf_op jit(solution)/shard_map/dot_general | solution.py:237
  3.5 0.1 compare_select_fusion.3
  3.6 0.2 concatenate.49
  3.9 1.0 all_to_all.49
  4.9 7.3 %all-to-all-start = ((f32[32,1,2304]{2,1,0:T(1,128)}), f32[32,1,2304]{2,1,0:T(1,128)S(1)}, u32[]{:S(2)}, u32[]{:S(2)}) async-start(f32[32,1,2304]{2,1,0:T(1,128)} %all_to_all.49), calls=%async_computation | async-start | bytes 589824 | tf_op jit(solution)/shard_map/all_to_all | solution.py:261
  12.4 0.1 pad_maximum_fusion
  12.5 0.1 broadcast_in_dim.8
  12.6 1.0 reshape.806.basis_ref
  13.6 0.7 broadcast_select_fusion.val_ref
  14.2 3.1 %shard_map.103 = f32[16,256]{1,0:T(8,128)} custom-call(f32[1,8192]{1,0:T(1,128)} %broadcast_select_fusion.val_ref, s32[1,8192]{1,0:T(1,128)} %bitcast.129, f32[16,8192]{1,0:T(8,128)} %reshape.806.basis_ref), custom_call_target="tpu_custom_call" | custom-call | tf_op jit(solution)/shard_map/pallas_call | solution.py:201
  17.3 0.8 slice_bitcast_fusion.5
  18.1 0.1 add_dynamic-update-slice_fusion.1
  18.3 0.1 fusion.17
  18.4 0.1 fusion.16
  18.7 4.1 %all-to-all-done = f32[32,1,2304]{2,1,0:T(1,128)S(1)} async-done(((f32[32,1,2304]{2,1,0:T(1,128)}), f32[32,1,2304]{2,1,0:T(1,128)S(1)}, u32[]{:S(2)}, u32[]{:S(2)}) %all-to-all-start) | async-done | bytes 294944 | tf_op jit(solution)/shard_map/all_to_all | solution.py:261
  22.8 0.7 reduce.24
  23.6 0.7 fusion.18
  24.3 0.8 all_to_all.38
  25.1 3.2 %all-to-all-start.1 = ((f32[32,1,1028]{2,1,0:T(1,128)}), f32[32,1,1028]{2,1,0:T(1,128)S(1)}, u32[]{:S(2)}, u32[]{:S(2)}) async-start(f32[32,1,1028]{2,1,0:T(1,128)} %all_to_all.38), calls=%async_computation.1 | async-start | bytes 294912 | tf_op jit(solution)/shard_map/all_to_all | solution.py:276
  28.3 0.7 multiply_add_fusion.3.ids_ref
  29.0 0.2 fusion.9
  29.1 0.7 broadcast_multiply_fusion.1.val_ref
  29.9 0.8 pad_maximum_fusion.2.basis_ref
  30.6 7.6 %shard_map.104 = (f32[640,256]{1,0:T(8,128)}, f32[1,1]{1,0:T(1,128)}) custom-call(f32[5,8192]{1,0:T(8,128)} %broadcast_multiply_fusion.1.val_ref, s32[1,8192]{1,0:T(1,128)} %ids_ref.7), custom_call_target="tpu_custom_call" | custom-call | tf_op jit(solution)/shard_map/pallas_call | solution.py:127
  38.3 7.9 %shard_map.105.zsrc_ref = f32[1,8192]{1,0:T(1,128)} custom-call(f32[640,256]{1,0:T(8,128)} %get-tuple-element.134.tab_ref, s32[1,8192]{1,0:T(1,128)} %ids_ref.7, f32[5,8192]{1,0:T(8,128)} %bitcast.106), custom_call_target="tpu_custom_call" | custom-call | tf_op jit(solution)/shard_map/pallas_call | solution.py:89
  46.2 0.1 reduce_sum.112
  46.3 0.4 scatter-add.40
  46.8 0.6 multiply_reduce_fusion.4
  47.6 0.1 pad_maximum_fusion.1
  47.7 0.7 reshape.813.tab_ref
  48.4 4.6 %shard_map.106 = (f32[1,8192]{1,0:T(1,128)}, f32[1,12288]{1,0:T(1,128)}) custom-call(f32[128,256]{1,0:T(8,128)} %reshape.813.tab_ref, s32[1,8192]{1,0:T(1,128)} %multiply_add_fusion.3.ids_ref, f32[4,8192]{1,0:T(4,128)} %pad_maximum_fusion.2.basis_ref, f32[1,8192]{1,0:T(1,128)} %shard_map.105.zsrc_ref, f32[1,8192]{1,0:T(1,128)} %bitcast.124, ...), custom_call_target="tpu_custom_call" | custom-call | tf_op jit(solution)/shard_map/pallas_call | solution.py:170
  53.0 5.7 %all-to-all-start.2 = ((f32[32,1,384]{2,1,0:T(1,128)}), f32[32,1,384]{2,1,0:T(1,128)S(1)}, u32[]{:S(2)}, u32[]{:S(2)}) async-start(f32[32,1,384]{2,1,0:T(1,128)} %bitcast.163), calls=%async_computation.2 | async-start | bytes 98304 | tf_op jit(solution)/shard_map/all_to_all | solution.py:288
  58.7 0.8 mul.384
  59.6 0.7 broadcast_multiply_fusion.val_ref
  60.3 7.7 %shard_map.108 = f32[640,256]{1,0:T(8,128)} custom-call(f32[5,8192]{1,0:T(8,128)} %broadcast_multiply_fusion.val_ref, s32[1,8192]{1,0:T(1,128)} %ids_ref.7), custom_call_target="tpu_custom_call" | custom-call | tf_op jit(solution)/shard_map/pallas_call | solution.py:126
  68.0 0.7 slice_reduce_fusion.2
  70.1 0.6 fusion.19
  72.1 0.7 multiply_subtract_fusion.2.val_ref
  72.7 3.1 %shard_map.107 = f32[16,256]{1,0:T(8,128)} custom-call(f32[1,8192]{1,0:T(1,128)} %multiply_subtract_fusion.2.val_ref, s32[1,8192]{1,0:T(1,128)} %bitcast.130, f32[16,8192]{1,0:T(8,128)} %reshape.806.basis_ref), custom_call_target="tpu_custom_call" | custom-call | tf_op jit(solution)/shard_map/pallas_call | solution.py:201
  75.9 0.8 slice_bitcast_fusion.1
  76.7 1.5 %multiply_reduce_fusion = (f32[]{:T(128)}, f32[640,256]{1,0:T(8,128)}) fusion(f32[640,256]{1,0:T(8,128)S(1)} %copy-done.3, f32[640,256]{1,0:T(8,128)S(1)} %copy-done.5, f32[]{:T(128)S(6)} %div.65), kind=kLoop, calls=%fused_computation.4 | loop fusion | flops 655359 | bytes 1966088 | tf_op jit(solution)/shard_map/reduce_sum | solution.py:315
  78.3 0.1 add_dynamic-update-slice_fusion
  78.4 0.1 fusion.15
  78.5 0.1 fusion.14
  78.7 0.7 pad_maximum_fusion.5
  79.4 0.7 broadcast_in_dim.11
  80.1 6.1 %all-to-all-start.3 = ((f32[32,1,1028]{2,1,0:T(1,128)}), f32[32,1,1028]{2,1,0:T(1,128)S(1)}, u32[]{:S(2)}, u32[]{:S(2)}) async-start(f32[32,1,1028]{2,1,0:T(1,128)} %broadcast_in_dim.11), calls=%async_computation.3 | async-start | bytes 294912 | tf_op jit(solution)/shard_map/all_to_all | solution.py:276
  86.2 7.9 %shard_map.109 = f32[1,8192]{1,0:T(1,128)} custom-call(f32[640,256]{1,0:T(8,128)} %get-tuple-element.142.tab_ref, s32[1,8192]{1,0:T(1,128)} %ids_ref.7, f32[5,8192]{1,0:T(8,128)} %bitcast.107), custom_call_target="tpu_custom_call" | custom-call | tf_op jit(solution)/shard_map/pallas_call | solution.py:89
  94.1 0.5 all-to-all-done.3
  94.6 0.7 slice_reduce_fusion.1
  95.4 0.1 reduce_sum.119
  95.5 0.4 scatter-add.49
  95.9 0.6 multiply_reduce_fusion.3
  98.1 0.7 multiply_add_fusion.1
  98.7 0.1 pad_maximum_fusion.3
  98.9 0.7 reshape.821.tab_ref
  99.6 3.9 %shard_map.110 = (f32[1,8192]{1,0:T(1,128)}, f32[1,12288]{1,0:T(1,128)}) custom-call(f32[128,256]{1,0:T(8,128)} %reshape.821.tab_ref, s32[1,8192]{1,0:T(1,128)} %multiply_add_fusion.3.ids_ref, f32[4,8192]{1,0:T(4,128)} %pad_maximum_fusion.2.basis_ref, f32[1,8192]{1,0:T(1,128)} %get-tuple-element.176.zsrc_ref, f32[1,8192]{1,0:T(1,128)} %bitcast.125, ...), custom_call_target="tpu_custom_call" | custom-call | tf_op jit(solution)/shard_map/pallas_call | solution.py:170
  103.5 5.1 %all-to-all-start.4 = ((f32[32,1,384]{2,1,0:T(1,128)}), f32[32,1,384]{2,1,0:T(1,128)S(1)}, u32[]{:S(2)}, u32[]{:S(2)}) async-start(f32[32,1,384]{2,1,0:T(1,128)} %bitcast.162), calls=%async_computation.4 | async-start | bytes 98304 | tf_op jit(solution)/shard_map/all_to_all | solution.py:288
  108.7 7.4 %all-to-all-done.4 = f32[32,1,384]{2,1,0:T(1,128)S(1)} async-done(((f32[32,1,384]{2,1,0:T(1,128)}), f32[32,1,384]{2,1,0:T(1,128)S(1)}, u32[]{:S(2)}, u32[]{:S(2)}) %all-to-all-start.4) | async-done | bytes 49184 | tf_op jit(solution)/shard_map/all_to_all | solution.py:288
  116.2 0.1 multiply_add_fusion
  116.4 0.6 fusion.13
  117.0 1.2 add.229
  118.2 0.9 multiply_subtract_fusion.1
  (68 shorter events, 1.1 us)
Async XLA Ops:
  0.6 0.9 copy-start
  0.6 2.8 %copy-start.12 = (s32[1,32]{1,0:T(1,128)S(1)}, s32[1,32]{1,0:T(1,128)}, u32[]{:S(2)}) copy-start(s32[1,32]{1,0:T(1,128)} %param.34) | copy-start | bytes 388
  0.7 3.0 %copy-start.10 = (f32[8192]{0:T(1024)S(1)}, f32[8192]{0:T(1024)}, u32[]{:S(2)}) copy-start(f32[8192]{0:T(1024)} %param.33) | copy-start | bytes 98308
  0.7 3.0 %copy-start.9 = (f32[5,8192]{1,0:T(8,128)S(1)}, f32[5,8192]{1,0:T(8,128)}, u32[]{:S(2)}) copy-start(f32[5,8192]{1,0:T(8,128)} %param.29) | copy-start | bytes 491524
  4.9 17.9 %all-to-all-start = ((f32[32,1,2304]{2,1,0:T(1,128)}), f32[32,1,2304]{2,1,0:T(1,128)S(1)}, u32[]{:S(2)}, u32[]{:S(2)}) async-start(f32[32,1,2304]{2,1,0:T(1,128)} %all_to_all.49), calls=%async_computation | async-start | bytes 589824 | tf_op jit(solution)/shard_map/all_to_all | solution.py:261
  24.3 14.0 %copy-start.1 = (f32[5,32,256]{2,0,1:T(8,128)}, f32[5,32,256]{2,0,1:T(8,128)S(1)}, u32[]{:S(2)}) copy-start(f32[5,32,256]{2,0,1:T(8,128)S(1)} %slice.331) | copy-start | bytes 491524
  25.1 21.1 %all-to-all-start.1 = ((f32[32,1,1028]{2,1,0:T(1,128)}), f32[32,1,1028]{2,1,0:T(1,128)S(1)}, u32[]{:S(2)}, u32[]{:S(2)}) async-start(f32[32,1,1028]{2,1,0:T(1,128)} %all_to_all.38), calls=%async_computation.1 | async-start | bytes 294912 | tf_op jit(solution)/shard_map/all_to_all | solution.py:276
  46.1 12.6 %copy-start.7 = (f32[1,32,256]{2,0,1:T(1,128)S(1)}, f32[1,32,256]{2,0,1:T(1,128)}, u32[]{:S(2)}) copy-start(f32[1,32,256]{2,0,1:T(1,128)} %get-tuple-element.144) | copy-start | bytes 98308
  46.2 13.4 %copy-start.2 = (f32[5,32,256]{2,0,1:T(8,128)S(1)}, f32[5,32,256]{2,0,1:T(8,128)}, u32[]{:S(2)}) copy-start(f32[5,32,256]{2,0,1:T(8,128)} %copy-done.1) | copy-start | bytes 491524
  53.0 16.9 %all-to-all-start.2 = ((f32[32,1,384]{2,1,0:T(1,128)}), f32[32,1,384]{2,1,0:T(1,128)S(1)}, u32[]{:S(2)}, u32[]{:S(2)}) async-start(f32[32,1,384]{2,1,0:T(1,128)} %bitcast.163), calls=%async_computation.2 | async-start | bytes 98304 | tf_op jit(solution)/shard_map/all_to_all | solution.py:288
  60.3 16.4 %copy-start.3 = (f32[640,256]{1,0:T(8,128)S(1)}, f32[640,256]{1,0:T(8,128)}, u32[]{:S(2)}) copy-start(f32[640,256]{1,0:T(8,128)} %get-tuple-element.134.tab_ref) | copy-start | bytes 1966084
  68.0 8.7 %copy-start.5 = (f32[640,256]{1,0:T(8,128)S(1)}, f32[640,256]{1,0:T(8,128)}, u32[]{:S(2)}) copy-start(f32[640,256]{1,0:T(8,128)} %shard_map.108) | copy-start | bytes 1966084
  80.1 14.5 %all-to-all-start.3 = ((f32[32,1,1028]{2,1,0:T(1,128)}), f32[32,1,1028]{2,1,0:T(1,128)S(1)}, u32[]{:S(2)}, u32[]{:S(2)}) async-start(f32[32,1,1028]{2,1,0:T(1,128)} %broadcast_in_dim.11), calls=%async_computation.3 | async-start | bytes 294912 | tf_op jit(solution)/shard_map/all_to_all | solution.py:276
  86.2 11.8 %copy-start.8 = (f32[1,8192]{1,0:T(1,128)S(1)}, f32[1,8192]{1,0:T(1,128)}, u32[]{:S(2)}) copy-start(f32[1,8192]{1,0:T(1,128)} %shard_map.105.zsrc_ref) | copy-start | bytes 98308
  94.1 4.0 %copy-start.11 = (f32[1,8192]{1,0:T(1,128)S(1)}, f32[1,8192]{1,0:T(1,128)}, u32[]{:S(2)}) copy-start(f32[1,8192]{1,0:T(1,128)} %shard_map.109) | copy-start | bytes 98308
  95.4 20.9 %copy-start.4 = (f32[640,256]{1,0:T(8,128)S(1)}, f32[640,256]{1,0:T(8,128)}, u32[]{:S(2)}) copy-start(f32[640,256]{1,0:T(8,128)} %get-tuple-element.142.tab_ref) | copy-start | bytes 1966084
  103.5 12.5 %all-to-all-start.4 = ((f32[32,1,384]{2,1,0:T(1,128)}), f32[32,1,384]{2,1,0:T(1,128)S(1)}, u32[]{:S(2)}, u32[]{:S(2)}) async-start(f32[32,1,384]{2,1,0:T(1,128)} %bitcast.162), calls=%async_computation.4 | async-start | bytes 98304 | tf_op jit(solution)/shard_map/all_to_all | solution.py:288
  116.4 1.8 %copy-start.6 = (f32[12,8192]{1,0:T(8,128)S(1)}, f32[12,8192]{1,0:T(8,128)}, u32[]{:S(2)}) copy-start(f32[12,8192]{1,0:T(8,128)} %param.28) | copy-start | bytes 1179652

commit v12 on v11

--- a/solution.py
+++ b/solution.py
@@ -177,13 +177,14 @@
     )(shifted.reshape(rows, HI), first_ids, basis, zsrc, weight, extra.reshape(1, 1))
 
 
-def knot_scatter(values, first_ids, basis16, knots):
+def knot_scatter(values, first_ids, basis16, s_norm, knots, parts):
     total = first_ids.shape[1]
     cols = knots // HI
     rows = 4 * cols
-
-    def kernel(val_ref, ids_ref, basis_ref, out_ref):
-        out_ref[...] = jnp.zeros(out_ref.shape, jnp.float32)
+    line = 128 + (cols + 1) * HI
+
+    def kernel(val_ref, ids_ref, basis_ref, norm_ref, pay_ref, acc_ref):
+        acc_ref[...] = jnp.zeros(acc_ref.shape, jnp.float32)
 
         def body(off):
             idc = ids_ref[:, pl.ds(off, CHUNK)]
@@ -194,18 +195,28 @@
                 spread, hot_rows(idc, CHUNK), (((1,), (1,)), ((), ())),
                 preferred_element_type=jnp.float32,
             )
-            out_ref[...] += res[:rows] + res[rows:]
+            acc_ref[...] += res[:rows] + res[rows:]
 
         chunks(total, body)
-
-    out = pl.pallas_call(
-        kernel, out_shape=jax.ShapeDtypeStruct((rows, HI), jnp.float32)
-    )(values, first_ids, basis16)
-    per_shift = out.reshape(4, knots)
-    grad = jnp.zeros((knots + 3,), jnp.float32)
-    for q in range(4):
-        grad = grad.at[q:q + knots].add(per_shift[q])
-    return grad
+        lane = lax.broadcasted_iota(jnp.int32, (cols, HI), 1)
+        same = acc_ref[0:cols, :]
+        carried = jnp.zeros((cols, HI), jnp.float32)
+        for q in range(1, 4):
+            moved = pltpu.roll(acc_ref[q * cols:(q + 1) * cols, :], q, 1)
+            same = same + jnp.where(lane >= q, moved, 0.0)
+            carried = carried + jnp.where(lane < q, moved, 0.0)
+        blank = jnp.zeros((1, HI), jnp.float32)
+        grid = jnp.concatenate([same, blank], axis=0) + jnp.concatenate([blank, carried], axis=0)
+        head = jnp.where(lax.broadcasted_iota(jnp.int32, (1, 128), 1) == 0, norm_ref[...], 0.0)
+        row = jnp.concatenate([head] + [grid[c:c + 1, :] for c in range(cols + 1)], axis=1)
+        for r in range(parts):
+            pay_ref[:, r * line:(r + 1) * line] = row
+
+    return pl.pallas_call(
+        kernel,
+        out_shape=jax.ShapeDtypeStruct((1, parts * line), jnp.float32),
+        scratch_shapes=[pltpu.VMEM((rows, HI), jnp.float32)],
+    )(values, first_ids, basis16, s_norm.reshape(1, 1)).reshape(parts, line)
 
 
 def per_device(
@@ -268,16 +279,12 @@
     base_own = (slot_device // n_share) * knots + got[n_params + 3:n_params + 4].astype(jnp.int32)
     table_rows = n_params * (owned // HI)
 
-    def outgoing(part_a, s_norm):
-        mine = jnp.concatenate([part_a, s_norm[None]])
-        return jnp.broadcast_to(mine[None, :], (n_ranks, knots + 4))
-
     def combine(sent):
         every = lax.all_to_all(sent, everyone, 0, 0, tiled=True)
-        block = jnp.sum(every[:, :knots + 3].reshape(n_time, n_share, knots + 3), axis=1)
+        block = jnp.sum(every[:, 128:128 + knots + 3].reshape(n_time, n_share, knots + 3), axis=1)
         main = block[:, :knots].at[1:, :3].add(block[:-1, knots:])
         grad_a = main.reshape(n_knots)
-        norm = jnp.sum(every[:, knots + 3]) + jnp.sum(grad_a * grad_a)
+        norm = jnp.sum(every[:, 0]) + jnp.sum(grad_a * grad_a)
         return grad_a, norm
 
     def forward(zsrc, dir_a, extra):
@@ -293,7 +300,7 @@
     sol_a = jnp.zeros((n_knots,), jnp.float32)
     resid = observed_residual
     zbar_slot = zbar0
-    sent = outgoing(knot_scatter(zbar_slot, first_ids, basis16, knots), jnp.zeros((), jnp.float32))
+    sent = knot_scatter(zbar_slot, first_ids, basis16, jnp.zeros((), jnp.float32), knots, n_ranks)
     sent, held, zbar0_own = lax.optimization_barrier((sent, held, zbar0_own))
     grad_a, gamma_a = combine(sent)
     grad_s, extra = source_scatter(held * zbar0_own, ids, owned, with_norm=True)
@@ -304,7 +311,7 @@
         if step == 0:
             gamma = extra_sum + gamma_a
         alpha = gamma / image_sq
-        sol_s = sol_s + alpha * dir_s.reshape(n_params, owned)
+        sol_s = sol_s + alpha * lax.optimization_barrier(dir_s.reshape(n_params, owned))
         sol_a = sol_a + alpha * dir_a
         resid = resid - alpha * (weight_factor * shift_slot)
         if step + 1 < ITERS:
@@ -312,7 +319,7 @@
             zbar_slot = zbar_slot - alpha * (weight_sq * shift_slot)
             grad_s = grad_s - alpha * pushed
             grad_a, fresh = combine(
-                outgoing(knot_scatter(zbar_slot, first_ids, basis16, knots), jnp.sum(grad_s * grad_s))
+                knot_scatter(zbar_slot, first_ids, basis16, jnp.sum(grad_s * grad_s), knots, n_ranks)
             )
             raw = source_gather(grad_s, ids, held)
             beta = fresh / gamma

time: 120 us -> 122 us (1.017)
  other arithmetic: 16.5 us -> 19.6 us
  waiting for transfers between devices: 12 us -> 9.95 us
    pallas_call x0 -> x1, other arithmetic: none -> 2.01 us  [knot_scatter(): pl.pallas_call(kernel, out_shape=jax.ShapeDtypeStruct((1, parts * line),...]
    all_to_all x1, waiting for transfers between devices: 4.14 us -> 2.74 us  [per_device(): got = lax.all_to_all(blocks, everyone, 0, 0, tiled=True)]
  transfers between devices with their start and end apart: 5 -> 5, of which waited for: 3 -> 3; matrix products, arithmetic and copies ran while one was open for 7% -> 8% of each run, Pallas kernels for 29% -> 28%
where the time goes in v12:
time: 122 us; the launch traced here: 121 us
  Pallas kernels  46.8 us (38%)
  starting transfers between devices  27.9 us (23%)
  other arithmetic  19.6 us (16%)
  waiting for transfers between devices  9.95 us (8%)
  local copies, waits for them, and re-layouts  9.59 us (8%)
  between operations  5.07 us (4%)
  matrix products  1.99 us (2%)
    pallas_call x2, Pallas kernels, source_gather(): pl.pallas_call(kernel, out_shape=jax.ShapeDtypeStruct((1, total), jnp.flo...  15.7 us
    all_to_all x2, starting transfers between devices, forward(): lax.all_to_all(payload.reshape(n_ranks, -1), everyone, 0, 0, tiled=True)  11.2 us
    all_to_all x2, starting transfers between devices, combine(): every = lax.all_to_all(sent, everyone, 0, 0, tiled=True)  9.34 us
    pallas_call x2, Pallas kernels, knot_gather(): pl.pallas_call(kernel, out_shape=(jax.ShapeDtypeStruct((1, total), jnp.fl...  8.53 us
    pallas_call x1, Pallas kernels, source_scatter(): return pl.pallas_call(kernel, out_shape=shape)(values, ids)  7.64 us
    pallas_call x1, Pallas kernels, source_scatter(): pl.pallas_call(kernel, out_shape=(shape, jax.ShapeDtypeStruct((1, 1), jnp...  7.64 us
    all_to_all x1, starting transfers between devices, per_device(): got = lax.all_to_all(blocks, everyone, 0, 0, tiled=True)  7.3 us
    pallas_call x2, Pallas kernels, knot_scatter(): pl.pallas_call(kernel, out_shape=jax.ShapeDtypeStruct((1, parts * line),...  7.2 us
  transfers between devices with their start and end apart: 5, of which 3 were waited for; matrix products, arithmetic and copies ran while one was open for 8% of the time, Pallas kernels for 28%

profile of v12, /device:TPU:0, one launch (start us, length us, event | category | flops | bytes accessed | tf_op | source)
XLA Modules:
  0.0 120.9 jit_solution(4110031412356416081)
XLA Ops:
  0.7 0.8 convert_element_type.32
  1.5 2.0 %multiply_reduce_fusion.1 = (f32[8192]{0:T(1024)S(1)}, f32[8192]{0:T(1024)S(1)}, f32[12,8192]{1,0:T(8,128)S(1)}) fusion(f32[12,8192]{1,0:T(8,128)} %param.12, f32[12,62]{1,0:T(8,128)S(1)} %copy-done, s32[8192]{0:T(1024)} %param.15), kind=kOutput, calls=%fused_computation.8 | convolution fusion | flops 74022912 | bytes 887712 | tf_op jit(solution)/shard_map/dot_general | solution.py:248
  3.5 0.1 compare_select_fusion.3
  3.6 0.2 concatenate.26
  3.9 1.0 all_to_all.52
  4.9 7.3 %all-to-all-start = ((f32[32,1,2304]{2,1,0:T(1,128)}), f32[32,1,2304]{2,1,0:T(1,128)S(1)}, u32[]{:S(2)}, u32[]{:S(2)}) async-start(f32[32,1,2304]{2,1,0:T(1,128)} %all_to_all.52), calls=%async_computation | async-start | bytes 589824 | tf_op jit(solution)/shard_map/all_to_all | solution.py:272
  12.2 0.1 fusion.11
  12.3 0.7 broadcast_select_fusion.val_ref
  13.0 0.1 pad_maximum_fusion
  13.1 0.1 broadcast_in_dim.2
  13.2 1.0 reshape.629.basis_ref
  14.2 3.3 %shard_map.103 = f32[1,45056]{1,0:T(1,128)} custom-call(f32[1,8192]{1,0:T(1,128)} %broadcast_select_fusion.val_ref, s32[1,8192]{1,0:T(1,128)} %bitcast.109, f32[16,8192]{1,0:T(8,128)} %reshape.629.basis_ref, f32[1,1]{1,0:T(1,128)} %constant.111.clone.1.norm_ref.extra_ref), custom_call_target="tpu_custom_call" | custom-call | tf_op jit(solution)/shard_map/pallas_call | solution.py:215
  17.5 0.5 broadcast.432
  18.0 2.0 %reduce.12 = f32[45056]{0:T(1024)S(1)} reduce(f32[1,45056]{1,0:T(1,128)} %shard_map.103, f32[]{:T(128)} %broadcast.432), dimensions={0}, to_apply=%pallas_call.36.reduce_sub_computation.3 | reduce | bytes 360452 | tf_op jit(solution)/shard_map/pallas_call | solution.py:215
  20.1 2.7 %all-to-all-done = f32[32,1,2304]{2,1,0:T(1,128)S(1)} async-done(((f32[32,1,2304]{2,1,0:T(1,128)}), f32[32,1,2304]{2,1,0:T(1,128)S(1)}, u32[]{:S(2)}, u32[]{:S(2)}) %all-to-all-start) | async-done | bytes 294944 | tf_op jit(solution)/shard_map/all_to_all | solution.py:272
  22.8 0.7 reduce.9
  23.6 0.7 fusion.14
  24.3 0.8 all_to_all.40
  25.1 3.3 %all-to-all-start.1 = ((f32[32,1,1408]{2,1,0:T(1,128)}), f32[32,1,1408]{2,1,0:T(1,128)S(1)}, u32[]{:S(2)}, u32[]{:S(2)}) async-start(f32[32,1,1408]{2,1,0:T(1,128)} %all_to_all.40), calls=%async_computation.1 | async-start | bytes 360448 | tf_op jit(solution)/shard_map/all_to_all | solution.py:283
  28.4 0.7 multiply_add_fusion.4.ids_ref
  29.0 0.2 fusion.9
  29.2 0.7 broadcast_multiply_fusion.1.val_ref
  29.9 0.8 pad_maximum_fusion.2.basis_ref
  30.7 7.6 %shard_map.104 = (f32[640,256]{1,0:T(8,128)}, f32[1,1]{1,0:T(1,128)}) custom-call(f32[5,8192]{1,0:T(8,128)} %broadcast_multiply_fusion.1.val_ref, s32[1,8192]{1,0:T(1,128)} %ids_ref.7), custom_call_target="tpu_custom_call" | custom-call | tf_op jit(solution)/shard_map/pallas_call | solution.py:127
  38.4 7.9 %shard_map.105.zsrc_ref = f32[1,8192]{1,0:T(1,128)} custom-call(f32[640,256]{1,0:T(8,128)} %get-tuple-element.38.tab_ref, s32[1,8192]{1,0:T(1,128)} %ids_ref.7, f32[5,8192]{1,0:T(8,128)} %bitcast.81), custom_call_target="tpu_custom_call" | custom-call | tf_op jit(solution)/shard_map/pallas_call | solution.py:89
  46.3 0.1 reduce_sum.112
  46.5 0.4 scatter-add.6
  46.9 0.6 multiply_reduce_fusion.4
  47.6 0.1 pad_slice_fusion.5
  47.7 0.5 copy-done.12
  48.2 0.1 pad_maximum_fusion.1
  48.3 0.8 reshape.634.tab_ref
  49.1 4.6 %shard_map.106 = (f32[1,8192]{1,0:T(1,128)}, f32[1,12288]{1,0:T(1,128)}) custom-call(f32[128,256]{1,0:T(8,128)} %reshape.634.tab_ref, s32[1,8192]{1,0:T(1,128)} %multiply_add_fusion.4.ids_ref, f32[4,8192]{1,0:T(4,128)} %pad_maximum_fusion.2.basis_ref, f32[1,8192]{1,0:T(1,128)} %shard_map.105.zsrc_ref, f32[1,8192]{1,0:T(1,128)} %bitcast.100, ...), custom_call_target="tpu_custom_call" | custom-call | tf_op jit(solution)/shard_map/pallas_call | solution.py:170
  53.7 5.7 %all-to-all-start.2 = ((f32[32,1,384]{2,1,0:T(1,128)}), f32[32,1,384]{2,1,0:T(1,128)S(1)}, u32[]{:S(2)}, u32[]{:S(2)}) async-start(f32[32,1,384]{2,1,0:T(1,128)} %bitcast.138), calls=%async_computation.2 | async-start | bytes 98304 | tf_op jit(solution)/shard_map/all_to_all | solution.py:295
  59.4 0.8 mul.385
  60.2 0.7 broadcast_multiply_fusion.val_ref
  60.9 7.6 %shard_map.107 = f32[640,256]{1,0:T(8,128)} custom-call(f32[5,8192]{1,0:T(8,128)} %broadcast_multiply_fusion.val_ref, s32[1,8192]{1,0:T(1,128)} %ids_ref.7), custom_call_target="tpu_custom_call" | custom-call | tf_op jit(solution)/shard_map/pallas_call | solution.py:126
  68.5 0.6 slice_reduce_fusion.2
  70.5 0.6 fusion.15
  72.4 2.6 %multiply_reduce_fusion = (f32[]{:T(128)}, f32[640,256]{1,0:T(8,128)}) fusion(f32[640,256]{1,0:T(8,128)S(1)} %copy-done.1, f32[640,256]{1,0:T(8,128)} %shard_map.107, f32[]{:T(128)S(6)} %div.65), kind=kLoop, calls=%fused_computation.5 | loop fusion | flops 655359 | bytes 1966088 | tf_op jit(solution)/shard_map/reduce_sum | solution.py:322
  75.0 0.7 multiply_subtract_fusion.2.val_ref
  75.7 3.9 %shard_map.108 = f32[1,45056]{1,0:T(1,128)} custom-call(f32[1,8192]{1,0:T(1,128)} %multiply_subtract_fusion.2.val_ref, s32[1,8192]{1,0:T(1,128)} %bitcast.110, f32[16,8192]{1,0:T(8,128)} %reshape.629.basis_ref, f32[1,1]{1,0:T(1,128)} %bitcast.29.norm_ref), custom_call_target="tpu_custom_call" | custom-call | tf_op jit(solution)/shard_map/pallas_call | solution.py:215
  79.7 6.1 %all-to-all-start.3 = ((f32[32,1,1408]{2,1,0:T(1,128)}), f32[32,1,1408]{2,1,0:T(1,128)S(1)}, u32[]{:S(2)}, u32[]{:S(2)}) async-start(f32[32,1,1408]{2,1,0:T(1,128)} %bitcast.90), calls=%async_computation.3 | async-start | bytes 360448 | tf_op jit(solution)/shard_map/all_to_all | solution.py:283
  85.7 0.2 reshape.635
  86.0 0.6 copy.27
  86.6 7.9 %shard_map.109 = f32[1,8192]{1,0:T(1,128)} custom-call(f32[640,256]{1,0:T(8,128)} %get-tuple-element.46.tab_ref, s32[1,8192]{1,0:T(1,128)} %ids_ref.7, f32[5,8192]{1,0:T(8,128)} %bitcast.82), custom_call_target="tpu_custom_call" | custom-call | tf_op jit(solution)/shard_map/pallas_call | solution.py:89
  94.5 0.1 all-to-all-done.3
  94.6 0.6 slice_reduce_fusion.1
  95.3 0.1 reduce_sum.119
  95.4 0.4 scatter-add.9
  95.9 0.7 multiply_reduce_fusion.3
  98.0 0.1 pad_slice_fusion.2
  98.1 0.7 multiply_add_fusion.2
  98.8 0.1 pad_maximum_fusion.3
  98.9 0.7 reshape.641.tab_ref
  99.6 3.9 %shard_map.110 = (f32[1,8192]{1,0:T(1,128)}, f32[1,12288]{1,0:T(1,128)}) custom-call(f32[128,256]{1,0:T(8,128)} %reshape.641.tab_ref, s32[1,8192]{1,0:T(1,128)} %multiply_add_fusion.4.ids_ref, f32[4,8192]{1,0:T(4,128)} %pad_maximum_fusion.2.basis_ref, f32[1,8192]{1,0:T(1,128)} %get-tuple-element.72.zsrc_ref, f32[1,8192]{1,0:T(1,128)} %bitcast.101, ...), custom_call_target="tpu_custom_call" | custom-call | tf_op jit(solution)/shard_map/pallas_call | solution.py:170
  103.6 5.6 %all-to-all-start.4 = ((f32[32,1,384]{2,1,0:T(1,128)}), f32[32,1,384]{2,1,0:T(1,128)}, u32[]{:S(2)}, u32[]{:S(2)}) async-start(f32[32,1,384]{2,1,0:T(1,128)} %bitcast.139), calls=%async_computation.4 | async-start | bytes 98304 | tf_op jit(solution)/shard_map/all_to_all | solution.py:295
  109.2 0.1 multiply_add_fusion.1
  109.3 0.2 reshape.642
  109.5 7.1 %all-to-all-done.4 = f32[32,1,384]{2,1,0:T(1,128)} async-done(((f32[32,1,384]{2,1,0:T(1,128)}), f32[32,1,384]{2,1,0:T(1,128)}, u32[]{:S(2)}, u32[]{:S(2)}) %all-to-all-start.4) | async-done | bytes 49184 | tf_op jit(solution)/shard_map/all_to_all | solution.py:295
  116.6 0.8 copy.39
  117.6 1.3 %fusion.13 = f32[1024]{0:T(1024)} fusion(f32[8192]{0:T(1024)} %copy-done.11, s32[]{:T(128)S(6)} %select_n.29, f32[8192]{0:T(1024)} %bitcast.117, f32[]{:T(128)S(6)} %div.67, f32[]{:T(128)S(6)} %div.65), kind=kLoop, calls=%fused_computation.76 | loop fusion | flops 3072 | bytes 12300 | tf_op jit(solution)/shard_map/add | solution.py:315
  118.9 1.1 multiply_add_fusion
  120.0 0.9 multiply_subtract_fusion.1
  (61 shorter events, 0.7 us)
Async XLA Ops:
  0.6 0.9 copy-start
  0.6 2.8 %copy-start.16 = (s32[1,32]{1,0:T(1,128)S(1)}, s32[1,32]{1,0:T(1,128)}, u32[]{:S(2)}) copy-start(s32[1,32]{1,0:T(1,128)} %param.18) | copy-start | bytes 388
  0.7 3.0 %copy-start.13 = (f32[8192]{0:T(1024)S(1)}, f32[8192]{0:T(1024)}, u32[]{:S(2)}) copy-start(f32[8192]{0:T(1024)} %param.17) | copy-start | bytes 98308
  0.7 3.0 %copy-start.10 = (f32[5,8192]{1,0:T(8,128)S(1)}, f32[5,8192]{1,0:T(8,128)}, u32[]{:S(2)}) copy-start(f32[5,8192]{1,0:T(8,128)} %param.13) | copy-start | bytes 491524
  4.9 17.9 %all-to-all-start = ((f32[32,1,2304]{2,1,0:T(1,128)}), f32[32,1,2304]{2,1,0:T(1,128)S(1)}, u32[]{:S(2)}, u32[]{:S(2)}) async-start(f32[32,1,2304]{2,1,0:T(1,128)} %all_to_all.52), calls=%async_computation | async-start | bytes 589824 | tf_op jit(solution)/shard_map/all_to_all | solution.py:272
  24.3 14.1 %copy-start.2 = (f32[5,32,256]{2,0,1:T(8,128)}, f32[5,32,256]{2,0,1:T(8,128)S(1)}, u32[]{:S(2)}) copy-start(f32[5,32,256]{2,0,1:T(8,128)S(1)} %slice.173) | copy-start | bytes 491524
  25.1 21.1 %all-to-all-start.1 = ((f32[32,1,1408]{2,1,0:T(1,128)}), f32[32,1,1408]{2,1,0:T(1,128)S(1)}, u32[]{:S(2)}, u32[]{:S(2)}) async-start(f32[32,1,1408]{2,1,0:T(1,128)} %all_to_all.40), calls=%async_computation.1 | async-start | bytes 360448 | tf_op jit(solution)/shard_map/all_to_all | solution.py:283
  46.2 13.1 %copy-start.6 = (f32[1,32,256]{2,0,1:T(1,128)S(1)}, f32[1,32,256]{2,0,1:T(1,128)}, u32[]{:S(2)}) copy-start(f32[1,32,256]{2,0,1:T(1,128)} %get-tuple-element.48) | copy-start | bytes 98308
  46.3 13.9 %copy-start.3 = (f32[5,32,256]{2,0,1:T(8,128)S(1)}, f32[5,32,256]{2,0,1:T(8,128)}, u32[]{:S(2)}) copy-start(f32[5,32,256]{2,0,1:T(8,128)} %copy-done.2) | copy-start | bytes 491524
  47.6 21.0 %copy-start.8 = (f32[1,1,8,1024]{3,1,2,0:T(1,128)}, f32[1,1,8,1024]{3,1,2,0:T(1,128)S(1)}, u32[]{:S(2)}) copy-start(f32[1,1,8,1024]{3,1,2,0:T(1,128)S(1)} %copy.22) | copy-start | bytes 98308
  47.6 0.6 copy-start.12
  53.7 18.7 %copy-start.1 = (f32[640,256]{1,0:T(8,128)S(1)}, f32[640,256]{1,0:T(8,128)}, u32[]{:S(2)}) copy-start(f32[640,256]{1,0:T(8,128)} %get-tuple-element.38.tab_ref) | copy-start | bytes 1966084
  53.7 16.7 %all-to-all-start.2 = ((f32[32,1,384]{2,1,0:T(1,128)}), f32[32,1,384]{2,1,0:T(1,128)S(1)}, u32[]{:S(2)}, u32[]{:S(2)}) async-start(f32[32,1,384]{2,1,0:T(1,128)} %bitcast.138), calls=%async_computation.2 | async-start | bytes 98304 | tf_op jit(solution)/shard_map/all_to_all | solution.py:295
  79.7 14.9 %all-to-all-start.3 = ((f32[32,1,1408]{2,1,0:T(1,128)}), f32[32,1,1408]{2,1,0:T(1,128)S(1)}, u32[]{:S(2)}, u32[]{:S(2)}) async-start(f32[32,1,1408]{2,1,0:T(1,128)} %bitcast.90), calls=%async_computation.3 | async-start | bytes 360448 | tf_op jit(solution)/shard_map/all_to_all | solution.py:283
  86.6 11.5 %copy-start.7 = (f32[1,8192]{1,0:T(1,128)S(1)}, f32[1,8192]{1,0:T(1,128)}, u32[]{:S(2)}) copy-start(f32[1,8192]{1,0:T(1,128)} %shard_map.105.zsrc_ref) | copy-start | bytes 98308
  86.6 11.5 %copy-start.9 = (f32[1,1,8,1024]{3,1,2,0:T(1,128)S(1)}, f32[1,1,8,1024]{3,1,2,0:T(1,128)}, u32[]{:S(2)}) copy-start(f32[1,1,8,1024]{3,1,2,0:T(1,128)} %copy-done.8) | copy-start | bytes 98308
  94.6 3.4 %copy-start.15 = (f32[1,8192]{1,0:T(1,128)S(1)}, f32[1,8192]{1,0:T(1,128)}, u32[]{:S(2)}) copy-start(f32[1,8192]{1,0:T(1,128)} %shard_map.109) | copy-start | bytes 98308
  95.3 13.9 %copy-start.4 = (f32[640,256]{1,0:T(8,128)S(1)}, f32[640,256]{1,0:T(8,128)}, u32[]{:S(2)}) copy-start(f32[640,256]{1,0:T(8,128)} %get-tuple-element.46.tab_ref) | copy-start | bytes 1966084
  97.9 5.6 %copy-start.11 = (f32[8192]{0:T(1024)}, f32[8192]{0:T(1024)S(1)}, u32[]{:S(2)}) copy-start(f32[8192]{0:T(1024)S(1)} %bitcast_add_fusion) | copy-start | bytes 98308
  103.6 13.0 %all-to-all-start.4 = ((f32[32,1,384]{2,1,0:T(1,128)}), f32[32,1,384]{2,1,0:T(1,128)}, u32[]{:S(2)}, u32[]{:S(2)}) async-start(f32[32,1,384]{2,1,0:T(1,128)} %bitcast.139), calls=%async_computation.4 | async-start | bytes 98304 | tf_op jit(solution)/shard_map/all_to_all | solution.py:295
  118.9 1.1 copy-start.5
  118.9 1.1 copy-start.14

commit v13 on v11

--- a/solution.py
+++ b/solution.py
@@ -93,17 +93,24 @@
     )(table, ids, held)
 
 
-def source_scatter(values, ids, width, with_norm=False):
+def source_scatter(values, scales, ids, width, with_norm=False):
     n, total = values.shape
     cols = width // HI
     rows = n * cols
-
-    def kernel(val_ref, ids_ref, out_ref, *norm_ref):
+    count = len(scales)
+
+    def kernel(val_ref, *refs):
+        scale_refs = refs[:count]
+        ids_ref, out_ref = refs[count:count + 2]
+        norm_ref = refs[count + 2:]
         out_ref[...] = jnp.zeros(out_ref.shape, jnp.float32)
 
         def body(off):
             idc = ids_ref[:, pl.ds(off, CHUNK)]
-            v = val_ref[:, pl.ds(off, CHUNK)]
+            scale = scale_refs[0][:, pl.ds(off, CHUNK)]
+            for other in scale_refs[1:]:
+                scale = scale * other[:, pl.ds(off, CHUNK)]
+            v = val_ref[:, pl.ds(off, CHUNK)] * scale
             sel = group_mask(idc, cols, CHUNK, cols)
             parts = []
             for piece in pieces(v):
@@ -123,10 +130,10 @@
 
     shape = jax.ShapeDtypeStruct((rows, HI), jnp.float32)
     if not with_norm:
-        return pl.pallas_call(kernel, out_shape=shape)(values, ids)
+        return pl.pallas_call(kernel, out_shape=shape)(values, *scales, ids)
     grad, norm = pl.pallas_call(
         kernel, out_shape=(shape, jax.ShapeDtypeStruct((1, 1), jnp.float32))
-    )(values, ids)
+    )(values, *scales, ids)
     return grad, norm.reshape(())
 
 
@@ -296,7 +303,7 @@
     sent = outgoing(knot_scatter(zbar_slot, first_ids, basis16, knots), jnp.zeros((), jnp.float32))
     sent, held, zbar0_own = lax.optimization_barrier((sent, held, zbar0_own))
     grad_a, gamma_a = combine(sent)
-    grad_s, extra = source_scatter(held * zbar0_own, ids, owned, with_norm=True)
+    grad_s, extra = source_scatter(held, [zbar0_own], ids, owned, with_norm=True)
     dir_s, dir_a = (grad_s, grad_a)
     pulled = source_gather(dir_s, ids, held)
     for step in range(ITERS):
@@ -308,7 +315,7 @@
         sol_a = sol_a + alpha * dir_a
         resid = resid - alpha * (weight_factor * shift_slot)
         if step + 1 < ITERS:
-            pushed = source_scatter(held * (weight_sq_own * shift_own), ids, owned)
+            pushed = source_scatter(held, [weight_sq_own, shift_own], ids, owned)
             zbar_slot = zbar_slot - alpha * (weight_sq * shift_slot)
             grad_s = grad_s - alpha * pushed
             grad_a, fresh = combine(

time: 120 us -> 118 us (0.983)
  other arithmetic: 16.5 us -> 14.3 us
    mul x3 -> x0, other arithmetic: 2.28 us -> none  [the longest x2 1.56 us: per_device(): pushed = source_scatter(held * (weight_sq_own * shift_own), ids, owned)]
  transfers between devices with their start and end apart: 5 -> 5, of which waited for: 3 -> 3; matrix products, arithmetic and copies ran while one was open for 7% -> 5% of each run, Pallas kernels for 29% -> 29%
where the time goes in v13:
time: 118 us; the launch traced here: 117 us
  Pallas kernels  45.9 us (39%)
  starting transfers between devices  27.1 us (23%)
  other arithmetic  14.3 us (12%)
  waiting for transfers between devices  12.2 us (10%)
  local copies, waits for them, and re-layouts  10.8 us (9%)
  between operations  5.01 us (4%)
  matrix products  2 us (2%)
    pallas_call x2, Pallas kernels, source_gather(): pl.pallas_call(kernel, out_shape=jax.ShapeDtypeStruct((1, total), jnp.flo...  15.7 us
    all_to_all x2, starting transfers between devices, forward(): lax.all_to_all(payload.reshape(n_ranks, -1), everyone, 0, 0, tiled=True)  10.9 us
    all_to_all x2, starting transfers between devices, combine(): every = lax.all_to_all(sent, everyone, 0, 0, tiled=True)  8.85 us
    pallas_call x2, Pallas kernels, knot_gather(): pl.pallas_call(kernel, out_shape=(jax.ShapeDtypeStruct((1, total), jnp.fl...  8.54 us
    pallas_call x1, Pallas kernels, source_scatter(): return pl.pallas_call(kernel, out_shape=shape)(values, *scales, ids)  7.74 us
    pallas_call x1, Pallas kernels, source_scatter(): pl.pallas_call(kernel, out_shape=(shape, jax.ShapeDtypeStruct((1, 1), jnp...  7.66 us
    all_to_all x2, waiting for transfers between devices, forward(): lax.all_to_all(payload.reshape(n_ranks, -1), everyone, 0, 0, tiled=True)  7.37 us
    all_to_all x1, starting transfers between devices, per_device(): got = lax.all_to_all(blocks, everyone, 0, 0, tiled=True)  7.3 us
  transfers between devices with their start and end apart: 5, of which 3 were waited for; matrix products, arithmetic and copies ran while one was open for 5% of the time, Pallas kernels for 29%

profile of v13, /device:TPU:0, one launch (start us, length us, event | category | flops | bytes accessed | tf_op | source)
XLA Modules:
  0.0 117.4 jit_solution(17824216345199892564)
XLA Ops:
  0.7 0.8 convert_element_type.32
  1.5 2.0 %multiply_reduce_fusion.1 = (f32[8192]{0:T(1024)S(1)}, f32[8192]{0:T(1024)S(1)}, f32[12,8192]{1,0:T(8,128)S(1)}) fusion(f32[12,8192]{1,0:T(8,128)} %param.28, f32[12,62]{1,0:T(8,128)S(1)} %copy-done, s32[8192]{0:T(1024)} %param.31), kind=kOutput, calls=%fused_computation.7 | convolution fusion | flops 74022912 | bytes 887712 | tf_op jit(solution)/shard_map/dot_general | solution.py:244
  3.5 0.1 compare_select_fusion.3
  3.6 0.2 concatenate.49
  3.9 1.0 all_to_all.49
  4.9 7.3 %all-to-all-start = ((f32[32,1,2304]{2,1,0:T(1,128)}), f32[32,1,2304]{2,1,0:T(1,128)S(1)}, u32[]{:S(2)}, u32[]{:S(2)}) async-start(f32[32,1,2304]{2,1,0:T(1,128)} %all_to_all.49), calls=%async_computation | async-start | bytes 589824 | tf_op jit(solution)/shard_map/all_to_all | solution.py:268
  12.4 0.1 pad_maximum_fusion
  12.5 0.1 broadcast_in_dim.8
  12.6 1.0 reshape.806.basis_ref
  13.6 0.7 broadcast_select_fusion.val_ref
  14.2 3.1 %shard_map.103 = f32[16,256]{1,0:T(8,128)} custom-call(f32[1,8192]{1,0:T(1,128)} %broadcast_select_fusion.val_ref, s32[1,8192]{1,0:T(1,128)} %bitcast.127, f32[16,8192]{1,0:T(8,128)} %reshape.806.basis_ref), custom_call_target="tpu_custom_call" | custom-call | tf_op jit(solution)/shard_map/pallas_call | solution.py:208
  17.4 0.8 slice_bitcast_fusion.5
  18.2 0.1 add_dynamic-update-slice_fusion.1
  18.3 0.1 fusion.17
  18.5 0.1 fusion.16
  18.7 4.1 %all-to-all-done = f32[32,1,2304]{2,1,0:T(1,128)S(1)} async-done(((f32[32,1,2304]{2,1,0:T(1,128)}), f32[32,1,2304]{2,1,0:T(1,128)S(1)}, u32[]{:S(2)}, u32[]{:S(2)}) %all-to-all-start) | async-done | bytes 294944 | tf_op jit(solution)/shard_map/all_to_all | solution.py:268
  22.8 0.7 reduce.24
  23.6 0.7 fusion.18
  24.3 0.7 slice.331
  25.1 0.8 all_to_all.38
  25.8 3.0 %all-to-all-start.1 = ((f32[32,1,1028]{2,1,0:T(1,128)}), f32[32,1,1028]{2,1,0:T(1,128)S(1)}, u32[]{:S(2)}, u32[]{:S(2)}) async-start(f32[32,1,1028]{2,1,0:T(1,128)} %all_to_all.38), calls=%async_computation.1 | async-start | bytes 294912 | tf_op jit(solution)/shard_map/all_to_all | solution.py:283
  28.8 0.7 multiply_add_fusion.3.ids_ref
  29.5 0.2 fusion.9
  29.7 0.8 pad_maximum_fusion.2.basis_ref
  30.4 7.7 %shard_map.104 = (f32[640,256]{1,0:T(8,128)}, f32[1,1]{1,0:T(1,128)}) custom-call(f32[5,8192]{1,0:T(8,128)} %bitcast.103, f32[1,8192]{1,0:T(1,128)} %bitcast.146, s32[1,8192]{1,0:T(1,128)} %ids_ref.3), custom_call_target="tpu_custom_call" | custom-call | tf_op jit(solution)/shard_map/pallas_call | solution.py:134
  38.1 7.9 %shard_map.105.zsrc_ref = f32[1,8192]{1,0:T(1,128)} custom-call(f32[640,256]{1,0:T(8,128)} %get-tuple-element.134.tab_ref, s32[1,8192]{1,0:T(1,128)} %ids_ref.3, f32[5,8192]{1,0:T(8,128)} %bitcast.104), custom_call_target="tpu_custom_call" | custom-call | tf_op jit(solution)/shard_map/pallas_call | solution.py:89
  46.0 0.1 reduce_sum.112
  46.2 0.4 scatter-add.40
  46.6 0.6 multiply_reduce_fusion.4
  47.2 0.1 pad_slice_fusion.5
  47.3 0.1 pad_maximum_fusion.1
  47.5 0.7 reshape.813.tab_ref
  48.2 4.6 %shard_map.106 = (f32[1,8192]{1,0:T(1,128)}, f32[1,12288]{1,0:T(1,128)}) custom-call(f32[128,256]{1,0:T(8,128)} %reshape.813.tab_ref, s32[1,8192]{1,0:T(1,128)} %multiply_add_fusion.3.ids_ref, f32[4,8192]{1,0:T(4,128)} %pad_maximum_fusion.2.basis_ref, f32[1,8192]{1,0:T(1,128)} %shard_map.105.zsrc_ref, f32[1,8192]{1,0:T(1,128)} %bitcast.122, ...), custom_call_target="tpu_custom_call" | custom-call | tf_op jit(solution)/shard_map/pallas_call | solution.py:177
  52.8 5.8 %all-to-all-start.2 = ((f32[32,1,384]{2,1,0:T(1,128)}), f32[32,1,384]{2,1,0:T(1,128)S(1)}, u32[]{:S(2)}, u32[]{:S(2)}) async-start(f32[32,1,384]{2,1,0:T(1,128)} %bitcast.160), calls=%async_computation.2 | async-start | bytes 98304 | tf_op jit(solution)/shard_map/all_to_all | solution.py:295
  58.7 7.7 %shard_map.108 = f32[640,256]{1,0:T(8,128)} custom-call(f32[5,8192]{1,0:T(8,128)} %bitcast.105, f32[1,8192]{1,0:T(1,128)} %bitcast.123, f32[1,8192]{1,0:T(1,128)} %get-tuple-element.137.refs_1_, s32[1,8192]{1,0:T(1,128)} %ids_ref.3), custom_call_target="tpu_custom_call" | custom-call | tf_op jit(solution)/shard_map/pallas_call | solution.py:133
  66.4 0.7 slice_reduce_fusion.2
  68.4 0.6 fusion.19
  70.3 0.7 multiply_subtract_fusion.2.val_ref
  71.0 3.1 %shard_map.107 = f32[16,256]{1,0:T(8,128)} custom-call(f32[1,8192]{1,0:T(1,128)} %multiply_subtract_fusion.2.val_ref, s32[1,8192]{1,0:T(1,128)} %bitcast.128, f32[16,8192]{1,0:T(8,128)} %reshape.806.basis_ref), custom_call_target="tpu_custom_call" | custom-call | tf_op jit(solution)/shard_map/pallas_call | solution.py:208
  74.1 0.8 slice_bitcast_fusion.1
  75.0 1.5 %multiply_reduce_fusion = (f32[]{:T(128)}, f32[640,256]{1,0:T(8,128)}) fusion(f32[640,256]{1,0:T(8,128)S(1)} %copy-done.1, f32[640,256]{1,0:T(8,128)S(1)} %copy-done.3, f32[]{:T(128)S(6)} %div.65), kind=kLoop, calls=%fused_computation.4 | loop fusion | flops 655359 | bytes 1966088 | tf_op jit(solution)/shard_map/reduce_sum | solution.py:322
  76.5 0.1 add_dynamic-update-slice_fusion
  76.7 0.1 fusion.15
  76.8 0.1 fusion.14
  76.9 0.7 pad_maximum_fusion.5
  77.7 0.7 broadcast_in_dim.11
  78.4 5.8 %all-to-all-start.3 = ((f32[32,1,1028]{2,1,0:T(1,128)}), f32[32,1,1028]{2,1,0:T(1,128)S(1)}, u32[]{:S(2)}, u32[]{:S(2)}) async-start(f32[32,1,1028]{2,1,0:T(1,128)} %broadcast_in_dim.11), calls=%async_computation.3 | async-start | bytes 294912 | tf_op jit(solution)/shard_map/all_to_all | solution.py:283
  84.2 7.9 %shard_map.109 = f32[1,8192]{1,0:T(1,128)} custom-call(f32[640,256]{1,0:T(8,128)} %get-tuple-element.142.tab_ref, s32[1,8192]{1,0:T(1,128)} %ids_ref.3, f32[5,8192]{1,0:T(8,128)} %bitcast.106), custom_call_target="tpu_custom_call" | custom-call | tf_op jit(solution)/shard_map/pallas_call | solution.py:89
  92.1 0.7 all-to-all-done.3
  92.9 0.7 slice_reduce_fusion.1
  93.6 0.1 reduce_sum.119
  93.7 0.4 scatter-add.49
  94.2 0.6 multiply_reduce_fusion.3
  96.2 0.1 pad_slice_fusion.2
  96.3 0.7 multiply_add_fusion.1
  97.0 0.1 pad_maximum_fusion.3
  97.1 0.7 reshape.821.tab_ref
  97.9 3.9 %shard_map.110 = (f32[1,8192]{1,0:T(1,128)}, f32[1,12288]{1,0:T(1,128)}) custom-call(f32[128,256]{1,0:T(8,128)} %reshape.821.tab_ref, s32[1,8192]{1,0:T(1,128)} %multiply_add_fusion.3.ids_ref, f32[4,8192]{1,0:T(4,128)} %pad_maximum_fusion.2.basis_ref, f32[1,8192]{1,0:T(1,128)} %get-tuple-element.176.zsrc_ref, f32[1,8192]{1,0:T(1,128)} %bitcast.124, ...), custom_call_target="tpu_custom_call" | custom-call | tf_op jit(solution)/shard_map/pallas_call | solution.py:177
  101.8 5.1 %all-to-all-start.4 = ((f32[32,1,384]{2,1,0:T(1,128)}), f32[32,1,384]{2,1,0:T(1,128)S(1)}, u32[]{:S(2)}, u32[]{:S(2)}) async-start(f32[32,1,384]{2,1,0:T(1,128)} %bitcast.159), calls=%async_computation.4 | async-start | bytes 98304 | tf_op jit(solution)/shard_map/all_to_all | solution.py:295
  107.0 7.4 %all-to-all-done.4 = f32[32,1,384]{2,1,0:T(1,128)S(1)} async-done(((f32[32,1,384]{2,1,0:T(1,128)}), f32[32,1,384]{2,1,0:T(1,128)S(1)}, u32[]{:S(2)}, u32[]{:S(2)}) %all-to-all-start.4) | async-done | bytes 49184 | tf_op jit(solution)/shard_map/all_to_all | solution.py:295
  114.5 0.1 multiply_add_fusion
  114.6 0.6 fusion.13
  115.3 1.2 %add.229 = f32[5,32768]{1,0:T(8,128)} reshape(f32[640,256]{1,0:T(8,128)S(1)} %multiply_add_fusion) | data formatting | bytes 1310720 | tf_op jit(solution)/shard_map/add | solution.py:314
  116.5 0.9 multiply_subtract_fusion.1
  (59 shorter events, 0.9 us)
Async XLA Ops:
  0.6 0.9 copy-start
  0.6 2.8 %copy-start.9 = (s32[1,32]{1,0:T(1,128)S(1)}, s32[1,32]{1,0:T(1,128)}, u32[]{:S(2)}) copy-start(s32[1,32]{1,0:T(1,128)} %param.34) | copy-start | bytes 388
  0.7 3.0 %copy-start.7 = (f32[8192]{0:T(1024)S(1)}, f32[8192]{0:T(1024)}, u32[]{:S(2)}) copy-start(f32[8192]{0:T(1024)} %param.33) | copy-start | bytes 98308
  0.7 3.0 %copy-start.6 = (f32[5,8192]{1,0:T(8,128)S(1)}, f32[5,8192]{1,0:T(8,128)}, u32[]{:S(2)}) copy-start(f32[5,8192]{1,0:T(8,128)} %param.29) | copy-start | bytes 491524
  4.9 17.9 %all-to-all-start = ((f32[32,1,2304]{2,1,0:T(1,128)}), f32[32,1,2304]{2,1,0:T(1,128)S(1)}, u32[]{:S(2)}, u32[]{:S(2)}) async-start(f32[32,1,2304]{2,1,0:T(1,128)} %all_to_all.49), calls=%async_computation | async-start | bytes 589824 | tf_op jit(solution)/shard_map/all_to_all | solution.py:268
  25.8 20.2 %all-to-all-start.1 = ((f32[32,1,1028]{2,1,0:T(1,128)}), f32[32,1,1028]{2,1,0:T(1,128)S(1)}, u32[]{:S(2)}, u32[]{:S(2)}) async-start(f32[32,1,1028]{2,1,0:T(1,128)} %all_to_all.38), calls=%async_computation.1 | async-start | bytes 294912 | tf_op jit(solution)/shard_map/all_to_all | solution.py:283
  52.8 15.5 %all-to-all-start.2 = ((f32[32,1,384]{2,1,0:T(1,128)}), f32[32,1,384]{2,1,0:T(1,128)S(1)}, u32[]{:S(2)}, u32[]{:S(2)}) async-start(f32[32,1,384]{2,1,0:T(1,128)} %bitcast.160), calls=%async_computation.2 | async-start | bytes 98304 | tf_op jit(solution)/shard_map/all_to_all | solution.py:295
  58.6 16.3 %copy-start.1 = (f32[640,256]{1,0:T(8,128)S(1)}, f32[640,256]{1,0:T(8,128)}, u32[]{:S(2)}) copy-start(f32[640,256]{1,0:T(8,128)} %get-tuple-element.134.tab_ref) | copy-start | bytes 1966084
  66.4 8.6 %copy-start.3 = (f32[640,256]{1,0:T(8,128)S(1)}, f32[640,256]{1,0:T(8,128)}, u32[]{:S(2)}) copy-start(f32[640,256]{1,0:T(8,128)} %shard_map.108) | copy-start | bytes 1966084
  78.4 14.5 %all-to-all-start.3 = ((f32[32,1,1028]{2,1,0:T(1,128)}), f32[32,1,1028]{2,1,0:T(1,128)S(1)}, u32[]{:S(2)}, u32[]{:S(2)}) async-start(f32[32,1,1028]{2,1,0:T(1,128)} %broadcast_in_dim.11), calls=%async_computation.3 | async-start | bytes 294912 | tf_op jit(solution)/shard_map/all_to_all | solution.py:283
  84.2 12.0 %copy-start.5 = (f32[1,8192]{1,0:T(1,128)S(1)}, f32[1,8192]{1,0:T(1,128)}, u32[]{:S(2)}) copy-start(f32[1,8192]{1,0:T(1,128)} %shard_map.105.zsrc_ref) | copy-start | bytes 98308
  92.1 4.2 %copy-start.8 = (f32[1,8192]{1,0:T(1,128)S(1)}, f32[1,8192]{1,0:T(1,128)}, u32[]{:S(2)}) copy-start(f32[1,8192]{1,0:T(1,128)} %shard_map.109) | copy-start | bytes 98308
  93.6 20.9 %copy-start.2 = (f32[640,256]{1,0:T(8,128)S(1)}, f32[640,256]{1,0:T(8,128)}, u32[]{:S(2)}) copy-start(f32[640,256]{1,0:T(8,128)} %get-tuple-element.142.tab_ref) | copy-start | bytes 1966084
  101.8 12.5 %all-to-all-start.4 = ((f32[32,1,384]{2,1,0:T(1,128)}), f32[32,1,384]{2,1,0:T(1,128)S(1)}, u32[]{:S(2)}, u32[]{:S(2)}) async-start(f32[32,1,384]{2,1,0:T(1,128)} %bitcast.159), calls=%async_computation.4 | async-start | bytes 98304 | tf_op jit(solution)/shard_map/all_to_all | solution.py:295
  114.6 1.8 %copy-start.4 = (f32[12,8192]{1,0:T(8,128)S(1)}, f32[12,8192]{1,0:T(8,128)}, u32[]{:S(2)}) copy-start(f32[12,8192]{1,0:T(8,128)} %param.28) | copy-start | bytes 1179652

commit v14 on v13

--- a/solution.py
+++ b/solution.py
@@ -184,18 +184,24 @@
     )(shifted.reshape(rows, HI), first_ids, basis, zsrc, weight, extra.reshape(1, 1))
 
 
-def knot_scatter(values, first_ids, basis16, knots):
+def knot_scatter(values, first_ids, basis16, knots, step=None):
     total = first_ids.shape[1]
     cols = knots // HI
     rows = 4 * cols
-
-    def kernel(val_ref, ids_ref, basis_ref, out_ref):
+    extras = [] if step is None else [step[0].reshape(1, 1), step[1], step[2]]
+
+    def kernel(val_ref, ids_ref, basis_ref, *refs):
+        out_ref = refs[-1]
         out_ref[...] = jnp.zeros(out_ref.shape, jnp.float32)
 
         def body(off):
             idc = ids_ref[:, pl.ds(off, CHUNK)]
             sel = group_mask(idc, rows, CHUNK, cols)
-            v = jnp.where(sel, basis_ref[:, pl.ds(off, CHUNK)] * val_ref[:, pl.ds(off, CHUNK)], 0.0)
+            z = val_ref[:, pl.ds(off, CHUNK)]
+            if step is not None:
+                alpha_ref, weight_ref, shift_ref = refs[:3]
+                z = z - alpha_ref[...] * (weight_ref[:, pl.ds(off, CHUNK)] * shift_ref[:, pl.ds(off, CHUNK)])
+            v = jnp.where(sel, basis_ref[:, pl.ds(off, CHUNK)] * z, 0.0)
             spread = jnp.concatenate(pieces(v), axis=0)
             res = lax.dot_general(
                 spread, hot_rows(idc, CHUNK), (((1,), (1,)), ((), ())),
@@ -207,7 +213,7 @@
 
     out = pl.pallas_call(
         kernel, out_shape=jax.ShapeDtypeStruct((rows, HI), jnp.float32)
-    )(values, first_ids, basis16)
+    )(values, first_ids, basis16, *extras)
     per_shift = out.reshape(4, knots)
     grad = jnp.zeros((knots + 3,), jnp.float32)
     for q in range(4):
@@ -316,10 +322,13 @@
         resid = resid - alpha * (weight_factor * shift_slot)
         if step + 1 < ITERS:
             pushed = source_scatter(held, [weight_sq_own, shift_own], ids, owned)
-            zbar_slot = zbar_slot - alpha * (weight_sq * shift_slot)
+            step_slot = (alpha, weight_sq, shift_slot)
+            zbar_next = zbar_slot - alpha * (weight_sq * shift_slot)
             grad_s = grad_s - alpha * pushed
             grad_a, fresh = combine(
-                outgoing(knot_scatter(zbar_slot, first_ids, basis16, knots), jnp.sum(grad_s * grad_s))
+                outgoing(
+                    knot_scatter(zbar_slot, first_ids, basis16, knots, step_slot), jnp.sum(grad_s * grad_s)
+                )
             )
             raw = source_gather(grad_s, ids, held)
             beta = fresh / gamma
@@ -327,6 +336,7 @@
             dir_a = grad_a + beta * dir_a
             pulled = raw + beta * pulled
             gamma = fresh
+            zbar_slot = zbar_next
             extra = jnp.zeros((), jnp.float32)
     mine_a = lax.dynamic_slice(sol_a, (lax.axis_index("tm") * knots,), (knots,))
     return (sol_s, mine_a, resid)

time: 118 us -> 119 us (level)
  no operation moved by 1% of the time
where the time goes in v14:
time: 119 us; the launch traced here: 118 us
  Pallas kernels  46.1 us (39%)
  starting transfers between devices  27.1 us (23%)
  other arithmetic  14.4 us (12%)
  waiting for transfers between devices  12.3 us (10%)
  local copies, waits for them, and re-layouts  10.8 us (9%)
  between operations  5.21 us (4%)
  matrix products  2 us (2%)
    pallas_call x2, Pallas kernels, source_gather(): pl.pallas_call(kernel, out_shape=jax.ShapeDtypeStruct((1, total), jnp.flo...  15.7 us
    all_to_all x2, starting transfers between devices, forward(): lax.all_to_all(payload.reshape(n_ranks, -1), everyone, 0, 0, tiled=True)  10.9 us
    all_to_all x2, starting transfers between devices, combine(): every = lax.all_to_all(sent, everyone, 0, 0, tiled=True)  8.85 us
    pallas_call x2, Pallas kernels, knot_gather(): pl.pallas_call(kernel, out_shape=(jax.ShapeDtypeStruct((1, total), jnp.fl...  8.54 us
    pallas_call x1, Pallas kernels, source_scatter(): return pl.pallas_call(kernel, out_shape=shape)(values, *scales, ids)  7.74 us
    pallas_call x1, Pallas kernels, source_scatter(): pl.pallas_call(kernel, out_shape=(shape, jax.ShapeDtypeStruct((1, 1), jnp...  7.66 us
    all_to_all x2, waiting for transfers between devices, forward(): lax.all_to_all(payload.reshape(n_ranks, -1), everyone, 0, 0, tiled=True)  7.37 us
    all_to_all x1, starting transfers between devices, per_device(): got = lax.all_to_all(blocks, everyone, 0, 0, tiled=True)  7.3 us
  transfers between devices with their start and end apart: 5, of which 3 were waited for; matrix products, arithmetic and copies ran while one was open for 5% of the time, Pallas kernels for 29%

profile of v14, /device:TPU:0, one launch (start us, length us, event | category | flops | bytes accessed | tf_op | source)
XLA Modules:
  0.0 117.8 jit_solution(17272442402103434070)
XLA Ops:
  0.7 0.8 convert_element_type.29
  1.5 2.0 %multiply_reduce_fusion.1 = (f32[8192]{0:T(1024)S(1)}, f32[8192]{0:T(1024)S(1)}, f32[12,8192]{1,0:T(8,128)S(1)}) fusion(f32[12,8192]{1,0:T(8,128)} %param.28, f32[12,62]{1,0:T(8,128)S(1)} %copy-done, s32[8192]{0:T(1024)} %param.31), kind=kOutput, calls=%fused_computation.7 | convolution fusion | flops 74022912 | bytes 887712 | tf_op jit(solution)/shard_map/dot_general | solution.py:250
  3.5 0.1 compare_select_fusion.3
  3.6 0.2 concatenate.49
  3.9 1.0 all_to_all.49
  4.9 7.3 %all-to-all-start = ((f32[32,1,2304]{2,1,0:T(1,128)}), f32[32,1,2304]{2,1,0:T(1,128)S(1)}, u32[]{:S(2)}, u32[]{:S(2)}) async-start(f32[32,1,2304]{2,1,0:T(1,128)} %all_to_all.49), calls=%async_computation | async-start | bytes 589824 | tf_op jit(solution)/shard_map/all_to_all | solution.py:274
  12.4 0.1 pad_maximum_fusion
  12.5 0.1 broadcast_in_dim.8
  12.6 1.0 reshape.788.basis_ref
  13.6 0.7 broadcast_select_fusion.2.val_ref
  14.2 3.1 %shard_map.103 = f32[16,256]{1,0:T(8,128)} custom-call(f32[1,8192]{1,0:T(1,128)} %broadcast_select_fusion.2.val_ref, s32[1,8192]{1,0:T(1,128)} %bitcast.125, f32[16,8192]{1,0:T(8,128)} %reshape.788.basis_ref), custom_call_target="tpu_custom_call" | custom-call | tf_op jit(solution)/shard_map/pallas_call | solution.py:214
  17.3 0.8 slice_bitcast_fusion.5
  18.1 0.1 add_dynamic-update-slice_fusion.1
  18.3 0.1 fusion.17
  18.4 0.1 fusion.16
  18.7 4.1 %all-to-all-done = f32[32,1,2304]{2,1,0:T(1,128)S(1)} async-done(((f32[32,1,2304]{2,1,0:T(1,128)}), f32[32,1,2304]{2,1,0:T(1,128)S(1)}, u32[]{:S(2)}, u32[]{:S(2)}) %all-to-all-start) | async-done | bytes 294944 | tf_op jit(solution)/shard_map/all_to_all | solution.py:274
  22.8 0.7 reduce.24
  23.6 0.7 fusion.18
  24.3 0.7 slice.331
  25.0 0.8 all_to_all.38
  25.8 3.0 %all-to-all-start.1 = ((f32[32,1,1028]{2,1,0:T(1,128)}), f32[32,1,1028]{2,1,0:T(1,128)S(1)}, u32[]{:S(2)}, u32[]{:S(2)}) async-start(f32[32,1,1028]{2,1,0:T(1,128)} %all_to_all.38), calls=%async_computation.1 | async-start | bytes 294912 | tf_op jit(solution)/shard_map/all_to_all | solution.py:289
  28.8 0.7 multiply_add_fusion.3.ids_ref
  29.5 0.2 fusion.9
  29.7 0.8 pad_maximum_fusion.2.basis_ref
  30.4 7.7 %shard_map.104 = (f32[640,256]{1,0:T(8,128)}, f32[1,1]{1,0:T(1,128)}) custom-call(f32[5,8192]{1,0:T(8,128)} %bitcast.104, f32[1,8192]{1,0:T(1,128)} %bitcast.146, s32[1,8192]{1,0:T(1,128)} %ids_ref.3), custom_call_target="tpu_custom_call" | custom-call | tf_op jit(solution)/shard_map/pallas_call | solution.py:134
  38.1 7.9 %shard_map.105.zsrc_ref = f32[1,8192]{1,0:T(1,128)} custom-call(f32[640,256]{1,0:T(8,128)} %get-tuple-element.134.tab_ref, s32[1,8192]{1,0:T(1,128)} %ids_ref.3, f32[5,8192]{1,0:T(8,128)} %bitcast.105), custom_call_target="tpu_custom_call" | custom-call | tf_op jit(solution)/shard_map/pallas_call | solution.py:89
  46.0 0.1 reduce_sum.112
  46.2 0.4 scatter-add.40
  46.6 0.7 multiply_reduce_fusion.4
  47.3 0.1 pad_slice_fusion.5
  47.4 0.1 pad_maximum_fusion.1
  47.6 0.7 reshape.795.tab_ref
  48.3 4.6 %shard_map.106 = (f32[1,8192]{1,0:T(1,128)}, f32[1,12288]{1,0:T(1,128)}) custom-call(f32[128,256]{1,0:T(8,128)} %reshape.795.tab_ref, s32[1,8192]{1,0:T(1,128)} %multiply_add_fusion.3.ids_ref, f32[4,8192]{1,0:T(4,128)} %pad_maximum_fusion.2.basis_ref, f32[1,8192]{1,0:T(1,128)} %shard_map.105.zsrc_ref, f32[1,8192]{1,0:T(1,128)} %bitcast.120, ...), custom_call_target="tpu_custom_call" | custom-call | tf_op jit(solution)/shard_map/pallas_call | solution.py:177
  52.9 5.8 %all-to-all-start.2 = ((f32[32,1,384]{2,1,0:T(1,128)}), f32[32,1,384]{2,1,0:T(1,128)S(1)}, u32[]{:S(2)}, u32[]{:S(2)}) async-start(f32[32,1,384]{2,1,0:T(1,128)} %bitcast.160), calls=%async_computation.2 | async-start | bytes 98304 | tf_op jit(solution)/shard_map/all_to_all | solution.py:301
  58.8 7.7 %shard_map.108 = f32[640,256]{1,0:T(8,128)} custom-call(f32[5,8192]{1,0:T(8,128)} %bitcast.106, f32[1,8192]{1,0:T(1,128)} %bitcast.121, f32[1,8192]{1,0:T(1,128)} %get-tuple-element.137.refs_1_, s32[1,8192]{1,0:T(1,128)} %ids_ref.3), custom_call_target="tpu_custom_call" | custom-call | tf_op jit(solution)/shard_map/pallas_call | solution.py:133
  66.5 0.7 slice_reduce_fusion.2
  68.6 0.6 fusion.19
  70.6 0.7 broadcast_select_fusion
  71.3 3.3 %shard_map.107 = f32[16,256]{1,0:T(8,128)} custom-call(f32[1,8192]{1,0:T(1,128)} %broadcast_select_fusion.2.val_ref, s32[1,8192]{1,0:T(1,128)} %bitcast.126, f32[16,8192]{1,0:T(8,128)} %reshape.788.basis_ref, f32[1,1]{1,0:T(1,128)} %bitcast.26.refs_0_, f32[1,8192]{1,0:T(1,128)} %get-tuple-element.153.refs_1_, f32[1,8192]{1,0:T(1,128)} %get-tuple-element.152.refs_2_), custom_call_target="tpu_custom_call" | custom-call | tf_op jit(solution)/shard_map/pallas_call | solution.py:214
  74.6 0.8 slice_bitcast_fusion.1
  75.4 1.5 %multiply_reduce_fusion = (f32[]{:T(128)}, f32[640,256]{1,0:T(8,128)}) fusion(f32[640,256]{1,0:T(8,128)S(1)} %copy-done.1, f32[640,256]{1,0:T(8,128)S(1)} %copy-done.3, f32[]{:T(128)} %div.65), kind=kLoop, calls=%fused_computation.4 | loop fusion | flops 655359 | bytes 1966088 | tf_op jit(solution)/shard_map/reduce_sum | solution.py:330
  77.0 0.1 add_dynamic-update-slice_fusion
  77.1 0.1 fusion.15
  77.2 0.1 fusion.14
  77.4 0.7 pad_maximum_fusion.5
  78.1 0.7 broadcast_in_dim.11
  78.9 5.8 %all-to-all-start.3 = ((f32[32,1,1028]{2,1,0:T(1,128)}), f32[32,1,1028]{2,1,0:T(1,128)S(1)}, u32[]{:S(2)}, u32[]{:S(2)}) async-start(f32[32,1,1028]{2,1,0:T(1,128)} %broadcast_in_dim.11), calls=%async_computation.3 | async-start | bytes 294912 | tf_op jit(solution)/shard_map/all_to_all | solution.py:289
  84.7 7.9 %shard_map.109 = f32[1,8192]{1,0:T(1,128)} custom-call(f32[640,256]{1,0:T(8,128)} %get-tuple-element.142.tab_ref, s32[1,8192]{1,0:T(1,128)} %ids_ref.3, f32[5,8192]{1,0:T(8,128)} %bitcast.107), custom_call_target="tpu_custom_call" | custom-call | tf_op jit(solution)/shard_map/pallas_call | solution.py:89
  92.6 0.8 all-to-all-done.3
  93.3 0.7 slice_reduce_fusion.1
  94.1 0.1 reduce_sum.119
  94.2 0.4 scatter-add.49
  94.6 0.6 multiply_reduce_fusion.3
  96.6 0.1 pad_slice_fusion.2
  96.8 0.7 multiply_add_fusion.1
  97.4 0.1 pad_maximum_fusion.3
  97.6 0.7 reshape.804.tab_ref
  98.3 3.9 %shard_map.110 = (f32[1,8192]{1,0:T(1,128)}, f32[1,12288]{1,0:T(1,128)}) custom-call(f32[128,256]{1,0:T(8,128)} %reshape.804.tab_ref, s32[1,8192]{1,0:T(1,128)} %multiply_add_fusion.3.ids_ref, f32[4,8192]{1,0:T(4,128)} %pad_maximum_fusion.2.basis_ref, f32[1,8192]{1,0:T(1,128)} %get-tuple-element.178.zsrc_ref, f32[1,8192]{1,0:T(1,128)} %bitcast.122, ...), custom_call_target="tpu_custom_call" | custom-call | tf_op jit(solution)/shard_map/pallas_call | solution.py:177
  102.3 5.1 %all-to-all-start.4 = ((f32[32,1,384]{2,1,0:T(1,128)}), f32[32,1,384]{2,1,0:T(1,128)S(1)}, u32[]{:S(2)}, u32[]{:S(2)}) async-start(f32[32,1,384]{2,1,0:T(1,128)} %bitcast.159), calls=%async_computation.4 | async-start | bytes 98304 | tf_op jit(solution)/shard_map/all_to_all | solution.py:301
  107.4 7.4 %all-to-all-done.4 = f32[32,1,384]{2,1,0:T(1,128)S(1)} async-done(((f32[32,1,384]{2,1,0:T(1,128)}), f32[32,1,384]{2,1,0:T(1,128)S(1)}, u32[]{:S(2)}, u32[]{:S(2)}) %all-to-all-start.4) | async-done | bytes 49184 | tf_op jit(solution)/shard_map/all_to_all | solution.py:301
  114.9 0.1 multiply_add_fusion
  115.1 0.6 fusion.13
  115.7 1.2 %add.229 = f32[5,32768]{1,0:T(8,128)} reshape(f32[640,256]{1,0:T(8,128)S(1)} %multiply_add_fusion) | data formatting | bytes 1310720 | tf_op jit(solution)/shard_map/add | solution.py:320
  116.9 0.9 multiply_subtract_fusion.1
  (59 shorter events, 0.9 us)
Async XLA Ops:
  0.6 0.9 copy-start
  0.6 2.8 %copy-start.9 = (s32[1,32]{1,0:T(1,128)S(1)}, s32[1,32]{1,0:T(1,128)}, u32[]{:S(2)}) copy-start(s32[1,32]{1,0:T(1,128)} %param.34) | copy-start | bytes 388
  0.7 3.0 %copy-start.7 = (f32[8192]{0:T(1024)S(1)}, f32[8192]{0:T(1024)}, u32[]{:S(2)}) copy-start(f32[8192]{0:T(1024)} %param.33) | copy-start | bytes 98308
  0.7 3.0 %copy-start.6 = (f32[5,8192]{1,0:T(8,128)S(1)}, f32[5,8192]{1,0:T(8,128)}, u32[]{:S(2)}) copy-start(f32[5,8192]{1,0:T(8,128)} %param.29) | copy-start | bytes 491524
  4.9 17.9 %all-to-all-start = ((f32[32,1,2304]{2,1,0:T(1,128)}), f32[32,1,2304]{2,1,0:T(1,128)S(1)}, u32[]{:S(2)}, u32[]{:S(2)}) async-start(f32[32,1,2304]{2,1,0:T(1,128)} %all_to_all.49), calls=%async_computation | async-start | bytes 589824 | tf_op jit(solution)/shard_map/all_to_all | solution.py:274
  25.8 20.2 %all-to-all-start.1 = ((f32[32,1,1028]{2,1,0:T(1,128)}), f32[32,1,1028]{2,1,0:T(1,128)S(1)}, u32[]{:S(2)}, u32[]{:S(2)}) async-start(f32[32,1,1028]{2,1,0:T(1,128)} %all_to_all.38), calls=%async_computation.1 | async-start | bytes 294912 | tf_op jit(solution)/shard_map/all_to_all | solution.py:289
  52.9 15.6 %all-to-all-start.2 = ((f32[32,1,384]{2,1,0:T(1,128)}), f32[32,1,384]{2,1,0:T(1,128)S(1)}, u32[]{:S(2)}, u32[]{:S(2)}) async-start(f32[32,1,384]{2,1,0:T(1,128)} %bitcast.160), calls=%async_computation.2 | async-start | bytes 98304 | tf_op jit(solution)/shard_map/all_to_all | solution.py:301
  58.7 16.7 %copy-start.1 = (f32[640,256]{1,0:T(8,128)S(1)}, f32[640,256]{1,0:T(8,128)}, u32[]{:S(2)}) copy-start(f32[640,256]{1,0:T(8,128)} %get-tuple-element.134.tab_ref) | copy-start | bytes 1966084
  66.5 8.9 %copy-start.3 = (f32[640,256]{1,0:T(8,128)S(1)}, f32[640,256]{1,0:T(8,128)}, u32[]{:S(2)}) copy-start(f32[640,256]{1,0:T(8,128)} %shard_map.108) | copy-start | bytes 1966084
  78.9 14.5 %all-to-all-start.3 = ((f32[32,1,1028]{2,1,0:T(1,128)}), f32[32,1,1028]{2,1,0:T(1,128)S(1)}, u32[]{:S(2)}, u32[]{:S(2)}) async-start(f32[32,1,1028]{2,1,0:T(1,128)} %broadcast_in_dim.11), calls=%async_computation.3 | async-start | bytes 294912 | tf_op jit(solution)/shard_map/all_to_all | solution.py:289
  84.7 12.0 %copy-start.5 = (f32[1,8192]{1,0:T(1,128)S(1)}, f32[1,8192]{1,0:T(1,128)}, u32[]{:S(2)}) copy-start(f32[1,8192]{1,0:T(1,128)} %shard_map.105.zsrc_ref) | copy-start | bytes 98308
  92.6 4.2 %copy-start.8 = (f32[1,8192]{1,0:T(1,128)S(1)}, f32[1,8192]{1,0:T(1,128)}, u32[]{:S(2)}) copy-start(f32[1,8192]{1,0:T(1,128)} %shard_map.109) | copy-start | bytes 98308
  94.1 20.9 %copy-start.2 = (f32[640,256]{1,0:T(8,128)S(1)}, f32[640,256]{1,0:T(8,128)}, u32[]{:S(2)}) copy-start(f32[640,256]{1,0:T(8,128)} %get-tuple-element.142.tab_ref) | copy-start | bytes 1966084
  102.3 12.5 %all-to-all-start.4 = ((f32[32,1,384]{2,1,0:T(1,128)}), f32[32,1,384]{2,1,0:T(1,128)S(1)}, u32[]{:S(2)}, u32[]{:S(2)}) async-start(f32[32,1,384]{2,1,0:T(1,128)} %bitcast.159), calls=%async_computation.4 | async-start | bytes 98304 | tf_op jit(solution)/shard_map/all_to_all | solution.py:301
  115.1 1.8 %copy-start.4 = (f32[12,8192]{1,0:T(8,128)S(1)}, f32[12,8192]{1,0:T(8,128)}, u32[]{:S(2)}) copy-start(f32[12,8192]{1,0:T(8,128)} %param.28) | copy-start | bytes 1179652

commit v15 on v13

--- a/solution.py
+++ b/solution.py
@@ -137,7 +137,7 @@
     return grad, norm.reshape(())
 
 
-def knot_gather(extended, first_ids, basis, zsrc, weight, extra, knots, parts, width):
+def knot_gather(extended, first_ids, basis, zsrc, weight, extra, knots, parts, width, carry=None):
     total = first_ids.shape[1]
     cols = knots // HI
     shifted = jnp.stack([extended[q:q + knots] for q in range(4)], axis=0)
@@ -145,7 +145,10 @@
     per_chunk = CHUNK // width
     line = 128 + -(-width // 128) * 128
 
-    def kernel(tab_ref, ids_ref, basis_ref, zsrc_ref, weight_ref, extra_ref, out_ref, pay_ref, big_ref, norm_ref):
+    extras = [] if carry is None else [carry[0].reshape(1, 1), carry[1]]
+
+    def kernel(tab_ref, ids_ref, basis_ref, zsrc_ref, weight_ref, extra_ref, *refs):
+        out_ref, pay_ref, big_ref, norm_ref = refs[-4:]
         split_into(tab_ref, big_ref)
         norm_ref[...] = jnp.zeros(norm_ref.shape, jnp.float32)
 
@@ -161,6 +164,8 @@
                 value = jnp.sum(jnp.where(sel, acc[q * cols:(q + 1) * cols], 0.0), axis=0, keepdims=True)
                 z = z + b[q:q + 1] * value
             shift = zsrc_ref[:, pl.ds(off, CHUNK)] + z
+            if carry is not None:
+                shift = shift + refs[0][...] * refs[1][:, pl.ds(off, CHUNK)]
             out_ref[:, pl.ds(off, CHUNK)] = shift
             for r in range(per_chunk):
                 start = (i * per_chunk + r) * line + 128
@@ -181,7 +186,7 @@
             jax.ShapeDtypeStruct((1, parts * line), jnp.float32),
         ),
         scratch_shapes=[pltpu.VMEM((2 * rows, HI), jnp.bfloat16), pltpu.VMEM((1, 1), jnp.float32)],
-    )(shifted.reshape(rows, HI), first_ids, basis, zsrc, weight, extra.reshape(1, 1))
+    )(shifted.reshape(rows, HI), first_ids, basis, zsrc, weight, extra.reshape(1, 1), *extras)
 
 
 def knot_scatter(values, first_ids, basis16, knots):
@@ -287,10 +292,10 @@
         norm = jnp.sum(every[:, knots + 3]) + jnp.sum(grad_a * grad_a)
         return grad_a, norm
 
-    def forward(zsrc, dir_a, extra):
+    def forward(zsrc, dir_a, extra, carry=None):
         extended = jnp.concatenate([dir_a, jnp.zeros((3,), jnp.float32)])
         shift_own, payload = knot_gather(
-            extended, base_own, basis_own, zsrc, weight_sq_own, extra, n_knots, n_ranks, capacity
+            extended, base_own, basis_own, zsrc, weight_sq_own, extra, n_knots, n_ranks, capacity, carry
         )
         back = lax.all_to_all(payload.reshape(n_ranks, -1), everyone, 0, 0, tiled=True)
         totals = jnp.sum(back[:, :2], axis=0)
@@ -305,9 +310,9 @@
     grad_a, gamma_a = combine(sent)
     grad_s, extra = source_scatter(held, [zbar0_own], ids, owned, with_norm=True)
     dir_s, dir_a = (grad_s, grad_a)
-    pulled = source_gather(dir_s, ids, held)
+    zsrc, att, carry = source_gather(dir_s, ids, held), dir_a, None
     for step in range(ITERS):
-        shift_own, shift_slot, image_sq, extra_sum = forward(pulled, dir_a, extra)
+        shift_own, shift_slot, image_sq, extra_sum = forward(zsrc, att, extra, carry)
         if step == 0:
             gamma = extra_sum + gamma_a
         alpha = gamma / image_sq
@@ -321,11 +326,11 @@
             grad_a, fresh = combine(
                 outgoing(knot_scatter(zbar_slot, first_ids, basis16, knots), jnp.sum(grad_s * grad_s))
             )
-            raw = source_gather(grad_s, ids, held)
+            zsrc, att = source_gather(grad_s, ids, held), grad_a
             beta = fresh / gamma
+            carry = (beta, shift_own)
             dir_s = grad_s + beta * dir_s
             dir_a = grad_a + beta * dir_a
-            pulled = raw + beta * pulled
             gamma = fresh
             extra = jnp.zeros((), jnp.float32)
     mine_a = lax.dynamic_slice(sol_a, (lax.axis_index("tm") * knots,), (knots,))

time: 118 us -> 118 us (level)
  no operation moved by 1% of the time
where the time goes in v15:
time: 118 us; the launch traced here: 117 us
  Pallas kernels  45.9 us (39%)
  starting transfers between devices  27 us (23%)
  other arithmetic  13.6 us (12%)
  waiting for transfers between devices  12.3 us (10%)
  local copies, waits for them, and re-layouts  10.9 us (9%)
  between operations  5.17 us (4%)
  matrix products  2 us (2%)
    pallas_call x2, Pallas kernels, source_gather(): pl.pallas_call(kernel, out_shape=jax.ShapeDtypeStruct((1, total), jnp.flo...  15.7 us
    all_to_all x2, starting transfers between devices, forward(): lax.all_to_all(payload.reshape(n_ranks, -1), everyone, 0, 0, tiled=True)  10.9 us
    all_to_all x2, starting transfers between devices, combine(): every = lax.all_to_all(sent, everyone, 0, 0, tiled=True)  8.85 us
    pallas_call x2, Pallas kernels, knot_gather(): pl.pallas_call(kernel, out_shape=(jax.ShapeDtypeStruct((1, total), jnp.fl...  8.56 us
    pallas_call x1, Pallas kernels, source_scatter(): return pl.pallas_call(kernel, out_shape=shape)(values, *scales, ids)  7.73 us
    pallas_call x1, Pallas kernels, source_scatter(): pl.pallas_call(kernel, out_shape=(shape, jax.ShapeDtypeStruct((1, 1), jnp...  7.66 us
    all_to_all x2, waiting for transfers between devices, forward(): lax.all_to_all(payload.reshape(n_ranks, -1), everyone, 0, 0, tiled=True)  7.37 us
    all_to_all x1, starting transfers between devices, per_device(): got = lax.all_to_all(blocks, everyone, 0, 0, tiled=True)  7.3 us
  transfers between devices with their start and end apart: 5, of which 3 were waited for; matrix products, arithmetic and copies ran while one was open for 5% of the time, Pallas kernels for 29%

profile of v15, /device:TPU:0, one launch (start us, length us, event | category | flops | bytes accessed | tf_op | source)
XLA Modules:
  0.0 116.9 jit_solution(6307916783814347952)
XLA Ops:
  0.7 0.8 convert_element_type.32
  1.5 2.0 %multiply_reduce_fusion.1 = (f32[8192]{0:T(1024)S(1)}, f32[8192]{0:T(1024)S(1)}, f32[12,8192]{1,0:T(8,128)S(1)}) fusion(f32[12,8192]{1,0:T(8,128)} %param.28, f32[12,62]{1,0:T(8,128)S(1)} %copy-done, s32[8192]{0:T(1024)} %param.31), kind=kOutput, calls=%fused_computation.7 | convolution fusion | flops 74022912 | bytes 887712 | tf_op jit(solution)/shard_map/dot_general | solution.py:249
  3.5 0.1 compare_select_fusion.3
  3.6 0.2 concatenate.49
  3.9 1.0 all_to_all.49
  4.9 7.3 %all-to-all-start = ((f32[32,1,2304]{2,1,0:T(1,128)}), f32[32,1,2304]{2,1,0:T(1,128)S(1)}, u32[]{:S(2)}, u32[]{:S(2)}) async-start(f32[32,1,2304]{2,1,0:T(1,128)} %all_to_all.49), calls=%async_computation | async-start | bytes 589824 | tf_op jit(solution)/shard_map/all_to_all | solution.py:273
  12.4 0.1 pad_maximum_fusion
  12.5 0.1 broadcast_in_dim.8
  12.6 1.0 reshape.787.basis_ref
  13.6 0.7 broadcast_select_fusion.val_ref
  14.2 3.1 %shard_map.103 = f32[16,256]{1,0:T(8,128)} custom-call(f32[1,8192]{1,0:T(1,128)} %broadcast_select_fusion.val_ref, s32[1,8192]{1,0:T(1,128)} %bitcast.126, f32[16,8192]{1,0:T(8,128)} %reshape.787.basis_ref), custom_call_target="tpu_custom_call" | custom-call | tf_op jit(solution)/shard_map/pallas_call | solution.py:213
  17.3 0.8 slice_bitcast_fusion.5
  18.1 0.1 add_dynamic-update-slice_fusion.1
  18.3 0.1 fusion.18
  18.4 0.1 fusion.17
  18.6 0.1 pad_maximum_fusion.4
  18.7 4.1 %all-to-all-done = f32[32,1,2304]{2,1,0:T(1,128)S(1)} async-done(((f32[32,1,2304]{2,1,0:T(1,128)}), f32[32,1,2304]{2,1,0:T(1,128)S(1)}, u32[]{:S(2)}, u32[]{:S(2)}) %all-to-all-start) | async-done | bytes 294944 | tf_op jit(solution)/shard_map/all_to_all | solution.py:273
  22.8 0.7 reduce.24
  23.6 0.7 fusion.19
  24.3 0.7 slice.331
  25.0 0.8 all_to_all.38
  25.8 3.0 %all-to-all-start.1 = ((f32[32,1,1028]{2,1,0:T(1,128)}), f32[32,1,1028]{2,1,0:T(1,128)S(1)}, u32[]{:S(2)}, u32[]{:S(2)}) async-start(f32[32,1,1028]{2,1,0:T(1,128)} %all_to_all.38), calls=%async_computation.1 | async-start | bytes 294912 | tf_op jit(solution)/shard_map/all_to_all | solution.py:288
  28.8 0.7 multiply_add_fusion.1.ids_ref
  29.5 0.2 fusion.9
  29.7 0.8 pad_maximum_fusion.2.basis_ref
  30.4 7.7 %shard_map.104 = (f32[640,256]{1,0:T(8,128)}, f32[1,1]{1,0:T(1,128)}) custom-call(f32[5,8192]{1,0:T(8,128)} %bitcast.103, f32[1,8192]{1,0:T(1,128)} %bitcast.144, s32[1,8192]{1,0:T(1,128)} %ids_ref.3), custom_call_target="tpu_custom_call" | custom-call | tf_op jit(solution)/shard_map/pallas_call | solution.py:134
  38.1 7.9 %shard_map.105.zsrc_ref = f32[1,8192]{1,0:T(1,128)} custom-call(f32[640,256]{1,0:T(8,128)} %get-tuple-element.134.tab_ref, s32[1,8192]{1,0:T(1,128)} %ids_ref.3, f32[5,8192]{1,0:T(8,128)} %bitcast.104), custom_call_target="tpu_custom_call" | custom-call | tf_op jit(solution)/shard_map/pallas_call | solution.py:89
  46.0 0.1 reduce_sum.112
  46.2 0.4 scatter-add.40
  46.6 0.6 multiply_reduce_fusion.4
  47.3 0.1 pad_slice_fusion.5
  47.4 0.1 pad_maximum_fusion.1
  47.5 0.7 reshape.794.tab_ref
  48.2 4.6 %shard_map.106 = (f32[1,8192]{1,0:T(1,128)}, f32[1,12288]{1,0:T(1,128)}) custom-call(f32[128,256]{1,0:T(8,128)} %reshape.794.tab_ref, s32[1,8192]{1,0:T(1,128)} %multiply_add_fusion.1.ids_ref, f32[4,8192]{1,0:T(4,128)} %pad_maximum_fusion.2.basis_ref, f32[1,8192]{1,0:T(1,128)} %shard_map.105.zsrc_ref, f32[1,8192]{1,0:T(1,128)} %bitcast.121, ...), custom_call_target="tpu_custom_call" | custom-call | tf_op jit(solution)/shard_map/pallas_call | solution.py:182
  52.8 5.8 %all-to-all-start.2 = ((f32[32,1,384]{2,1,0:T(1,128)}), f32[32,1,384]{2,1,0:T(1,128)S(1)}, u32[]{:S(2)}, u32[]{:S(2)}) async-start(f32[32,1,384]{2,1,0:T(1,128)} %bitcast.160), calls=%async_computation.2 | async-start | bytes 98304 | tf_op jit(solution)/shard_map/all_to_all | solution.py:300
  58.7 7.7 %shard_map.108 = f32[640,256]{1,0:T(8,128)} custom-call(f32[5,8192]{1,0:T(8,128)} %bitcast.105, f32[1,8192]{1,0:T(1,128)} %bitcast.122, f32[1,8192]{1,0:T(1,128)} %get-tuple-element.137.refs_1_, s32[1,8192]{1,0:T(1,128)} %ids_ref.3), custom_call_target="tpu_custom_call" | custom-call | tf_op jit(solution)/shard_map/pallas_call | solution.py:133
  66.4 0.7 slice_reduce_fusion.2
  68.5 0.7 fusion.20
  70.6 0.7 multiply_subtract_fusion.2.val_ref
  71.2 3.1 %shard_map.107 = f32[16,256]{1,0:T(8,128)} custom-call(f32[1,8192]{1,0:T(1,128)} %multiply_subtract_fusion.2.val_ref, s32[1,8192]{1,0:T(1,128)} %bitcast.127, f32[16,8192]{1,0:T(8,128)} %reshape.787.basis_ref), custom_call_target="tpu_custom_call" | custom-call | tf_op jit(solution)/shard_map/pallas_call | solution.py:213
  74.4 0.8 slice_bitcast_fusion.1
  75.2 1.5 %multiply_reduce_fusion = (f32[]{:T(128)}, f32[640,256]{1,0:T(8,128)}) fusion(f32[640,256]{1,0:T(8,128)S(1)} %copy-done.1, f32[640,256]{1,0:T(8,128)S(1)} %copy-done.3, f32[]{:T(128)S(6)} %div.65), kind=kLoop, calls=%fused_computation.4 | loop fusion | flops 655359 | bytes 1966088 | tf_op jit(solution)/shard_map/reduce_sum | solution.py:327
  76.8 0.1 add_dynamic-update-slice_fusion
  76.9 0.1 fusion.16
  77.0 0.1 fusion.15
  77.2 0.7 pad_maximum_fusion.5
  77.9 0.7 broadcast_in_dim.11
  78.6 5.8 %all-to-all-start.3 = ((f32[32,1,1028]{2,1,0:T(1,128)}), f32[32,1,1028]{2,1,0:T(1,128)S(1)}, u32[]{:S(2)}, u32[]{:S(2)}) async-start(f32[32,1,1028]{2,1,0:T(1,128)} %broadcast_in_dim.11), calls=%async_computation.3 | async-start | bytes 294912 | tf_op jit(solution)/shard_map/all_to_all | solution.py:288
  84.5 7.9 %shard_map.109.zsrc_ref = f32[1,8192]{1,0:T(1,128)} custom-call(f32[640,256]{1,0:T(8,128)} %get-tuple-element.142.tab_ref, s32[1,8192]{1,0:T(1,128)} %ids_ref.3, f32[5,8192]{1,0:T(8,128)} %bitcast.106), custom_call_target="tpu_custom_call" | custom-call | tf_op jit(solution)/shard_map/pallas_call | solution.py:89
  92.4 0.8 all-to-all-done.3
  93.1 0.7 slice_reduce_fusion.1
  93.9 0.1 reduce_sum.119
  94.0 0.4 scatter-add.49
  94.4 0.6 multiply_reduce_fusion.3
  96.4 0.1 pad_slice_fusion.2
  96.5 0.1 pad_maximum_fusion.3
  96.7 0.7 reshape.801.tab_ref
  97.4 4.0 %shard_map.110 = (f32[1,8192]{1,0:T(1,128)}, f32[1,12288]{1,0:T(1,128)}) custom-call(f32[128,256]{1,0:T(8,128)} %reshape.801.tab_ref, s32[1,8192]{1,0:T(1,128)} %multiply_add_fusion.1.ids_ref, f32[4,8192]{1,0:T(4,128)} %pad_maximum_fusion.2.basis_ref, f32[1,8192]{1,0:T(1,128)} %shard_map.109.zsrc_ref, f32[1,8192]{1,0:T(1,128)} %bitcast.123, ...), custom_call_target="tpu_custom_call" | custom-call | tf_op jit(solution)/shard_map/pallas_call | solution.py:182
  101.4 5.1 %all-to-all-start.4 = ((f32[32,1,384]{2,1,0:T(1,128)}), f32[32,1,384]{2,1,0:T(1,128)S(1)}, u32[]{:S(2)}, u32[]{:S(2)}) async-start(f32[32,1,384]{2,1,0:T(1,128)} %bitcast.159), calls=%async_computation.4 | async-start | bytes 98304 | tf_op jit(solution)/shard_map/all_to_all | solution.py:300
  106.5 7.4 %all-to-all-done.4 = f32[32,1,384]{2,1,0:T(1,128)S(1)} async-done(((f32[32,1,384]{2,1,0:T(1,128)}), f32[32,1,384]{2,1,0:T(1,128)S(1)}, u32[]{:S(2)}, u32[]{:S(2)}) %all-to-all-start.4) | async-done | bytes 49184 | tf_op jit(solution)/shard_map/all_to_all | solution.py:300
  114.0 0.1 multiply_add_fusion
  114.2 0.6 fusion.14
  114.8 1.2 %add.214 = f32[5,32768]{1,0:T(8,128)} reshape(f32[640,256]{1,0:T(8,128)S(1)} %multiply_add_fusion) | data formatting | bytes 1310720 | tf_op jit(solution)/shard_map/add | solution.py:319
  116.0 0.9 multiply_subtract_fusion.1
  (54 shorter events, 0.8 us)
Async XLA Ops:
  0.6 0.9 copy-start
  0.6 2.8 %copy-start.7 = (s32[1,32]{1,0:T(1,128)S(1)}, s32[1,32]{1,0:T(1,128)}, u32[]{:S(2)}) copy-start(s32[1,32]{1,0:T(1,128)} %param.34) | copy-start | bytes 388
  0.7 3.0 %copy-start.6 = (f32[8192]{0:T(1024)S(1)}, f32[8192]{0:T(1024)}, u32[]{:S(2)}) copy-start(f32[8192]{0:T(1024)} %param.33) | copy-start | bytes 98308
  0.7 3.0 %copy-start.5 = (f32[5,8192]{1,0:T(8,128)S(1)}, f32[5,8192]{1,0:T(8,128)}, u32[]{:S(2)}) copy-start(f32[5,8192]{1,0:T(8,128)} %param.29) | copy-start | bytes 491524
  4.9 17.9 %all-to-all-start = ((f32[32,1,2304]{2,1,0:T(1,128)}), f32[32,1,2304]{2,1,0:T(1,128)S(1)}, u32[]{:S(2)}, u32[]{:S(2)}) async-start(f32[32,1,2304]{2,1,0:T(1,128)} %all_to_all.49), calls=%async_computation | async-start | bytes 589824 | tf_op jit(solution)/shard_map/all_to_all | solution.py:273
  25.8 20.2 %all-to-all-start.1 = ((f32[32,1,1028]{2,1,0:T(1,128)}), f32[32,1,1028]{2,1,0:T(1,128)S(1)}, u32[]{:S(2)}, u32[]{:S(2)}) async-start(f32[32,1,1028]{2,1,0:T(1,128)} %all_to_all.38), calls=%async_computation.1 | async-start | bytes 294912 | tf_op jit(solution)/shard_map/all_to_all | solution.py:288
  52.8 15.5 %all-to-all-start.2 = ((f32[32,1,384]{2,1,0:T(1,128)}), f32[32,1,384]{2,1,0:T(1,128)S(1)}, u32[]{:S(2)}, u32[]{:S(2)}) async-start(f32[32,1,384]{2,1,0:T(1,128)} %bitcast.160), calls=%async_computation.2 | async-start | bytes 98304 | tf_op jit(solution)/shard_map/all_to_all | solution.py:300
  58.7 16.5 %copy-start.1 = (f32[640,256]{1,0:T(8,128)S(1)}, f32[640,256]{1,0:T(8,128)}, u32[]{:S(2)}) copy-start(f32[640,256]{1,0:T(8,128)} %get-tuple-element.134.tab_ref) | copy-start | bytes 1966084
  66.4 8.8 %copy-start.3 = (f32[640,256]{1,0:T(8,128)S(1)}, f32[640,256]{1,0:T(8,128)}, u32[]{:S(2)}) copy-start(f32[640,256]{1,0:T(8,128)} %shard_map.108) | copy-start | bytes 1966084
  78.6 14.5 %all-to-all-start.3 = ((f32[32,1,1028]{2,1,0:T(1,128)}), f32[32,1,1028]{2,1,0:T(1,128)S(1)}, u32[]{:S(2)}, u32[]{:S(2)}) async-start(f32[32,1,1028]{2,1,0:T(1,128)} %broadcast_in_dim.11), calls=%async_computation.3 | async-start | bytes 294912 | tf_op jit(solution)/shard_map/all_to_all | solution.py:288
  93.8 20.2 %copy-start.2 = (f32[640,256]{1,0:T(8,128)S(1)}, f32[640,256]{1,0:T(8,128)}, u32[]{:S(2)}) copy-start(f32[640,256]{1,0:T(8,128)} %get-tuple-element.142.tab_ref) | copy-start | bytes 1966084
  101.4 12.5 %all-to-all-start.4 = ((f32[32,1,384]{2,1,0:T(1,128)}), f32[32,1,384]{2,1,0:T(1,128)S(1)}, u32[]{:S(2)}, u32[]{:S(2)}) async-start(f32[32,1,384]{2,1,0:T(1,128)} %bitcast.159), calls=%async_computation.4 | async-start | bytes 98304 | tf_op jit(solution)/shard_map/all_to_all | solution.py:300
  114.1 1.8 %copy-start.4 = (f32[12,8192]{1,0:T(8,128)S(1)}, f32[12,8192]{1,0:T(8,128)}, u32[]{:S(2)}) copy-start(f32[12,8192]{1,0:T(8,128)} %param.28) | copy-start | bytes 1179652

commit v16 on v12

--- a/solution.py
+++ b/solution.py
@@ -93,17 +93,24 @@
     )(table, ids, held)
 
 
-def source_scatter(values, ids, width, with_norm=False):
+def source_scatter(values, scales, ids, width, with_norm=False):
     n, total = values.shape
     cols = width // HI
     rows = n * cols
-
-    def kernel(val_ref, ids_ref, out_ref, *norm_ref):
+    count = len(scales)
+
+    def kernel(val_ref, *refs):
+        scale_refs = refs[:count]
+        ids_ref, out_ref = refs[count:count + 2]
+        norm_ref = refs[count + 2:]
         out_ref[...] = jnp.zeros(out_ref.shape, jnp.float32)
 
         def body(off):
             idc = ids_ref[:, pl.ds(off, CHUNK)]
-            v = val_ref[:, pl.ds(off, CHUNK)]
+            scale = scale_refs[0][:, pl.ds(off, CHUNK)]
+            for other in scale_refs[1:]:
+                scale = scale * other[:, pl.ds(off, CHUNK)]
+            v = val_ref[:, pl.ds(off, CHUNK)] * scale
             sel = group_mask(idc, cols, CHUNK, cols)
             parts = []
             for piece in pieces(v):
@@ -123,10 +130,10 @@
 
     shape = jax.ShapeDtypeStruct((rows, HI), jnp.float32)
     if not with_norm:
-        return pl.pallas_call(kernel, out_shape=shape)(values, ids)
+        return pl.pallas_call(kernel, out_shape=shape)(values, *scales, ids)
     grad, norm = pl.pallas_call(
         kernel, out_shape=(shape, jax.ShapeDtypeStruct((1, 1), jnp.float32))
-    )(values, ids)
+    )(values, *scales, ids)
     return grad, norm.reshape(())
 
 
@@ -303,7 +310,7 @@
     sent = knot_scatter(zbar_slot, first_ids, basis16, jnp.zeros((), jnp.float32), knots, n_ranks)
     sent, held, zbar0_own = lax.optimization_barrier((sent, held, zbar0_own))
     grad_a, gamma_a = combine(sent)
-    grad_s, extra = source_scatter(held * zbar0_own, ids, owned, with_norm=True)
+    grad_s, extra = source_scatter(held, [zbar0_own], ids, owned, with_norm=True)
     dir_s, dir_a = (grad_s, grad_a)
     pulled = source_gather(dir_s, ids, held)
     for step in range(ITERS):
@@ -311,11 +318,11 @@
         if step == 0:
             gamma = extra_sum + gamma_a
         alpha = gamma / image_sq
-        sol_s = sol_s + alpha * lax.optimization_barrier(dir_s.reshape(n_params, owned))
+        sol_s = sol_s + alpha * dir_s.reshape(n_params, owned)
         sol_a = sol_a + alpha * dir_a
         resid = resid - alpha * (weight_factor * shift_slot)
         if step + 1 < ITERS:
-            pushed = source_scatter(held * (weight_sq_own * shift_own), ids, owned)
+            pushed = source_scatter(held, [weight_sq_own, shift_own], ids, owned)
             zbar_slot = zbar_slot - alpha * (weight_sq * shift_slot)
             grad_s = grad_s - alpha * pushed
             grad_a, fresh = combine(

time: 122 us -> 117 us (0.959)
  other arithmetic: 19.6 us -> 15.7 us
    mul x3 -> x0, other arithmetic: 2.24 us -> none  [the longest x2 1.52 us: per_device(): pushed = source_scatter(held * (weight_sq_own * shift_own), ids, owned)]
    unnamed x45 -> x29, local copies, waits for them, and re-layouts: 2.22 us -> 0.27 us
  transfers between devices with their start and end apart: 5 -> 5, of which waited for: 3 -> 3; matrix products, arithmetic and copies ran while one was open for 8% -> 6% of each run, Pallas kernels for 28% -> 29%
where the time goes in v16:
time: 117 us
  Pallas kernels  46.8 us (40%)
  starting transfers between devices  27 us (23%)
  other arithmetic  15.7 us (13%)
  waiting for transfers between devices  11.1 us (9%)
  local copies, waits for them, and re-layouts  8.97 us (8%)
  between operations  5.2 us (4%)
  matrix products  2 us (2%)
    pallas_call x2, Pallas kernels, source_gather(): pl.pallas_call(kernel, out_shape=jax.ShapeDtypeStruct((1, total), jnp.flo...  15.8 us
    all_to_all x2, starting transfers between devices, forward(): lax.all_to_all(payload.reshape(n_ranks, -1), everyone, 0, 0, tiled=True)  10.3 us
    all_to_all x2, starting transfers between devices, combine(): every = lax.all_to_all(sent, everyone, 0, 0, tiled=True)  9.35 us
    pallas_call x2, Pallas kernels, knot_gather(): pl.pallas_call(kernel, out_shape=(jax.ShapeDtypeStruct((1, total), jnp.fl...  8.54 us
    pallas_call x1, Pallas kernels, source_scatter(): return pl.pallas_call(kernel, out_shape=shape)(values, *scales, ids)  7.66 us
    pallas_call x1, Pallas kernels, source_scatter(): pl.pallas_call(kernel, out_shape=(shape, jax.ShapeDtypeStruct((1, 1), jnp...  7.66 us
    all_to_all x2, waiting for transfers between devices, forward(): lax.all_to_all(payload.reshape(n_ranks, -1), everyone, 0, 0, tiled=True)  7.37 us
    all_to_all x1, starting transfers between devices, per_device(): got = lax.all_to_all(blocks, everyone, 0, 0, tiled=True)  7.3 us
  transfers between devices with their start and end apart: 5, of which 3 were waited for; matrix products, arithmetic and copies ran while one was open for 6% of the time, Pallas kernels for 29%

profile of v16, /device:TPU:0, one launch (start us, length us, event | category | flops | bytes accessed | tf_op | source)
XLA Modules:
  0.0 116.7 jit_solution(1480297027173437066)
XLA Ops:
  0.6 0.0 copy-start
  0.7 0.8 convert_element_type.32
  1.5 2.0 %multiply_reduce_fusion.1 = (f32[8192]{0:T(1024)S(1)}, f32[8192]{0:T(1024)S(1)}, f32[12,8192]{1,0:T(8,128)S(1)}) fusion(f32[12,8192]{1,0:T(8,128)} %param.12, f32[12,62]{1,0:T(8,128)S(1)} %copy-done, s32[8192]{0:T(1024)} %param.15), kind=kOutput, calls=%fused_computation.7 | convolution fusion | flops 74022912 | bytes 887712 | tf_op jit(solution)/shard_map/dot_general | solution.py:255
  3.5 0.1 compare_select_fusion.3
  3.6 0.2 concatenate.26
  3.9 1.0 all_to_all.52
  4.9 7.3 %all-to-all-start = ((f32[32,1,2304]{2,1,0:T(1,128)}), f32[32,1,2304]{2,1,0:T(1,128)S(1)}, u32[]{:S(2)}, u32[]{:S(2)}) async-start(f32[32,1,2304]{2,1,0:T(1,128)} %all_to_all.52), calls=%async_computation | async-start | bytes 589824 | tf_op jit(solution)/shard_map/all_to_all | solution.py:279
  12.2 0.1 fusion.11
  12.4 0.7 broadcast_select_fusion.val_ref
  13.0 0.1 pad_maximum_fusion
  13.2 0.1 broadcast_in_dim.2
  13.3 1.0 reshape.630.basis_ref
  14.2 3.3 %shard_map.103 = f32[1,45056]{1,0:T(1,128)} custom-call(f32[1,8192]{1,0:T(1,128)} %broadcast_select_fusion.val_ref, s32[1,8192]{1,0:T(1,128)} %bitcast.107, f32[16,8192]{1,0:T(8,128)} %reshape.630.basis_ref, f32[1,1]{1,0:T(1,128)} %constant.111.clone.1.norm_ref.extra_ref), custom_call_target="tpu_custom_call" | custom-call | tf_op jit(solution)/shard_map/pallas_call | solution.py:222
  17.5 0.5 broadcast.436
  18.0 2.0 %reduce.12 = f32[45056]{0:T(1024)S(1)} reduce(f32[1,45056]{1,0:T(1,128)} %shard_map.103, f32[]{:T(128)} %broadcast.436), dimensions={0}, to_apply=%pallas_call.36.reduce_sub_computation.3 | reduce | bytes 360452 | tf_op jit(solution)/shard_map/pallas_call | solution.py:222
  20.1 2.7 %all-to-all-done = f32[32,1,2304]{2,1,0:T(1,128)S(1)} async-done(((f32[32,1,2304]{2,1,0:T(1,128)}), f32[32,1,2304]{2,1,0:T(1,128)S(1)}, u32[]{:S(2)}, u32[]{:S(2)}) %all-to-all-start) | async-done | bytes 294944 | tf_op jit(solution)/shard_map/all_to_all | solution.py:279
  22.8 0.7 reduce.9
  23.5 0.1 reshape.632
  23.6 0.7 fusion.14
  24.3 0.7 slice.173
  25.0 0.8 all_to_all.40
  25.8 3.3 %all-to-all-start.1 = ((f32[32,1,1408]{2,1,0:T(1,128)}), f32[32,1,1408]{2,1,0:T(1,128)S(1)}, u32[]{:S(2)}, u32[]{:S(2)}) async-start(f32[32,1,1408]{2,1,0:T(1,128)} %all_to_all.40), calls=%async_computation.1 | async-start | bytes 360448 | tf_op jit(solution)/shard_map/all_to_all | solution.py:290
  29.1 0.2 fusion.9
  29.3 0.7 multiply_add_fusion.3.ids_ref
  30.0 0.8 pad_maximum_fusion.2.basis_ref
  30.7 7.7 %shard_map.104 = (f32[640,256]{1,0:T(8,128)}, f32[1,1]{1,0:T(1,128)}) custom-call(f32[5,8192]{1,0:T(8,128)} %bitcast.78, f32[1,8192]{1,0:T(1,128)} %bitcast.122, s32[1,8192]{1,0:T(1,128)} %ids_ref.3), custom_call_target="tpu_custom_call" | custom-call | tf_op jit(solution)/shard_map/pallas_call | solution.py:134
  38.4 7.9 %shard_map.105.zsrc_ref = f32[1,8192]{1,0:T(1,128)} custom-call(f32[640,256]{1,0:T(8,128)} %get-tuple-element.38.tab_ref, s32[1,8192]{1,0:T(1,128)} %ids_ref.3, f32[5,8192]{1,0:T(8,128)} %bitcast.79), custom_call_target="tpu_custom_call" | custom-call | tf_op jit(solution)/shard_map/pallas_call | solution.py:89
  46.4 0.1 reduce_sum.112
  46.5 0.4 scatter-add.6
  46.9 0.6 multiply_reduce_fusion.4
  47.6 0.1 pad_slice_fusion.5
  47.7 0.1 pad_maximum_fusion.1
  47.8 0.0 copy-start.1
  47.9 0.7 reshape.635.tab_ref
  48.6 4.6 %shard_map.106 = (f32[1,8192]{1,0:T(1,128)}, f32[1,12288]{1,0:T(1,128)}) custom-call(f32[128,256]{1,0:T(8,128)} %reshape.635.tab_ref, s32[1,8192]{1,0:T(1,128)} %multiply_add_fusion.3.ids_ref, f32[4,8192]{1,0:T(4,128)} %pad_maximum_fusion.2.basis_ref, f32[1,8192]{1,0:T(1,128)} %shard_map.105.zsrc_ref, f32[1,8192]{1,0:T(1,128)} %bitcast.98, ...), custom_call_target="tpu_custom_call" | custom-call | tf_op jit(solution)/shard_map/pallas_call | solution.py:177
  53.2 5.7 %all-to-all-start.2 = ((f32[32,1,384]{2,1,0:T(1,128)}), f32[32,1,384]{2,1,0:T(1,128)S(1)}, u32[]{:S(2)}, u32[]{:S(2)}) async-start(f32[32,1,384]{2,1,0:T(1,128)} %bitcast.136), calls=%async_computation.2 | async-start | bytes 98304 | tf_op jit(solution)/shard_map/all_to_all | solution.py:302
  58.9 7.7 %shard_map.107 = f32[640,256]{1,0:T(8,128)} custom-call(f32[5,8192]{1,0:T(8,128)} %bitcast.80, f32[1,8192]{1,0:T(1,128)} %bitcast.99, f32[1,8192]{1,0:T(1,128)} %get-tuple-element.41.refs_1_, s32[1,8192]{1,0:T(1,128)} %ids_ref.3), custom_call_target="tpu_custom_call" | custom-call | tf_op jit(solution)/shard_map/pallas_call | solution.py:133
  66.5 0.6 slice_reduce_fusion.2
  68.5 0.1 select_bitcast_fusion
  68.5 0.7 fusion.15
  70.6 2.6 %multiply_reduce_fusion = (f32[]{:T(128)}, f32[640,256]{1,0:T(8,128)}) fusion(f32[640,256]{1,0:T(8,128)S(1)} %copy-done.1, f32[640,256]{1,0:T(8,128)} %shard_map.107, f32[]{:T(128)S(6)} %div.65), kind=kLoop, calls=%fused_computation.4 | loop fusion | flops 655359 | bytes 1966088 | tf_op jit(solution)/shard_map/reduce_sum | solution.py:329
  73.2 0.7 multiply_subtract_fusion.2.val_ref
  73.9 3.9 %shard_map.108 = f32[1,45056]{1,0:T(1,128)} custom-call(f32[1,8192]{1,0:T(1,128)} %multiply_subtract_fusion.2.val_ref, s32[1,8192]{1,0:T(1,128)} %bitcast.108, f32[16,8192]{1,0:T(8,128)} %reshape.630.basis_ref, f32[1,1]{1,0:T(1,128)} %bitcast.27.norm_ref), custom_call_target="tpu_custom_call" | custom-call | tf_op jit(solution)/shard_map/pallas_call | solution.py:222
  77.9 6.1 %all-to-all-start.3 = ((f32[32,1,1408]{2,1,0:T(1,128)}), f32[32,1,1408]{2,1,0:T(1,128)S(1)}, u32[]{:S(2)}, u32[]{:S(2)}) async-start(f32[32,1,1408]{2,1,0:T(1,128)} %bitcast.88), calls=%async_computation.3 | async-start | bytes 360448 | tf_op jit(solution)/shard_map/all_to_all | solution.py:290
  83.9 7.9 %shard_map.109 = f32[1,8192]{1,0:T(1,128)} custom-call(f32[640,256]{1,0:T(8,128)} %get-tuple-element.46.tab_ref, s32[1,8192]{1,0:T(1,128)} %ids_ref.3, f32[5,8192]{1,0:T(8,128)} %bitcast.81), custom_call_target="tpu_custom_call" | custom-call | tf_op jit(solution)/shard_map/pallas_call | solution.py:89
  91.8 1.0 all-to-all-done.3
  92.9 0.0 copy-start.2
  92.9 0.1 reduce_sum.119
  93.0 0.6 slice_reduce_fusion.1
  93.6 0.3 scatter-add.9
  93.9 0.7 multiply_reduce_fusion.3
  96.0 0.1 pad_slice_fusion.2
  96.1 0.7 multiply_add_fusion.1
  96.8 0.1 pad_maximum_fusion.3
  96.9 0.7 reshape.641.tab_ref
  97.7 3.9 %shard_map.110 = (f32[1,8192]{1,0:T(1,128)}, f32[1,12288]{1,0:T(1,128)}) custom-call(f32[128,256]{1,0:T(8,128)} %reshape.641.tab_ref, s32[1,8192]{1,0:T(1,128)} %multiply_add_fusion.3.ids_ref, f32[4,8192]{1,0:T(4,128)} %pad_maximum_fusion.2.basis_ref, f32[1,8192]{1,0:T(1,128)} %get-tuple-element.72.zsrc_ref, f32[1,8192]{1,0:T(1,128)} %bitcast.100, ...), custom_call_target="tpu_custom_call" | custom-call | tf_op jit(solution)/shard_map/pallas_call | solution.py:177
  101.6 4.6 %all-to-all-start.4 = ((f32[32,1,384]{2,1,0:T(1,128)}), f32[32,1,384]{2,1,0:T(1,128)S(1)}, u32[]{:S(2)}, u32[]{:S(2)}) async-start(f32[32,1,384]{2,1,0:T(1,128)} %bitcast.135), calls=%async_computation.4 | async-start | bytes 98304 | tf_op jit(solution)/shard_map/all_to_all | solution.py:302
  106.3 7.4 %all-to-all-done.4 = f32[32,1,384]{2,1,0:T(1,128)S(1)} async-done(((f32[32,1,384]{2,1,0:T(1,128)}), f32[32,1,384]{2,1,0:T(1,128)S(1)}, u32[]{:S(2)}, u32[]{:S(2)}) %all-to-all-start.4) | async-done | bytes 49184 | tf_op jit(solution)/shard_map/all_to_all | solution.py:302
  113.7 0.1 fusion.10
  113.9 0.1 multiply_add_fusion
  114.0 0.0 copy-start.3
  114.0 0.6 fusion.13
  114.6 1.2 %add.161 = f32[5,32768]{1,0:T(8,128)} reshape(f32[640,256]{1,0:T(8,128)S(1)} %multiply_add_fusion) | data formatting | bytes 1310720 | tf_op jit(solution)/shard_map/add | solution.py:321
  115.8 0.9 multiply_subtract_fusion.1
  (40 shorter events, 0.5 us)
Async XLA Ops:
  0.6 0.9 copy-start
  0.6 2.8 %copy-start.8 = (s32[1,32]{1,0:T(1,128)S(1)}, s32[1,32]{1,0:T(1,128)}, u32[]{:S(2)}) copy-start(s32[1,32]{1,0:T(1,128)} %param.18) | copy-start | bytes 388
  0.7 3.0 %copy-start.6 = (f32[8192]{0:T(1024)S(1)}, f32[8192]{0:T(1024)}, u32[]{:S(2)}) copy-start(f32[8192]{0:T(1024)} %param.17) | copy-start | bytes 98308
  0.7 3.0 %copy-start.5 = (f32[5,8192]{1,0:T(8,128)S(1)}, f32[5,8192]{1,0:T(8,128)}, u32[]{:S(2)}) copy-start(f32[5,8192]{1,0:T(8,128)} %param.13) | copy-start | bytes 491524
  4.9 17.9 %all-to-all-start = ((f32[32,1,2304]{2,1,0:T(1,128)}), f32[32,1,2304]{2,1,0:T(1,128)S(1)}, u32[]{:S(2)}, u32[]{:S(2)}) async-start(f32[32,1,2304]{2,1,0:T(1,128)} %all_to_all.52), calls=%async_computation | async-start | bytes 589824 | tf_op jit(solution)/shard_map/all_to_all | solution.py:279
  25.8 20.5 %all-to-all-start.1 = ((f32[32,1,1408]{2,1,0:T(1,128)}), f32[32,1,1408]{2,1,0:T(1,128)S(1)}, u32[]{:S(2)}, u32[]{:S(2)}) async-start(f32[32,1,1408]{2,1,0:T(1,128)} %all_to_all.40), calls=%async_computation.1 | async-start | bytes 360448 | tf_op jit(solution)/shard_map/all_to_all | solution.py:290
  47.8 22.8 %copy-start.1 = (f32[640,256]{1,0:T(8,128)S(1)}, f32[640,256]{1,0:T(8,128)}, u32[]{:S(2)}) copy-start(f32[640,256]{1,0:T(8,128)} %get-tuple-element.38.tab_ref) | copy-start | bytes 1966084
  53.2 15.2 %all-to-all-start.2 = ((f32[32,1,384]{2,1,0:T(1,128)}), f32[32,1,384]{2,1,0:T(1,128)S(1)}, u32[]{:S(2)}, u32[]{:S(2)}) async-start(f32[32,1,384]{2,1,0:T(1,128)} %bitcast.136), calls=%async_computation.2 | async-start | bytes 98304 | tf_op jit(solution)/shard_map/all_to_all | solution.py:302
  77.9 14.9 %all-to-all-start.3 = ((f32[32,1,1408]{2,1,0:T(1,128)}), f32[32,1,1408]{2,1,0:T(1,128)S(1)}, u32[]{:S(2)}, u32[]{:S(2)}) async-start(f32[32,1,1408]{2,1,0:T(1,128)} %bitcast.88), calls=%async_computation.3 | async-start | bytes 360448 | tf_op jit(solution)/shard_map/all_to_all | solution.py:290
  83.9 12.2 %copy-start.4 = (f32[1,8192]{1,0:T(1,128)S(1)}, f32[1,8192]{1,0:T(1,128)}, u32[]{:S(2)}) copy-start(f32[1,8192]{1,0:T(1,128)} %shard_map.105.zsrc_ref) | copy-start | bytes 98308
  91.8 4.3 %copy-start.7 = (f32[1,8192]{1,0:T(1,128)S(1)}, f32[1,8192]{1,0:T(1,128)}, u32[]{:S(2)}) copy-start(f32[1,8192]{1,0:T(1,128)} %shard_map.109) | copy-start | bytes 98308
  92.9 21.0 %copy-start.2 = (f32[640,256]{1,0:T(8,128)S(1)}, f32[640,256]{1,0:T(8,128)}, u32[]{:S(2)}) copy-start(f32[640,256]{1,0:T(8,128)} %get-tuple-element.46.tab_ref) | copy-start | bytes 1966084
  101.6 12.0 %all-to-all-start.4 = ((f32[32,1,384]{2,1,0:T(1,128)}), f32[32,1,384]{2,1,0:T(1,128)S(1)}, u32[]{:S(2)}, u32[]{:S(2)}) async-start(f32[32,1,384]{2,1,0:T(1,128)} %bitcast.135), calls=%async_computation.4 | async-start | bytes 98304 | tf_op jit(solution)/shard_map/all_to_all | solution.py:302
  114.0 1.8 %copy-start.3 = (f32[12,8192]{1,0:T(8,128)S(1)}, f32[12,8192]{1,0:T(8,128)}, u32[]{:S(2)}) copy-start(f32[12,8192]{1,0:T(8,128)} %param.12) | copy-start | bytes 1179652

commit v17 on v16

--- a/solution.py
+++ b/solution.py
@@ -255,7 +255,7 @@
     weight_factor = jnp.dot(
         spread_derivative_table,
         indicator,
-        precision=lax.Precision.HIGHEST,
+        precision=lax.Precision.HIGH,
         preferred_element_type=jnp.float32,
     )
     weight_sq = live * jnp.sum(weight_factor * weight_factor, axis=0, keepdims=True)

time: 117 us -> 117 us (level)
  no operation moved by 1% of the time
where the time goes in v17:
time: 117 us
  Pallas kernels  46.8 us (40%)
  starting transfers between devices  27 us (23%)
  other arithmetic  15.7 us (13%)
  waiting for transfers between devices  11.1 us (9%)
  local copies, waits for them, and re-layouts  8.97 us (8%)
  between operations  5.2 us (4%)
  matrix products  1.82 us (2%)
    pallas_call x2, Pallas kernels, source_gather(): pl.pallas_call(kernel, out_shape=jax.ShapeDtypeStruct((1, total), jnp.flo...  15.8 us
    all_to_all x2, starting transfers between devices, forward(): lax.all_to_all(payload.reshape(n_ranks, -1), everyone, 0, 0, tiled=True)  10.3 us
    all_to_all x2, starting transfers between devices, combine(): every = lax.all_to_all(sent, everyone, 0, 0, tiled=True)  9.36 us
    pallas_call x2, Pallas kernels, knot_gather(): pl.pallas_call(kernel, out_shape=(jax.ShapeDtypeStruct((1, total), jnp.fl...  8.54 us
    pallas_call x1, Pallas kernels, source_scatter(): return pl.pallas_call(kernel, out_shape=shape)(values, *scales, ids)  7.66 us
    pallas_call x1, Pallas kernels, source_scatter(): pl.pallas_call(kernel, out_shape=(shape, jax.ShapeDtypeStruct((1, 1), jnp...  7.66 us
    all_to_all x2, waiting for transfers between devices, forward(): lax.all_to_all(payload.reshape(n_ranks, -1), everyone, 0, 0, tiled=True)  7.37 us
    all_to_all x1, starting transfers between devices, per_device(): got = lax.all_to_all(blocks, everyone, 0, 0, tiled=True)  7.3 us
  transfers between devices with their start and end apart: 5, of which 3 were waited for; matrix products, arithmetic and copies ran while one was open for 6% of the time, Pallas kernels for 29%

profile of v17, /device:TPU:0, one launch (start us, length us, event | category | flops | bytes accessed | tf_op | source)
XLA Modules:
  0.0 116.5 jit_solution(4957124475613672804)
XLA Ops:
  0.6 0.0 copy-start
  0.7 0.8 convert_element_type.32
  1.5 1.8 %multiply_reduce_fusion.1 = (f32[8192]{0:T(1024)S(1)}, f32[8192]{0:T(1024)S(1)}, f32[12,8192]{1,0:T(8,128)S(1)}) fusion(f32[12,8192]{1,0:T(8,128)} %param.12, f32[12,62]{1,0:T(8,128)S(1)} %copy-done, s32[8192]{0:T(1024)} %param.15), kind=kOutput, calls=%fused_computation.7 | convolution fusion | flops 37453824 | bytes 887712 | tf_op jit(solution)/shard_map/dot_general | solution.py:255
  3.3 0.1 compare_select_fusion.3
  3.5 0.2 concatenate.26
  3.7 1.0 all_to_all.52
  4.7 7.3 %all-to-all-start = ((f32[32,1,2304]{2,1,0:T(1,128)}), f32[32,1,2304]{2,1,0:T(1,128)S(1)}, u32[]{:S(2)}, u32[]{:S(2)}) async-start(f32[32,1,2304]{2,1,0:T(1,128)} %all_to_all.52), calls=%async_computation | async-start | bytes 589824 | tf_op jit(solution)/shard_map/all_to_all | solution.py:279
  12.1 0.1 fusion.11
  12.2 0.7 broadcast_select_fusion.val_ref
  12.9 0.1 pad_maximum_fusion
  13.0 0.1 broadcast_in_dim.2
  13.1 1.0 reshape.630.basis_ref
  14.1 3.3 %shard_map.103 = f32[1,45056]{1,0:T(1,128)} custom-call(f32[1,8192]{1,0:T(1,128)} %broadcast_select_fusion.val_ref, s32[1,8192]{1,0:T(1,128)} %bitcast.107, f32[16,8192]{1,0:T(8,128)} %reshape.630.basis_ref, f32[1,1]{1,0:T(1,128)} %constant.111.clone.1.norm_ref.extra_ref), custom_call_target="tpu_custom_call" | custom-call | tf_op jit(solution)/shard_map/pallas_call | solution.py:222
  17.3 0.5 broadcast.436
  17.9 2.0 %reduce.12 = f32[45056]{0:T(1024)S(1)} reduce(f32[1,45056]{1,0:T(1,128)} %shard_map.103, f32[]{:T(128)} %broadcast.436), dimensions={0}, to_apply=%pallas_call.36.reduce_sub_computation.3 | reduce | bytes 360452 | tf_op jit(solution)/shard_map/pallas_call | solution.py:222
  19.9 2.7 %all-to-all-done = f32[32,1,2304]{2,1,0:T(1,128)S(1)} async-done(((f32[32,1,2304]{2,1,0:T(1,128)}), f32[32,1,2304]{2,1,0:T(1,128)S(1)}, u32[]{:S(2)}, u32[]{:S(2)}) %all-to-all-start) | async-done | bytes 294944 | tf_op jit(solution)/shard_map/all_to_all | solution.py:279
  22.6 0.7 reduce.9
  23.3 0.1 reshape.632
  23.4 0.7 fusion.14
  24.1 0.7 slice.173
  24.9 0.8 all_to_all.40
  25.6 3.3 %all-to-all-start.1 = ((f32[32,1,1408]{2,1,0:T(1,128)}), f32[32,1,1408]{2,1,0:T(1,128)S(1)}, u32[]{:S(2)}, u32[]{:S(2)}) async-start(f32[32,1,1408]{2,1,0:T(1,128)} %all_to_all.40), calls=%async_computation.1 | async-start | bytes 360448 | tf_op jit(solution)/shard_map/all_to_all | solution.py:290
  29.0 0.2 fusion.9
  29.1 0.7 multiply_add_fusion.3.ids_ref
  29.8 0.8 pad_maximum_fusion.2.basis_ref
  30.6 7.7 %shard_map.104 = (f32[640,256]{1,0:T(8,128)}, f32[1,1]{1,0:T(1,128)}) custom-call(f32[5,8192]{1,0:T(8,128)} %bitcast.78, f32[1,8192]{1,0:T(1,128)} %bitcast.122, s32[1,8192]{1,0:T(1,128)} %ids_ref.3), custom_call_target="tpu_custom_call" | custom-call | tf_op jit(solution)/shard_map/pallas_call | solution.py:134
  38.2 7.9 %shard_map.105.zsrc_ref = f32[1,8192]{1,0:T(1,128)} custom-call(f32[640,256]{1,0:T(8,128)} %get-tuple-element.38.tab_ref, s32[1,8192]{1,0:T(1,128)} %ids_ref.3, f32[5,8192]{1,0:T(8,128)} %bitcast.79), custom_call_target="tpu_custom_call" | custom-call | tf_op jit(solution)/shard_map/pallas_call | solution.py:89
  46.2 0.1 reduce_sum.112
  46.3 0.4 scatter-add.6
  46.8 0.6 multiply_reduce_fusion.4
  47.4 0.1 pad_slice_fusion.5
  47.5 0.1 pad_maximum_fusion.1
  47.7 0.0 copy-start.1
  47.7 0.7 reshape.635.tab_ref
  48.4 4.6 %shard_map.106 = (f32[1,8192]{1,0:T(1,128)}, f32[1,12288]{1,0:T(1,128)}) custom-call(f32[128,256]{1,0:T(8,128)} %reshape.635.tab_ref, s32[1,8192]{1,0:T(1,128)} %multiply_add_fusion.3.ids_ref, f32[4,8192]{1,0:T(4,128)} %pad_maximum_fusion.2.basis_ref, f32[1,8192]{1,0:T(1,128)} %shard_map.105.zsrc_ref, f32[1,8192]{1,0:T(1,128)} %bitcast.98, ...), custom_call_target="tpu_custom_call" | custom-call | tf_op jit(solution)/shard_map/pallas_call | solution.py:177
  53.0 5.7 %all-to-all-start.2 = ((f32[32,1,384]{2,1,0:T(1,128)}), f32[32,1,384]{2,1,0:T(1,128)S(1)}, u32[]{:S(2)}, u32[]{:S(2)}) async-start(f32[32,1,384]{2,1,0:T(1,128)} %bitcast.136), calls=%async_computation.2 | async-start | bytes 98304 | tf_op jit(solution)/shard_map/all_to_all | solution.py:302
  58.7 7.7 %shard_map.107 = f32[640,256]{1,0:T(8,128)} custom-call(f32[5,8192]{1,0:T(8,128)} %bitcast.80, f32[1,8192]{1,0:T(1,128)} %bitcast.99, f32[1,8192]{1,0:T(1,128)} %get-tuple-element.41.refs_1_, s32[1,8192]{1,0:T(1,128)} %ids_ref.3), custom_call_target="tpu_custom_call" | custom-call | tf_op jit(solution)/shard_map/pallas_call | solution.py:133
  66.3 0.6 slice_reduce_fusion.2
  68.3 0.1 select_bitcast_fusion
  68.3 0.7 fusion.15
  70.4 2.6 %multiply_reduce_fusion = (f32[]{:T(128)}, f32[640,256]{1,0:T(8,128)}) fusion(f32[640,256]{1,0:T(8,128)S(1)} %copy-done.1, f32[640,256]{1,0:T(8,128)} %shard_map.107, f32[]{:T(128)S(6)} %div.65), kind=kLoop, calls=%fused_computation.4 | loop fusion | flops 655359 | bytes 1966088 | tf_op jit(solution)/shard_map/reduce_sum | solution.py:329
  73.1 0.7 multiply_subtract_fusion.2.val_ref
  73.8 3.9 %shard_map.108 = f32[1,45056]{1,0:T(1,128)} custom-call(f32[1,8192]{1,0:T(1,128)} %multiply_subtract_fusion.2.val_ref, s32[1,8192]{1,0:T(1,128)} %bitcast.108, f32[16,8192]{1,0:T(8,128)} %reshape.630.basis_ref, f32[1,1]{1,0:T(1,128)} %bitcast.27.norm_ref), custom_call_target="tpu_custom_call" | custom-call | tf_op jit(solution)/shard_map/pallas_call | solution.py:222
  77.7 6.1 %all-to-all-start.3 = ((f32[32,1,1408]{2,1,0:T(1,128)}), f32[32,1,1408]{2,1,0:T(1,128)S(1)}, u32[]{:S(2)}, u32[]{:S(2)}) async-start(f32[32,1,1408]{2,1,0:T(1,128)} %bitcast.88), calls=%async_computation.3 | async-start | bytes 360448 | tf_op jit(solution)/shard_map/all_to_all | solution.py:290
  83.8 7.9 %shard_map.109 = f32[1,8192]{1,0:T(1,128)} custom-call(f32[640,256]{1,0:T(8,128)} %get-tuple-element.46.tab_ref, s32[1,8192]{1,0:T(1,128)} %ids_ref.3, f32[5,8192]{1,0:T(8,128)} %bitcast.81), custom_call_target="tpu_custom_call" | custom-call | tf_op jit(solution)/shard_map/pallas_call | solution.py:89
  91.6 1.0 all-to-all-done.3
  92.7 0.0 copy-start.2
  92.7 0.1 reduce_sum.119
  92.8 0.6 slice_reduce_fusion.1
  93.4 0.3 scatter-add.9
  93.7 0.7 multiply_reduce_fusion.3
  95.8 0.1 pad_slice_fusion.2
  95.9 0.7 multiply_add_fusion.1
  96.6 0.1 pad_maximum_fusion.3
  96.7 0.7 reshape.641.tab_ref
  97.5 3.9 %shard_map.110 = (f32[1,8192]{1,0:T(1,128)}, f32[1,12288]{1,0:T(1,128)}) custom-call(f32[128,256]{1,0:T(8,128)} %reshape.641.tab_ref, s32[1,8192]{1,0:T(1,128)} %multiply_add_fusion.3.ids_ref, f32[4,8192]{1,0:T(4,128)} %pad_maximum_fusion.2.basis_ref, f32[1,8192]{1,0:T(1,128)} %get-tuple-element.72.zsrc_ref, f32[1,8192]{1,0:T(1,128)} %bitcast.100, ...), custom_call_target="tpu_custom_call" | custom-call | tf_op jit(solution)/shard_map/pallas_call | solution.py:177
  101.4 4.6 %all-to-all-start.4 = ((f32[32,1,384]{2,1,0:T(1,128)}), f32[32,1,384]{2,1,0:T(1,128)S(1)}, u32[]{:S(2)}, u32[]{:S(2)}) async-start(f32[32,1,384]{2,1,0:T(1,128)} %bitcast.135), calls=%async_computation.4 | async-start | bytes 98304 | tf_op jit(solution)/shard_map/all_to_all | solution.py:302
  106.1 7.4 %all-to-all-done.4 = f32[32,1,384]{2,1,0:T(1,128)S(1)} async-done(((f32[32,1,384]{2,1,0:T(1,128)}), f32[32,1,384]{2,1,0:T(1,128)S(1)}, u32[]{:S(2)}, u32[]{:S(2)}) %all-to-all-start.4) | async-done | bytes 49184 | tf_op jit(solution)/shard_map/all_to_all | solution.py:302
  113.5 0.1 fusion.10
  113.7 0.1 multiply_add_fusion
  113.8 0.0 copy-start.3
  113.8 0.6 fusion.13
  114.4 1.2 %add.161 = f32[5,32768]{1,0:T(8,128)} reshape(f32[640,256]{1,0:T(8,128)S(1)} %multiply_add_fusion) | data formatting | bytes 1310720 | tf_op jit(solution)/shard_map/add | solution.py:321
  115.6 0.9 multiply_subtract_fusion.1
  (40 shorter events, 0.5 us)
Async XLA Ops:
  0.6 0.9 copy-start
  0.6 2.7 %copy-start.8 = (s32[1,32]{1,0:T(1,128)S(1)}, s32[1,32]{1,0:T(1,128)}, u32[]{:S(2)}) copy-start(s32[1,32]{1,0:T(1,128)} %param.18) | copy-start | bytes 388
  0.7 2.8 %copy-start.6 = (f32[8192]{0:T(1024)S(1)}, f32[8192]{0:T(1024)}, u32[]{:S(2)}) copy-start(f32[8192]{0:T(1024)} %param.17) | copy-start | bytes 98308
  0.7 2.8 %copy-start.5 = (f32[5,8192]{1,0:T(8,128)S(1)}, f32[5,8192]{1,0:T(8,128)}, u32[]{:S(2)}) copy-start(f32[5,8192]{1,0:T(8,128)} %param.13) | copy-start | bytes 491524
  4.7 17.9 %all-to-all-start = ((f32[32,1,2304]{2,1,0:T(1,128)}), f32[32,1,2304]{2,1,0:T(1,128)S(1)}, u32[]{:S(2)}, u32[]{:S(2)}) async-start(f32[32,1,2304]{2,1,0:T(1,128)} %all_to_all.52), calls=%async_computation | async-start | bytes 589824 | tf_op jit(solution)/shard_map/all_to_all | solution.py:279
  25.6 20.5 %all-to-all-start.1 = ((f32[32,1,1408]{2,1,0:T(1,128)}), f32[32,1,1408]{2,1,0:T(1,128)S(1)}, u32[]{:S(2)}, u32[]{:S(2)}) async-start(f32[32,1,1408]{2,1,0:T(1,128)} %all_to_all.40), calls=%async_computation.1 | async-start | bytes 360448 | tf_op jit(solution)/shard_map/all_to_all | solution.py:290
  47.7 22.8 %copy-start.1 = (f32[640,256]{1,0:T(8,128)S(1)}, f32[640,256]{1,0:T(8,128)}, u32[]{:S(2)}) copy-start(f32[640,256]{1,0:T(8,128)} %get-tuple-element.38.tab_ref) | copy-start | bytes 1966084
  53.0 15.2 %all-to-all-start.2 = ((f32[32,1,384]{2,1,0:T(1,128)}), f32[32,1,384]{2,1,0:T(1,128)S(1)}, u32[]{:S(2)}, u32[]{:S(2)}) async-start(f32[32,1,384]{2,1,0:T(1,128)} %bitcast.136), calls=%async_computation.2 | async-start | bytes 98304 | tf_op jit(solution)/shard_map/all_to_all | solution.py:302
  77.7 14.9 %all-to-all-start.3 = ((f32[32,1,1408]{2,1,0:T(1,128)}), f32[32,1,1408]{2,1,0:T(1,128)S(1)}, u32[]{:S(2)}, u32[]{:S(2)}) async-start(f32[32,1,1408]{2,1,0:T(1,128)} %bitcast.88), calls=%async_computation.3 | async-start | bytes 360448 | tf_op jit(solution)/shard_map/all_to_all | solution.py:290
  83.7 12.2 %copy-start.4 = (f32[1,8192]{1,0:T(1,128)S(1)}, f32[1,8192]{1,0:T(1,128)}, u32[]{:S(2)}) copy-start(f32[1,8192]{1,0:T(1,128)} %shard_map.105.zsrc_ref) | copy-start | bytes 98308
  91.6 4.3 %copy-start.7 = (f32[1,8192]{1,0:T(1,128)S(1)}, f32[1,8192]{1,0:T(1,128)}, u32[]{:S(2)}) copy-start(f32[1,8192]{1,0:T(1,128)} %shard_map.109) | copy-start | bytes 98308
  92.7 21.0 %copy-start.2 = (f32[640,256]{1,0:T(8,128)S(1)}, f32[640,256]{1,0:T(8,128)}, u32[]{:S(2)}) copy-start(f32[640,256]{1,0:T(8,128)} %get-tuple-element.46.tab_ref) | copy-start | bytes 1966084
  101.4 12.0 %all-to-all-start.4 = ((f32[32,1,384]{2,1,0:T(1,128)}), f32[32,1,384]{2,1,0:T(1,128)S(1)}, u32[]{:S(2)}, u32[]{:S(2)}) async-start(f32[32,1,384]{2,1,0:T(1,128)} %bitcast.135), calls=%async_computation.4 | async-start | bytes 98304 | tf_op jit(solution)/shard_map/all_to_all | solution.py:302
  113.8 1.8 %copy-start.3 = (f32[12,8192]{1,0:T(8,128)S(1)}, f32[12,8192]{1,0:T(8,128)}, u32[]{:S(2)}) copy-start(f32[12,8192]{1,0:T(8,128)} %param.12) | copy-start | bytes 1179652

commit v18 on v16

--- a/solution.py
+++ b/solution.py
@@ -137,7 +137,7 @@
     return grad, norm.reshape(())
 
 
-def knot_gather(extended, first_ids, basis, zsrc, weight, extra, knots, parts, width):
+def knot_gather(extended, first_ids, basis, zsrc, weight, extra, knots, parts, width, carry=None):
     total = first_ids.shape[1]
     cols = knots // HI
     shifted = jnp.stack([extended[q:q + knots] for q in range(4)], axis=0)
@@ -145,7 +145,10 @@
     per_chunk = CHUNK // width
     line = 128 + -(-width // 128) * 128
 
-    def kernel(tab_ref, ids_ref, basis_ref, zsrc_ref, weight_ref, extra_ref, out_ref, pay_ref, big_ref, norm_ref):
+    extras = [] if carry is None else [carry[0].reshape(1, 1), carry[1]]
+
+    def kernel(tab_ref, ids_ref, basis_ref, zsrc_ref, weight_ref, extra_ref, *refs):
+        out_ref, pay_ref, big_ref, norm_ref = refs[-4:]
         split_into(tab_ref, big_ref)
         norm_ref[...] = jnp.zeros(norm_ref.shape, jnp.float32)
 
@@ -161,6 +164,8 @@
                 value = jnp.sum(jnp.where(sel, acc[q * cols:(q + 1) * cols], 0.0), axis=0, keepdims=True)
                 z = z + b[q:q + 1] * value
             shift = zsrc_ref[:, pl.ds(off, CHUNK)] + z
+            if carry is not None:
+                shift = shift + refs[0][...] * refs[1][:, pl.ds(off, CHUNK)]
             out_ref[:, pl.ds(off, CHUNK)] = shift
             for r in range(per_chunk):
                 start = (i * per_chunk + r) * line + 128
@@ -181,7 +186,7 @@
             jax.ShapeDtypeStruct((1, parts * line), jnp.float32),
         ),
         scratch_shapes=[pltpu.VMEM((2 * rows, HI), jnp.bfloat16), pltpu.VMEM((1, 1), jnp.float32)],
-    )(shifted.reshape(rows, HI), first_ids, basis, zsrc, weight, extra.reshape(1, 1))
+    )(shifted.reshape(rows, HI), first_ids, basis, zsrc, weight, extra.reshape(1, 1), *extras)
 
 
 def knot_scatter(values, first_ids, basis16, s_norm, knots, parts):
@@ -294,10 +299,10 @@
         norm = jnp.sum(every[:, 0]) + jnp.sum(grad_a * grad_a)
         return grad_a, norm
 
-    def forward(zsrc, dir_a, extra):
+    def forward(zsrc, dir_a, extra, carry=None):
         extended = jnp.concatenate([dir_a, jnp.zeros((3,), jnp.float32)])
         shift_own, payload = knot_gather(
-            extended, base_own, basis_own, zsrc, weight_sq_own, extra, n_knots, n_ranks, capacity
+            extended, base_own, basis_own, zsrc, weight_sq_own, extra, n_knots, n_ranks, capacity, carry
         )
         back = lax.all_to_all(payload.reshape(n_ranks, -1), everyone, 0, 0, tiled=True)
         totals = jnp.sum(back[:, :2], axis=0)
@@ -312,9 +317,9 @@
     grad_a, gamma_a = combine(sent)
     grad_s, extra = source_scatter(held, [zbar0_own], ids, owned, with_norm=True)
     dir_s, dir_a = (grad_s, grad_a)
-    pulled = source_gather(dir_s, ids, held)
+    zsrc, att, carry = source_gather(dir_s, ids, held), dir_a, None
     for step in range(ITERS):
-        shift_own, shift_slot, image_sq, extra_sum = forward(pulled, dir_a, extra)
+        shift_own, shift_slot, image_sq, extra_sum = forward(zsrc, att, extra, carry)
         if step == 0:
             gamma = extra_sum + gamma_a
         alpha = gamma / image_sq
@@ -328,11 +333,11 @@
             grad_a, fresh = combine(
                 knot_scatter(zbar_slot, first_ids, basis16, jnp.sum(grad_s * grad_s), knots, n_ranks)
             )
-            raw = source_gather(grad_s, ids, held)
+            zsrc, att = source_gather(grad_s, ids, held), grad_a
             beta = fresh / gamma
+            carry = (beta, shift_own)
             dir_s = grad_s + beta * dir_s
             dir_a = grad_a + beta * dir_a
-            pulled = raw + beta * pulled
             gamma = fresh
             extra = jnp.zeros((), jnp.float32)
     mine_a = lax.dynamic_slice(sol_a, (lax.axis_index("tm") * knots,), (knots,))

time: 117 us -> 117 us (level)
  transfers between devices with their start and end apart: 5 -> 5, of which waited for: 3 -> 3; matrix products, arithmetic and copies ran while one was open for 6% -> 6% of each run, Pallas kernels for 29% -> 30%
where the time goes in v18:
time: 117 us; the launch traced here: 116 us
  Pallas kernels  46.8 us (40%)
  starting transfers between devices  26.9 us (23%)
  other arithmetic  14.9 us (13%)
  waiting for transfers between devices  11.1 us (9%)
  local copies, waits for them, and re-layouts  8.97 us (8%)
  between operations  5.11 us (4%)
  matrix products  2 us (2%)
    pallas_call x2, Pallas kernels, source_gather(): pl.pallas_call(kernel, out_shape=jax.ShapeDtypeStruct((1, total), jnp.flo...  15.7 us
    all_to_all x2, starting transfers between devices, forward(): lax.all_to_all(payload.reshape(n_ranks, -1), everyone, 0, 0, tiled=True)  10.3 us
    all_to_all x2, starting transfers between devices, combine(): every = lax.all_to_all(sent, everyone, 0, 0, tiled=True)  9.35 us
    pallas_call x2, Pallas kernels, knot_gather(): pl.pallas_call(kernel, out_shape=(jax.ShapeDtypeStruct((1, total), jnp.fl...  8.55 us
    pallas_call x1, Pallas kernels, source_scatter(): return pl.pallas_call(kernel, out_shape=shape)(values, *scales, ids)  7.66 us
    pallas_call x1, Pallas kernels, source_scatter(): pl.pallas_call(kernel, out_shape=(shape, jax.ShapeDtypeStruct((1, 1), jnp...  7.66 us
    all_to_all x2, waiting for transfers between devices, forward(): lax.all_to_all(payload.reshape(n_ranks, -1), everyone, 0, 0, tiled=True)  7.37 us
    all_to_all x1, starting transfers between devices, per_device(): got = lax.all_to_all(blocks, everyone, 0, 0, tiled=True)  7.3 us
  transfers between devices with their start and end apart: 5, of which 3 were waited for; matrix products, arithmetic and copies ran while one was open for 6% of the time, Pallas kernels for 30%

profile of v18, /device:TPU:0, one launch (start us, length us, event | category | flops | bytes accessed | tf_op | source)
XLA Modules:
  0.0 115.9 jit_solution(17169889498564177088)
XLA Ops:
  0.6 0.0 copy-start
  0.7 0.8 convert_element_type.32
  1.5 2.0 %multiply_reduce_fusion.1 = (f32[8192]{0:T(1024)S(1)}, f32[8192]{0:T(1024)S(1)}, f32[12,8192]{1,0:T(8,128)S(1)}) fusion(f32[12,8192]{1,0:T(8,128)} %param.12, f32[12,62]{1,0:T(8,128)S(1)} %copy-done, s32[8192]{0:T(1024)} %param.15), kind=kOutput, calls=%fused_computation.7 | convolution fusion | flops 74022912 | bytes 887712 | tf_op jit(solution)/shard_map/dot_general | solution.py:260
  3.5 0.1 compare_select_fusion.3
  3.6 0.2 concatenate.26
  3.9 1.0 all_to_all.52
  4.9 7.3 %all-to-all-start = ((f32[32,1,2304]{2,1,0:T(1,128)}), f32[32,1,2304]{2,1,0:T(1,128)S(1)}, u32[]{:S(2)}, u32[]{:S(2)}) async-start(f32[32,1,2304]{2,1,0:T(1,128)} %all_to_all.52), calls=%async_computation | async-start | bytes 589824 | tf_op jit(solution)/shard_map/all_to_all | solution.py:284
  12.2 0.1 fusion.11
  12.4 0.7 broadcast_select_fusion.val_ref
  13.0 0.1 pad_maximum_fusion
  13.2 0.1 broadcast_in_dim.2
  13.3 1.0 reshape.611.basis_ref
  14.2 3.3 %shard_map.103 = f32[1,45056]{1,0:T(1,128)} custom-call(f32[1,8192]{1,0:T(1,128)} %broadcast_select_fusion.val_ref, s32[1,8192]{1,0:T(1,128)} %bitcast.104, f32[16,8192]{1,0:T(8,128)} %reshape.611.basis_ref, f32[1,1]{1,0:T(1,128)} %constant.111.clone.1.norm_ref.extra_ref), custom_call_target="tpu_custom_call" | custom-call | tf_op jit(solution)/shard_map/pallas_call | solution.py:227
  17.5 0.5 broadcast.429
  18.0 2.0 %reduce.12 = f32[45056]{0:T(1024)S(1)} reduce(f32[1,45056]{1,0:T(1,128)} %shard_map.103, f32[]{:T(128)} %broadcast.429), dimensions={0}, to_apply=%pallas_call.36.reduce_sub_computation.3 | reduce | bytes 360452 | tf_op jit(solution)/shard_map/pallas_call | solution.py:227
  20.1 2.7 %all-to-all-done = f32[32,1,2304]{2,1,0:T(1,128)S(1)} async-done(((f32[32,1,2304]{2,1,0:T(1,128)}), f32[32,1,2304]{2,1,0:T(1,128)S(1)}, u32[]{:S(2)}, u32[]{:S(2)}) %all-to-all-start) | async-done | bytes 294944 | tf_op jit(solution)/shard_map/all_to_all | solution.py:284
  22.8 0.7 reduce.9
  23.5 0.1 reshape.613
  23.6 0.7 fusion.15
  24.3 0.7 slice.173
  25.0 0.8 all_to_all.40
  25.8 3.3 %all-to-all-start.1 = ((f32[32,1,1408]{2,1,0:T(1,128)}), f32[32,1,1408]{2,1,0:T(1,128)S(1)}, u32[]{:S(2)}, u32[]{:S(2)}) async-start(f32[32,1,1408]{2,1,0:T(1,128)} %all_to_all.40), calls=%async_computation.1 | async-start | bytes 360448 | tf_op jit(solution)/shard_map/all_to_all | solution.py:295
  29.1 0.2 fusion.9
  29.3 0.7 multiply_add_fusion.1.ids_ref
  30.0 0.8 pad_maximum_fusion.2.basis_ref
  30.7 7.7 %shard_map.104 = (f32[640,256]{1,0:T(8,128)}, f32[1,1]{1,0:T(1,128)}) custom-call(f32[5,8192]{1,0:T(8,128)} %bitcast.78, f32[1,8192]{1,0:T(1,128)} %bitcast.120, s32[1,8192]{1,0:T(1,128)} %ids_ref.3), custom_call_target="tpu_custom_call" | custom-call | tf_op jit(solution)/shard_map/pallas_call | solution.py:134
  38.4 7.9 %shard_map.105.zsrc_ref = f32[1,8192]{1,0:T(1,128)} custom-call(f32[640,256]{1,0:T(8,128)} %get-tuple-element.38.tab_ref, s32[1,8192]{1,0:T(1,128)} %ids_ref.3, f32[5,8192]{1,0:T(8,128)} %bitcast.79), custom_call_target="tpu_custom_call" | custom-call | tf_op jit(solution)/shard_map/pallas_call | solution.py:89
  46.4 0.1 reduce_sum.112
  46.5 0.4 scatter-add.6
  46.9 0.6 multiply_reduce_fusion.4
  47.6 0.1 pad_slice_fusion.5
  47.7 0.1 pad_maximum_fusion.1
  47.8 0.0 copy-start.1
  47.9 0.7 reshape.616.tab_ref
  48.6 4.6 %shard_map.106 = (f32[1,8192]{1,0:T(1,128)}, f32[1,12288]{1,0:T(1,128)}) custom-call(f32[128,256]{1,0:T(8,128)} %reshape.616.tab_ref, s32[1,8192]{1,0:T(1,128)} %multiply_add_fusion.1.ids_ref, f32[4,8192]{1,0:T(4,128)} %pad_maximum_fusion.2.basis_ref, f32[1,8192]{1,0:T(1,128)} %shard_map.105.zsrc_ref, f32[1,8192]{1,0:T(1,128)} %bitcast.97, ...), custom_call_target="tpu_custom_call" | custom-call | tf_op jit(solution)/shard_map/pallas_call | solution.py:182
  53.2 5.7 %all-to-all-start.2 = ((f32[32,1,384]{2,1,0:T(1,128)}), f32[32,1,384]{2,1,0:T(1,128)S(1)}, u32[]{:S(2)}, u32[]{:S(2)}) async-start(f32[32,1,384]{2,1,0:T(1,128)} %bitcast.136), calls=%async_computation.2 | async-start | bytes 98304 | tf_op jit(solution)/shard_map/all_to_all | solution.py:307
  58.8 7.7 %shard_map.107 = f32[640,256]{1,0:T(8,128)} custom-call(f32[5,8192]{1,0:T(8,128)} %bitcast.80, f32[1,8192]{1,0:T(1,128)} %bitcast.98, f32[1,8192]{1,0:T(1,128)} %get-tuple-element.41.refs_1_, s32[1,8192]{1,0:T(1,128)} %ids_ref.3), custom_call_target="tpu_custom_call" | custom-call | tf_op jit(solution)/shard_map/pallas_call | solution.py:133
  66.5 0.6 slice_reduce_fusion.2
  68.4 0.0 all-to-all-done.2
  68.4 0.1 select_bitcast_fusion
  68.5 0.7 fusion.16
  70.6 2.6 %multiply_reduce_fusion = (f32[]{:T(128)}, f32[640,256]{1,0:T(8,128)}) fusion(f32[640,256]{1,0:T(8,128)S(1)} %copy-done.1, f32[640,256]{1,0:T(8,128)} %shard_map.107, f32[]{:T(128)S(6)} %div.65), kind=kLoop, calls=%fused_computation.4 | loop fusion | flops 655359 | bytes 1966088 | tf_op jit(solution)/shard_map/reduce_sum | solution.py:334
  73.2 0.7 multiply_subtract_fusion.2.val_ref
  73.9 3.9 %shard_map.108 = f32[1,45056]{1,0:T(1,128)} custom-call(f32[1,8192]{1,0:T(1,128)} %multiply_subtract_fusion.2.val_ref, s32[1,8192]{1,0:T(1,128)} %bitcast.105, f32[16,8192]{1,0:T(8,128)} %reshape.611.basis_ref, f32[1,1]{1,0:T(1,128)} %bitcast.27.norm_ref), custom_call_target="tpu_custom_call" | custom-call | tf_op jit(solution)/shard_map/pallas_call | solution.py:227
  77.8 6.1 %all-to-all-start.3 = ((f32[32,1,1408]{2,1,0:T(1,128)}), f32[32,1,1408]{2,1,0:T(1,128)S(1)}, u32[]{:S(2)}, u32[]{:S(2)}) async-start(f32[32,1,1408]{2,1,0:T(1,128)} %bitcast.85), calls=%async_computation.3 | async-start | bytes 360448 | tf_op jit(solution)/shard_map/all_to_all | solution.py:295
  83.9 7.9 %shard_map.109.zsrc_ref = f32[1,8192]{1,0:T(1,128)} custom-call(f32[640,256]{1,0:T(8,128)} %get-tuple-element.46.tab_ref, s32[1,8192]{1,0:T(1,128)} %ids_ref.3, f32[5,8192]{1,0:T(8,128)} %bitcast.81), custom_call_target="tpu_custom_call" | custom-call | tf_op jit(solution)/shard_map/pallas_call | solution.py:89
  91.8 1.0 all-to-all-done.3
  92.9 0.0 copy-start.2
  92.9 0.1 reduce_sum.119
  93.0 0.6 slice_reduce_fusion.1
  93.6 0.3 scatter-add.9
  93.9 0.6 multiply_reduce_fusion.3
  94.5 0.1 pad_slice_fusion.2
  94.6 0.1 pad_maximum_fusion.3
  94.8 0.7 reshape.621.tab_ref
  96.9 4.0 %shard_map.110 = (f32[1,8192]{1,0:T(1,128)}, f32[1,12288]{1,0:T(1,128)}) custom-call(f32[128,256]{1,0:T(8,128)} %reshape.621.tab_ref, s32[1,8192]{1,0:T(1,128)} %multiply_add_fusion.1.ids_ref, f32[4,8192]{1,0:T(4,128)} %pad_maximum_fusion.2.basis_ref, f32[1,8192]{1,0:T(1,128)} %shard_map.109.zsrc_ref, f32[1,8192]{1,0:T(1,128)} %bitcast.99, ...), custom_call_target="tpu_custom_call" | custom-call | tf_op jit(solution)/shard_map/pallas_call | solution.py:182
  100.8 4.6 %all-to-all-start.4 = ((f32[32,1,384]{2,1,0:T(1,128)}), f32[32,1,384]{2,1,0:T(1,128)S(1)}, u32[]{:S(2)}, u32[]{:S(2)}) async-start(f32[32,1,384]{2,1,0:T(1,128)} %bitcast.135), calls=%async_computation.4 | async-start | bytes 98304 | tf_op jit(solution)/shard_map/all_to_all | solution.py:307
  105.5 7.4 %all-to-all-done.4 = f32[32,1,384]{2,1,0:T(1,128)S(1)} async-done(((f32[32,1,384]{2,1,0:T(1,128)}), f32[32,1,384]{2,1,0:T(1,128)S(1)}, u32[]{:S(2)}, u32[]{:S(2)}) %all-to-all-start.4) | async-done | bytes 49184 | tf_op jit(solution)/shard_map/all_to_all | solution.py:307
  112.8 0.1 fusion.10
  113.0 0.1 multiply_add_fusion
  113.2 0.0 copy-start.3
  113.2 0.6 fusion.14
  113.8 1.2 %add.146 = f32[5,32768]{1,0:T(8,128)} reshape(f32[640,256]{1,0:T(8,128)S(1)} %multiply_add_fusion) | data formatting | bytes 1310720 | tf_op jit(solution)/shard_map/add | solution.py:326
  115.0 0.9 multiply_subtract_fusion.1
  (35 shorter events, 0.5 us)
Async XLA Ops:
  0.6 0.9 copy-start
  0.6 2.8 %copy-start.6 = (s32[1,32]{1,0:T(1,128)S(1)}, s32[1,32]{1,0:T(1,128)}, u32[]{:S(2)}) copy-start(s32[1,32]{1,0:T(1,128)} %param.18) | copy-start | bytes 388
  0.7 3.0 %copy-start.5 = (f32[8192]{0:T(1024)S(1)}, f32[8192]{0:T(1024)}, u32[]{:S(2)}) copy-start(f32[8192]{0:T(1024)} %param.17) | copy-start | bytes 98308
  0.7 3.0 %copy-start.4 = (f32[5,8192]{1,0:T(8,128)S(1)}, f32[5,8192]{1,0:T(8,128)}, u32[]{:S(2)}) copy-start(f32[5,8192]{1,0:T(8,128)} %param.13) | copy-start | bytes 491524
  4.9 17.9 %all-to-all-start = ((f32[32,1,2304]{2,1,0:T(1,128)}), f32[32,1,2304]{2,1,0:T(1,128)S(1)}, u32[]{:S(2)}, u32[]{:S(2)}) async-start(f32[32,1,2304]{2,1,0:T(1,128)} %all_to_all.52), calls=%async_computation | async-start | bytes 589824 | tf_op jit(solution)/shard_map/all_to_all | solution.py:284
  25.8 20.5 %all-to-all-start.1 = ((f32[32,1,1408]{2,1,0:T(1,128)}), f32[32,1,1408]{2,1,0:T(1,128)S(1)}, u32[]{:S(2)}, u32[]{:S(2)}) async-start(f32[32,1,1408]{2,1,0:T(1,128)} %all_to_all.40), calls=%async_computation.1 | async-start | bytes 360448 | tf_op jit(solution)/shard_map/all_to_all | solution.py:295
  47.8 22.7 %copy-start.1 = (f32[640,256]{1,0:T(8,128)S(1)}, f32[640,256]{1,0:T(8,128)}, u32[]{:S(2)}) copy-start(f32[640,256]{1,0:T(8,128)} %get-tuple-element.38.tab_ref) | copy-start | bytes 1966084
  53.2 15.2 %all-to-all-start.2 = ((f32[32,1,384]{2,1,0:T(1,128)}), f32[32,1,384]{2,1,0:T(1,128)S(1)}, u32[]{:S(2)}, u32[]{:S(2)}) async-start(f32[32,1,384]{2,1,0:T(1,128)} %bitcast.136), calls=%async_computation.2 | async-start | bytes 98304 | tf_op jit(solution)/shard_map/all_to_all | solution.py:307
  77.8 14.9 %all-to-all-start.3 = ((f32[32,1,1408]{2,1,0:T(1,128)}), f32[32,1,1408]{2,1,0:T(1,128)S(1)}, u32[]{:S(2)}, u32[]{:S(2)}) async-start(f32[32,1,1408]{2,1,0:T(1,128)} %bitcast.85), calls=%async_computation.3 | async-start | bytes 360448 | tf_op jit(solution)/shard_map/all_to_all | solution.py:295
  92.9 20.2 %copy-start.2 = (f32[640,256]{1,0:T(8,128)S(1)}, f32[640,256]{1,0:T(8,128)}, u32[]{:S(2)}) copy-start(f32[640,256]{1,0:T(8,128)} %get-tuple-element.46.tab_ref) | copy-start | bytes 1966084
  100.8 12.0 %all-to-all-start.4 = ((f32[32,1,384]{2,1,0:T(1,128)}), f32[32,1,384]{2,1,0:T(1,128)S(1)}, u32[]{:S(2)}, u32[]{:S(2)}) async-start(f32[32,1,384]{2,1,0:T(1,128)} %bitcast.135), calls=%async_computation.4 | async-start | bytes 98304 | tf_op jit(solution)/shard_map/all_to_all | solution.py:307
  113.2 1.8 %copy-start.3 = (f32[12,8192]{1,0:T(8,128)S(1)}, f32[12,8192]{1,0:T(8,128)}, u32[]{:S(2)}) copy-start(f32[12,8192]{1,0:T(8,128)} %param.12) | copy-start | bytes 1179652

commit v19 on v18

--- a/solution.py
+++ b/solution.py
@@ -137,8 +137,8 @@
     return grad, norm.reshape(())
 
 
-def knot_gather(extended, first_ids, basis, zsrc, weight, extra, knots, parts, width, carry=None):
-    total = first_ids.shape[1]
+def knot_gather(extended, frac, first, block_knots, share, zsrc, weight, extra, knots, parts, width, carry=None):
+    total = frac.shape[1]
     cols = knots // HI
     shifted = jnp.stack([extended[q:q + knots] for q in range(4)], axis=0)
     rows = 4 * cols
@@ -147,22 +147,23 @@
 
     extras = [] if carry is None else [carry[0].reshape(1, 1), carry[1]]
 
-    def kernel(tab_ref, ids_ref, basis_ref, zsrc_ref, weight_ref, extra_ref, *refs):
+    def kernel(tab_ref, frac_ref, first_ref, zsrc_ref, weight_ref, extra_ref, *refs):
         out_ref, pay_ref, big_ref, norm_ref = refs[-4:]
         split_into(tab_ref, big_ref)
         norm_ref[...] = jnp.zeros(norm_ref.shape, jnp.float32)
 
         for i in range(total // CHUNK):
             off = i * CHUNK
-            idc = ids_ref[:, pl.ds(off, CHUNK)]
+            slot = lax.broadcasted_iota(jnp.int32, (1, CHUNK), 1) + off
+            idc = (slot // width // share) * block_knots + first_ref[:, pl.ds(off, CHUNK)].astype(jnp.int32)
             picked = jnp.dot(big_ref[...], hot_rows(idc, CHUNK), preferred_element_type=jnp.float32)
             acc = picked[:rows] + picked[rows:]
             sel = group_mask(idc, cols, CHUNK, cols)
-            b = basis_ref[:, pl.ds(off, CHUNK)]
+            b = spline_basis(frac_ref[:, pl.ds(off, CHUNK)])
             z = jnp.zeros((1, CHUNK), jnp.float32)
             for q in range(4):
                 value = jnp.sum(jnp.where(sel, acc[q * cols:(q + 1) * cols], 0.0), axis=0, keepdims=True)
-                z = z + b[q:q + 1] * value
+                z = z + b[q] * value
             shift = zsrc_ref[:, pl.ds(off, CHUNK)] + z
             if carry is not None:
                 shift = shift + refs[0][...] * refs[1][:, pl.ds(off, CHUNK)]
@@ -186,7 +187,7 @@
             jax.ShapeDtypeStruct((1, parts * line), jnp.float32),
         ),
         scratch_shapes=[pltpu.VMEM((2 * rows, HI), jnp.bfloat16), pltpu.VMEM((1, 1), jnp.float32)],
-    )(shifted.reshape(rows, HI), first_ids, basis, zsrc, weight, extra.reshape(1, 1), *extras)
+    )(shifted.reshape(rows, HI), frac, first, zsrc, weight, extra.reshape(1, 1), *extras)
 
 
 def knot_scatter(values, first_ids, basis16, s_norm, knots, parts):
@@ -286,9 +287,8 @@
     held = got[:n_params]
     zbar0_own = got[n_params:n_params + 1]
     weight_sq_own = got[n_params + 1:n_params + 2]
-    basis_own = jnp.concatenate(spline_basis(got[n_params + 2:n_params + 3]), axis=0)
-    slot_device = jnp.arange(rows, dtype=jnp.int32)[None, :] // capacity
-    base_own = (slot_device // n_share) * knots + got[n_params + 3:n_params + 4].astype(jnp.int32)
+    frac_own = got[n_params + 2:n_params + 3]
+    first_own = got[n_params + 3:n_params + 4]
     table_rows = n_params * (owned // HI)
 
     def combine(sent):
@@ -302,7 +302,8 @@
     def forward(zsrc, dir_a, extra, carry=None):
         extended = jnp.concatenate([dir_a, jnp.zeros((3,), jnp.float32)])
         shift_own, payload = knot_gather(
-            extended, base_own, basis_own, zsrc, weight_sq_own, extra, n_knots, n_ranks, capacity, carry
+            extended, frac_own, first_own, knots, n_share, zsrc, weight_sq_own, extra, n_knots, n_ranks,
+            capacity, carry,
         )
         back = lax.all_to_all(payload.reshape(n_ranks, -1), everyone, 0, 0, tiled=True)
         totals = jnp.sum(back[:, :2], axis=0)

time: 117 us -> 115 us (0.983)
  other arithmetic: 14.9 us -> 12.7 us
  transfers between devices with their start and end apart: 5 -> 5, of which waited for: 3 -> 3; matrix products, arithmetic and copies ran while one was open for 6% -> 5% of each run, Pallas kernels for 30% -> 30%
where the time goes in v19:
time: 115 us; the launch traced here: 114 us
  Pallas kernels  46.6 us (41%)
  starting transfers between devices  26.9 us (23%)
  other arithmetic  12.7 us (11%)
  waiting for transfers between devices  11.1 us (10%)
  local copies, waits for them, and re-layouts  9.65 us (8%)
  between operations  5.01 us (4%)
  matrix products  2 us (2%)
    pallas_call x2, Pallas kernels, source_gather(): pl.pallas_call(kernel, out_shape=jax.ShapeDtypeStruct((1, total), jnp.flo...  15.7 us
    all_to_all x2, starting transfers between devices, forward(): lax.all_to_all(payload.reshape(n_ranks, -1), everyone, 0, 0, tiled=True)  10.2 us
    all_to_all x2, starting transfers between devices, combine(): every = lax.all_to_all(sent, everyone, 0, 0, tiled=True)  9.35 us
    pallas_call x2, Pallas kernels, knot_gather(): pl.pallas_call(kernel, out_shape=(jax.ShapeDtypeStruct((1, total), jnp.fl...  8.33 us
    pallas_call x1, Pallas kernels, source_scatter(): pl.pallas_call(kernel, out_shape=(shape, jax.ShapeDtypeStruct((1, 1), jnp...  7.66 us
    pallas_call x1, Pallas kernels, source_scatter(): return pl.pallas_call(kernel, out_shape=shape)(values, *scales, ids)  7.66 us
    all_to_all x2, waiting for transfers between devices, forward(): lax.all_to_all(payload.reshape(n_ranks, -1), everyone, 0, 0, tiled=True)  7.37 us
    all_to_all x1, starting transfers between devices, per_device(): got = lax.all_to_all(blocks, everyone, 0, 0, tiled=True)  7.3 us
  transfers between devices with their start and end apart: 5, of which 3 were waited for; matrix products, arithmetic and copies ran while one was open for 5% of the time, Pallas kernels for 30%

profile of v19, /device:TPU:0, one launch (start us, length us, event | category | flops | bytes accessed | tf_op | source)
XLA Modules:
  0.0 113.9 jit_solution(9760335277887589714)
XLA Ops:
  0.6 0.0 copy-start
  0.7 0.8 convert_element_type.18
  1.5 2.0 %multiply_reduce_fusion.1 = (f32[8192]{0:T(1024)S(1)}, f32[8192]{0:T(1024)S(1)}, f32[12,8192]{1,0:T(8,128)S(1)}) fusion(f32[12,8192]{1,0:T(8,128)} %param.12, f32[12,62]{1,0:T(8,128)S(1)} %copy-done, s32[8192]{0:T(1024)} %param.15), kind=kOutput, calls=%fused_computation.7 | convolution fusion | flops 74022912 | bytes 887712 | tf_op jit(solution)/shard_map/dot_general | solution.py:261
  3.5 0.0 copy-done.6
  3.5 0.1 compare_select_fusion
  3.6 0.2 concatenate.23
  3.9 1.0 all_to_all.52
  4.9 7.3 %all-to-all-start = ((f32[32,1,2304]{2,1,0:T(1,128)}), f32[32,1,2304]{2,1,0:T(1,128)S(1)}, u32[]{:S(2)}, u32[]{:S(2)}) async-start(f32[32,1,2304]{2,1,0:T(1,128)} %all_to_all.52), calls=%async_computation | async-start | bytes 589824 | tf_op jit(solution)/shard_map/all_to_all | solution.py:285
  12.2 0.1 fusion.10
  12.4 0.7 broadcast_select_fusion.val_ref
  13.0 0.1 pad_maximum_fusion
  13.2 0.1 broadcast_in_dim.2
  13.3 1.0 reshape.345.basis_ref
  14.2 3.3 %shard_map.103 = f32[1,45056]{1,0:T(1,128)} custom-call(f32[1,8192]{1,0:T(1,128)} %broadcast_select_fusion.val_ref, s32[1,8192]{1,0:T(1,128)} %bitcast.108, f32[16,8192]{1,0:T(8,128)} %reshape.345.basis_ref, f32[1,1]{1,0:T(1,128)} %constant.79.clone.1.norm_ref.extra_ref), custom_call_target="tpu_custom_call" | custom-call | tf_op jit(solution)/shard_map/pallas_call | solution.py:228
  17.5 0.5 broadcast.191
  18.0 2.0 %reduce.12 = f32[45056]{0:T(1024)S(1)} reduce(f32[1,45056]{1,0:T(1,128)} %shard_map.103, f32[]{:T(128)} %broadcast.191), dimensions={0}, to_apply=%pallas_call.36.reduce_sub_computation.3 | reduce | bytes 360452 | tf_op jit(solution)/shard_map/pallas_call | solution.py:228
  20.1 2.7 %all-to-all-done = f32[32,1,2304]{2,1,0:T(1,128)S(1)} async-done(((f32[32,1,2304]{2,1,0:T(1,128)}), f32[32,1,2304]{2,1,0:T(1,128)S(1)}, u32[]{:S(2)}, u32[]{:S(2)}) %all-to-all-start) | async-done | bytes 294944 | tf_op jit(solution)/shard_map/all_to_all | solution.py:285
  22.8 0.7 reduce.9
  23.5 0.1 reshape.347
  23.6 0.7 fusion.14
  24.3 0.7 slice.176
  25.0 0.8 all_to_all.40
  25.8 3.3 %all-to-all-start.1 = ((f32[32,1,1408]{2,1,0:T(1,128)}), f32[32,1,1408]{2,1,0:T(1,128)S(1)}, u32[]{:S(2)}, u32[]{:S(2)}) async-start(f32[32,1,1408]{2,1,0:T(1,128)} %all_to_all.40), calls=%async_computation.1 | async-start | bytes 360448 | tf_op jit(solution)/shard_map/all_to_all | solution.py:295
  29.1 7.7 %shard_map.104 = (f32[640,256]{1,0:T(8,128)}, f32[1,1]{1,0:T(1,128)}) custom-call(f32[5,8192]{1,0:T(8,128)} %bitcast.78, f32[1,8192]{1,0:T(1,128)} %bitcast.124, s32[1,8192]{1,0:T(1,128)} %ids_ref.3), custom_call_target="tpu_custom_call" | custom-call | tf_op jit(solution)/shard_map/pallas_call | solution.py:134
  36.8 7.9 %shard_map.105.zsrc_ref = f32[1,8192]{1,0:T(1,128)} custom-call(f32[640,256]{1,0:T(8,128)} %get-tuple-element.38.tab_ref, s32[1,8192]{1,0:T(1,128)} %ids_ref.3, f32[5,8192]{1,0:T(8,128)} %bitcast.79), custom_call_target="tpu_custom_call" | custom-call | tf_op jit(solution)/shard_map/pallas_call | solution.py:89
  44.7 0.0 all-to-all-done.1
  44.7 0.1 reduce_sum.112
  44.9 0.4 scatter-add.6
  45.3 0.7 multiply_reduce_fusion.4
  46.0 0.1 pad_slice_fusion.5
  46.1 0.1 pad_maximum_fusion.1
  46.3 0.0 copy-start.1
  46.3 0.7 reshape.350.tab_ref
  47.0 4.5 %shard_map.106 = (f32[1,8192]{1,0:T(1,128)}, f32[1,12288]{1,0:T(1,128)}) custom-call(f32[128,256]{1,0:T(8,128)} %reshape.350.tab_ref, f32[1,8192]{1,0:T(1,128)} %bitcast.106, f32[1,8192]{1,0:T(1,128)} %bitcast.104, f32[1,8192]{1,0:T(1,128)} %shard_map.105.zsrc_ref, f32[1,8192]{1,0:T(1,128)} %bitcast.97, f32[1,1]{1,0:T(1,128)} %get-tuple-element.39.extra_ref), custom_call_target="tpu_custom_call" | custom-call | tf_op jit(solution)/shard_map/pallas_call | solution.py:183
  51.5 5.7 %all-to-all-start.2 = ((f32[32,1,384]{2,1,0:T(1,128)}), f32[32,1,384]{2,1,0:T(1,128)S(1)}, u32[]{:S(2)}, u32[]{:S(2)}) async-start(f32[32,1,384]{2,1,0:T(1,128)} %bitcast.138), calls=%async_computation.2 | async-start | bytes 98304 | tf_op jit(solution)/shard_map/all_to_all | solution.py:308
  57.1 7.7 %shard_map.107 = f32[640,256]{1,0:T(8,128)} custom-call(f32[5,8192]{1,0:T(8,128)} %bitcast.80, f32[1,8192]{1,0:T(1,128)} %bitcast.98, f32[1,8192]{1,0:T(1,128)} %get-tuple-element.41.refs_1_, s32[1,8192]{1,0:T(1,128)} %ids_ref.3), custom_call_target="tpu_custom_call" | custom-call | tf_op jit(solution)/shard_map/pallas_call | solution.py:133
  64.8 0.6 slice_reduce_fusion.2
  66.7 0.0 all-to-all-done.2
  66.7 0.1 select_bitcast_fusion
  66.8 0.6 fusion.15
  68.7 0.0 copy-done.1
  68.8 2.6 %multiply_reduce_fusion = (f32[]{:T(128)}, f32[640,256]{1,0:T(8,128)}) fusion(f32[640,256]{1,0:T(8,128)S(1)} %copy-done.1, f32[640,256]{1,0:T(8,128)} %shard_map.107, f32[]{:T(128)S(6)} %div.25), kind=kLoop, calls=%fused_computation.4 | loop fusion | flops 655359 | bytes 1966088 | tf_op jit(solution)/shard_map/reduce_sum | solution.py:335
  71.4 0.7 multiply_subtract_fusion.2.val_ref
  72.1 3.9 %shard_map.108 = f32[1,45056]{1,0:T(1,128)} custom-call(f32[1,8192]{1,0:T(1,128)} %multiply_subtract_fusion.2.val_ref, s32[1,8192]{1,0:T(1,128)} %bitcast.109, f32[16,8192]{1,0:T(8,128)} %reshape.345.basis_ref, f32[1,1]{1,0:T(1,128)} %bitcast.27.norm_ref), custom_call_target="tpu_custom_call" | custom-call | tf_op jit(solution)/shard_map/pallas_call | solution.py:228
  76.0 6.1 %all-to-all-start.3 = ((f32[32,1,1408]{2,1,0:T(1,128)}), f32[32,1,1408]{2,1,0:T(1,128)S(1)}, u32[]{:S(2)}, u32[]{:S(2)}) async-start(f32[32,1,1408]{2,1,0:T(1,128)} %bitcast.85), calls=%async_computation.3 | async-start | bytes 360448 | tf_op jit(solution)/shard_map/all_to_all | solution.py:295
  82.1 7.9 %shard_map.109.zsrc_ref = f32[1,8192]{1,0:T(1,128)} custom-call(f32[640,256]{1,0:T(8,128)} %get-tuple-element.46.tab_ref, s32[1,8192]{1,0:T(1,128)} %ids_ref.3, f32[5,8192]{1,0:T(8,128)} %bitcast.81), custom_call_target="tpu_custom_call" | custom-call | tf_op jit(solution)/shard_map/pallas_call | solution.py:89
  89.9 1.0 all-to-all-done.3
  91.0 0.0 copy-start.2
  91.0 0.1 reduce_sum.119
  91.2 0.6 slice_reduce_fusion.1
  91.8 0.3 scatter-add.9
  92.0 0.7 multiply_reduce_fusion.3
  92.7 0.1 pad_slice_fusion.2
  92.8 0.1 pad_maximum_fusion.2
  93.0 0.7 reshape.355.tab_ref
  95.0 3.9 %shard_map.110 = (f32[1,8192]{1,0:T(1,128)}, f32[1,12288]{1,0:T(1,128)}) custom-call(f32[128,256]{1,0:T(8,128)} %reshape.355.tab_ref, f32[1,8192]{1,0:T(1,128)} %bitcast.107, f32[1,8192]{1,0:T(1,128)} %bitcast.105, f32[1,8192]{1,0:T(1,128)} %shard_map.109.zsrc_ref, f32[1,8192]{1,0:T(1,128)} %bitcast.99, f32[1,1]{1,0:T(1,128)} %constant.79.clone.1.norm_ref.extra_ref, ...), custom_call_target="tpu_custom_call" | custom-call | tf_op jit(solution)/shard_map/pallas_call | solution.py:183
  98.9 4.6 %all-to-all-start.4 = ((f32[32,1,384]{2,1,0:T(1,128)}), f32[32,1,384]{2,1,0:T(1,128)S(1)}, u32[]{:S(2)}, u32[]{:S(2)}) async-start(f32[32,1,384]{2,1,0:T(1,128)} %bitcast.137), calls=%async_computation.4 | async-start | bytes 98304 | tf_op jit(solution)/shard_map/all_to_all | solution.py:308
  103.5 7.4 %all-to-all-done.4 = f32[32,1,384]{2,1,0:T(1,128)S(1)} async-done(((f32[32,1,384]{2,1,0:T(1,128)}), f32[32,1,384]{2,1,0:T(1,128)S(1)}, u32[]{:S(2)}, u32[]{:S(2)}) %all-to-all-start.4) | async-done | bytes 49184 | tf_op jit(solution)/shard_map/all_to_all | solution.py:308
  110.9 0.1 fusion.9
  111.1 0.1 multiply_add_fusion
  111.2 0.0 copy-start.3
  111.2 0.6 fusion.13
  111.9 1.2 %add.72 = f32[5,32768]{1,0:T(8,128)} reshape(f32[640,256]{1,0:T(8,128)S(1)} %multiply_add_fusion) | data formatting | bytes 1310720 | tf_op jit(solution)/shard_map/add | solution.py:327
  113.0 0.9 multiply_subtract_fusion.1
  (32 shorter events, 0.5 us)
Async XLA Ops:
  0.6 0.9 copy-start
  0.6 2.8 %copy-start.6 = (s32[1,32]{1,0:T(1,128)S(1)}, s32[1,32]{1,0:T(1,128)}, u32[]{:S(2)}) copy-start(s32[1,32]{1,0:T(1,128)} %param.18) | copy-start | bytes 388
  0.7 3.0 %copy-start.5 = (f32[8192]{0:T(1024)S(1)}, f32[8192]{0:T(1024)}, u32[]{:S(2)}) copy-start(f32[8192]{0:T(1024)} %param.17) | copy-start | bytes 98308
  0.7 3.0 %copy-start.4 = (f32[5,8192]{1,0:T(8,128)S(1)}, f32[5,8192]{1,0:T(8,128)}, u32[]{:S(2)}) copy-start(f32[5,8192]{1,0:T(8,128)} %param.13) | copy-start | bytes 491524
  4.9 17.9 %all-to-all-start = ((f32[32,1,2304]{2,1,0:T(1,128)}), f32[32,1,2304]{2,1,0:T(1,128)S(1)}, u32[]{:S(2)}, u32[]{:S(2)}) async-start(f32[32,1,2304]{2,1,0:T(1,128)} %all_to_all.52), calls=%async_computation | async-start | bytes 589824 | tf_op jit(solution)/shard_map/all_to_all | solution.py:285
  25.8 18.9 %all-to-all-start.1 = ((f32[32,1,1408]{2,1,0:T(1,128)}), f32[32,1,1408]{2,1,0:T(1,128)S(1)}, u32[]{:S(2)}, u32[]{:S(2)}) async-start(f32[32,1,1408]{2,1,0:T(1,128)} %all_to_all.40), calls=%async_computation.1 | async-start | bytes 360448 | tf_op jit(solution)/shard_map/all_to_all | solution.py:295
  46.3 22.5 %copy-start.1 = (f32[640,256]{1,0:T(8,128)S(1)}, f32[640,256]{1,0:T(8,128)}, u32[]{:S(2)}) copy-start(f32[640,256]{1,0:T(8,128)} %get-tuple-element.38.tab_ref) | copy-start | bytes 1966084
  51.5 15.2 %all-to-all-start.2 = ((f32[32,1,384]{2,1,0:T(1,128)}), f32[32,1,384]{2,1,0:T(1,128)S(1)}, u32[]{:S(2)}, u32[]{:S(2)}) async-start(f32[32,1,384]{2,1,0:T(1,128)} %bitcast.138), calls=%async_computation.2 | async-start | bytes 98304 | tf_op jit(solution)/shard_map/all_to_all | solution.py:308
  76.0 14.9 %all-to-all-start.3 = ((f32[32,1,1408]{2,1,0:T(1,128)}), f32[32,1,1408]{2,1,0:T(1,128)S(1)}, u32[]{:S(2)}, u32[]{:S(2)}) async-start(f32[32,1,1408]{2,1,0:T(1,128)} %bitcast.85), calls=%async_computation.3 | async-start | bytes 360448 | tf_op jit(solution)/shard_map/all_to_all | solution.py:295
  91.0 20.1 %copy-start.2 = (f32[640,256]{1,0:T(8,128)S(1)}, f32[640,256]{1,0:T(8,128)}, u32[]{:S(2)}) copy-start(f32[640,256]{1,0:T(8,128)} %get-tuple-element.46.tab_ref) | copy-start | bytes 1966084
  98.9 12.0 %all-to-all-start.4 = ((f32[32,1,384]{2,1,0:T(1,128)}), f32[32,1,384]{2,1,0:T(1,128)S(1)}, u32[]{:S(2)}, u32[]{:S(2)}) async-start(f32[32,1,384]{2,1,0:T(1,128)} %bitcast.137), calls=%async_computation.4 | async-start | bytes 98304 | tf_op jit(solution)/shard_map/all_to_all | solution.py:308
  111.2 1.8 %copy-start.3 = (f32[12,8192]{1,0:T(8,128)S(1)}, f32[12,8192]{1,0:T(8,128)}, u32[]{:S(2)}) copy-start(f32[12,8192]{1,0:T(8,128)} %param.12) | copy-start | bytes 1179652

commit v20 on v19

--- a/solution.py
+++ b/solution.py
@@ -190,13 +190,14 @@
     )(shifted.reshape(rows, HI), frac, first, zsrc, weight, extra.reshape(1, 1), *extras)
 
 
-def knot_scatter(values, first_ids, basis16, s_norm, knots, parts):
+def knot_scatter(values, first_ids, basis16, s_norm, knots, parts, norm_of=None):
     total = first_ids.shape[1]
     cols = knots // HI
     rows = 4 * cols
     line = 128 + (cols + 1) * HI
 
-    def kernel(val_ref, ids_ref, basis_ref, norm_ref, pay_ref, acc_ref):
+    def kernel(val_ref, ids_ref, basis_ref, norm_ref, *refs):
+        pay_ref, acc_ref = refs[-2:]
         acc_ref[...] = jnp.zeros(acc_ref.shape, jnp.float32)
 
         def body(off):
@@ -220,16 +221,21 @@
             carried = carried + jnp.where(lane < q, moved, 0.0)
         blank = jnp.zeros((1, HI), jnp.float32)
         grid = jnp.concatenate([same, blank], axis=0) + jnp.concatenate([blank, carried], axis=0)
-        head = jnp.where(lax.broadcasted_iota(jnp.int32, (1, 128), 1) == 0, norm_ref[...], 0.0)
+        norm = norm_ref[...]
+        if norm_of is not None:
+            grad = refs[0][...] - refs[2][...] * refs[1][...]
+            norm = jnp.sum(jnp.sum(grad * grad, axis=0, keepdims=True), axis=1, keepdims=True)
+        head = jnp.where(lax.broadcasted_iota(jnp.int32, (1, 128), 1) == 0, norm, 0.0)
         row = jnp.concatenate([head] + [grid[c:c + 1, :] for c in range(cols + 1)], axis=1)
         for r in range(parts):
             pay_ref[:, r * line:(r + 1) * line] = row
 
+    extras = [] if norm_of is None else [norm_of[0], norm_of[1], norm_of[2].reshape(1, 1)]
     return pl.pallas_call(
         kernel,
         out_shape=jax.ShapeDtypeStruct((1, parts * line), jnp.float32),
         scratch_shapes=[pltpu.VMEM((rows, HI), jnp.float32)],
-    )(values, first_ids, basis16, s_norm.reshape(1, 1)).reshape(parts, line)
+    )(values, first_ids, basis16, s_norm.reshape(1, 1), *extras).reshape(parts, line)
 
 
 def per_device(
@@ -330,9 +336,13 @@
         if step + 1 < ITERS:
             pushed = source_scatter(held, [weight_sq_own, shift_own], ids, owned)
             zbar_slot = zbar_slot - alpha * (weight_sq * shift_slot)
+            grad_before = grad_s
             grad_s = grad_s - alpha * pushed
             grad_a, fresh = combine(
-                knot_scatter(zbar_slot, first_ids, basis16, jnp.sum(grad_s * grad_s), knots, n_ranks)
+                knot_scatter(
+                    zbar_slot, first_ids, basis16, jnp.zeros((), jnp.float32), knots, n_ranks,
+                    (grad_before, pushed, alpha),
+                )
             )
             zsrc, att = source_gather(grad_s, ids, held), grad_a
             beta = fresh / gamma

time: 115 us -> 113 us (0.983)
  other arithmetic: 12.7 us -> 10.9 us
    reduce_sum x1 -> x0, other arithmetic: 2.63 us -> none  [per_device(): jnp.sum(grad_s * grad_s)]
  transfers between devices with their start and end apart: 5 -> 5, of which waited for: 3 -> 3; matrix products, arithmetic and copies ran while one was open for 5% -> 5% of each run, Pallas kernels for 30% -> 31%
where the time goes in v20:
time: 113 us; the launch traced here: 112 us
  Pallas kernels  46.6 us (41%)
  starting transfers between devices  27.8 us (25%)
  other arithmetic  10.9 us (10%)
  waiting for transfers between devices  10.2 us (9%)
  local copies, waits for them, and re-layouts  9.84 us (9%)
  between operations  4.96 us (4%)
  matrix products  2 us (2%)
    pallas_call x2, Pallas kernels, source_gather(): pl.pallas_call(kernel, out_shape=jax.ShapeDtypeStruct((1, total), jnp.flo...  15.7 us
    all_to_all x2, starting transfers between devices, forward(): lax.all_to_all(payload.reshape(n_ranks, -1), everyone, 0, 0, tiled=True)  11.2 us
    all_to_all x2, starting transfers between devices, combine(): every = lax.all_to_all(sent, everyone, 0, 0, tiled=True)  9.35 us
    pallas_call x2, Pallas kernels, knot_gather(): pl.pallas_call(kernel, out_shape=(jax.ShapeDtypeStruct((1, total), jnp.fl...  8.34 us
    pallas_call x1, Pallas kernels, source_scatter(): pl.pallas_call(kernel, out_shape=(shape, jax.ShapeDtypeStruct((1, 1), jnp...  7.66 us
    pallas_call x1, Pallas kernels, source_scatter(): return pl.pallas_call(kernel, out_shape=shape)(values, *scales, ids)  7.66 us
    all_to_all x2, waiting for transfers between devices, forward(): lax.all_to_all(payload.reshape(n_ranks, -1), everyone, 0, 0, tiled=True)  7.37 us
    all_to_all x1, starting transfers between devices, per_device(): got = lax.all_to_all(blocks, everyone, 0, 0, tiled=True)  7.3 us
  transfers between devices with their start and end apart: 5, of which 3 were waited for; matrix products, arithmetic and copies ran while one was open for 5% of the time, Pallas kernels for 31%

profile of v20, /device:TPU:0, one launch (start us, length us, event | category | flops | bytes accessed | tf_op | source)
XLA Modules:
  0.0 112.2 jit_solution(11850257102162450027)
XLA Ops:
  0.6 0.0 copy-start
  0.6 0.0 copy-start.6
  0.7 0.8 convert_element_type.18
  1.5 2.0 %multiply_reduce_fusion = (f32[8192]{0:T(1024)S(1)}, f32[8192]{0:T(1024)S(1)}, f32[12,8192]{1,0:T(8,128)S(1)}) fusion(f32[12,8192]{1,0:T(8,128)} %param.12, f32[12,62]{1,0:T(8,128)S(1)} %copy-done, s32[8192]{0:T(1024)} %param.15), kind=kOutput, calls=%fused_computation.6 | convolution fusion | flops 74022912 | bytes 887712 | tf_op jit(solution)/shard_map/dot_general | solution.py:267
  3.5 0.1 compare_select_fusion
  3.6 0.2 concatenate.23
  3.9 1.0 all_to_all.52
  4.9 7.3 %all-to-all-start = ((f32[32,1,2304]{2,1,0:T(1,128)}), f32[32,1,2304]{2,1,0:T(1,128)S(1)}, u32[]{:S(2)}, u32[]{:S(2)}) async-start(f32[32,1,2304]{2,1,0:T(1,128)} %all_to_all.52), calls=%async_computation | async-start | bytes 589824 | tf_op jit(solution)/shard_map/all_to_all | solution.py:291
  12.2 0.1 fusion.10
  12.4 0.7 broadcast_select_fusion.val_ref
  13.0 0.1 pad_maximum_fusion
  13.2 0.1 broadcast_in_dim.2
  13.3 1.0 reshape.345.basis_ref
  14.2 3.3 %shard_map.103 = f32[1,45056]{1,0:T(1,128)} custom-call(f32[1,8192]{1,0:T(1,128)} %broadcast_select_fusion.val_ref, s32[1,8192]{1,0:T(1,128)} %bitcast.108, f32[16,8192]{1,0:T(8,128)} %reshape.345.basis_ref, f32[1,1]{1,0:T(1,128)} %constant.79.clone.1.norm_ref.extra_ref), custom_call_target="tpu_custom_call" | custom-call | tf_op jit(solution)/shard_map/pallas_call | solution.py:234
  17.5 0.5 broadcast.191
  18.0 2.0 %reduce.12 = f32[45056]{0:T(1024)S(1)} reduce(f32[1,45056]{1,0:T(1,128)} %shard_map.103, f32[]{:T(128)} %broadcast.191), dimensions={0}, to_apply=%pallas_call.36.reduce_sub_computation.3 | reduce | bytes 360452 | tf_op jit(solution)/shard_map/pallas_call | solution.py:234
  20.1 2.7 %all-to-all-done = f32[32,1,2304]{2,1,0:T(1,128)S(1)} async-done(((f32[32,1,2304]{2,1,0:T(1,128)}), f32[32,1,2304]{2,1,0:T(1,128)S(1)}, u32[]{:S(2)}, u32[]{:S(2)}) %all-to-all-start) | async-done | bytes 294944 | tf_op jit(solution)/shard_map/all_to_all | solution.py:291
  22.8 0.7 reduce.9
  23.5 0.1 reshape.347
  23.6 0.7 slice.176
  24.3 0.7 fusion.14
  25.0 0.8 all_to_all.40
  25.8 3.3 %all-to-all-start.1 = ((f32[32,1,1408]{2,1,0:T(1,128)}), f32[32,1,1408]{2,1,0:T(1,128)S(1)}, u32[]{:S(2)}, u32[]{:S(2)}) async-start(f32[32,1,1408]{2,1,0:T(1,128)} %all_to_all.40), calls=%async_computation.1 | async-start | bytes 360448 | tf_op jit(solution)/shard_map/all_to_all | solution.py:301
  29.1 7.7 %shard_map.104 = (f32[640,256]{1,0:T(8,128)}, f32[1,1]{1,0:T(1,128)}) custom-call(f32[5,8192]{1,0:T(8,128)} %bitcast.78, f32[1,8192]{1,0:T(1,128)} %bitcast.124, s32[1,8192]{1,0:T(1,128)} %ids_ref.3), custom_call_target="tpu_custom_call" | custom-call | tf_op jit(solution)/shard_map/pallas_call | solution.py:134
  36.8 7.9 %shard_map.105.zsrc_ref = f32[1,8192]{1,0:T(1,128)} custom-call(f32[640,256]{1,0:T(8,128)} %get-tuple-element.38.tab_ref.refs_0_, s32[1,8192]{1,0:T(1,128)} %ids_ref.3, f32[5,8192]{1,0:T(8,128)} %bitcast.79), custom_call_target="tpu_custom_call" | custom-call | tf_op jit(solution)/shard_map/pallas_call | solution.py:89
  44.7 0.0 all-to-all-done.1
  44.8 0.1 reduce_sum.103
  44.9 0.4 scatter-add.6
  45.3 0.6 multiply_reduce_fusion.3
  45.9 0.1 pad_slice_fusion.5
  46.0 0.1 pad_maximum_fusion.1
  46.2 0.7 reshape.350.tab_ref
  46.9 4.5 %shard_map.106 = (f32[1,8192]{1,0:T(1,128)}, f32[1,12288]{1,0:T(1,128)}) custom-call(f32[128,256]{1,0:T(8,128)} %reshape.350.tab_ref, f32[1,8192]{1,0:T(1,128)} %bitcast.106, f32[1,8192]{1,0:T(1,128)} %bitcast.104, f32[1,8192]{1,0:T(1,128)} %shard_map.105.zsrc_ref, f32[1,8192]{1,0:T(1,128)} %bitcast.97, f32[1,1]{1,0:T(1,128)} %get-tuple-element.39.extra_ref), custom_call_target="tpu_custom_call" | custom-call | tf_op jit(solution)/shard_map/pallas_call | solution.py:183
  51.4 5.7 %all-to-all-start.2 = ((f32[32,1,384]{2,1,0:T(1,128)}), f32[32,1,384]{2,1,0:T(1,128)S(1)}, u32[]{:S(2)}, u32[]{:S(2)}) async-start(f32[32,1,384]{2,1,0:T(1,128)} %bitcast.138), calls=%async_computation.2 | async-start | bytes 98304 | tf_op jit(solution)/shard_map/all_to_all | solution.py:314
  57.0 7.7 %shard_map.107.refs_1_ = f32[640,256]{1,0:T(8,128)} custom-call(f32[5,8192]{1,0:T(8,128)} %bitcast.80, f32[1,8192]{1,0:T(1,128)} %bitcast.98, f32[1,8192]{1,0:T(1,128)} %get-tuple-element.41.refs_1_, s32[1,8192]{1,0:T(1,128)} %ids_ref.3), custom_call_target="tpu_custom_call" | custom-call | tf_op jit(solution)/shard_map/pallas_call | solution.py:133
  64.7 0.6 slice_reduce_fusion.2
  66.5 0.0 all-to-all-done.2
  66.5 0.1 select_bitcast_fusion
  66.7 0.6 fusion.15
  68.6 0.7 multiply_subtract_fusion.2.val_ref
  69.3 3.9 %shard_map.108 = f32[1,45056]{1,0:T(1,128)} custom-call(f32[1,8192]{1,0:T(1,128)} %multiply_subtract_fusion.2.val_ref, s32[1,8192]{1,0:T(1,128)} %bitcast.109, f32[16,8192]{1,0:T(8,128)} %reshape.345.basis_ref, f32[1,1]{1,0:T(1,128)} %constant.79.clone.1.norm_ref.extra_ref, f32[640,256]{1,0:T(8,128)} %get-tuple-element.38.tab_ref.refs_0_, ...), custom_call_target="tpu_custom_call" | custom-call | tf_op jit(solution)/shard_map/pallas_call | solution.py:234
  73.2 6.1 %all-to-all-start.3 = ((f32[32,1,1408]{2,1,0:T(1,128)}), f32[32,1,1408]{2,1,0:T(1,128)S(1)}, u32[]{:S(2)}, u32[]{:S(2)}) async-start(f32[32,1,1408]{2,1,0:T(1,128)} %bitcast.85), calls=%async_computation.3 | async-start | bytes 360448 | tf_op jit(solution)/shard_map/all_to_all | solution.py:301
  79.2 0.0 copy-done.1
  79.3 0.0 copy-done.2
  79.3 0.9 multiply_subtract_fusion.tab_ref
  80.2 7.9 %shard_map.109.zsrc_ref = f32[1,8192]{1,0:T(1,128)} custom-call(f32[640,256]{1,0:T(8,128)} %multiply_subtract_fusion.tab_ref, s32[1,8192]{1,0:T(1,128)} %ids_ref.3, f32[5,8192]{1,0:T(8,128)} %bitcast.81), custom_call_target="tpu_custom_call" | custom-call | tf_op jit(solution)/shard_map/pallas_call | solution.py:89
  88.0 0.1 all-to-all-done.3
  88.1 0.6 slice_reduce_fusion.1
  88.8 0.1 reduce_sum.109
  88.9 0.4 scatter-add.9
  89.4 0.6 multiply_reduce_fusion.2
  91.3 0.1 pad_slice_fusion.2
  91.5 0.1 pad_maximum_fusion.2
  91.6 0.7 reshape.355.tab_ref
  92.3 3.9 %shard_map.110 = (f32[1,8192]{1,0:T(1,128)}, f32[1,12288]{1,0:T(1,128)}) custom-call(f32[128,256]{1,0:T(8,128)} %reshape.355.tab_ref, f32[1,8192]{1,0:T(1,128)} %bitcast.107, f32[1,8192]{1,0:T(1,128)} %bitcast.105, f32[1,8192]{1,0:T(1,128)} %shard_map.109.zsrc_ref, f32[1,8192]{1,0:T(1,128)} %bitcast.99, f32[1,1]{1,0:T(1,128)} %constant.79.clone.1.norm_ref.extra_ref, ...), custom_call_target="tpu_custom_call" | custom-call | tf_op jit(solution)/shard_map/pallas_call | solution.py:183
  96.2 5.5 %all-to-all-start.4 = ((f32[32,1,384]{2,1,0:T(1,128)}), f32[32,1,384]{2,1,0:T(1,128)S(1)}, u32[]{:S(2)}, u32[]{:S(2)}) async-start(f32[32,1,384]{2,1,0:T(1,128)} %bitcast.137), calls=%async_computation.4 | async-start | bytes 98304 | tf_op jit(solution)/shard_map/all_to_all | solution.py:314
  101.8 7.4 %all-to-all-done.4 = f32[32,1,384]{2,1,0:T(1,128)S(1)} async-done(((f32[32,1,384]{2,1,0:T(1,128)}), f32[32,1,384]{2,1,0:T(1,128)S(1)}, u32[]{:S(2)}, u32[]{:S(2)}) %all-to-all-start.4) | async-done | bytes 49184 | tf_op jit(solution)/shard_map/all_to_all | solution.py:314
  109.2 0.1 fusion.9
  109.3 0.2 multiply_add_fusion
  109.5 0.0 copy-start.3
  109.5 1.2 %add.72 = f32[5,32768]{1,0:T(8,128)} reshape(f32[640,256]{1,0:T(8,128)S(1)} %multiply_add_fusion) | data formatting | bytes 1310720 | tf_op jit(solution)/shard_map/add | solution.py:333
  110.7 0.6 fusion.13
  111.3 0.0 copy-done.3
  111.3 0.9 multiply_subtract_fusion.1
  (32 shorter events, 0.5 us)
Async XLA Ops:
  0.6 0.9 copy-start
  0.6 2.8 %copy-start.6 = (s32[1,32]{1,0:T(1,128)S(1)}, s32[1,32]{1,0:T(1,128)}, u32[]{:S(2)}) copy-start(s32[1,32]{1,0:T(1,128)} %param.18) | copy-start | bytes 388
  0.7 3.0 %copy-start.4 = (f32[5,8192]{1,0:T(8,128)S(1)}, f32[5,8192]{1,0:T(8,128)}, u32[]{:S(2)}) copy-start(f32[5,8192]{1,0:T(8,128)} %param.13) | copy-start | bytes 491524
  0.7 3.0 %copy-start.5 = (f32[8192]{0:T(1024)S(1)}, f32[8192]{0:T(1024)}, u32[]{:S(2)}) copy-start(f32[8192]{0:T(1024)} %param.17) | copy-start | bytes 98308
  4.9 17.9 %all-to-all-start = ((f32[32,1,2304]{2,1,0:T(1,128)}), f32[32,1,2304]{2,1,0:T(1,128)S(1)}, u32[]{:S(2)}, u32[]{:S(2)}) async-start(f32[32,1,2304]{2,1,0:T(1,128)} %all_to_all.52), calls=%async_computation | async-start | bytes 589824 | tf_op jit(solution)/shard_map/all_to_all | solution.py:291
  25.8 18.8 %all-to-all-start.1 = ((f32[32,1,1408]{2,1,0:T(1,128)}), f32[32,1,1408]{2,1,0:T(1,128)S(1)}, u32[]{:S(2)}, u32[]{:S(2)}) async-start(f32[32,1,1408]{2,1,0:T(1,128)} %all_to_all.40), calls=%async_computation.1 | async-start | bytes 360448 | tf_op jit(solution)/shard_map/all_to_all | solution.py:301
  51.4 15.1 %all-to-all-start.2 = ((f32[32,1,384]{2,1,0:T(1,128)}), f32[32,1,384]{2,1,0:T(1,128)S(1)}, u32[]{:S(2)}, u32[]{:S(2)}) async-start(f32[32,1,384]{2,1,0:T(1,128)} %bitcast.138), calls=%async_computation.2 | async-start | bytes 98304 | tf_op jit(solution)/shard_map/all_to_all | solution.py:314
  69.3 10.0 %copy-start.1 = (f32[640,256]{1,0:T(8,128)S(1)}, f32[640,256]{1,0:T(8,128)}, u32[]{:S(2)}) copy-start(f32[640,256]{1,0:T(8,128)} %get-tuple-element.38.tab_ref.refs_0_) | copy-start | bytes 1966084
  69.3 10.0 %copy-start.2 = (f32[640,256]{1,0:T(8,128)S(1)}, f32[640,256]{1,0:T(8,128)}, u32[]{:S(2)}) copy-start(f32[640,256]{1,0:T(8,128)} %shard_map.107.refs_1_) | copy-start | bytes 1966084
  73.2 14.9 %all-to-all-start.3 = ((f32[32,1,1408]{2,1,0:T(1,128)}), f32[32,1,1408]{2,1,0:T(1,128)S(1)}, u32[]{:S(2)}, u32[]{:S(2)}) async-start(f32[32,1,1408]{2,1,0:T(1,128)} %bitcast.85), calls=%async_computation.3 | async-start | bytes 360448 | tf_op jit(solution)/shard_map/all_to_all | solution.py:301
  96.2 12.9 %all-to-all-start.4 = ((f32[32,1,384]{2,1,0:T(1,128)}), f32[32,1,384]{2,1,0:T(1,128)S(1)}, u32[]{:S(2)}, u32[]{:S(2)}) async-start(f32[32,1,384]{2,1,0:T(1,128)} %bitcast.137), calls=%async_computation.4 | async-start | bytes 98304 | tf_op jit(solution)/shard_map/all_to_all | solution.py:314
  109.5 1.8 %copy-start.3 = (f32[12,8192]{1,0:T(8,128)S(1)}, f32[12,8192]{1,0:T(8,128)}, u32[]{:S(2)}) copy-start(f32[12,8192]{1,0:T(8,128)} %param.12) | copy-start | bytes 1179652

commit v21 on v20

--- a/solution.py
+++ b/solution.py
@@ -145,12 +145,16 @@
     per_chunk = CHUNK // width
     line = 128 + -(-width // 128) * 128
 
-    extras = [] if carry is None else [carry[0].reshape(1, 1), carry[1]]
+    extras = [] if carry is None else [carry[0].reshape(1, 1), carry[1].reshape(1, 1), carry[2]]
 
     def kernel(tab_ref, frac_ref, first_ref, zsrc_ref, weight_ref, extra_ref, *refs):
         out_ref, pay_ref, big_ref, norm_ref = refs[-4:]
         split_into(tab_ref, big_ref)
         norm_ref[...] = jnp.zeros(norm_ref.shape, jnp.float32)
+        if carry is not None:
+            first_shift = tab_ref[0:cols, :]
+            a_norm = jnp.sum(jnp.sum(first_shift * first_shift, axis=0, keepdims=True), axis=1, keepdims=True)
+            beta = (refs[0][...] + a_norm) / refs[1][...]
 
         for i in range(total // CHUNK):
             off = i * CHUNK
@@ -166,7 +170,7 @@
                 z = z + b[q] * value
             shift = zsrc_ref[:, pl.ds(off, CHUNK)] + z
             if carry is not None:
-                shift = shift + refs[0][...] * refs[1][:, pl.ds(off, CHUNK)]
+                shift = shift + beta * refs[2][:, pl.ds(off, CHUNK)]
             out_ref[:, pl.ds(off, CHUNK)] = shift
             for r in range(per_chunk):
                 start = (i * per_chunk + r) * line + 128
@@ -302,8 +306,8 @@
         block = jnp.sum(every[:, 128:128 + knots + 3].reshape(n_time, n_share, knots + 3), axis=1)
         main = block[:, :knots].at[1:, :3].add(block[:-1, knots:])
         grad_a = main.reshape(n_knots)
-        norm = jnp.sum(every[:, 0]) + jnp.sum(grad_a * grad_a)
-        return grad_a, norm
+        s_sum = jnp.sum(every[:, 0])
+        return grad_a, s_sum + jnp.sum(grad_a * grad_a), s_sum
 
     def forward(zsrc, dir_a, extra, carry=None):
         extended = jnp.concatenate([dir_a, jnp.zeros((3,), jnp.float32)])
@@ -321,7 +325,7 @@
     zbar_slot = zbar0
     sent = knot_scatter(zbar_slot, first_ids, basis16, jnp.zeros((), jnp.float32), knots, n_ranks)
     sent, held, zbar0_own = lax.optimization_barrier((sent, held, zbar0_own))
-    grad_a, gamma_a = combine(sent)
+    grad_a, gamma_a, unused = combine(sent)
     grad_s, extra = source_scatter(held, [zbar0_own], ids, owned, with_norm=True)
     dir_s, dir_a = (grad_s, grad_a)
     zsrc, att, carry = source_gather(dir_s, ids, held), dir_a, None
@@ -338,7 +342,7 @@
             zbar_slot = zbar_slot - alpha * (weight_sq * shift_slot)
             grad_before = grad_s
             grad_s = grad_s - alpha * pushed
-            grad_a, fresh = combine(
+            grad_a, fresh, s_sum = combine(
                 knot_scatter(
                     zbar_slot, first_ids, basis16, jnp.zeros((), jnp.float32), knots, n_ranks,
                     (grad_before, pushed, alpha),
@@ -346,7 +350,7 @@
             )
             zsrc, att = source_gather(grad_s, ids, held), grad_a
             beta = fresh / gamma
-            carry = (beta, shift_own)
+            carry = (s_sum, gamma, shift_own)
             dir_s = grad_s + beta * dir_s
             dir_a = grad_a + beta * dir_a
             gamma = fresh

time: 113 us -> 112 us (level)
  waiting for transfers between devices: 10.2 us -> 8.23 us
    all_to_all x2, waiting for transfers between devices: 7.37 us -> 5.45 us  [forward(): lax.all_to_all(payload.reshape(n_ranks, -1), everyone, 0, 0, tiled=True)]
  transfers between devices with their start and end apart: 5 -> 5, of which waited for: 3 -> 3; matrix products, arithmetic and copies ran while one was open for 5% -> 6% of each run, Pallas kernels for 31% -> 31%
where the time goes in v21:
time: 112 us; the launch traced here: 111 us
  Pallas kernels  47.2 us (42%)
  starting transfers between devices  27.9 us (25%)
  other arithmetic  10.9 us (10%)
  local copies, waits for them, and re-layouts  9.83 us (9%)
  waiting for transfers between devices  8.23 us (7%)
  between operations  4.98 us (4%)
  matrix products  2 us (2%)
    pallas_call x2, Pallas kernels, source_gather(): pl.pallas_call(kernel, out_shape=jax.ShapeDtypeStruct((1, total), jnp.flo...  15.7 us
    all_to_all x2, starting transfers between devices, forward(): lax.all_to_all(payload.reshape(n_ranks, -1), everyone, 0, 0, tiled=True)  11.3 us
    all_to_all x2, starting transfers between devices, combine(): every = lax.all_to_all(sent, everyone, 0, 0, tiled=True)  9.35 us
    pallas_call x2, Pallas kernels, knot_gather(): pl.pallas_call(kernel, out_shape=(jax.ShapeDtypeStruct((1, total), jnp.fl...  8.95 us
    pallas_call x1, Pallas kernels, source_scatter(): pl.pallas_call(kernel, out_shape=(shape, jax.ShapeDtypeStruct((1, 1), jnp...  7.66 us
    pallas_call x1, Pallas kernels, source_scatter(): return pl.pallas_call(kernel, out_shape=shape)(values, *scales, ids)  7.66 us
    all_to_all x1, starting transfers between devices, per_device(): got = lax.all_to_all(blocks, everyone, 0, 0, tiled=True)  7.3 us
    pallas_call x2, Pallas kernels, knot_scatter(): pl.pallas_call(kernel, out_shape=jax.ShapeDtypeStruct((1, parts * line),...  7.17 us
  transfers between devices with their start and end apart: 5, of which 3 were waited for; matrix products, arithmetic and copies ran while one was open for 6% of the time, Pallas kernels for 31%

profile of v21, /device:TPU:0, one launch (start us, length us, event | category | flops | bytes accessed | tf_op | source)
XLA Modules:
  0.0 111.0 jit_solution(3321880712851737861)
XLA Ops:
  0.6 0.0 copy-start
  0.6 0.0 copy-start.6
  0.7 0.0 copy-start.4
  0.7 0.0 copy-start.5
  0.7 0.8 convert_element_type.18
  1.5 2.0 %multiply_reduce_fusion = (f32[8192]{0:T(1024)S(1)}, f32[8192]{0:T(1024)S(1)}, f32[12,8192]{1,0:T(8,128)S(1)}) fusion(f32[12,8192]{1,0:T(8,128)} %param.12, f32[12,62]{1,0:T(8,128)S(1)} %copy-done, s32[8192]{0:T(1024)} %param.15), kind=kOutput, calls=%fused_computation.6 | convolution fusion | flops 74022912 | bytes 887712 | tf_op jit(solution)/shard_map/dot_general | solution.py:271
  3.5 0.1 compare_select_fusion
  3.6 0.2 concatenate.23
  3.9 1.0 all_to_all.52
  4.9 7.3 %all-to-all-start = ((f32[32,1,2304]{2,1,0:T(1,128)}), f32[32,1,2304]{2,1,0:T(1,128)S(1)}, u32[]{:S(2)}, u32[]{:S(2)}) async-start(f32[32,1,2304]{2,1,0:T(1,128)} %all_to_all.52), calls=%async_computation | async-start | bytes 589824 | tf_op jit(solution)/shard_map/all_to_all | solution.py:295
  12.2 0.1 fusion.10
  12.4 0.7 broadcast_select_fusion.val_ref
  13.0 0.1 pad_maximum_fusion
  13.2 0.1 broadcast_in_dim.2
  13.3 1.0 reshape.348.basis_ref
  14.2 3.3 %shard_map.103 = f32[1,45056]{1,0:T(1,128)} custom-call(f32[1,8192]{1,0:T(1,128)} %broadcast_select_fusion.val_ref, s32[1,8192]{1,0:T(1,128)} %bitcast.109, f32[16,8192]{1,0:T(8,128)} %reshape.348.basis_ref, f32[1,1]{1,0:T(1,128)} %constant.79.clone.1.norm_ref.extra_ref), custom_call_target="tpu_custom_call" | custom-call | tf_op jit(solution)/shard_map/pallas_call | solution.py:238
  17.5 0.5 broadcast.191
  18.0 2.0 %reduce.12 = f32[45056]{0:T(1024)S(1)} reduce(f32[1,45056]{1,0:T(1,128)} %shard_map.103, f32[]{:T(128)} %broadcast.191), dimensions={0}, to_apply=%pallas_call.36.reduce_sub_computation.3 | reduce | bytes 360452 | tf_op jit(solution)/shard_map/pallas_call | solution.py:238
  20.1 2.7 %all-to-all-done = f32[32,1,2304]{2,1,0:T(1,128)S(1)} async-done(((f32[32,1,2304]{2,1,0:T(1,128)}), f32[32,1,2304]{2,1,0:T(1,128)S(1)}, u32[]{:S(2)}, u32[]{:S(2)}) %all-to-all-start) | async-done | bytes 294944 | tf_op jit(solution)/shard_map/all_to_all | solution.py:295
  22.8 0.7 reduce.9
  23.5 0.1 reshape.350
  23.6 0.7 slice.176
  24.3 0.7 fusion.14
  25.0 0.8 all_to_all.40
  25.8 3.3 %all-to-all-start.1 = ((f32[32,1,1408]{2,1,0:T(1,128)}), f32[32,1,1408]{2,1,0:T(1,128)S(1)}, u32[]{:S(2)}, u32[]{:S(2)}) async-start(f32[32,1,1408]{2,1,0:T(1,128)} %all_to_all.40), calls=%async_computation.1 | async-start | bytes 360448 | tf_op jit(solution)/shard_map/all_to_all | solution.py:305
  29.1 7.7 %shard_map.104 = (f32[640,256]{1,0:T(8,128)}, f32[1,1]{1,0:T(1,128)}) custom-call(f32[5,8192]{1,0:T(8,128)} %bitcast.79, f32[1,8192]{1,0:T(1,128)} %bitcast.125, s32[1,8192]{1,0:T(1,128)} %ids_ref.3), custom_call_target="tpu_custom_call" | custom-call | tf_op jit(solution)/shard_map/pallas_call | solution.py:134
  36.8 7.9 %shard_map.105.zsrc_ref = f32[1,8192]{1,0:T(1,128)} custom-call(f32[640,256]{1,0:T(8,128)} %get-tuple-element.38.tab_ref.refs_0_, s32[1,8192]{1,0:T(1,128)} %ids_ref.3, f32[5,8192]{1,0:T(8,128)} %bitcast.80), custom_call_target="tpu_custom_call" | custom-call | tf_op jit(solution)/shard_map/pallas_call | solution.py:89
  44.7 0.0 all-to-all-done.1
  44.8 0.1 reduce_sum.103
  44.9 0.4 scatter-add.6
  45.3 0.6 multiply_reduce_fusion.3
  45.9 0.1 pad_slice_fusion.5
  46.0 0.1 pad_maximum_fusion.1
  46.2 0.7 reshape.353.tab_ref
  46.9 4.5 %shard_map.106 = (f32[1,8192]{1,0:T(1,128)}, f32[1,12288]{1,0:T(1,128)}) custom-call(f32[128,256]{1,0:T(8,128)} %reshape.353.tab_ref, f32[1,8192]{1,0:T(1,128)} %bitcast.107, f32[1,8192]{1,0:T(1,128)} %bitcast.105, f32[1,8192]{1,0:T(1,128)} %shard_map.105.zsrc_ref, f32[1,8192]{1,0:T(1,128)} %bitcast.98, f32[1,1]{1,0:T(1,128)} %get-tuple-element.39.extra_ref), custom_call_target="tpu_custom_call" | custom-call | tf_op jit(solution)/shard_map/pallas_call | solution.py:187
  51.4 5.7 %all-to-all-start.2 = ((f32[32,1,384]{2,1,0:T(1,128)}), f32[32,1,384]{2,1,0:T(1,128)S(1)}, u32[]{:S(2)}, u32[]{:S(2)}) async-start(f32[32,1,384]{2,1,0:T(1,128)} %bitcast.139), calls=%async_computation.2 | async-start | bytes 98304 | tf_op jit(solution)/shard_map/all_to_all | solution.py:318
  57.0 7.7 %shard_map.107.refs_1_ = f32[640,256]{1,0:T(8,128)} custom-call(f32[5,8192]{1,0:T(8,128)} %bitcast.81, f32[1,8192]{1,0:T(1,128)} %bitcast.99, f32[1,8192]{1,0:T(1,128)} %get-tuple-element.41.refs_1_.refs_2_, s32[1,8192]{1,0:T(1,128)} %ids_ref.3), custom_call_target="tpu_custom_call" | custom-call | tf_op jit(solution)/shard_map/pallas_call | solution.py:133
  64.7 0.6 slice_reduce_fusion.2
  66.5 0.0 all-to-all-done.2
  66.5 0.1 select_bitcast_fusion
  66.7 0.6 fusion.15
  68.6 0.7 multiply_subtract_fusion.2.val_ref
  69.3 3.9 %shard_map.108 = f32[1,45056]{1,0:T(1,128)} custom-call(f32[1,8192]{1,0:T(1,128)} %multiply_subtract_fusion.2.val_ref, s32[1,8192]{1,0:T(1,128)} %bitcast.110, f32[16,8192]{1,0:T(8,128)} %reshape.348.basis_ref, f32[1,1]{1,0:T(1,128)} %constant.79.clone.1.norm_ref.extra_ref, f32[640,256]{1,0:T(8,128)} %get-tuple-element.38.tab_ref.refs_0_, ...), custom_call_target="tpu_custom_call" | custom-call | tf_op jit(solution)/shard_map/pallas_call | solution.py:238
  73.2 6.1 %all-to-all-start.3 = ((f32[32,1,1408]{2,1,0:T(1,128)}), f32[32,1,1408]{2,1,0:T(1,128)S(1)}, u32[]{:S(2)}, u32[]{:S(2)}) async-start(f32[32,1,1408]{2,1,0:T(1,128)} %bitcast.86), calls=%async_computation.3 | async-start | bytes 360448 | tf_op jit(solution)/shard_map/all_to_all | solution.py:305
  79.3 0.9 multiply_subtract_fusion.tab_ref
  80.2 7.9 %shard_map.109.zsrc_ref = f32[1,8192]{1,0:T(1,128)} custom-call(f32[640,256]{1,0:T(8,128)} %multiply_subtract_fusion.tab_ref, s32[1,8192]{1,0:T(1,128)} %ids_ref.3, f32[5,8192]{1,0:T(8,128)} %bitcast.82), custom_call_target="tpu_custom_call" | custom-call | tf_op jit(solution)/shard_map/pallas_call | solution.py:89
  88.1 0.1 all-to-all-done.3
  88.2 0.6 slice_reduce_fusion.1
  88.8 0.1 reduce_sum.109
  89.0 0.4 scatter-add.9
  89.4 0.1 pad_slice_fusion.2
  89.5 0.1 pad_maximum_fusion.2
  89.7 0.7 reshape.358.tab_ref
  90.4 4.5 %shard_map.110 = (f32[1,8192]{1,0:T(1,128)}, f32[1,12288]{1,0:T(1,128)}) custom-call(f32[128,256]{1,0:T(8,128)} %reshape.358.tab_ref, f32[1,8192]{1,0:T(1,128)} %bitcast.108, f32[1,8192]{1,0:T(1,128)} %bitcast.106, f32[1,8192]{1,0:T(1,128)} %shard_map.109.zsrc_ref, f32[1,8192]{1,0:T(1,128)} %bitcast.100, f32[1,1]{1,0:T(1,128)} %constant.79.clone.1.norm_ref.extra_ref, ...), custom_call_target="tpu_custom_call" | custom-call | tf_op jit(solution)/shard_map/pallas_call | solution.py:187
  94.9 5.6 %all-to-all-start.4 = ((f32[32,1,384]{2,1,0:T(1,128)}), f32[32,1,384]{2,1,0:T(1,128)S(1)}, u32[]{:S(2)}, u32[]{:S(2)}) async-start(f32[32,1,384]{2,1,0:T(1,128)} %bitcast.138), calls=%async_computation.4 | async-start | bytes 98304 | tf_op jit(solution)/shard_map/all_to_all | solution.py:318
  100.5 0.6 multiply_reduce_fusion.2
  102.5 5.4 %all-to-all-done.4 = f32[32,1,384]{2,1,0:T(1,128)S(1)} async-done(((f32[32,1,384]{2,1,0:T(1,128)}), f32[32,1,384]{2,1,0:T(1,128)S(1)}, u32[]{:S(2)}, u32[]{:S(2)}) %all-to-all-start.4) | async-done | bytes 49184 | tf_op jit(solution)/shard_map/all_to_all | solution.py:318
  107.9 0.1 fusion.9
  108.1 0.2 multiply_add_fusion
  108.3 0.0 copy-start.3
  108.3 1.2 %add.72 = f32[5,32768]{1,0:T(8,128)} reshape(f32[640,256]{1,0:T(8,128)S(1)} %multiply_add_fusion) | data formatting | bytes 1310720 | tf_op jit(solution)/shard_map/add | solution.py:337
  109.5 0.6 fusion.13
  110.1 0.0 copy-done.3
  110.1 0.9 multiply_subtract_fusion.1
  (32 shorter events, 0.5 us)
Async XLA Ops:
  0.6 0.9 copy-start
  0.6 2.8 %copy-start.6 = (s32[1,32]{1,0:T(1,128)S(1)}, s32[1,32]{1,0:T(1,128)}, u32[]{:S(2)}) copy-start(s32[1,32]{1,0:T(1,128)} %param.18) | copy-start | bytes 388
  0.7 3.0 %copy-start.4 = (f32[5,8192]{1,0:T(8,128)S(1)}, f32[5,8192]{1,0:T(8,128)}, u32[]{:S(2)}) copy-start(f32[5,8192]{1,0:T(8,128)} %param.13) | copy-start | bytes 491524
  0.7 3.0 %copy-start.5 = (f32[8192]{0:T(1024)S(1)}, f32[8192]{0:T(1024)}, u32[]{:S(2)}) copy-start(f32[8192]{0:T(1024)} %param.17) | copy-start | bytes 98308
  4.9 17.9 %all-to-all-start = ((f32[32,1,2304]{2,1,0:T(1,128)}), f32[32,1,2304]{2,1,0:T(1,128)S(1)}, u32[]{:S(2)}, u32[]{:S(2)}) async-start(f32[32,1,2304]{2,1,0:T(1,128)} %all_to_all.52), calls=%async_computation | async-start | bytes 589824 | tf_op jit(solution)/shard_map/all_to_all | solution.py:295
  25.8 18.8 %all-to-all-start.1 = ((f32[32,1,1408]{2,1,0:T(1,128)}), f32[32,1,1408]{2,1,0:T(1,128)S(1)}, u32[]{:S(2)}, u32[]{:S(2)}) async-start(f32[32,1,1408]{2,1,0:T(1,128)} %all_to_all.40), calls=%async_computation.1 | async-start | bytes 360448 | tf_op jit(solution)/shard_map/all_to_all | solution.py:305
  51.4 15.1 %all-to-all-start.2 = ((f32[32,1,384]{2,1,0:T(1,128)}), f32[32,1,384]{2,1,0:T(1,128)S(1)}, u32[]{:S(2)}, u32[]{:S(2)}) async-start(f32[32,1,384]{2,1,0:T(1,128)} %bitcast.139), calls=%async_computation.2 | async-start | bytes 98304 | tf_op jit(solution)/shard_map/all_to_all | solution.py:318
  69.3 10.0 %copy-start.1 = (f32[640,256]{1,0:T(8,128)S(1)}, f32[640,256]{1,0:T(8,128)}, u32[]{:S(2)}) copy-start(f32[640,256]{1,0:T(8,128)} %get-tuple-element.38.tab_ref.refs_0_) | copy-start | bytes 1966084
  69.3 10.0 %copy-start.2 = (f32[640,256]{1,0:T(8,128)S(1)}, f32[640,256]{1,0:T(8,128)}, u32[]{:S(2)}) copy-start(f32[640,256]{1,0:T(8,128)} %shard_map.107.refs_1_) | copy-start | bytes 1966084
  73.2 14.9 %all-to-all-start.3 = ((f32[32,1,1408]{2,1,0:T(1,128)}), f32[32,1,1408]{2,1,0:T(1,128)S(1)}, u32[]{:S(2)}, u32[]{:S(2)}) async-start(f32[32,1,1408]{2,1,0:T(1,128)} %bitcast.86), calls=%async_computation.3 | async-start | bytes 360448 | tf_op jit(solution)/shard_map/all_to_all | solution.py:305
  94.9 13.0 %all-to-all-start.4 = ((f32[32,1,384]{2,1,0:T(1,128)}), f32[32,1,384]{2,1,0:T(1,128)S(1)}, u32[]{:S(2)}, u32[]{:S(2)}) async-start(f32[32,1,384]{2,1,0:T(1,128)} %bitcast.138), calls=%async_computation.4 | async-start | bytes 98304 | tf_op jit(solution)/shard_map/all_to_all | solution.py:318
  108.3 1.8 %copy-start.3 = (f32[12,8192]{1,0:T(8,128)S(1)}, f32[12,8192]{1,0:T(8,128)}, u32[]{:S(2)}) copy-start(f32[12,8192]{1,0:T(8,128)} %param.12) | copy-start | bytes 1179652
